TPU v7x, 32 devices: a whole 2x2x4 slice. The times are simulated.
32 devices in a mesh: shot: 2 (over y), real: 4 (over x, core), tile: 4 (over z).
Axes of the slice: x: 2, y: 2, z: 4, core: 2. Of those that a mesh axis runs over, the one named last changes fastest.
Arguments:
- courant: float32 [4, 64, 160, 128], P('real', 'tile'), may hold values from 0.01 to 0.05
- prev_field: float32 [8, 64, 160, 128], P(('shot', 'real'), 'tile'), parts along dimension 0, may hold values from -6 to 6
- cur_field: float32 [8, 64, 160, 128], P(('shot', 'real'), 'tile'), parts along dimension 0, may hold values from -6 to 6
- adj_prev: float32 [8, 64, 160, 128], P(('shot', 'real'), 'tile'), parts along dimension 0, may hold values from -6 to 6
- adj_cur: float32 [8, 64, 160, 128], P(('shot', 'real'), 'tile'), parts along dimension 0, may hold values from -6 to 6
- buoyancy: float32 [64, 160, 128], P('tile'), may hold values from 0.4 to 2.5
- wavelet: float32 [4], P('shot'), parts along dimension 0, may hold values from -16 to 16
- src_cell: int32 [2], P('shot'), parts along dimension 0, may hold values from 0 to 1310719
- rec_cell: int32 [512], P('shot'), parts along dimension 0, may hold values from 0 to 1310719
- observed: float32 [4, 256], P('shot'), parts along dimension 0, may hold values from -6 to 6
Outputs:
- image: float32 [128, 160, 128], P(('shot', 'tile')), parts along dimension 0
- adj_state: float32 [8, 64, 160, 128], P(('shot', 'real'), 'tile'), parts along dimension 0
There are 2 independent parts, one for each index of `shot`. A program takes and returns all parts, laid end to end along the dimension named above; an argument that names none is the same for every part. Nothing has to cross between parts.
Inputs may be any that keep to these rules, and one draw needn't show every extreme that they name: `src_cell`: A flattened cell index x * 160 * 128 + y * 128 + z. `rec_cell`: flattened cell indices x * 160 * 128 + y * 128 + z; several receivers may share a cell.
All inputs are finite; a program needn't handle non-finite values.
Results may differ from a plain program's by a relative error of at most 0.00002.
Values sent between devices are 32-bit elements; how exact they have to be, the bound alone decides.
No kernel may reach another device: no remote copies, remote signals or barrier semaphores. Data moves between devices by JAX's collectives and lax.ppermute only.
A program may use at most 128 MiB of HBM per device.

v0:
```python
import jax
import jax.numpy as jnp
from jax import lax
from jax.sharding import PartitionSpec as P

SECOND = (-205.0 / 72.0, 8.0 / 5.0, -1.0 / 5.0, 8.0 / 315.0, -1.0 / 560.0)
FIRST = (4.0 / 5.0, -1.0 / 5.0, 4.0 / 105.0, -1.0 / 280.0)


def extended(block, sides, width):
    for axis, dim in sides:
        count = lax.axis_size(axis)
        forward = [(i, i + 1) for i in range(count - 1)]
        backward = [(target, source) for source, target in forward]
        low = lax.ppermute(
            lax.slice_in_dim(block, block.shape[dim] - width, None, axis=dim), axis, forward
        )
        high = lax.ppermute(lax.slice_in_dim(block, 0, width, axis=dim), axis, backward)
        block = jnp.concatenate([low, block, high], axis=dim)
    return block


def window(padded, axis, shift):
    starts = [4, 4, 4]
    starts[axis] = starts[axis] + shift
    dims = [padded.shape[0] - 8, padded.shape[1] - 8, padded.shape[2] - 8]
    return lax.slice(
        padded, starts, [starts[0] + dims[0], starts[1] + dims[1], starts[2] + dims[2]]
    )


def stencil(padded):
    centre = window(padded, 0, 0)
    lap = 3.0 * SECOND[0] * centre
    grads = []
    for axis in range(3):
        for k in range(1, 5):
            lap = lap + SECOND[k] * (window(padded, axis, k) + window(padded, axis, -k))
        slope = FIRST[0] * (window(padded, axis, 1) - window(padded, axis, -1))
        for k in range(2, 5):
            slope = slope + FIRST[k - 1] * (window(padded, axis, k) - window(padded, axis, -k))
        grads.append(slope)
    return (lap, grads)


def side_pad(slab):
    return jnp.pad(slab, ((0, 0), (4, 4), (4, 4)))


def operate_slab(field, buoyancy, grad_b):
    padded = side_pad(extended(field, (("tile", 0),), 4))
    lap, grads = stencil(padded)
    return buoyancy * lap + (grad_b[0] * grads[0] + grad_b[1] * grads[1] + grad_b[2] * grads[2])


def inject(field, where, valid, values):
    flat = field.reshape(-1).at[where].add(jnp.where(valid, values, 0.0))
    return flat.reshape(field.shape)


def shards(
    courant,
    prev_field,
    cur_field,
    adj_prev,
    adj_cur,
    buoyancy,
    wavelet,
    src_cell,
    rec_cell,
    observed,
):
    speed = courant[0]
    planes, height, depth = buoyancy.shape
    volume = planes * height * depth
    offset = lax.axis_index("tile") * volume
    steps = wavelet.shape[0]

    def locate(cells):
        local = cells - offset
        valid = (local >= 0) & (local < volume)
        return (jnp.clip(local, 0, volume - 1), valid)

    src_local, src_valid = locate(src_cell)
    rec_local, rec_valid = locate(rec_cell)
    b_padded = side_pad(extended(buoyancy, (("tile", 0),), 4))
    _, grad_b = stencil(b_padded)
    older, now = (prev_field[0], cur_field[0])
    forces = []
    samples = []
    for k in range(steps):
        force = operate_slab(now, buoyancy, grad_b)
        newer = 2.0 * now - older + speed * force
        newer = inject(newer, src_local, src_valid, jnp.full((1,), wavelet[k], jnp.float32))
        samples.append(jnp.where(rec_valid, newer.reshape(-1)[rec_local], 0.0))
        forces.append(force)
        older, now = (now, newer)
    traces = lax.psum(jnp.stack(samples), "tile")
    residual = traces - observed
    older, now = (adj_prev[0], adj_cur[0])
    image_part = jnp.zeros(buoyancy.shape, jnp.float32)
    for j in range(steps):
        force = operate_slab(now, buoyancy, grad_b)
        newer = 2.0 * now - older + speed * force
        newer = inject(newer, rec_local, rec_valid, residual[steps - 1 - j])
        image_part = image_part + newer * forces[steps - 1 - j]
        older, now = (now, newer)
    members = lax.axis_size("real")
    image = lax.psum(image_part, "real") / members
    return (image, now[None])


def solution(mesh):
    in_specs = (
        P("real", "tile", None, None),
        P(("shot", "real"), "tile", None, None),
        P(("shot", "real"), "tile", None, None),
        P(("shot", "real"), "tile", None, None),
        P(("shot", "real"), "tile", None, None),
        P("tile", None, None),
        P("shot"),
        P("shot"),
        P("shot"),
        P("shot", None),
    )
    out_specs = (P(("shot", "tile"), None, None), P(("shot", "real"), "tile", None, None))
    return jax.shard_map(shards, mesh=mesh, in_specs=in_specs, out_specs=out_specs, check_vma=False)
```

profile of v0, /device:TPU:9, one launch (start us, length us, event | category | flops | bytes accessed | tf_op | source)
XLA Modules:
  0.0 236.2 jit_solution(11216864384527946837)
XLA Ops:
  9.4 3.2 %collective-permute-start.3 = (f32[4,160,128]{2,1,0:T(8,128)}, f32[4,160,128]{2,1,0:T(8,128)S(1)}, u32[]{:S(2)}, u32[]{:S(2)}) collective-permute-start(f32[4,160,128]{2,1,0:T(8,128)} %get-tuple-element.42), channel_id=1, source_target_pairs={{0,1},{1,2},{2,3},{4,5},{5,6},{6,7},{8,9},{9,10},{10,11},{12,13},{... | collective-permute-start | bytes 983048 | tf_op jit(solution)/shard_map/ppermute | solution.py:15
  17.6 3.4 %collective-permute-start.5 = (f32[4,160,128]{2,1,0:T(8,128)}, f32[4,160,128]{2,1,0:T(8,128)}, u32[]{:S(2)}, u32[]{:S(2)}) collective-permute-start(f32[4,160,128]{2,1,0:T(8,128)} %get-tuple-element.45), channel_id=1, source_target_pairs={{0,1},{1,2},{2,3},{4,5},{5,6},{6,7},{8,9},{9,10},{10,11},{12,13},{... | collective-permute-start | bytes 983048 | tf_op jit(solution)/shard_map/ppermute | solution.py:15
  21.9 2.6 %collective-permute-start = (f32[4,160,128]{2,1,0:T(8,128)}, f32[4,160,128]{2,1,0:T(8,128)S(1)}, u32[]{:S(2)}, u32[]{:S(2)}) collective-permute-start(f32[4,160,128]{2,1,0:T(8,128)} %get-tuple-element.40), channel_id=1, source_target_pairs={{1,0},{2,1},{3,2},{5,4},{6,5},{7,6},{9,8},{10,9},{11,10},{13,12},{... | collective-permute-start | bytes 983048 | tf_op jit(solution)/shard_map/ppermute | solution.py:18
  26.5 3.3 %collective-permute-start.1 = (f32[4,160,128]{2,1,0:T(8,128)}, f32[4,160,128]{2,1,0:T(8,128)S(1)}, u32[]{:S(2)}, u32[]{:S(2)}) collective-permute-start(f32[4,160,128]{2,1,0:T(8,128)} %get-tuple-element.39), channel_id=1, source_target_pairs={{0,1},{1,2},{2,3},{4,5},{5,6},{6,7},{8,9},{9,10},{10,11},{12,13},{... | collective-permute-start | bytes 983048 | tf_op jit(solution)/shard_map/ppermute | solution.py:15
  29.8 5.0 %select_maximum_fusion.6 = f32[24,168,136]{2,1,0:T(8,128)} fusion(f32[4,160,128]{2,1,0:T(8,128)} %collective-permute-done.2, f32[16,160,128]{2,1,0:T(8,128)S(1)} %copy-done, f32[4,160,128]{2,1,0:T(8,128)} %copy-done.18), kind=kLoop, calls=%fused_computation.14 | loop fusion | flops 8225280 | bytes 4159488 | tf_op jit(solution)/shard_map/concatenate | solution.py:19
  39.2 5.1 %select_maximum_fusion.4 = f32[24,168,136]{2,1,0:T(8,128)} fusion(f32[4,160,128]{2,1,0:T(8,128)} %collective-permute-done.4, f32[16,160,128]{2,1,0:T(8,128)S(1)} %bitcast.56, f32[4,160,128]{2,1,0:T(8,128)} %collective-permute-done.5), kind=kLoop, calls=%fused_computation.12 | loop fusion | flops 8225280 | bytes 4159488 | tf_op jit(solution)/shard_map/concatenate | solution.py:19
  44.2 42.8 %fusion.48 = (f32[16,160,128]{2,1,0:T(8,128)}, f32[16,160,128]{2,1,0:T(8,128)}, f32[16,160,128]{2,1,0:T(8,128)}, f32[16,160,128]{2,1,0:T(8,128)}, f32[16,160,128]{2,1,0:T(8,128)}) fusion(f32[1,16,160,128]{3,2,1,0:T(8,128)} %param.15, f32[1,16,160,128]{3,2,1,0:T(8,128)} %param.14, f32[1,16,160,128]{3,2,1,0:T(8,128)S(1)} %copy-done.1, ...), kind=kLoop, calls=%fused_computation.135 | loop fusion | flops 39976960 | bytes 66191360 | tf_op jit(solution)/shard_map/add | solution.py:93
  87.0 2.8 %fusion.52 = f32[327680]{0:T(1024)} fusion(f32[327680]{0:T(1024)} %bitcast.58, s32[]{:T(128)} %bitcast.12, s32[1]{0:T(128)} %maximum_minimum_fusion, f32[2]{0:T(128)S(1)} %copy-done.22, s32[1]{0:T(128)S(6)} %copy.19, s32[1]{0:T(128)} %bitcast.11), kind=kLoop, calls=%fused_computation.163 | loop fusion | flops 8 | bytes 2568 | tf_op jit(solution)/shard_map/scatter-add | solution.py:57
  93.8 3.4 %collective-permute-start.7 = (f32[4,160,128]{2,1,0:T(8,128)}, f32[4,160,128]{2,1,0:T(8,128)}, u32[]{:S(2)}, u32[]{:S(2)}) collective-permute-start(f32[4,160,128]{2,1,0:T(8,128)} %bitcast.16), channel_id=1, source_target_pairs={{0,1},{1,2},{2,3},{4,5},{5,6},{6,7},{8,9},{9,10},{10,11},{12,13},{... | collective-permute-start | bytes 983048 | tf_op jit(solution)/shard_map/ppermute | solution.py:15
  97.3 2.9 %select_maximum_fusion.8 = f32[24,168,136]{2,1,0:T(8,128)S(1)} fusion(f32[4,160,128]{2,1,0:T(8,128)S(1)} %collective-permute-done, f32[16,160,128]{2,1,0:T(8,128)S(1)} %bitcast.61, f32[4,160,128]{2,1,0:T(8,128)S(1)} %collective-permute-done.1), kind=kLoop, calls=%fused_computation.16 | loop fusion | flops 8225280 | bytes 4159488 | tf_op jit(solution)/shard_map/concatenate | solution.py:19
  100.3 9.3 %fusion.49 = f32[16,160,128]{2,1,0:T(8,128)S(1)} fusion(f32[1,16,160,128]{3,2,1,0:T(8,128)S(1)} %copy-done.4, f32[1,16,160,128]{3,2,1,0:T(8,128)} %param.17, f32[16,160,128]{2,1,0:T(8,128)S(1)} %copy-done.12, f32[16,160,128]{2,1,0:T(8,128)S(1)} %copy-done.10, f32[16,160,128]{2,1,0:T(8,128)S(1)} %copy-done.7, f32[16,160,128]{2,1,0:T(8,128)S(1)} %copy-done, ...), kind=kLoop, calls=%fused_computation.140 | loop fusion | flops 29163520 | bytes 32112640 | tf_op jit(solution)/shard_map/add | solution.py:104
  109.5 5.9 %gather_fusion = f32[256]{0:T(256)S(1)} fusion(f32[327680]{0:T(1024)} %fusion.52, s32[1024]{0:T(1024)S(1)} %pad_clamp_fusion), kind=kCustom, calls=%fused_computation | custom fusion | bytes 3072 | tf_op jit(solution)/shard_map/gather | solution.py:95
  115.6 4.1 %select_maximum_fusion.2 = f32[24,168,136]{2,1,0:T(8,128)S(1)} fusion(f32[4,160,128]{2,1,0:T(8,128)} %collective-permute-done.6, f32[16,160,128]{2,1,0:T(8,128)} %bitcast.59, f32[4,160,128]{2,1,0:T(8,128)} %collective-permute-done.7), kind=kLoop, calls=%fused_computation.10 | loop fusion | flops 8225280 | bytes 4159488 | tf_op jit(solution)/shard_map/concatenate | solution.py:19
  119.7 8.1 %fusion.50 = (f32[16,160,128]{2,1,0:T(8,128)}, f32[16,160,128]{2,1,0:T(8,128)}) fusion(f32[1,16,160,128]{3,2,1,0:T(8,128)S(1)} %copy-done.5, f32[16,160,128]{2,1,0:T(8,128)S(1)} %bitcast.60, f32[1,16,160,128]{3,2,1,0:T(8,128)S(1)} %copy-done.2, f32[16,160,128]{2,1,0:T(8,128)} %get-tuple-element.34, f32[16,160,128]{2,1,0:T(8,128)} %get-tuple-element.33, ...), kind=kLoop, calls=%fused_computation.141 | loop fusion | flops 29163520 | bytes 33423360 | tf_op jit(solution)/shard_map/add | solution.py:93
  127.8 2.7 %fusion.53 = f32[327680]{0:T(1024)} fusion(f32[327680]{0:T(1024)} %bitcast.17, s32[]{:T(128)} %bitcast.12, s32[1]{0:T(128)} %maximum_minimum_fusion, f32[2]{0:T(128)S(1)} %copy-done.22, s32[1]{0:T(128)S(6)} %copy.19, s32[1]{0:T(128)} %bitcast.11), kind=kLoop, calls=%fused_computation.164 | loop fusion | flops 8 | bytes 2568 | tf_op jit(solution)/shard_map/scatter-add | solution.py:57
  130.4 5.9 %gather_fusion.1 = f32[256]{0:T(256)S(1)} fusion(f32[327680]{0:T(1024)} %fusion.53, s32[1024]{0:T(1024)S(1)} %pad_clamp_fusion), kind=kCustom, calls=%fused_computation.1 | custom fusion | bytes 3072 | tf_op jit(solution)/shard_map/gather | solution.py:95
  136.4 11.8 %psum.14 = f32[2,256]{1,0:T(2,128)S(1)} all-reduce(f32[2,256]{1,0:T(2,128)S(1)} %pad_maximum_fusion.8), channel_id=1, replica_groups=mesh['shot'=2,'real'=4,'tile'=4] {'tile'}, use_global_device_ids=true, to_apply=%region_0.1 | all-reduce | flops 512 | bytes 4096 | tf_op jit(solution)/shard_map/psum | solution.py:98
  150.7 5.0 %collective-permute-start.8 = (f32[4,160,128]{2,1,0:T(8,128)S(1)}, f32[4,160,128]{2,1,0:T(8,128)S(1)}, u32[]{:S(2)}, u32[]{:S(2)}) collective-permute-start(f32[4,160,128]{2,1,0:T(8,128)S(1)} %bitcast.67), channel_id=1, source_target_pairs={{1,0},{2,1},{3,2},{5,4},{6,5},{7,6},{9,8},{10,9},{11,10},{13,12},{... | collective-permute-start | bytes 983048 | tf_op jit(solution)/shard_map/ppermute | solution.py:18
  159.7 4.1 %collective-permute-done.9 = f32[4,160,128]{2,1,0:T(8,128)S(1)} collective-permute-done((f32[4,160,128]{2,1,0:T(8,128)S(1)}, f32[4,160,128]{2,1,0:T(8,128)S(1)}, u32[]{:S(2)}, u32[]{:S(2)}) %collective-permute-start.9) | collective-permute-done | bytes 327712 | tf_op jit(solution)/shard_map/ppermute | solution.py:15
  163.9 2.9 %select_maximum_fusion = f32[24,168,136]{2,1,0:T(8,128)S(1)} fusion(f32[4,160,128]{2,1,0:T(8,128)S(1)} %collective-permute-done.8, f32[16,160,128]{2,1,0:T(8,128)S(1)} %bitcast.53, f32[4,160,128]{2,1,0:T(8,128)S(1)} %collective-permute-done.9), kind=kLoop, calls=%fused_computation.8 | loop fusion | flops 8225280 | bytes 4159488 | tf_op jit(solution)/shard_map/concatenate | solution.py:19
  166.8 9.2 %fusion.51 = f32[16,160,128]{2,1,0:T(8,128)} fusion(f32[1,16,160,128]{3,2,1,0:T(8,128)S(1)} %copy-done.6, f32[16,160,128]{2,1,0:T(8,128)S(1)} %copy-done.13, f32[16,160,128]{2,1,0:T(8,128)S(1)} %copy-done.11, f32[16,160,128]{2,1,0:T(8,128)S(1)} %copy-done.9, f32[16,160,128]{2,1,0:T(8,128)S(1)} %copy-done, f32[24,168,136]{2,1,0:T(8,128)S(1)} %select_maximum_fusion, ...), kind=kLoop, calls=%fused_computation.142 | loop fusion | flops 29163520 | bytes 32112640 | tf_op jit(solution)/shard_map/add | solution.py:104
  176.1 4.4 %scatter_fusion.1 = f32[327680]{0:T(1024)} fusion(f32[327680]{0:T(1024)} %bitcast.63, s32[256]{0:T(256)S(1)} %compare_select_fusion, f32[256]{0:T(256)S(1)} %get-tuple-element.49), kind=kCustom, calls=%fused_computation.3 | custom fusion | flops 256 | bytes 4096 | tf_op jit(solution)/shard_map/scatter-add | solution.py:57
  180.4 3.1 %multiply_add_fusion = f32[16,160,128]{2,1,0:T(8,128)} fusion(f32[16,160,128]{2,1,0:T(8,128)} %bitcast.64, f32[16,160,128]{2,1,0:T(8,128)} %get-tuple-element.31, f32[16,160,128]{2,1,0:T(8,128)S(1)} %bitcast.55, f32[16,160,128]{2,1,0:T(8,128)S(1)} %copy-done.17), kind=kLoop, calls=%fused_computation.144 | loop fusion | flops 983040 | bytes 6553600 | tf_op jit(solution)/shard_map/add | solution.py:106
  183.6 43.3 %all-reduce.7.cloned.1.call-done = f32[16,160,128]{2,1,0:T(8,128)} async-done(((f32[16,160,128]{2,1,0:T(8,128)}), f32[16,160,128]{2,1,0:T(8,128)}) %all-reduce.7.cloned.1.call-update) | async-done | bytes 1310736 | tf_op jit(solution)/shard_map/psum | solution.py:109
  (79 shorter events, 26.4 us)
Async XLA Ops:
  7.2 7.7 %copy-start.1 = (f32[1,16,160,128]{3,2,1,0:T(8,128)S(1)}, f32[1,16,160,128]{3,2,1,0:T(8,128)}, u32[]{:S(2)}) copy-start(f32[1,16,160,128]{3,2,1,0:T(8,128)} %param.16) | copy-start | bytes 3932164
  7.2 219.7 %all-reduce.7.cloned.1.call-start = ((), (), s32[]{:S(2)}) async-start(), calls=%async_computation | async-start | bytes 2621440 | tf_op jit(solution)/shard_map/psum | solution.py:109
  7.2 13.8 %copy-start.14 = (f32[1,16,160,128]{3,2,1,0:T(8,128)S(1)}, f32[1,16,160,128]{3,2,1,0:T(8,128)}, u32[]{:S(2)}) copy-start(f32[1,16,160,128]{3,2,1,0:T(8,128)} %param.18) | copy-start | bytes 3932164
  9.4 16.3 %collective-permute-start.3 = (f32[4,160,128]{2,1,0:T(8,128)}, f32[4,160,128]{2,1,0:T(8,128)S(1)}, u32[]{:S(2)}, u32[]{:S(2)}) collective-permute-start(f32[4,160,128]{2,1,0:T(8,128)} %get-tuple-element.42), channel_id=1, source_target_pairs={{0,1},{1,2},{2,3},{4,5},{5,6},{6,7},{8,9},{9,10},{10,11},{12,13},{... | collective-permute-start | bytes 983048 | tf_op jit(solution)/shard_map/ppermute | solution.py:15
  12.6 13.1 %copy-start.20 = (s32[256]{0:T(256)S(1)}, s32[256]{0:T(256)}, u32[]{:S(2)}) copy-start(s32[256]{0:T(256)} %param.22) | copy-start | bytes 3076
  12.6 17.2 %copy-start = (f32[16,160,128]{2,1,0:T(8,128)S(1)}, f32[16,160,128]{2,1,0:T(8,128)}, u32[]{:S(2)}) copy-start(f32[16,160,128]{2,1,0:T(8,128)} %param.19) | copy-start | bytes 3932164
  12.6 17.2 %collective-permute-start.2 = (f32[4,160,128]{2,1,0:T(8,128)}, f32[4,160,128]{2,1,0:T(8,128)}, u32[]{:S(2)}, u32[]{:S(2)}) collective-permute-start(f32[4,160,128]{2,1,0:T(8,128)} %get-tuple-element.41), channel_id=1, source_target_pairs={{1,0},{2,1},{3,2},{5,4},{6,5},{7,6},{9,8},{10,9},{11,10},{13,12},{... | collective-permute-start | bytes 983048 | tf_op jit(solution)/shard_map/ppermute | solution.py:18
  15.7 23.4 %collective-permute-start.4 = (f32[4,160,128]{2,1,0:T(8,128)}, f32[4,160,128]{2,1,0:T(8,128)}, u32[]{:S(2)}, u32[]{:S(2)}) collective-permute-start(f32[4,160,128]{2,1,0:T(8,128)} %get-tuple-element.46), channel_id=1, source_target_pairs={{1,0},{2,1},{3,2},{5,4},{6,5},{7,6},{9,8},{10,9},{11,10},{13,12},{... | collective-permute-start | bytes 983048 | tf_op jit(solution)/shard_map/ppermute | solution.py:18
  17.6 21.5 %collective-permute-start.5 = (f32[4,160,128]{2,1,0:T(8,128)}, f32[4,160,128]{2,1,0:T(8,128)}, u32[]{:S(2)}, u32[]{:S(2)}) collective-permute-start(f32[4,160,128]{2,1,0:T(8,128)} %get-tuple-element.45), channel_id=1, source_target_pairs={{0,1},{1,2},{2,3},{4,5},{5,6},{6,7},{8,9},{9,10},{10,11},{12,13},{... | collective-permute-start | bytes 983048 | tf_op jit(solution)/shard_map/ppermute | solution.py:15
  21.9 75.3 %collective-permute-start = (f32[4,160,128]{2,1,0:T(8,128)}, f32[4,160,128]{2,1,0:T(8,128)S(1)}, u32[]{:S(2)}, u32[]{:S(2)}) collective-permute-start(f32[4,160,128]{2,1,0:T(8,128)} %get-tuple-element.40), channel_id=1, source_target_pairs={{1,0},{2,1},{3,2},{5,4},{6,5},{7,6},{9,8},{10,9},{11,10},{13,12},{... | collective-permute-start | bytes 983048 | tf_op jit(solution)/shard_map/ppermute | solution.py:18
  26.5 8.4 %copy-start.19 = (f32[4,160,128]{2,1,0:T(8,128)S(1)}, f32[4,160,128]{2,1,0:T(8,128)}, u32[]{:S(2)}) copy-start(f32[4,160,128]{2,1,0:T(8,128)} %copy-done.18) | copy-start | bytes 983044
  26.5 70.8 %collective-permute-start.1 = (f32[4,160,128]{2,1,0:T(8,128)}, f32[4,160,128]{2,1,0:T(8,128)S(1)}, u32[]{:S(2)}, u32[]{:S(2)}) collective-permute-start(f32[4,160,128]{2,1,0:T(8,128)} %get-tuple-element.39), channel_id=1, source_target_pairs={{0,1},{1,2},{2,3},{4,5},{5,6},{6,7},{8,9},{9,10},{10,11},{12,13},{... | collective-permute-start | bytes 983048 | tf_op jit(solution)/shard_map/ppermute | solution.py:15
  44.2 42.8 %copy-start.22 = (f32[2]{0:T(128)S(1)}, f32[2]{0:T(128)}, u32[]{:S(2)}) copy-start(f32[2]{0:T(128)} %param.20) | copy-start | bytes 28
  87.0 10.2 %copy-start.15 = (f32[1,16,160,128]{3,2,1,0:T(8,128)S(1)}, f32[1,16,160,128]{3,2,1,0:T(8,128)}, u32[]{:S(2)}) copy-start(f32[1,16,160,128]{3,2,1,0:T(8,128)} %param.18) | copy-start | bytes 3932164
  91.7 23.8 %collective-permute-start.6 = (f32[4,160,128]{2,1,0:T(8,128)}, f32[4,160,128]{2,1,0:T(8,128)}, u32[]{:S(2)}, u32[]{:S(2)}) collective-permute-start(f32[4,160,128]{2,1,0:T(8,128)} %bitcast.15), channel_id=1, source_target_pairs={{1,0},{2,1},{3,2},{5,4},{6,5},{7,6},{9,8},{10,9},{11,10},{13,12},{... | collective-permute-start | bytes 983048 | tf_op jit(solution)/shard_map/ppermute | solution.py:18
  93.8 21.7 %collective-permute-start.7 = (f32[4,160,128]{2,1,0:T(8,128)}, f32[4,160,128]{2,1,0:T(8,128)}, u32[]{:S(2)}, u32[]{:S(2)}) collective-permute-start(f32[4,160,128]{2,1,0:T(8,128)} %bitcast.16), channel_id=1, source_target_pairs={{0,1},{1,2},{2,3},{4,5},{5,6},{6,7},{8,9},{9,10},{10,11},{12,13},{... | collective-permute-start | bytes 983048 | tf_op jit(solution)/shard_map/ppermute | solution.py:15
  115.5 4.1 %copy-start.2 = (f32[1,16,160,128]{3,2,1,0:T(8,128)S(1)}, f32[1,16,160,128]{3,2,1,0:T(8,128)}, u32[]{:S(2)}) copy-start(f32[1,16,160,128]{3,2,1,0:T(8,128)} %param.16) | copy-start | bytes 3932164
  115.5 4.1 %copy-start.3 = (f32[327680]{0:T(1024)S(1)}, f32[327680]{0:T(1024)}, u32[]{:S(2)}) copy-start(f32[327680]{0:T(1024)} %fusion.52) | copy-start | bytes 3932164
  115.5 4.1 %copy-start.5 = (f32[1,16,160,128]{3,2,1,0:T(8,128)S(1)}, f32[1,16,160,128]{3,2,1,0:T(8,128)}, u32[]{:S(2)}) copy-start(f32[1,16,160,128]{3,2,1,0:T(8,128)} %param.14) | copy-start | bytes 3932164
  119.7 28.5 %copy-start.21 = (f32[2,256]{1,0:T(2,128)S(1)}, f32[2,256]{1,0:T(2,128)}, u32[]{:S(2)}) copy-start(f32[2,256]{1,0:T(2,128)} %param.23) | copy-start | bytes 6148
  150.7 16.1 %copy-start.16 = (f32[1,16,160,128]{3,2,1,0:T(8,128)S(1)}, f32[1,16,160,128]{3,2,1,0:T(8,128)}, u32[]{:S(2)}) copy-start(f32[1,16,160,128]{3,2,1,0:T(8,128)} %param.18) | copy-start | bytes 3932164
  150.7 9.0 %collective-permute-start.8 = (f32[4,160,128]{2,1,0:T(8,128)S(1)}, f32[4,160,128]{2,1,0:T(8,128)S(1)}, u32[]{:S(2)}, u32[]{:S(2)}) collective-permute-start(f32[4,160,128]{2,1,0:T(8,128)S(1)} %bitcast.67), channel_id=1, source_target_pairs={{1,0},{2,1},{3,2},{5,4},{6,5},{7,6},{9,8},{10,9},{11,10},{13,12},{... | collective-permute-start | bytes 983048 | tf_op jit(solution)/shard_map/ppermute | solution.py:18
  155.7 8.1 %collective-permute-start.9 = (f32[4,160,128]{2,1,0:T(8,128)S(1)}, f32[4,160,128]{2,1,0:T(8,128)S(1)}, u32[]{:S(2)}, u32[]{:S(2)}) collective-permute-start(f32[4,160,128]{2,1,0:T(8,128)S(1)} %bitcast.66), channel_id=1, source_target_pairs={{0,1},{1,2},{2,3},{4,5},{5,6},{6,7},{8,9},{9,10},{10,11},{12,13},{... | collective-permute-start | bytes 983048 | tf_op jit(solution)/shard_map/ppermute | solution.py:15
  176.1 4.4 %copy-start.17 = (f32[16,160,128]{2,1,0:T(8,128)S(1)}, f32[16,160,128]{2,1,0:T(8,128)}, u32[]{:S(2)}) copy-start(f32[16,160,128]{2,1,0:T(8,128)} %get-tuple-element.29) | copy-start | bytes 3932164
  (10 other events, 28.6 us)
Sparse Core Ops, SparseCore 0:
  183.7 43.1 all-reduce.6
where the time goes:
time: 239 us; the launch traced here: 236 us
  other arithmetic  107 us (45%)
  waiting for transfers between devices  49.3 us (21%)
  starting transfers between devices  29.3 us (12%)
  local copies, waits for them, and re-layouts  23 us (10%)
  between operations  15.7 us (7%)
  blocking collectives  11.8 us (5%)
    add x4, other arithmetic, shards(): newer = 2.0 * now - older + speed * force  69.3 us
    psum x1, waiting for transfers between devices, shards(): image = lax.psum(image_part, 'real') / members  43.3 us
    concatenate x5, other arithmetic, extended(): block = jnp.concatenate([low, block, high], axis=dim)  20 us
    ppermute x5, starting transfers between devices, extended(): lax.ppermute(lax.slice_in_dim(block, block.shape[dim] - width, None, axis...  15.4 us
    ppermute x5, starting transfers between devices, extended(): lax.ppermute(lax.slice_in_dim(block, 0, width, axis=dim), axis, backward)  13.8 us
    scatter-add x4, other arithmetic, inject(): flat = field.reshape(-1).at[where].add(jnp.where(valid, values, 0.0))  12.2 us
    gather x2, local copies, waits for them, and re-layouts, shards(): samples.append(jnp.where(rec_valid, newer.reshape(-1)[rec_local], 0.0))  11.9 us
    psum x1, blocking collectives, shards(): traces = lax.psum(jnp.stack(samples), 'tile')  11.8 us
  transfers between devices with their start and end apart: 11, of which 3 were waited for; matrix products, arithmetic and copies ran while one was open for 35% of the time, Pallas kernels for 0%

commit v1 on v0

--- a/solution.py
+++ b/solution.py
@@ -58,6 +58,31 @@
     return flat.reshape(field.shape)
 
 
+def reduce_members(part, axis):
+    members = lax.axis_size(axis)
+    if members & (members - 1) or part.size % (members * 1024):
+        return lax.psum(part, axis) / members
+    me = lax.axis_index(axis)
+    rows = part.reshape(-1, 128)
+    bits = members.bit_length() - 1
+    for b in range(bits):
+        mask = 1 << b
+        half = rows.shape[0] // 2
+        upper = (me // mask) % 2
+        keep = lax.dynamic_slice_in_dim(rows, upper * half, half, 0)
+        give = lax.dynamic_slice_in_dim(rows, (1 - upper) * half, half, 0)
+        pairs = [(i, i ^ mask) for i in range(members)]
+        rows = keep + lax.ppermute(give, axis, pairs)
+    rows = rows / members
+    for b in reversed(range(bits)):
+        mask = 1 << b
+        upper = (me // mask) % 2
+        pairs = [(i, i ^ mask) for i in range(members)]
+        other = lax.ppermute(rows, axis, pairs)
+        rows = jnp.where(upper == 1, jnp.concatenate([other, rows]), jnp.concatenate([rows, other]))
+    return rows.reshape(part.shape)
+
+
 def shards(
     courant,
     prev_field,
@@ -95,8 +120,7 @@
         samples.append(jnp.where(rec_valid, newer.reshape(-1)[rec_local], 0.0))
         forces.append(force)
         older, now = (now, newer)
-    traces = lax.psum(jnp.stack(samples), "tile")
-    residual = traces - observed
+    residual = jnp.where(rec_valid, jnp.stack(samples) - observed, 0.0)
     older, now = (adj_prev[0], adj_cur[0])
     image_part = jnp.zeros(buoyancy.shape, jnp.float32)
     for j in range(steps):
@@ -105,8 +129,7 @@
         newer = inject(newer, rec_local, rec_valid, residual[steps - 1 - j])
         image_part = image_part + newer * forces[steps - 1 - j]
         older, now = (now, newer)
-    members = lax.axis_size("real")
-    image = lax.psum(image_part, "real") / members
+    image = reduce_members(image_part, "real")
     return (image, now[None])
 
 

time: 239 us -> 200 us (0.84)
  waiting for transfers between devices: 49.3 us -> 24.2 us
  between operations: 15.7 us -> 2.36 us
  blocking collectives: 11.8 us -> 0 us
  starting transfers between devices: 29.3 us -> 40 us
  local copies, waits for them, and re-layouts: 23 us -> 25.9 us
    psum x1 -> x0, waiting for transfers between devices: 43.3 us -> none  [shards(): image = lax.psum(image_part, 'real') / members]
    ppermute x0 -> x4, waiting for transfers between devices: none -> 18 us  [the longest x2 9.44 us: reduce_members(): rows = keep + lax.ppermute(give, axis, pairs)]
    psum x1 -> x0, blocking collectives: 11.8 us -> none  [shards(): traces = lax.psum(jnp.stack(samples), 'tile')]
    ppermute x0 -> x4, starting transfers between devices: none -> 8.65 us  [the longest x2 5.18 us: reduce_members(): rows = keep + lax.ppermute(give, axis, pairs)]
    div x1, other arithmetic: 2.48 us -> 0.04 us  [reduce_members(): rows = rows / members]
  transfers between devices with their start and end apart: 11 -> 14, of which waited for: 3 -> 6; matrix products, arithmetic and copies ran while one was open for 35% -> 41% of each run, Pallas kernels for 0% -> 0%
where the time goes in v1:
time: 200 us; the launch traced here: 199 us
  other arithmetic  107 us (54%)
  starting transfers between devices  40 us (20%)
  local copies, waits for them, and re-layouts  25.9 us (13%)
  waiting for transfers between devices  24.2 us (12%)
  between operations  2.36 us (1%)
    add x4, other arithmetic, shards(): newer = 2.0 * now - older + speed * force  69.6 us
    concatenate x5, other arithmetic, extended(): block = jnp.concatenate([low, block, high], axis=dim)  20 us
    ppermute x5, starting transfers between devices, extended(): lax.ppermute(lax.slice_in_dim(block, 0, width, axis=dim), axis, backward)  16 us
    ppermute x5, starting transfers between devices, extended(): lax.ppermute(lax.slice_in_dim(block, block.shape[dim] - width, None, axis...  15.4 us
    gather x2, local copies, waits for them, and re-layouts, shards(): samples.append(jnp.where(rec_valid, newer.reshape(-1)[rec_local], 0.0))  12.9 us
    scatter-add x4, other arithmetic, inject(): flat = field.reshape(-1).at[where].add(jnp.where(valid, values, 0.0))  12.4 us
    ppermute x2, waiting for transfers between devices, reduce_members(): rows = keep + lax.ppermute(give, axis, pairs)  9.44 us
    ppermute x2, waiting for transfers between devices, reduce_members(): other = lax.ppermute(rows, axis, pairs)  8.52 us
  transfers between devices with their start and end apart: 14, of which 6 were waited for; matrix products, arithmetic and copies ran while one was open for 41% of the time, Pallas kernels for 0%

profile of v1, /device:TPU:9, one launch (start us, length us, event | category | flops | bytes accessed | tf_op | source)
XLA Modules:
  0.0 199.0 jit_solution(14190720909573653301)
XLA Ops:
  2.8 3.2 %collective-permute-start.3 = (f32[4,160,128]{2,1,0:T(8,128)}, f32[4,160,128]{2,1,0:T(8,128)S(1)}, u32[]{:S(2)}, u32[]{:S(2)}) collective-permute-start(f32[4,160,128]{2,1,0:T(8,128)} %get-tuple-element.42), channel_id=1, source_target_pairs={{0,1},{1,2},{2,3},{4,5},{5,6},{6,7},{8,9},{9,10},{10,11},{12,13},{... | collective-permute-start | bytes 983048 | tf_op jit(solution)/shard_map/ppermute | solution.py:15
  11.1 3.4 %collective-permute-start.5 = (f32[4,160,128]{2,1,0:T(8,128)}, f32[4,160,128]{2,1,0:T(8,128)}, u32[]{:S(2)}, u32[]{:S(2)}) collective-permute-start(f32[4,160,128]{2,1,0:T(8,128)} %get-tuple-element.45), channel_id=1, source_target_pairs={{0,1},{1,2},{2,3},{4,5},{5,6},{6,7},{8,9},{9,10},{10,11},{12,13},{... | collective-permute-start | bytes 983048 | tf_op jit(solution)/shard_map/ppermute | solution.py:15
  15.3 2.6 %collective-permute-start = (f32[4,160,128]{2,1,0:T(8,128)}, f32[4,160,128]{2,1,0:T(8,128)S(1)}, u32[]{:S(2)}, u32[]{:S(2)}) collective-permute-start(f32[4,160,128]{2,1,0:T(8,128)} %get-tuple-element.40), channel_id=1, source_target_pairs={{1,0},{2,1},{3,2},{5,4},{6,5},{7,6},{9,8},{10,9},{11,10},{13,12},{... | collective-permute-start | bytes 983048 | tf_op jit(solution)/shard_map/ppermute | solution.py:18
  19.9 3.3 %collective-permute-start.1 = (f32[4,160,128]{2,1,0:T(8,128)}, f32[4,160,128]{2,1,0:T(8,128)S(1)}, u32[]{:S(2)}, u32[]{:S(2)}) collective-permute-start(f32[4,160,128]{2,1,0:T(8,128)} %get-tuple-element.39), channel_id=1, source_target_pairs={{0,1},{1,2},{2,3},{4,5},{5,6},{6,7},{8,9},{9,10},{10,11},{12,13},{... | collective-permute-start | bytes 983048 | tf_op jit(solution)/shard_map/ppermute | solution.py:15
  23.3 5.0 %select_maximum_fusion.6 = f32[24,168,136]{2,1,0:T(8,128)} fusion(f32[4,160,128]{2,1,0:T(8,128)} %collective-permute-done.2, f32[16,160,128]{2,1,0:T(8,128)S(1)} %copy-done, f32[4,160,128]{2,1,0:T(8,128)} %copy-done.18), kind=kLoop, calls=%fused_computation.14 | loop fusion | flops 8225280 | bytes 4159488 | tf_op jit(solution)/shard_map/concatenate | solution.py:19
  32.6 5.1 %select_maximum_fusion.4 = f32[24,168,136]{2,1,0:T(8,128)} fusion(f32[4,160,128]{2,1,0:T(8,128)} %collective-permute-done.4, f32[16,160,128]{2,1,0:T(8,128)S(1)} %bitcast.58, f32[4,160,128]{2,1,0:T(8,128)} %collective-permute-done.5), kind=kLoop, calls=%fused_computation.12 | loop fusion | flops 8225280 | bytes 4159488 | tf_op jit(solution)/shard_map/concatenate | solution.py:19
  37.6 42.3 %fusion.48 = (f32[16,160,128]{2,1,0:T(8,128)}, f32[16,160,128]{2,1,0:T(8,128)}, f32[16,160,128]{2,1,0:T(8,128)}, f32[16,160,128]{2,1,0:T(8,128)}, f32[16,160,128]{2,1,0:T(8,128)}) fusion(f32[1,16,160,128]{3,2,1,0:T(8,128)} %param.15, f32[1,16,160,128]{3,2,1,0:T(8,128)} %param.14, f32[1,16,160,128]{3,2,1,0:T(8,128)S(1)} %copy-done.1, ...), kind=kLoop, calls=%fused_computation.136 | loop fusion | flops 39976960 | bytes 66191360 | tf_op jit(solution)/shard_map/add | solution.py:118
  80.0 2.9 %fusion.53 = f32[327680]{0:T(1024)} fusion(f32[327680]{0:T(1024)} %bitcast.60, s32[]{:T(128)} %bitcast.12, s32[1]{0:T(128)} %maximum_minimum_fusion, f32[2]{0:T(128)S(1)} %copy-done.21, s32[1]{0:T(128)S(6)} %copy.18, s32[1]{0:T(128)} %bitcast.11), kind=kLoop, calls=%fused_computation.169 | loop fusion | flops 8 | bytes 2568 | tf_op jit(solution)/shard_map/scatter-add | solution.py:57
  86.9 3.4 %collective-permute-start.7 = (f32[4,160,128]{2,1,0:T(8,128)}, f32[4,160,128]{2,1,0:T(8,128)}, u32[]{:S(2)}, u32[]{:S(2)}) collective-permute-start(f32[4,160,128]{2,1,0:T(8,128)} %bitcast.16), channel_id=1, source_target_pairs={{0,1},{1,2},{2,3},{4,5},{5,6},{6,7},{8,9},{9,10},{10,11},{12,13},{... | collective-permute-start | bytes 983048 | tf_op jit(solution)/shard_map/ppermute | solution.py:15
  90.4 2.9 %select_maximum_fusion.8 = f32[24,168,136]{2,1,0:T(8,128)S(1)} fusion(f32[4,160,128]{2,1,0:T(8,128)S(1)} %collective-permute-done, f32[16,160,128]{2,1,0:T(8,128)S(1)} %bitcast.63, f32[4,160,128]{2,1,0:T(8,128)S(1)} %collective-permute-done.1), kind=kLoop, calls=%fused_computation.16 | loop fusion | flops 8225280 | bytes 4159488 | tf_op jit(solution)/shard_map/concatenate | solution.py:19
  93.3 9.3 %fusion.49 = f32[16,160,128]{2,1,0:T(8,128)S(1)} fusion(f32[1,16,160,128]{3,2,1,0:T(8,128)S(1)} %copy-done.4, f32[1,16,160,128]{3,2,1,0:T(8,128)} %param.17, f32[16,160,128]{2,1,0:T(8,128)S(1)} %copy-done.12, f32[16,160,128]{2,1,0:T(8,128)S(1)} %copy-done.10, f32[16,160,128]{2,1,0:T(8,128)S(1)} %copy-done.7, f32[16,160,128]{2,1,0:T(8,128)S(1)} %copy-done, ...), kind=kLoop, calls=%fused_computation.141 | loop fusion | flops 29163520 | bytes 32112640 | tf_op jit(solution)/shard_map/add | solution.py:128
  102.6 6.4 %gather_fusion = f32[256]{0:T(256)S(1)} fusion(f32[327680]{0:T(1024)} %fusion.53, s32[1024]{0:T(1024)S(1)} %pad_clamp_fusion), kind=kCustom, calls=%fused_computation | custom fusion | bytes 3072 | tf_op jit(solution)/shard_map/gather | solution.py:120
  109.1 4.1 %select_maximum_fusion.2 = f32[24,168,136]{2,1,0:T(8,128)S(1)} fusion(f32[4,160,128]{2,1,0:T(8,128)} %collective-permute-done.6, f32[16,160,128]{2,1,0:T(8,128)} %bitcast.61, f32[4,160,128]{2,1,0:T(8,128)} %collective-permute-done.7), kind=kLoop, calls=%fused_computation.10 | loop fusion | flops 8225280 | bytes 4159488 | tf_op jit(solution)/shard_map/concatenate | solution.py:19
  113.3 8.1 %fusion.50 = (f32[16,160,128]{2,1,0:T(8,128)}, f32[16,160,128]{2,1,0:T(8,128)}) fusion(f32[1,16,160,128]{3,2,1,0:T(8,128)S(1)} %copy-done.5, f32[16,160,128]{2,1,0:T(8,128)S(1)} %bitcast.62, f32[1,16,160,128]{3,2,1,0:T(8,128)S(1)} %copy-done.2, f32[16,160,128]{2,1,0:T(8,128)} %get-tuple-element.34, f32[16,160,128]{2,1,0:T(8,128)} %get-tuple-element.33, ...), kind=kLoop, calls=%fused_computation.142 | loop fusion | flops 29163520 | bytes 33423360 | tf_op jit(solution)/shard_map/add | solution.py:118
  121.4 2.8 %fusion.54 = f32[327680]{0:T(1024)} fusion(f32[327680]{0:T(1024)} %bitcast.17, s32[]{:T(128)} %bitcast.12, s32[1]{0:T(128)} %maximum_minimum_fusion, f32[2]{0:T(128)S(1)} %copy-done.21, s32[1]{0:T(128)S(6)} %copy.18, s32[1]{0:T(128)} %bitcast.11), kind=kLoop, calls=%fused_computation.170 | loop fusion | flops 8 | bytes 2568 | tf_op jit(solution)/shard_map/scatter-add | solution.py:57
  124.2 6.4 %gather_fusion.1 = f32[256]{0:T(256)S(1)} fusion(f32[327680]{0:T(1024)} %fusion.54, s32[1024]{0:T(1024)S(1)} %pad_clamp_fusion), kind=kCustom, calls=%fused_computation.1 | custom fusion | bytes 3072 | tf_op jit(solution)/shard_map/gather | solution.py:120
  134.0 7.1 %collective-permute-start.8 = (f32[4,160,128]{2,1,0:T(8,128)}, f32[4,160,128]{2,1,0:T(8,128)S(1)}, u32[]{:S(2)}, u32[]{:S(2)}) collective-permute-start(f32[4,160,128]{2,1,0:T(8,128)} %bitcast.21), channel_id=1, source_target_pairs={{1,0},{2,1},{3,2},{5,4},{6,5},{7,6},{9,8},{10,9},{11,10},{13,12},{... | collective-permute-start | bytes 983048 | tf_op jit(solution)/shard_map/ppermute | solution.py:18
  145.8 3.7 %collective-permute-done.9 = f32[4,160,128]{2,1,0:T(8,128)S(1)} collective-permute-done((f32[4,160,128]{2,1,0:T(8,128)}, f32[4,160,128]{2,1,0:T(8,128)S(1)}, u32[]{:S(2)}, u32[]{:S(2)}) %collective-permute-start.9) | collective-permute-done | bytes 327712 | tf_op jit(solution)/shard_map/ppermute | solution.py:15
  149.5 2.9 %select_maximum_fusion = f32[24,168,136]{2,1,0:T(8,128)S(1)} fusion(f32[4,160,128]{2,1,0:T(8,128)S(1)} %collective-permute-done.8, f32[16,160,128]{2,1,0:T(8,128)S(1)} %bitcast.55, f32[4,160,128]{2,1,0:T(8,128)S(1)} %collective-permute-done.9), kind=kLoop, calls=%fused_computation.8 | loop fusion | flops 8225280 | bytes 4159488 | tf_op jit(solution)/shard_map/concatenate | solution.py:19
  152.5 9.9 %fusion.51 = f32[16,160,128]{2,1,0:T(8,128)} fusion(f32[1,16,160,128]{3,2,1,0:T(8,128)S(1)} %copy-done.6, f32[16,160,128]{2,1,0:T(8,128)S(1)} %copy-done.13, f32[16,160,128]{2,1,0:T(8,128)S(1)} %copy-done.11, f32[16,160,128]{2,1,0:T(8,128)S(1)} %copy-done.9, f32[16,160,128]{2,1,0:T(8,128)S(1)} %copy-done, f32[24,168,136]{2,1,0:T(8,128)S(1)} %select_maximum_fusion, ...), kind=kLoop, calls=%fused_computation.143 | loop fusion | flops 29163520 | bytes 32112640 | tf_op jit(solution)/shard_map/add | solution.py:128
  162.4 4.4 %scatter_fusion.1 = f32[327680]{0:T(1024)} fusion(f32[327680]{0:T(1024)} %bitcast.65, s32[256]{0:T(256)S(1)} %compare_select_fusion, f32[256]{0:T(256)S(1)} %get-tuple-element.49), kind=kCustom, calls=%fused_computation.3 | custom fusion | flops 256 | bytes 4096 | tf_op jit(solution)/shard_map/scatter-add | solution.py:57
  170.0 3.9 %collective-permute-start.10 = (f32[1280,128]{1,0:T(8,128)S(1)}, f32[1280,128]{1,0:T(8,128)S(1)}, u32[]{:S(2)}, u32[]{:S(2)}) collective-permute-start(f32[1280,128]{1,0:T(8,128)S(1)} %constant_dynamic-slice_fusion.1), channel_id=1, source_target_pairs={{0,4},{4,0},{8,12},{12,8},{1,5},{5,1},{9,13},{13,9},{2,6},{6,2},{1... | collective-permute-start | bytes 1966088 | tf_op jit(solution)/shard_map/ppermute | solution.py:75
  178.1 7.7 %collective-permute-done.11 = f32[640,128]{1,0:T(8,128)S(1)} collective-permute-done((f32[640,128]{1,0:T(8,128)S(1)}, f32[640,128]{1,0:T(8,128)S(1)}, u32[]{:S(2)}, u32[]{:S(2)}) %collective-permute-start.11) | collective-permute-done | bytes 327712 | tf_op jit(solution)/shard_map/ppermute | solution.py:75
  187.1 6.8 %collective-permute-done.12 = f32[640,128]{1,0:T(8,128)S(1)} collective-permute-done((f32[640,128]{1,0:T(8,128)S(1)}, f32[640,128]{1,0:T(8,128)S(1)}, u32[]{:S(2)}, u32[]{:S(2)}) %collective-permute-start.12) | collective-permute-done | bytes 327712 | tf_op jit(solution)/shard_map/ppermute | solution.py:81
  (87 shorter events, 39.1 us)
Async XLA Ops:
  0.6 7.6 %copy-start.1 = (f32[1,16,160,128]{3,2,1,0:T(8,128)S(1)}, f32[1,16,160,128]{3,2,1,0:T(8,128)}, u32[]{:S(2)}) copy-start(f32[1,16,160,128]{3,2,1,0:T(8,128)} %param.16) | copy-start | bytes 3932164
  0.6 13.8 %copy-start.14 = (f32[1,16,160,128]{3,2,1,0:T(8,128)S(1)}, f32[1,16,160,128]{3,2,1,0:T(8,128)}, u32[]{:S(2)}) copy-start(f32[1,16,160,128]{3,2,1,0:T(8,128)} %param.18) | copy-start | bytes 3932164
  2.8 16.4 %collective-permute-start.3 = (f32[4,160,128]{2,1,0:T(8,128)}, f32[4,160,128]{2,1,0:T(8,128)S(1)}, u32[]{:S(2)}, u32[]{:S(2)}) collective-permute-start(f32[4,160,128]{2,1,0:T(8,128)} %get-tuple-element.42), channel_id=1, source_target_pairs={{0,1},{1,2},{2,3},{4,5},{5,6},{6,7},{8,9},{9,10},{10,11},{12,13},{... | collective-permute-start | bytes 983048 | tf_op jit(solution)/shard_map/ppermute | solution.py:15
  6.0 13.2 %copy-start.20 = (s32[256]{0:T(256)S(1)}, s32[256]{0:T(256)}, u32[]{:S(2)}) copy-start(s32[256]{0:T(256)} %param.22) | copy-start | bytes 3076
  6.0 17.2 %copy-start = (f32[16,160,128]{2,1,0:T(8,128)S(1)}, f32[16,160,128]{2,1,0:T(8,128)}, u32[]{:S(2)}) copy-start(f32[16,160,128]{2,1,0:T(8,128)} %param.19) | copy-start | bytes 3932164
  6.0 17.2 %collective-permute-start.2 = (f32[4,160,128]{2,1,0:T(8,128)}, f32[4,160,128]{2,1,0:T(8,128)}, u32[]{:S(2)}, u32[]{:S(2)}) collective-permute-start(f32[4,160,128]{2,1,0:T(8,128)} %get-tuple-element.41), channel_id=1, source_target_pairs={{1,0},{2,1},{3,2},{5,4},{6,5},{7,6},{9,8},{10,9},{11,10},{13,12},{... | collective-permute-start | bytes 983048 | tf_op jit(solution)/shard_map/ppermute | solution.py:18
  9.1 23.4 %collective-permute-start.4 = (f32[4,160,128]{2,1,0:T(8,128)}, f32[4,160,128]{2,1,0:T(8,128)}, u32[]{:S(2)}, u32[]{:S(2)}) collective-permute-start(f32[4,160,128]{2,1,0:T(8,128)} %get-tuple-element.46), channel_id=1, source_target_pairs={{1,0},{2,1},{3,2},{5,4},{6,5},{7,6},{9,8},{10,9},{11,10},{13,12},{... | collective-permute-start | bytes 983048 | tf_op jit(solution)/shard_map/ppermute | solution.py:18
  11.1 21.5 %collective-permute-start.5 = (f32[4,160,128]{2,1,0:T(8,128)}, f32[4,160,128]{2,1,0:T(8,128)}, u32[]{:S(2)}, u32[]{:S(2)}) collective-permute-start(f32[4,160,128]{2,1,0:T(8,128)} %get-tuple-element.45), channel_id=1, source_target_pairs={{0,1},{1,2},{2,3},{4,5},{5,6},{6,7},{8,9},{9,10},{10,11},{12,13},{... | collective-permute-start | bytes 983048 | tf_op jit(solution)/shard_map/ppermute | solution.py:15
  15.3 74.9 %collective-permute-start = (f32[4,160,128]{2,1,0:T(8,128)}, f32[4,160,128]{2,1,0:T(8,128)S(1)}, u32[]{:S(2)}, u32[]{:S(2)}) collective-permute-start(f32[4,160,128]{2,1,0:T(8,128)} %get-tuple-element.40), channel_id=1, source_target_pairs={{1,0},{2,1},{3,2},{5,4},{6,5},{7,6},{9,8},{10,9},{11,10},{13,12},{... | collective-permute-start | bytes 983048 | tf_op jit(solution)/shard_map/ppermute | solution.py:18
  19.9 8.4 %copy-start.19 = (f32[4,160,128]{2,1,0:T(8,128)S(1)}, f32[4,160,128]{2,1,0:T(8,128)}, u32[]{:S(2)}) copy-start(f32[4,160,128]{2,1,0:T(8,128)} %copy-done.18) | copy-start | bytes 983044
  19.9 70.4 %collective-permute-start.1 = (f32[4,160,128]{2,1,0:T(8,128)}, f32[4,160,128]{2,1,0:T(8,128)S(1)}, u32[]{:S(2)}, u32[]{:S(2)}) collective-permute-start(f32[4,160,128]{2,1,0:T(8,128)} %get-tuple-element.39), channel_id=1, source_target_pairs={{0,1},{1,2},{2,3},{4,5},{5,6},{6,7},{8,9},{9,10},{10,11},{12,13},{... | collective-permute-start | bytes 983048 | tf_op jit(solution)/shard_map/ppermute | solution.py:15
  37.6 42.3 %copy-start.21 = (f32[2]{0:T(128)S(1)}, f32[2]{0:T(128)}, u32[]{:S(2)}) copy-start(f32[2]{0:T(128)} %param.20) | copy-start | bytes 28
  80.0 10.3 %copy-start.15 = (f32[1,16,160,128]{3,2,1,0:T(8,128)S(1)}, f32[1,16,160,128]{3,2,1,0:T(8,128)}, u32[]{:S(2)}) copy-start(f32[1,16,160,128]{3,2,1,0:T(8,128)} %param.18) | copy-start | bytes 3932164
  84.8 24.3 %collective-permute-start.6 = (f32[4,160,128]{2,1,0:T(8,128)}, f32[4,160,128]{2,1,0:T(8,128)}, u32[]{:S(2)}, u32[]{:S(2)}) collective-permute-start(f32[4,160,128]{2,1,0:T(8,128)} %bitcast.15), channel_id=1, source_target_pairs={{1,0},{2,1},{3,2},{5,4},{6,5},{7,6},{9,8},{10,9},{11,10},{13,12},{... | collective-permute-start | bytes 983048 | tf_op jit(solution)/shard_map/ppermute | solution.py:18
  86.9 22.1 %collective-permute-start.7 = (f32[4,160,128]{2,1,0:T(8,128)}, f32[4,160,128]{2,1,0:T(8,128)}, u32[]{:S(2)}, u32[]{:S(2)}) collective-permute-start(f32[4,160,128]{2,1,0:T(8,128)} %bitcast.16), channel_id=1, source_target_pairs={{0,1},{1,2},{2,3},{4,5},{5,6},{6,7},{8,9},{9,10},{10,11},{12,13},{... | collective-permute-start | bytes 983048 | tf_op jit(solution)/shard_map/ppermute | solution.py:15
  109.1 4.1 %copy-start.2 = (f32[1,16,160,128]{3,2,1,0:T(8,128)S(1)}, f32[1,16,160,128]{3,2,1,0:T(8,128)}, u32[]{:S(2)}) copy-start(f32[1,16,160,128]{3,2,1,0:T(8,128)} %param.16) | copy-start | bytes 3932164
  113.3 17.4 %copy-start.22 = (f32[2,256]{1,0:T(2,128)S(1)}, f32[2,256]{1,0:T(2,128)}, u32[]{:S(2)}) copy-start(f32[2,256]{1,0:T(2,128)} %param.23) | copy-start | bytes 6148
  134.0 11.8 %collective-permute-start.8 = (f32[4,160,128]{2,1,0:T(8,128)}, f32[4,160,128]{2,1,0:T(8,128)S(1)}, u32[]{:S(2)}, u32[]{:S(2)}) collective-permute-start(f32[4,160,128]{2,1,0:T(8,128)} %bitcast.21), channel_id=1, source_target_pairs={{1,0},{2,1},{3,2},{5,4},{6,5},{7,6},{9,8},{10,9},{11,10},{13,12},{... | collective-permute-start | bytes 983048 | tf_op jit(solution)/shard_map/ppermute | solution.py:18
  141.1 8.4 %collective-permute-start.9 = (f32[4,160,128]{2,1,0:T(8,128)}, f32[4,160,128]{2,1,0:T(8,128)S(1)}, u32[]{:S(2)}, u32[]{:S(2)}) collective-permute-start(f32[4,160,128]{2,1,0:T(8,128)} %bitcast.22), channel_id=1, source_target_pairs={{0,1},{1,2},{2,3},{4,5},{5,6},{6,7},{8,9},{9,10},{10,11},{12,13},{... | collective-permute-start | bytes 983048 | tf_op jit(solution)/shard_map/ppermute | solution.py:15
  162.4 4.4 %copy-start.16 = (f32[16,160,128]{2,1,0:T(8,128)S(1)}, f32[16,160,128]{2,1,0:T(8,128)}, u32[]{:S(2)}) copy-start(f32[16,160,128]{2,1,0:T(8,128)} %get-tuple-element.29) | copy-start | bytes 3932164
  170.0 5.6 %collective-permute-start.10 = (f32[1280,128]{1,0:T(8,128)S(1)}, f32[1280,128]{1,0:T(8,128)S(1)}, u32[]{:S(2)}, u32[]{:S(2)}) collective-permute-start(f32[1280,128]{1,0:T(8,128)S(1)} %constant_dynamic-slice_fusion.1), channel_id=1, source_target_pairs={{0,4},{4,0},{8,12},{12,8},{1,5},{5,1},{9,13},{13,9},{2,6},{6,2},{1... | collective-permute-start | bytes 1966088 | tf_op jit(solution)/shard_map/ppermute | solution.py:75
  176.8 9.0 %collective-permute-start.11 = (f32[640,128]{1,0:T(8,128)S(1)}, f32[640,128]{1,0:T(8,128)S(1)}, u32[]{:S(2)}, u32[]{:S(2)}) collective-permute-start(f32[640,128]{1,0:T(8,128)S(1)} %constant_dynamic-slice_fusion), channel_id=1, source_target_pairs={{0,8},{4,12},{8,0},{12,4},{1,9},{5,13},{9,1},{13,5},{2,10},{6,14},... | collective-permute-start | bytes 983048 | tf_op jit(solution)/shard_map/ppermute | solution.py:75
  185.8 8.1 %collective-permute-start.12 = (f32[640,128]{1,0:T(8,128)S(1)}, f32[640,128]{1,0:T(8,128)S(1)}, u32[]{:S(2)}, u32[]{:S(2)}) collective-permute-start(f32[640,128]{1,0:T(8,128)S(1)} %add_multiply_fusion), channel_id=1, source_target_pairs={{0,8},{4,12},{8,0},{12,4},{1,9},{5,13},{9,1},{13,5},{2,10},{6,14},... | collective-permute-start | bytes 983048 | tf_op jit(solution)/shard_map/ppermute | solution.py:81
  193.9 3.9 %collective-permute-start.13 = (f32[1280,128]{1,0:T(8,128)S(1)}, f32[1280,128]{1,0:T(8,128)S(1)}, u32[]{:S(2)}, u32[]{:S(2)}) collective-permute-start(f32[1280,128]{1,0:T(8,128)S(1)} %maximum_select_fusion.1), channel_id=1, source_target_pairs={{0,4},{4,0},{8,12},{12,8},{1,5},{5,1},{9,13},{13,9},{2,6},{6,2},{1... | collective-permute-start | bytes 1966088 | tf_op jit(solution)/shard_map/ppermute | solution.py:81
  (13 other events, 37.9 us)

commit v2 on v1

v2 whole, which is shorter than its diff:
```python
import functools
import jax
import jax.numpy as jnp
from jax import lax
from jax.experimental import pallas as pl
from jax.experimental.pallas import tpu as pltpu
from jax.sharding import PartitionSpec as P

SECOND = (-205.0 / 72.0, 8.0 / 5.0, -1.0 / 5.0, 8.0 / 315.0, -1.0 / 560.0)
FIRST = (4.0 / 5.0, -1.0 / 5.0, 4.0 / 105.0, -1.0 / 280.0)
HALO = 4
PADY = 8


def lane_shift(v, k, lane):
    width = v.shape[-1]
    if k > 0:
        rolled = pltpu.roll(v, width - k, 1)
        return jnp.where(lane < width - k, rolled, 0.0)
    rolled = pltpu.roll(v, -k, 1)
    return jnp.where(lane >= -k, rolled, 0.0)


def fill_padded(pad_ref, lo_ref, mid_ref, hi_ref):
    planes, height, depth = mid_ref.shape
    pad_ref[...] = jnp.zeros(pad_ref.shape, jnp.float32)
    pad_ref[0:HALO, PADY:PADY + height, :] = lo_ref[...]
    pad_ref[HALO:HALO + planes, PADY:PADY + height, :] = mid_ref[...]
    pad_ref[HALO + planes:, PADY:PADY + height, :] = hi_ref[...]


def taps(pad_ref, plane, y0, rows, lane):
    def at(dx, dy):
        return pad_ref[plane + dx, pl.ds(PADY + y0 + dy, rows), :]
    centre = at(0, 0)
    lap = 3.0 * SECOND[0] * centre
    grads = []
    for axis in range(3):
        if axis == 0:
            get = lambda k: at(k, 0)
        elif axis == 1:
            get = lambda k: at(0, k)
        else:
            get = lambda k: lane_shift(centre, k, lane)
        vals = {k: get(k) for k in (1, 2, 3, 4, -1, -2, -3, -4)}
        for k in range(1, 5):
            lap = lap + SECOND[k] * (vals[k] + vals[-k])
        slope = FIRST[0] * (vals[1] - vals[-1])
        for k in range(2, 5):
            slope = slope + FIRST[k - 1] * (vals[k] - vals[-k])
        grads.append(slope)
    return centre, lap, grads


def step_kernel(lo_ref, mid_ref, hi_ref, b_ref, g0_ref, g1_ref, g2_ref, c_ref, old_ref,
                force_ref, new_ref, pad_ref, *, block, rows):
    i = pl.program_id(0)

    @pl.when(i == 0)
    def _():
        fill_padded(pad_ref, lo_ref, mid_ref, hi_ref)

    height = b_ref.shape[1]
    lane = lax.broadcasted_iota(jnp.int32, (rows, b_ref.shape[2]), 1)
    for p in range(block):
        plane = i * block + p + HALO
        for y0 in range(0, height, rows):
            sl = (p, pl.ds(y0, rows), slice(None))
            centre, lap, grads = taps(pad_ref, plane, y0, rows, lane)
            force = b_ref[sl] * lap + (g0_ref[sl] * grads[0] + g1_ref[sl] * grads[1] + g2_ref[sl] * grads[2])
            force_ref[sl] = force
            new_ref[sl] = 2.0 * centre - old_ref[sl] + c_ref[sl] * force


def grad_kernel(lo_ref, mid_ref, hi_ref, g0_ref, g1_ref, g2_ref, pad_ref, *, block, rows):
    i = pl.program_id(0)

    @pl.when(i == 0)
    def _():
        fill_padded(pad_ref, lo_ref, mid_ref, hi_ref)

    height = mid_ref.shape[1]
    lane = lax.broadcasted_iota(jnp.int32, (rows, mid_ref.shape[2]), 1)
    for p in range(block):
        plane = i * block + p + HALO
        for y0 in range(0, height, rows):
            sl = (p, pl.ds(y0, rows), slice(None))
            _, _, grads = taps(pad_ref, plane, y0, rows, lane)
            g0_ref[sl] = grads[0]
            g1_ref[sl] = grads[1]
            g2_ref[sl] = grads[2]


def pick_block(planes):
    for b in (4, 2, 1):
        if planes % b == 0:
            return b


def specs(shape, block):
    planes, height, depth = shape
    full = lambda s: pl.BlockSpec(s, lambda i: (0, 0, 0))
    blk = pl.BlockSpec((block, height, depth), lambda i: (i, 0, 0))
    return full, blk


def apply_step(lo, mid, hi, b, g, c, old, rows=40):
    planes, height, depth = mid.shape
    block = pick_block(planes)
    full, blk = specs(mid.shape, block)
    out = jax.ShapeDtypeStruct(mid.shape, jnp.float32)
    return pl.pallas_call(
        functools.partial(step_kernel, block=block, rows=rows),
        grid=(planes // block,),
        in_specs=[full(lo.shape), full(mid.shape), full(hi.shape)] + [blk] * 6,
        out_specs=[blk, blk],
        out_shape=[out, out],
        scratch_shapes=[pltpu.VMEM((planes + 2 * HALO, height + 2 * PADY, depth), jnp.float32)],
        compiler_params=pltpu.CompilerParams(dimension_semantics=("arbitrary",)),
    )(lo, mid, hi, b, g[0], g[1], g[2], c, old)


def apply_grad(lo, mid, hi, rows=40):
    planes, height, depth = mid.shape
    block = pick_block(planes)
    full, blk = specs(mid.shape, block)
    out = jax.ShapeDtypeStruct(mid.shape, jnp.float32)
    return pl.pallas_call(
        functools.partial(grad_kernel, block=block, rows=rows),
        grid=(planes // block,),
        in_specs=[full(lo.shape), full(mid.shape), full(hi.shape)],
        out_specs=[blk, blk, blk],
        out_shape=[out, out, out],
        scratch_shapes=[pltpu.VMEM((planes + 2 * HALO, height + 2 * PADY, depth), jnp.float32)],
        compiler_params=pltpu.CompilerParams(dimension_semantics=("arbitrary",)),
    )(lo, mid, hi)


def reduce_members(part, axis):
    members = lax.axis_size(axis)
    if members & (members - 1) or part.size % (members * 1024):
        return lax.psum(part, axis) / members
    me = lax.axis_index(axis)
    rows = part.reshape(-1, 128)
    bits = members.bit_length() - 1
    for b in range(bits):
        mask = 1 << b
        half = rows.shape[0] // 2
        upper = (me // mask) % 2
        keep = lax.dynamic_slice_in_dim(rows, upper * half, half, 0)
        give = lax.dynamic_slice_in_dim(rows, (1 - upper) * half, half, 0)
        pairs = [(i, i ^ mask) for i in range(members)]
        rows = keep + lax.ppermute(give, axis, pairs)
    rows = rows / members
    for b in reversed(range(bits)):
        mask = 1 << b
        upper = (me // mask) % 2
        pairs = [(i, i ^ mask) for i in range(members)]
        other = lax.ppermute(rows, axis, pairs)
        rows = jnp.where(upper == 1, jnp.concatenate([other, rows]), jnp.concatenate([rows, other]))
    return rows.reshape(part.shape)


def halos(block, axis):
    count = lax.axis_size(axis)
    forward = [(i, i + 1) for i in range(count - 1)]
    backward = [(target, source) for source, target in forward]
    planes = block.shape[0]
    low = lax.ppermute(block[planes - HALO:], axis, forward)
    high = lax.ppermute(block[:HALO], axis, backward)
    return low, high


def inject(field, where, valid, values):
    flat = field.reshape(-1).at[where].add(jnp.where(valid, values, 0.0))
    return flat.reshape(field.shape)


def shards(
    courant,
    prev_field,
    cur_field,
    adj_prev,
    adj_cur,
    buoyancy,
    wavelet,
    src_cell,
    rec_cell,
    observed,
):
    speed = courant[0]
    planes, height, depth = buoyancy.shape
    volume = planes * height * depth
    offset = lax.axis_index("tile") * volume
    steps = wavelet.shape[0]

    def locate(cells):
        local = cells - offset
        valid = (local >= 0) & (local < volume)
        return (jnp.clip(local, 0, volume - 1), valid)

    src_local, src_valid = locate(src_cell)
    rec_local, rec_valid = locate(rec_cell)
    b_lo, b_hi = halos(buoyancy, "tile")
    grad_b = apply_grad(b_lo, buoyancy, b_hi)
    older, now = (prev_field[0], cur_field[0])
    forces = []
    samples = []
    for k in range(steps):
        lo, hi = halos(now, "tile")
        force, newer = apply_step(lo, now, hi, buoyancy, grad_b, speed, older)
        newer = inject(newer, src_local, src_valid, jnp.full((1,), wavelet[k], jnp.float32))
        samples.append(jnp.where(rec_valid, newer.reshape(-1)[rec_local], 0.0))
        forces.append(force)
        older, now = (now, newer)
    residual = jnp.where(rec_valid, jnp.stack(samples) - observed, 0.0)
    older, now = (adj_prev[0], adj_cur[0])
    image_part = jnp.zeros(buoyancy.shape, jnp.float32)
    for j in range(steps):
        lo, hi = halos(now, "tile")
        _, newer = apply_step(lo, now, hi, buoyancy, grad_b, speed, older)
        newer = inject(newer, rec_local, rec_valid, residual[steps - 1 - j])
        image_part = image_part + newer * forces[steps - 1 - j]
        older, now = (now, newer)
    image = reduce_members(image_part, "real")
    return (image, now[None])


def solution(mesh):
    in_specs = (
        P("real", "tile", None, None),
        P(("shot", "real"), "tile", None, None),
        P(("shot", "real"), "tile", None, None),
        P(("shot", "real"), "tile", None, None),
        P(("shot", "real"), "tile", None, None),
        P("tile", None, None),
        P("shot"),
        P("shot"),
        P("shot"),
        P("shot", None),
    )
    out_specs = (P(("shot", "tile"), None, None), P(("shot", "real"), "tile", None, None))
    return jax.shard_map(shards, mesh=mesh, in_specs=in_specs, out_specs=out_specs, check_vma=False)
```

time: 200 us -> 136 us (0.68)
  other arithmetic: 107 us -> 16.1 us
  Pallas kernels: 0 us -> 39.3 us
  local copies, waits for them, and re-layouts: 25.9 us -> 14.6 us
  starting transfers between devices: 40 us -> 35.9 us
  waiting for transfers between devices: 24.2 us -> 26.5 us
    add x4 -> x0, other arithmetic: 69.6 us -> none  [shards(): newer = 2.0 * now - older + speed * force]
    pallas_call x0 -> x5, Pallas kernels: none -> 39.3 us  [the longest x4 33 us: apply_step(): pl.pallas_call(functools.partial(step_kernel, block=block, rows=rows), gr...]
    concatenate x5 -> x0, other arithmetic: 20 us -> none  [extended(): block = jnp.concatenate([low, block, high], axis=dim)]
    gather x2, local copies, waits for them, and re-layouts: 12.9 us -> 7.72 us  [shards(): samples.append(jnp.where(rec_valid, newer.reshape(-1)[rec_local], 0.0))]
    ppermute x10, starting transfers between devices: 31.3 us -> 27.3 us  [the longest x5 17.3 us: halos(): low = lax.ppermute(block[planes - HALO:], axis, forward)]
    slice x5, local copies, waits for them, and re-layouts: 6.78 us -> 3.48 us  [halos(): high = lax.ppermute(block[:HALO], axis, backward)]
    ppermute x10, waiting for transfers between devices: 6.24 us -> 8.52 us  [the longest x5 5.74 us: halos(): high = lax.ppermute(block[:HALO], axis, backward)]
    unnamed x48 -> x36, local copies, waits for them, and re-layouts: 4.44 us -> 3.3 us
  transfers between devices with their start and end apart: 14 -> 14, of which waited for: 6 -> 6; matrix products, arithmetic and copies ran while one was open for 41% -> 5% of each run, Pallas kernels for 0% -> 17%
where the time goes in v2:
time: 136 us; the launch traced here: 135 us
  Pallas kernels  39.3 us (29%)
  starting transfers between devices  35.9 us (26%)
  waiting for transfers between devices  26.5 us (19%)
  other arithmetic  16.1 us (12%)
  local copies, waits for them, and re-layouts  14.6 us (11%)
  between operations  2.25 us (2%)
    pallas_call x4, Pallas kernels, apply_step(): pl.pallas_call(functools.partial(step_kernel, block=block, rows=rows), gr...  33 us
    ppermute x5, starting transfers between devices, halos(): low = lax.ppermute(block[planes - HALO:], axis, forward)  17.3 us
    scatter-add x4, other arithmetic, inject(): flat = field.reshape(-1).at[where].add(jnp.where(valid, values, 0.0))  12.3 us
    ppermute x5, starting transfers between devices, halos(): high = lax.ppermute(block[:HALO], axis, backward)  9.97 us
    ppermute x2, waiting for transfers between devices, reduce_members(): rows = keep + lax.ppermute(give, axis, pairs)  9.44 us
    ppermute x2, waiting for transfers between devices, reduce_members(): other = lax.ppermute(rows, axis, pairs)  8.52 us
    gather x2, local copies, waits for them, and re-layouts, shards(): samples.append(jnp.where(rec_valid, newer.reshape(-1)[rec_local], 0.0))  7.72 us
    pallas_call x1, Pallas kernels, apply_grad(): pl.pallas_call(functools.partial(grad_kernel, block=block, rows=rows), gr...  6.33 us
  transfers between devices with their start and end apart: 14, of which 6 were waited for; matrix products, arithmetic and copies ran while one was open for 5% of the time, Pallas kernels for 17%

profile of v2, /device:TPU:9, one launch (start us, length us, event | category | flops | bytes accessed | tf_op | source)
XLA Modules:
  0.0 134.6 jit_solution(9521291817665782412)
XLA Ops:
  1.9 3.2 %collective-permute-start.2 = (f32[4,160,128]{2,1,0:T(8,128)S(1)}, f32[4,160,128]{2,1,0:T(8,128)S(1)}, u32[]{:S(2)}, u32[]{:S(2)}) collective-permute-start(f32[4,160,128]{2,1,0:T(8,128)S(1)} %get-tuple-element.53), channel_id=1, source_target_pairs={{0,1},{1,2},{2,3},{4,5},{5,6},{6,7},{8,9},{9,10},{10,11},{12,13},{... | collective-permute-start | bytes 983048 | tf_op jit(solution)/shard_map/ppermute | solution.py:169
  5.2 2.1 %collective-permute-start.3 = (f32[4,160,128]{2,1,0:T(8,128)S(1)}, f32[4,160,128]{2,1,0:T(8,128)}, u32[]{:S(2)}, u32[]{:S(2)}) collective-permute-start(f32[4,160,128]{2,1,0:T(8,128)S(1)} %get-tuple-element.52), channel_id=1, source_target_pairs={{1,0},{2,1},{3,2},{5,4},{6,5},{7,6},{9,8},{10,9},{11,10},{13,12},{... | collective-permute-start | bytes 983048 | tf_op jit(solution)/shard_map/ppermute | solution.py:170
  7.3 3.2 %collective-permute-start.4 = (f32[4,160,128]{2,1,0:T(8,128)S(1)}, f32[4,160,128]{2,1,0:T(8,128)S(1)}, u32[]{:S(2)}, u32[]{:S(2)}) collective-permute-start(f32[4,160,128]{2,1,0:T(8,128)S(1)} %get-tuple-element.51), channel_id=1, source_target_pairs={{0,1},{1,2},{2,3},{4,5},{5,6},{6,7},{8,9},{9,10},{10,11},{12,13},{... | collective-permute-start | bytes 983048 | tf_op jit(solution)/shard_map/ppermute | solution.py:169
  10.5 2.1 %collective-permute-start.5 = (f32[4,160,128]{2,1,0:T(8,128)S(1)}, f32[4,160,128]{2,1,0:T(8,128)S(1)}, u32[]{:S(2)}, u32[]{:S(2)}) collective-permute-start(f32[4,160,128]{2,1,0:T(8,128)S(1)} %get-tuple-element.50), channel_id=1, source_target_pairs={{1,0},{2,1},{3,2},{5,4},{6,5},{7,6},{9,8},{10,9},{11,10},{13,12},{... | collective-permute-start | bytes 983048 | tf_op jit(solution)/shard_map/ppermute | solution.py:170
  12.7 3.7 %collective-permute-start = (f32[4,160,128]{2,1,0:T(8,128)S(1)}, f32[4,160,128]{2,1,0:T(8,128)S(1)}, u32[]{:S(2)}, u32[]{:S(2)}) collective-permute-start(f32[4,160,128]{2,1,0:T(8,128)S(1)} %get-tuple-element.55), channel_id=1, source_target_pairs={{0,1},{1,2},{2,3},{4,5},{5,6},{6,7},{8,9},{9,10},{10,11},{12,13},{... | collective-permute-start | bytes 983048 | tf_op jit(solution)/shard_map/ppermute | solution.py:169
  19.6 6.3 %shard_map.113 = (f32[16,160,128]{2,1,0:T(8,128)}, f32[16,160,128]{2,1,0:T(8,128)}, f32[16,160,128]{2,1,0:T(8,128)}) custom-call(f32[4,160,128]{2,1,0:T(8,128)} %copy-done.14, f32[16,160,128]{2,1,0:T(8,128)} %b_ref.7, f32[4,160,128]{2,1,0:T(8,128)} %collective-permute-done.3.hi_ref), custom_call_target="tpu_custom_call" | custom-call | tf_op jit(solution)/shard_map/pallas_call | solution.py:128
  26.8 8.3 %shard_map.115 = (f32[16,160,128]{2,1,0:T(8,128)}, f32[16,160,128]{2,1,0:T(8,128)}) custom-call(f32[4,160,128]{2,1,0:T(8,128)} %copy-done.8, f32[16,160,128]{2,1,0:T(8,128)} %bitcast.40, f32[4,160,128]{2,1,0:T(8,128)} %copy-done.11, f32[16,160,128]{2,1,0:T(8,128)} %b_ref.7, f32[16,160,128]{2,1,0:T(8,128)} %get-tuple-element.35.g0_ref, ...), custom_call_target="tpu_custom_call" | custom-call | tf_op jit(solution)/shard_map/pallas_call | solution.py:112
  35.0 2.7 %fusion.1 = f32[327680]{0:T(1024)} fusion(f32[327680]{0:T(1024)} %bitcast.44, s32[]{:T(128)} %bitcast.12, s32[1]{0:T(128)} %maximum_minimum_fusion, f32[2]{0:T(128)S(1)} %copy-done.16, s32[1]{0:T(128)S(6)} %copy.16, s32[1]{0:T(128)} %bitcast.11), kind=kLoop, calls=%fused_computation.23 | loop fusion | flops 8 | bytes 2568 | tf_op jit(solution)/shard_map/scatter-add | solution.py:175
  39.8 3.4 %collective-permute-start.6 = (f32[4,160,128]{2,1,0:T(8,128)}, f32[4,160,128]{2,1,0:T(8,128)S(1)}, u32[]{:S(2)}, u32[]{:S(2)}) collective-permute-start(f32[4,160,128]{2,1,0:T(8,128)} %bitcast.14), channel_id=1, source_target_pairs={{0,1},{1,2},{2,3},{4,5},{5,6},{6,7},{8,9},{9,10},{10,11},{12,13},{... | collective-permute-start | bytes 983048 | tf_op jit(solution)/shard_map/ppermute | solution.py:169
  47.7 8.2 %shard_map.114 = (f32[16,160,128]{2,1,0:T(8,128)}, f32[16,160,128]{2,1,0:T(8,128)}) custom-call(f32[4,160,128]{2,1,0:T(8,128)} %copy-done.6, f32[16,160,128]{2,1,0:T(8,128)} %bitcast.42, f32[4,160,128]{2,1,0:T(8,128)} %copy-done.9, f32[16,160,128]{2,1,0:T(8,128)} %b_ref.7, f32[16,160,128]{2,1,0:T(8,128)} %get-tuple-element.35.g0_ref, ...), custom_call_target="tpu_custom_call" | custom-call | tf_op jit(solution)/shard_map/pallas_call | solution.py:112
  56.9 8.3 %shard_map.116 = (f32[16,160,128]{2,1,0:T(8,128)}, f32[16,160,128]{2,1,0:T(8,128)}) custom-call(f32[4,160,128]{2,1,0:T(8,128)} %copy-done.12, f32[16,160,128]{2,1,0:T(8,128)} %bitcast.45, f32[4,160,128]{2,1,0:T(8,128)} %copy-done.13, f32[16,160,128]{2,1,0:T(8,128)} %b_ref.7, f32[16,160,128]{2,1,0:T(8,128)} %get-tuple-element.35.g0_ref, ...), custom_call_target="tpu_custom_call" | custom-call | tf_op jit(solution)/shard_map/pallas_call | solution.py:112
  65.2 2.7 %fusion.2 = f32[327680]{0:T(1024)} fusion(f32[327680]{0:T(1024)} %bitcast.54, s32[]{:T(128)} %bitcast.12, s32[1]{0:T(128)} %maximum_minimum_fusion, f32[2]{0:T(128)S(1)} %copy-done.16, s32[1]{0:T(128)S(6)} %copy.16, s32[1]{0:T(128)} %bitcast.11), kind=kLoop, calls=%fused_computation.24 | loop fusion | flops 8 | bytes 2568 | tf_op jit(solution)/shard_map/scatter-add | solution.py:175
  67.9 6.0 %gather_fusion.1 = f32[256]{0:T(256)S(1)} fusion(f32[327680]{0:T(1024)} %fusion.2, s32[1024]{0:T(1024)S(1)} %pad_clamp_fusion), kind=kCustom, calls=%fused_computation.1 | custom fusion | bytes 3072 | tf_op jit(solution)/shard_map/gather | solution.py:213
  74.0 2.4 %scatter_fusion = f32[327680]{0:T(1024)S(1)} fusion(f32[327680]{0:T(1024)S(1)} %bitcast.37, s32[256]{0:T(256)S(1)} %compare_select_fusion, f32[256]{0:T(256)S(1)} %get-tuple-element.59), kind=kCustom, calls=%fused_computation.2 | custom fusion | flops 256 | bytes 4096 | tf_op jit(solution)/shard_map/scatter-add | solution.py:175
  76.5 3.8 %collective-permute-start.8 = (f32[4,160,128]{2,1,0:T(8,128)S(1)}, f32[4,160,128]{2,1,0:T(8,128)S(1)}, u32[]{:S(2)}, u32[]{:S(2)}) collective-permute-start(f32[4,160,128]{2,1,0:T(8,128)S(1)} %bitcast.56), channel_id=1, source_target_pairs={{0,1},{1,2},{2,3},{4,5},{5,6},{6,7},{8,9},{9,10},{10,11},{12,13},{... | collective-permute-start | bytes 983048 | tf_op jit(solution)/shard_map/ppermute | solution.py:169
  82.3 2.8 %collective-permute-done.8.lo_ref = f32[4,160,128]{2,1,0:T(8,128)S(1)} collective-permute-done((f32[4,160,128]{2,1,0:T(8,128)S(1)}, f32[4,160,128]{2,1,0:T(8,128)S(1)}, u32[]{:S(2)}, u32[]{:S(2)}) %collective-permute-start.8) | collective-permute-done | bytes 327712 | tf_op jit(solution)/shard_map/ppermute | solution.py:169
  85.0 5.7 %collective-permute-done.9.hi_ref = f32[4,160,128]{2,1,0:T(8,128)S(1)} collective-permute-done((f32[4,160,128]{2,1,0:T(8,128)S(1)}, f32[4,160,128]{2,1,0:T(8,128)S(1)}, u32[]{:S(2)}, u32[]{:S(2)}) %collective-permute-start.9) | collective-permute-done | bytes 327712 | tf_op jit(solution)/shard_map/ppermute | solution.py:170
  91.5 8.2 %shard_map.117 = (f32[16,160,128]{2,1,0:T(8,128)}, f32[16,160,128]{2,1,0:T(8,128)}) custom-call(f32[4,160,128]{2,1,0:T(8,128)} %copy-done.7, f32[16,160,128]{2,1,0:T(8,128)} %bitcast.38, f32[4,160,128]{2,1,0:T(8,128)} %copy-done.10, f32[16,160,128]{2,1,0:T(8,128)} %b_ref.7, f32[16,160,128]{2,1,0:T(8,128)} %get-tuple-element.35.g0_ref, ...), custom_call_target="tpu_custom_call" | custom-call | tf_op jit(solution)/shard_map/pallas_call | solution.py:112
  99.7 4.4 %scatter_fusion.1 = f32[327680]{0:T(1024)} fusion(f32[327680]{0:T(1024)} %bitcast.48, s32[256]{0:T(256)S(1)} %compare_select_fusion, f32[256]{0:T(256)S(1)} %get-tuple-element.58), kind=kCustom, calls=%fused_computation.3 | custom fusion | flops 256 | bytes 4096 | tf_op jit(solution)/shard_map/scatter-add | solution.py:175
  104.1 2.5 %multiply_add_fusion = f32[16,160,128]{2,1,0:T(8,128)S(1)} fusion(f32[16,160,128]{2,1,0:T(8,128)} %bitcast.49, f32[16,160,128]{2,1,0:T(8,128)} %get-tuple-element.43, f32[16,160,128]{2,1,0:T(8,128)S(1)} %bitcast.39, f32[16,160,128]{2,1,0:T(8,128)} %get-tuple-element.41), kind=kLoop, calls=%fused_computation.5 | loop fusion | flops 983040 | bytes 6553600 | tf_op jit(solution)/shard_map/add | solution.py:223
  106.6 3.9 %collective-permute-start.10 = (f32[1280,128]{1,0:T(8,128)S(1)}, f32[1280,128]{1,0:T(8,128)S(1)}, u32[]{:S(2)}, u32[]{:S(2)}) collective-permute-start(f32[1280,128]{1,0:T(8,128)S(1)} %constant_dynamic-slice_fusion.1), channel_id=1, source_target_pairs={{0,4},{4,0},{8,12},{12,8},{1,5},{5,1},{9,13},{13,9},{2,6},{6,2},{1... | collective-permute-start | bytes 1966088 | tf_op jit(solution)/shard_map/ppermute | solution.py:153
  113.7 7.7 %collective-permute-done.11 = f32[640,128]{1,0:T(8,128)S(1)} collective-permute-done((f32[640,128]{1,0:T(8,128)S(1)}, f32[640,128]{1,0:T(8,128)S(1)}, u32[]{:S(2)}, u32[]{:S(2)}) %collective-permute-start.11) | collective-permute-done | bytes 327712 | tf_op jit(solution)/shard_map/ppermute | solution.py:153
  122.7 6.8 %collective-permute-done.12 = f32[640,128]{1,0:T(8,128)S(1)} collective-permute-done((f32[640,128]{1,0:T(8,128)S(1)}, f32[640,128]{1,0:T(8,128)S(1)}, u32[]{:S(2)}, u32[]{:S(2)}) %collective-permute-start.12) | collective-permute-done | bytes 327712 | tf_op jit(solution)/shard_map/ppermute | solution.py:159
  129.5 2.2 %collective-permute-start.13 = (f32[1280,128]{1,0:T(8,128)S(1)}, f32[1280,128]{1,0:T(8,128)S(1)}, u32[]{:S(2)}, u32[]{:S(2)}) collective-permute-start(f32[1280,128]{1,0:T(8,128)S(1)} %maximum_select_fusion.1), channel_id=1, source_target_pairs={{0,4},{4,0},{8,12},{12,8},{1,5},{5,1},{9,13},{13,9},{2,6},{6,2},{1... | collective-permute-start | bytes 1966088 | tf_op jit(solution)/shard_map/ppermute | solution.py:159
  (70 shorter events, 21.8 us)
Async XLA Ops:
  0.6 6.6 %copy-start.3 = (f32[1,16,160,128]{3,2,1,0:T(8,128)S(1)}, f32[1,16,160,128]{3,2,1,0:T(8,128)}, u32[]{:S(2)}) copy-start(f32[1,16,160,128]{3,2,1,0:T(8,128)} %param.16) | copy-start | bytes 3932164
  0.6 12.0 %copy-start.4 = (f32[1,16,160,128]{3,2,1,0:T(8,128)S(1)}, f32[1,16,160,128]{3,2,1,0:T(8,128)}, u32[]{:S(2)}) copy-start(f32[1,16,160,128]{3,2,1,0:T(8,128)} %param.18) | copy-start | bytes 3932164
  1.9 15.7 %collective-permute-start.2 = (f32[4,160,128]{2,1,0:T(8,128)S(1)}, f32[4,160,128]{2,1,0:T(8,128)S(1)}, u32[]{:S(2)}, u32[]{:S(2)}) collective-permute-start(f32[4,160,128]{2,1,0:T(8,128)S(1)} %get-tuple-element.53), channel_id=1, source_target_pairs={{0,1},{1,2},{2,3},{4,5},{5,6},{6,7},{8,9},{9,10},{10,11},{12,13},{... | collective-permute-start | bytes 983048 | tf_op jit(solution)/shard_map/ppermute | solution.py:169
  5.1 12.5 %copy-start.15 = (s32[256]{0:T(256)S(1)}, s32[256]{0:T(256)}, u32[]{:S(2)}) copy-start(s32[256]{0:T(256)} %param.22) | copy-start | bytes 3076
  5.2 14.4 %collective-permute-start.3 = (f32[4,160,128]{2,1,0:T(8,128)S(1)}, f32[4,160,128]{2,1,0:T(8,128)}, u32[]{:S(2)}, u32[]{:S(2)}) collective-permute-start(f32[4,160,128]{2,1,0:T(8,128)S(1)} %get-tuple-element.52), channel_id=1, source_target_pairs={{1,0},{2,1},{3,2},{5,4},{6,5},{7,6},{9,8},{10,9},{11,10},{13,12},{... | collective-permute-start | bytes 983048 | tf_op jit(solution)/shard_map/ppermute | solution.py:170
  7.3 18.6 %collective-permute-start.4 = (f32[4,160,128]{2,1,0:T(8,128)S(1)}, f32[4,160,128]{2,1,0:T(8,128)S(1)}, u32[]{:S(2)}, u32[]{:S(2)}) collective-permute-start(f32[4,160,128]{2,1,0:T(8,128)S(1)} %get-tuple-element.51), channel_id=1, source_target_pairs={{0,1},{1,2},{2,3},{4,5},{5,6},{6,7},{8,9},{9,10},{10,11},{12,13},{... | collective-permute-start | bytes 983048 | tf_op jit(solution)/shard_map/ppermute | solution.py:169
  10.5 15.4 %collective-permute-start.5 = (f32[4,160,128]{2,1,0:T(8,128)S(1)}, f32[4,160,128]{2,1,0:T(8,128)S(1)}, u32[]{:S(2)}, u32[]{:S(2)}) collective-permute-start(f32[4,160,128]{2,1,0:T(8,128)S(1)} %get-tuple-element.50), channel_id=1, source_target_pairs={{1,0},{2,1},{3,2},{5,4},{6,5},{7,6},{9,8},{10,9},{11,10},{13,12},{... | collective-permute-start | bytes 983048 | tf_op jit(solution)/shard_map/ppermute | solution.py:170
  12.7 34.2 %collective-permute-start = (f32[4,160,128]{2,1,0:T(8,128)S(1)}, f32[4,160,128]{2,1,0:T(8,128)S(1)}, u32[]{:S(2)}, u32[]{:S(2)}) collective-permute-start(f32[4,160,128]{2,1,0:T(8,128)S(1)} %get-tuple-element.55), channel_id=1, source_target_pairs={{0,1},{1,2},{2,3},{4,5},{5,6},{6,7},{8,9},{9,10},{10,11},{12,13},{... | collective-permute-start | bytes 983048 | tf_op jit(solution)/shard_map/ppermute | solution.py:169
  17.6 29.3 %collective-permute-start.1 = (f32[4,160,128]{2,1,0:T(8,128)S(1)}, f32[4,160,128]{2,1,0:T(8,128)S(1)}, u32[]{:S(2)}, u32[]{:S(2)}) collective-permute-start(f32[4,160,128]{2,1,0:T(8,128)S(1)} %get-tuple-element.54), channel_id=1, source_target_pairs={{1,0},{2,1},{3,2},{5,4},{6,5},{7,6},{9,8},{10,9},{11,10},{13,12},{... | collective-permute-start | bytes 983048 | tf_op jit(solution)/shard_map/ppermute | solution.py:170
  26.8 8.3 %copy-start.16 = (f32[2]{0:T(128)S(1)}, f32[2]{0:T(128)}, u32[]{:S(2)}) copy-start(f32[2]{0:T(128)} %param.20) | copy-start | bytes 28
  37.7 7.4 %copy-start.5 = (f32[327680]{0:T(1024)S(1)}, f32[327680]{0:T(1024)}, u32[]{:S(2)}) copy-start(f32[327680]{0:T(1024)} %fusion.1) | copy-start | bytes 3932164
  39.8 16.1 %collective-permute-start.6 = (f32[4,160,128]{2,1,0:T(8,128)}, f32[4,160,128]{2,1,0:T(8,128)S(1)}, u32[]{:S(2)}, u32[]{:S(2)}) collective-permute-start(f32[4,160,128]{2,1,0:T(8,128)} %bitcast.14), channel_id=1, source_target_pairs={{0,1},{1,2},{2,3},{4,5},{5,6},{6,7},{8,9},{9,10},{10,11},{12,13},{... | collective-permute-start | bytes 983048 | tf_op jit(solution)/shard_map/ppermute | solution.py:169
  43.2 12.8 %collective-permute-start.7 = (f32[4,160,128]{2,1,0:T(8,128)}, f32[4,160,128]{2,1,0:T(8,128)S(1)}, u32[]{:S(2)}, u32[]{:S(2)}) collective-permute-start(f32[4,160,128]{2,1,0:T(8,128)} %bitcast.16), channel_id=1, source_target_pairs={{1,0},{2,1},{3,2},{5,4},{6,5},{7,6},{9,8},{10,9},{11,10},{13,12},{... | collective-permute-start | bytes 983048 | tf_op jit(solution)/shard_map/ppermute | solution.py:170
  56.9 17.1 %copy-start.17 = (f32[2,256]{1,0:T(2,128)S(1)}, f32[2,256]{1,0:T(2,128)}, u32[]{:S(2)}) copy-start(f32[2,256]{1,0:T(2,128)} %param.23) | copy-start | bytes 6148
  56.9 17.1 %copy-start = (f32[16,160,128]{2,1,0:T(8,128)S(1)}, f32[16,160,128]{2,1,0:T(8,128)}, u32[]{:S(2)}) copy-start(f32[16,160,128]{2,1,0:T(8,128)} %get-tuple-element.38) | copy-start | bytes 3932164
  76.4 14.3 %copy-start.1 = (f32[327680]{0:T(1024)}, f32[327680]{0:T(1024)S(1)}, u32[]{:S(2)}) copy-start(f32[327680]{0:T(1024)S(1)} %scatter_fusion) | copy-start | bytes 3932164
  76.5 8.5 %collective-permute-start.8 = (f32[4,160,128]{2,1,0:T(8,128)S(1)}, f32[4,160,128]{2,1,0:T(8,128)S(1)}, u32[]{:S(2)}, u32[]{:S(2)}) collective-permute-start(f32[4,160,128]{2,1,0:T(8,128)S(1)} %bitcast.56), channel_id=1, source_target_pairs={{0,1},{1,2},{2,3},{4,5},{5,6},{6,7},{8,9},{9,10},{10,11},{12,13},{... | collective-permute-start | bytes 983048 | tf_op jit(solution)/shard_map/ppermute | solution.py:169
  80.3 10.5 %collective-permute-start.9 = (f32[4,160,128]{2,1,0:T(8,128)S(1)}, f32[4,160,128]{2,1,0:T(8,128)S(1)}, u32[]{:S(2)}, u32[]{:S(2)}) collective-permute-start(f32[4,160,128]{2,1,0:T(8,128)S(1)} %bitcast.55), channel_id=1, source_target_pairs={{1,0},{2,1},{3,2},{5,4},{6,5},{7,6},{9,8},{10,9},{11,10},{13,12},{... | collective-permute-start | bytes 983048 | tf_op jit(solution)/shard_map/ppermute | solution.py:170
  85.0 5.7 %copy-start.7 = (f32[4,160,128]{2,1,0:T(8,128)}, f32[4,160,128]{2,1,0:T(8,128)S(1)}, u32[]{:S(2)}) copy-start(f32[4,160,128]{2,1,0:T(8,128)S(1)} %collective-permute-done.8.lo_ref) | copy-start | bytes 983044
  99.7 4.4 %copy-start.2 = (f32[327680]{0:T(1024)S(1)}, f32[327680]{0:T(1024)}, u32[]{:S(2)}) copy-start(f32[327680]{0:T(1024)} %copy-done.1) | copy-start | bytes 3932164
  106.6 5.6 %collective-permute-start.10 = (f32[1280,128]{1,0:T(8,128)S(1)}, f32[1280,128]{1,0:T(8,128)S(1)}, u32[]{:S(2)}, u32[]{:S(2)}) collective-permute-start(f32[1280,128]{1,0:T(8,128)S(1)} %constant_dynamic-slice_fusion.1), channel_id=1, source_target_pairs={{0,4},{4,0},{8,12},{12,8},{1,5},{5,1},{9,13},{13,9},{2,6},{6,2},{1... | collective-permute-start | bytes 1966088 | tf_op jit(solution)/shard_map/ppermute | solution.py:153
  112.4 9.0 %collective-permute-start.11 = (f32[640,128]{1,0:T(8,128)S(1)}, f32[640,128]{1,0:T(8,128)S(1)}, u32[]{:S(2)}, u32[]{:S(2)}) collective-permute-start(f32[640,128]{1,0:T(8,128)S(1)} %constant_dynamic-slice_fusion), channel_id=1, source_target_pairs={{0,8},{4,12},{8,0},{12,4},{1,9},{5,13},{9,1},{13,5},{2,10},{6,14},... | collective-permute-start | bytes 983048 | tf_op jit(solution)/shard_map/ppermute | solution.py:153
  121.4 8.1 %collective-permute-start.12 = (f32[640,128]{1,0:T(8,128)S(1)}, f32[640,128]{1,0:T(8,128)S(1)}, u32[]{:S(2)}, u32[]{:S(2)}) collective-permute-start(f32[640,128]{1,0:T(8,128)S(1)} %add_multiply_fusion), channel_id=1, source_target_pairs={{0,8},{4,12},{8,0},{12,4},{1,9},{5,13},{9,1},{13,5},{2,10},{6,14},... | collective-permute-start | bytes 983048 | tf_op jit(solution)/shard_map/ppermute | solution.py:159
  129.5 3.9 %collective-permute-start.13 = (f32[1280,128]{1,0:T(8,128)S(1)}, f32[1280,128]{1,0:T(8,128)S(1)}, u32[]{:S(2)}, u32[]{:S(2)}) collective-permute-start(f32[1280,128]{1,0:T(8,128)S(1)} %maximum_select_fusion.1), channel_id=1, source_target_pairs={{0,4},{4,0},{8,12},{12,8},{1,5},{5,1},{9,13},{13,9},{2,6},{6,2},{1... | collective-permute-start | bytes 1966088 | tf_op jit(solution)/shard_map/ppermute | solution.py:159
  (8 other events, 7.4 us)

commit v3 on v2

--- a/solution.py
+++ b/solution.py
@@ -52,16 +52,28 @@
     return centre, lap, grads
 
 
-def step_kernel(lo_ref, mid_ref, hi_ref, b_ref, g0_ref, g1_ref, g2_ref, c_ref, old_ref,
-                force_ref, new_ref, pad_ref, *, block, rows):
+def step_kernel(*refs, block, rows, inject, edges):
+    lo_ref, mid_ref, hi_ref, b_ref, g0_ref, g1_ref, g2_ref, c_ref, old_ref = refs[:9]
+    refs = refs[9:]
+    if inject:
+        where_ref, amount_ref = refs[:2]
+        refs = refs[2:]
+    force_ref, new_ref = refs[:2]
+    refs = refs[2:]
+    if edges:
+        edge_lo_ref, edge_hi_ref = refs[:2]
+        refs = refs[2:]
+    (pad_ref,) = refs
     i = pl.program_id(0)
 
     @pl.when(i == 0)
     def _():
         fill_padded(pad_ref, lo_ref, mid_ref, hi_ref)
 
+    planes = mid_ref.shape[0]
     height = b_ref.shape[1]
     lane = lax.broadcasted_iota(jnp.int32, (rows, b_ref.shape[2]), 1)
+    row = lax.broadcasted_iota(jnp.int32, (rows, b_ref.shape[2]), 0)
     for p in range(block):
         plane = i * block + p + HALO
         for y0 in range(0, height, rows):
@@ -69,7 +81,22 @@
             centre, lap, grads = taps(pad_ref, plane, y0, rows, lane)
             force = b_ref[sl] * lap + (g0_ref[sl] * grads[0] + g1_ref[sl] * grads[1] + g2_ref[sl] * grads[2])
             force_ref[sl] = force
-            new_ref[sl] = 2.0 * centre - old_ref[sl] + c_ref[sl] * force
+            newer = 2.0 * centre - old_ref[sl] + c_ref[sl] * force
+            if inject:
+                hit = (where_ref[3] == 1) & (where_ref[0] == plane - HALO)
+                mask = hit & (row == where_ref[1] - y0) & (lane == where_ref[2])
+                newer = jnp.where(mask, newer + amount_ref[0], newer)
+            new_ref[sl] = newer
+            if edges:
+                g = plane - HALO
+
+                @pl.when(g < HALO)
+                def _():
+                    edge_lo_ref[pl.ds(g, 1), pl.ds(y0, rows), :] = newer[None]
+
+                @pl.when(g >= planes - HALO)
+                def _():
+                    edge_hi_ref[pl.ds(g - (planes - HALO), 1), pl.ds(y0, rows), :] = newer[None]
 
 
 def grad_kernel(lo_ref, mid_ref, hi_ref, g0_ref, g1_ref, g2_ref, pad_ref, *, block, rows):
@@ -104,31 +131,45 @@
     return full, blk
 
 
-def apply_step(lo, mid, hi, b, g, c, old, rows=40):
+def apply_step(lo, lo_at, mid, hi, hi_at, b, g, c, old, source=None, edges=False, rows=40):
     planes, height, depth = mid.shape
     block = pick_block(planes)
     full, blk = specs(mid.shape, block)
+    halo = lambda at: pl.BlockSpec((HALO, height, depth), lambda i: (at, 0, 0))
     out = jax.ShapeDtypeStruct(mid.shape, jnp.float32)
+    in_specs = [halo(lo_at), full(mid.shape), halo(hi_at)] + [blk] * 6
+    args = [lo, mid, hi, b, g[0], g[1], g[2], c, old]
+    if source is not None:
+        smem = pl.BlockSpec(memory_space=pltpu.SMEM)
+        in_specs += [smem, smem]
+        args += list(source)
+    out_specs = [blk, blk]
+    out_shape = [out, out]
+    if edges:
+        edge = jax.ShapeDtypeStruct((HALO, height, depth), jnp.float32)
+        out_specs += [full(edge.shape), full(edge.shape)]
+        out_shape += [edge, edge]
     return pl.pallas_call(
-        functools.partial(step_kernel, block=block, rows=rows),
+        functools.partial(step_kernel, block=block, rows=rows, inject=source is not None, edges=edges),
         grid=(planes // block,),
-        in_specs=[full(lo.shape), full(mid.shape), full(hi.shape)] + [blk] * 6,
-        out_specs=[blk, blk],
-        out_shape=[out, out],
+        in_specs=in_specs,
+        out_specs=out_specs,
+        out_shape=out_shape,
         scratch_shapes=[pltpu.VMEM((planes + 2 * HALO, height + 2 * PADY, depth), jnp.float32)],
         compiler_params=pltpu.CompilerParams(dimension_semantics=("arbitrary",)),
-    )(lo, mid, hi, b, g[0], g[1], g[2], c, old)
-
-
-def apply_grad(lo, mid, hi, rows=40):
+    )(*args)
+
+
+def apply_grad(lo, lo_at, mid, hi, hi_at, rows=40):
     planes, height, depth = mid.shape
     block = pick_block(planes)
     full, blk = specs(mid.shape, block)
+    halo = lambda at: pl.BlockSpec((HALO, height, depth), lambda i: (at, 0, 0))
     out = jax.ShapeDtypeStruct(mid.shape, jnp.float32)
     return pl.pallas_call(
         functools.partial(grad_kernel, block=block, rows=rows),
         grid=(planes // block,),
-        in_specs=[full(lo.shape), full(mid.shape), full(hi.shape)],
+        in_specs=[halo(lo_at), full(mid.shape), halo(hi_at)],
         out_specs=[blk, blk, blk],
         out_shape=[out, out, out],
         scratch_shapes=[pltpu.VMEM((planes + 2 * HALO, height + 2 * PADY, depth), jnp.float32)],
@@ -161,14 +202,21 @@
     return rows.reshape(part.shape)
 
 
-def halos(block, axis):
+def halos(blocks, axis):
     count = lax.axis_size(axis)
     forward = [(i, i + 1) for i in range(count - 1)]
     backward = [(target, source) for source, target in forward]
-    planes = block.shape[0]
-    low = lax.ppermute(block[planes - HALO:], axis, forward)
-    high = lax.ppermute(block[:HALO], axis, backward)
-    return low, high
+    planes = blocks[0].shape[0]
+    tops = jnp.concatenate([block[planes - HALO:] for block in blocks])
+    bottoms = jnp.concatenate([block[:HALO] for block in blocks])
+    return lax.ppermute(tops, axis, forward), lax.ppermute(bottoms, axis, backward)
+
+
+def edge_halos(low_edge, high_edge, axis):
+    count = lax.axis_size(axis)
+    forward = [(i, i + 1) for i in range(count - 1)]
+    backward = [(target, source) for source, target in forward]
+    return lax.ppermute(high_edge, axis, forward), lax.ppermute(low_edge, axis, backward)
 
 
 def inject(field, where, valid, values):
@@ -201,24 +249,34 @@
 
     src_local, src_valid = locate(src_cell)
     rec_local, rec_valid = locate(rec_cell)
-    b_lo, b_hi = halos(buoyancy, "tile")
-    grad_b = apply_grad(b_lo, buoyancy, b_hi)
+    first_lo, first_hi = halos([buoyancy, cur_field[0], adj_cur[0]], "tile")
+    grad_b = apply_grad(first_lo, 0, buoyancy, first_hi, 0)
+    sx = src_local // (height * depth)
+    sy = (src_local // depth) % height
+    sz = src_local % depth
+    where = jnp.concatenate([sx, sy, sz, src_valid.astype(jnp.int32)])
     older, now = (prev_field[0], cur_field[0])
+    lo, lo_at, hi, hi_at = first_lo, 1, first_hi, 1
     forces = []
     samples = []
     for k in range(steps):
-        lo, hi = halos(now, "tile")
-        force, newer = apply_step(lo, now, hi, buoyancy, grad_b, speed, older)
-        newer = inject(newer, src_local, src_valid, jnp.full((1,), wavelet[k], jnp.float32))
+        source = (where, wavelet[k:k + 1])
+        outs = apply_step(lo, lo_at, now, hi, hi_at, buoyancy, grad_b, speed, older, source, edges=k + 1 < steps)
+        force, newer = outs[:2]
+        if k + 1 < steps:
+            lo, hi = edge_halos(outs[2], outs[3], "tile")
+            lo_at, hi_at = 0, 0
         samples.append(jnp.where(rec_valid, newer.reshape(-1)[rec_local], 0.0))
         forces.append(force)
         older, now = (now, newer)
     residual = jnp.where(rec_valid, jnp.stack(samples) - observed, 0.0)
     older, now = (adj_prev[0], adj_cur[0])
+    lo, lo_at, hi, hi_at = first_lo, 2, first_hi, 2
     image_part = jnp.zeros(buoyancy.shape, jnp.float32)
     for j in range(steps):
-        lo, hi = halos(now, "tile")
-        _, newer = apply_step(lo, now, hi, buoyancy, grad_b, speed, older)
+        if j > 0:
+            (lo, hi), lo_at, hi_at = halos([now], "tile"), 0, 0
+        _, newer = apply_step(lo, lo_at, now, hi, hi_at, buoyancy, grad_b, speed, older)
         newer = inject(newer, rec_local, rec_valid, residual[steps - 1 - j])
         image_part = image_part + newer * forces[steps - 1 - j]
         older, now = (now, newer)

time: 136 us -> 151 us (1.11)
  waiting for transfers between devices: 26.5 us -> 47.3 us
  starting transfers between devices: 35.9 us -> 26.6 us
  Pallas kernels: 39.3 us -> 44.2 us
  other arithmetic: 16.1 us -> 12.4 us
  local copies, waits for them, and re-layouts: 14.6 us -> 17.4 us
    ppermute x10 -> x6, waiting for transfers between devices: 8.52 us -> 29.4 us  [the longest x2 20.1 us: halos(): lax.ppermute(tops, axis, forward)]
    ppermute x10 -> x6, starting transfers between devices: 27.3 us -> 18.7 us  [the longest x2 8.54 us: halos(): lax.ppermute(tops, axis, forward)]
    scatter-add x4 -> x2, other arithmetic: 12.3 us -> 6.83 us  [inject(): flat = field.reshape(-1).at[where].add(jnp.where(valid, values, 0.0))]
    pallas_call x4, Pallas kernels: 33 us -> 37.9 us  [apply_step(): pl.pallas_call(functools.partial(step_kernel, block=block, rows=rows, inj...]
    gather x2, local copies, waits for them, and re-layouts: 7.72 us -> 11.3 us  [shards(): samples.append(jnp.where(rec_valid, newer.reshape(-1)[rec_local], 0.0))]
    concatenate x0 -> x3, other arithmetic: none -> 1.72 us  [the longest x1 1.01 us: halos(): bottoms = jnp.concatenate([block[:HALO] for block in blocks])]
    slice x5 -> x4, local copies, waits for them, and re-layouts: 3.48 us -> 3.04 us  [the longest x3 2.43 us: halos(): bottoms = jnp.concatenate([block[:HALO] for block in blocks])]
    unnamed x36 -> x26, local copies, waits for them, and re-layouts: 3.3 us -> 2.94 us
  transfers between devices with their start and end apart: 14 -> 10, of which waited for: 6 -> 8; matrix products, arithmetic and copies ran while one was open for 5% -> 5% of each run, Pallas kernels for 17% -> 6%
where the time goes in v3:
time: 151 us; the launch traced here: 150 us
  waiting for transfers between devices  47.3 us (31%)
  Pallas kernels  44.2 us (29%)
  starting transfers between devices  26.6 us (18%)
  local copies, waits for them, and re-layouts  17.4 us (12%)
  other arithmetic  12.4 us (8%)
  between operations  1.63 us (1%)
    pallas_call x4, Pallas kernels, apply_step(): pl.pallas_call(functools.partial(step_kernel, block=block, rows=rows, inj...  37.9 us
    ppermute x2, waiting for transfers between devices, halos(): lax.ppermute(tops, axis, forward)  20.1 us
    gather x2, local copies, waits for them, and re-layouts, shards(): samples.append(jnp.where(rec_valid, newer.reshape(-1)[rec_local], 0.0))  11.3 us
    ppermute x2, waiting for transfers between devices, reduce_members(): rows = keep + lax.ppermute(give, axis, pairs)  9.44 us
    ppermute x2, waiting for transfers between devices, halos(): lax.ppermute(bottoms, axis, backward)  9.3 us
    ppermute x2, starting transfers between devices, halos(): lax.ppermute(tops, axis, forward)  8.54 us
    ppermute x2, waiting for transfers between devices, reduce_members(): other = lax.ppermute(rows, axis, pairs)  8.52 us
    scatter-add x2, other arithmetic, inject(): flat = field.reshape(-1).at[where].add(jnp.where(valid, values, 0.0))  6.83 us
  transfers between devices with their start and end apart: 10, of which 8 were waited for; matrix products, arithmetic and copies ran while one was open for 5% of the time, Pallas kernels for 6%

profile of v3, /device:TPU:9, one launch (start us, length us, event | category | flops | bytes accessed | tf_op | source)
XLA Modules:
  0.0 149.6 jit_solution(16347917313543308329)
XLA Ops:
  3.4 3.2 %collective-permute-start = (f32[12,160,128]{2,1,0:T(8,128)S(1)}, f32[12,160,128]{2,1,0:T(8,128)S(1)}, u32[]{:S(2)}, u32[]{:S(2)}) collective-permute-start(f32[12,160,128]{2,1,0:T(8,128)S(1)} %pad_maximum_fusion), channel_id=1, source_target_pairs={{0,1},{1,2},{2,3},{4,5},{5,6},{6,7},{8,9},{9,10},{10,11},{12,13},{... | collective-permute-start | bytes 2949128 | tf_op jit(solution)/shard_map/ppermute | solution.py:212
  7.6 2.1 %collective-permute-start.1 = (f32[12,160,128]{2,1,0:T(8,128)}, f32[12,160,128]{2,1,0:T(8,128)S(1)}, u32[]{:S(2)}, u32[]{:S(2)}) collective-permute-start(f32[12,160,128]{2,1,0:T(8,128)} %pad_maximum_fusion.1), channel_id=1, source_target_pairs={{1,0},{2,1},{3,2},{5,4},{6,5},{7,6},{9,8},{10,9},{11,10},{13,12},{... | collective-permute-start | bytes 2949128 | tf_op jit(solution)/shard_map/ppermute | solution.py:212
  11.7 16.2 %collective-permute-done.lo_ref.refs_0_ = f32[12,160,128]{2,1,0:T(8,128)S(1)} collective-permute-done((f32[12,160,128]{2,1,0:T(8,128)S(1)}, f32[12,160,128]{2,1,0:T(8,128)S(1)}, u32[]{:S(2)}, u32[]{:S(2)}) %collective-permute-start) | collective-permute-done | bytes 983072 | tf_op jit(solution)/shard_map/ppermute | solution.py:212
  27.9 4.1 %collective-permute-done.1.hi_ref.refs_2_ = f32[12,160,128]{2,1,0:T(8,128)S(1)} collective-permute-done((f32[12,160,128]{2,1,0:T(8,128)}, f32[12,160,128]{2,1,0:T(8,128)S(1)}, u32[]{:S(2)}, u32[]{:S(2)}) %collective-permute-start.1) | collective-permute-done | bytes 983072 | tf_op jit(solution)/shard_map/ppermute | solution.py:212
  33.1 6.3 %shard_map.113 = (f32[16,160,128]{2,1,0:T(8,128)}, f32[16,160,128]{2,1,0:T(8,128)}, f32[16,160,128]{2,1,0:T(8,128)}) custom-call(f32[12,160,128]{2,1,0:T(8,128)} %copy-done.3, f32[16,160,128]{2,1,0:T(8,128)} %refs_3_.7, f32[12,160,128]{2,1,0:T(8,128)} %copy-done.4), custom_call_target="tpu_custom_call" | custom-call | tf_op jit(solution)/shard_map/pallas_call | solution.py:169
  39.4 12.3 %shard_map.115 = (f32[16,160,128]{2,1,0:T(8,128)}, f32[16,160,128]{2,1,0:T(8,128)}, f32[4,160,128]{2,1,0:T(8,128)}, f32[4,160,128]{2,1,0:T(8,128)}) custom-call(f32[12,160,128]{2,1,0:T(8,128)} %copy-done.3, f32[16,160,128]{2,1,0:T(8,128)} %bitcast.36, f32[12,160,128]{2,1,0:T(8,128)} %copy-done.4, f32[16,160,128]{2,1,0:T(8,128)} %refs_3_.7, ...), custom_call_target="tpu_custom_call" | custom-call | tf_op jit(solution)/shard_map/pallas_call | solution.py:152
  51.7 3.2 %collective-permute-start.2 = (f32[4,160,128]{2,1,0:T(8,128)}, f32[4,160,128]{2,1,0:T(8,128)S(1)}, u32[]{:S(2)}, u32[]{:S(2)}) collective-permute-start(f32[4,160,128]{2,1,0:T(8,128)} %get-tuple-element.18), channel_id=1, source_target_pairs={{0,1},{1,2},{2,3},{4,5},{5,6},{6,7},{8,9},{9,10},{10,11},{12,13},{... | collective-permute-start | bytes 983048 | tf_op jit(solution)/shard_map/ppermute | solution.py:219
  54.9 2.1 %collective-permute-start.3 = (f32[4,160,128]{2,1,0:T(8,128)}, f32[4,160,128]{2,1,0:T(8,128)S(1)}, u32[]{:S(2)}, u32[]{:S(2)}) collective-permute-start(f32[4,160,128]{2,1,0:T(8,128)} %get-tuple-element.19), channel_id=1, source_target_pairs={{1,0},{2,1},{3,2},{5,4},{6,5},{7,6},{9,8},{10,9},{11,10},{13,12},{... | collective-permute-start | bytes 983048 | tf_op jit(solution)/shard_map/ppermute | solution.py:219
  57.1 5.7 %gather_fusion = f32[256]{0:T(256)S(1)} fusion(f32[327680]{0:T(1024)} %bitcast.42, s32[1024]{0:T(1024)S(1)} %pad_clamp_fusion), kind=kCustom, calls=%fused_computation | custom fusion | bytes 3072 | tf_op jit(solution)/shard_map/gather | solution.py:269
  62.8 8.2 %shard_map.114 = (f32[16,160,128]{2,1,0:T(8,128)}, f32[16,160,128]{2,1,0:T(8,128)}) custom-call(f32[12,160,128]{2,1,0:T(8,128)} %copy-done.3, f32[16,160,128]{2,1,0:T(8,128)} %bitcast.38, f32[12,160,128]{2,1,0:T(8,128)} %copy-done.4, f32[16,160,128]{2,1,0:T(8,128)} %refs_3_.7, f32[16,160,128]{2,1,0:T(8,128)} %get-tuple-element.13.refs_4_, ...), custom_call_target="tpu_custom_call" | custom-call | tf_op jit(solution)/shard_map/pallas_call | solution.py:152
  71.9 9.1 %shard_map.116 = (f32[16,160,128]{2,1,0:T(8,128)}, f32[16,160,128]{2,1,0:T(8,128)}) custom-call(f32[4,160,128]{2,1,0:T(8,128)} %copy-done.8, f32[16,160,128]{2,1,0:T(8,128)} %get-tuple-element.17.refs_1_, f32[4,160,128]{2,1,0:T(8,128)} %copy-done.9, f32[16,160,128]{2,1,0:T(8,128)} %refs_3_.7, f32[16,160,128]{2,1,0:T(8,128)} %get-tuple-element.13.refs_4_, ...), custom_call_target="tpu_custom_call" | custom-call | tf_op jit(solution)/shard_map/pallas_call | solution.py:152
  81.0 5.7 %gather_fusion.1 = f32[256]{0:T(256)S(1)} fusion(f32[327680]{0:T(1024)} %bitcast.49, s32[1024]{0:T(1024)S(1)} %pad_clamp_fusion), kind=kCustom, calls=%fused_computation.1 | custom fusion | bytes 3072 | tf_op jit(solution)/shard_map/gather | solution.py:269
  86.8 2.4 %scatter_fusion = f32[327680]{0:T(1024)S(1)} fusion(f32[327680]{0:T(1024)S(1)} %bitcast.33, s32[256]{0:T(256)S(1)} %compare_select_fusion, f32[256]{0:T(256)S(1)} %get-tuple-element.37), kind=kCustom, calls=%fused_computation.2 | custom fusion | flops 256 | bytes 4096 | tf_op jit(solution)/shard_map/scatter-add | solution.py:223
  89.3 5.3 %collective-permute-start.4 = (f32[4,160,128]{2,1,0:T(8,128)S(1)}, f32[4,160,128]{2,1,0:T(8,128)S(1)}, u32[]{:S(2)}, u32[]{:S(2)}) collective-permute-start(f32[4,160,128]{2,1,0:T(8,128)S(1)} %bitcast.51), channel_id=1, source_target_pairs={{0,1},{1,2},{2,3},{4,5},{5,6},{6,7},{8,9},{9,10},{10,11},{12,13},{... | collective-permute-start | bytes 983048 | tf_op jit(solution)/shard_map/ppermute | solution.py:212
  94.6 2.8 %collective-permute-start.5 = (f32[4,160,128]{2,1,0:T(8,128)S(1)}, f32[4,160,128]{2,1,0:T(8,128)S(1)}, u32[]{:S(2)}, u32[]{:S(2)}) collective-permute-start(f32[4,160,128]{2,1,0:T(8,128)S(1)} %bitcast.50), channel_id=1, source_target_pairs={{1,0},{2,1},{3,2},{5,4},{6,5},{7,6},{9,8},{10,9},{11,10},{13,12},{... | collective-permute-start | bytes 983048 | tf_op jit(solution)/shard_map/ppermute | solution.py:212
  97.5 3.9 %collective-permute-done.4.refs_0_ = f32[4,160,128]{2,1,0:T(8,128)S(1)} collective-permute-done((f32[4,160,128]{2,1,0:T(8,128)S(1)}, f32[4,160,128]{2,1,0:T(8,128)S(1)}, u32[]{:S(2)}, u32[]{:S(2)}) %collective-permute-start.4) | collective-permute-done | bytes 327712 | tf_op jit(solution)/shard_map/ppermute | solution.py:212
  101.4 5.2 %collective-permute-done.5.refs_2_ = f32[4,160,128]{2,1,0:T(8,128)S(1)} collective-permute-done((f32[4,160,128]{2,1,0:T(8,128)S(1)}, f32[4,160,128]{2,1,0:T(8,128)S(1)}, u32[]{:S(2)}, u32[]{:S(2)}) %collective-permute-start.5) | collective-permute-done | bytes 327712 | tf_op jit(solution)/shard_map/ppermute | solution.py:212
  107.3 8.2 %shard_map.117 = (f32[16,160,128]{2,1,0:T(8,128)}, f32[16,160,128]{2,1,0:T(8,128)}) custom-call(f32[4,160,128]{2,1,0:T(8,128)} %copy-done.6, f32[16,160,128]{2,1,0:T(8,128)} %bitcast.34, f32[4,160,128]{2,1,0:T(8,128)} %copy-done.7, f32[16,160,128]{2,1,0:T(8,128)} %refs_3_.7, f32[16,160,128]{2,1,0:T(8,128)} %get-tuple-element.13.refs_4_, ...), custom_call_target="tpu_custom_call" | custom-call | tf_op jit(solution)/shard_map/pallas_call | solution.py:152
  115.5 4.4 %scatter_fusion.1 = f32[327680]{0:T(1024)} fusion(f32[327680]{0:T(1024)} %bitcast.43, s32[256]{0:T(256)S(1)} %compare_select_fusion, f32[256]{0:T(256)S(1)} %get-tuple-element.36), kind=kCustom, calls=%fused_computation.3 | custom fusion | flops 256 | bytes 4096 | tf_op jit(solution)/shard_map/scatter-add | solution.py:223
  119.9 2.5 %multiply_add_fusion = f32[16,160,128]{2,1,0:T(8,128)S(1)} fusion(f32[16,160,128]{2,1,0:T(8,128)} %bitcast.44, f32[16,160,128]{2,1,0:T(8,128)} %get-tuple-element.23, f32[16,160,128]{2,1,0:T(8,128)S(1)} %bitcast.35, f32[16,160,128]{2,1,0:T(8,128)} %get-tuple-element.21), kind=kLoop, calls=%fused_computation.5 | loop fusion | flops 983040 | bytes 6553600 | tf_op jit(solution)/shard_map/add | solution.py:281
  122.4 3.1 %collective-permute-start.6 = (f32[1280,128]{1,0:T(8,128)S(1)}, f32[1280,128]{1,0:T(8,128)S(1)}, u32[]{:S(2)}, u32[]{:S(2)}) collective-permute-start(f32[1280,128]{1,0:T(8,128)S(1)} %constant_dynamic-slice_fusion.1), channel_id=1, source_target_pairs={{0,4},{4,0},{8,12},{12,8},{1,5},{5,1},{9,13},{13,9},{2,6},{6,2},{1... | collective-permute-start | bytes 1966088 | tf_op jit(solution)/shard_map/ppermute | solution.py:194
  128.7 7.7 %collective-permute-done.7 = f32[640,128]{1,0:T(8,128)S(1)} collective-permute-done((f32[640,128]{1,0:T(8,128)S(1)}, f32[640,128]{1,0:T(8,128)S(1)}, u32[]{:S(2)}, u32[]{:S(2)}) %collective-permute-start.7) | collective-permute-done | bytes 327712 | tf_op jit(solution)/shard_map/ppermute | solution.py:194
  137.7 6.8 %collective-permute-done.8 = f32[640,128]{1,0:T(8,128)S(1)} collective-permute-done((f32[640,128]{1,0:T(8,128)S(1)}, f32[640,128]{1,0:T(8,128)S(1)}, u32[]{:S(2)}, u32[]{:S(2)}) %collective-permute-start.8) | collective-permute-done | bytes 327712 | tf_op jit(solution)/shard_map/ppermute | solution.py:200
  144.5 2.2 %collective-permute-start.9 = (f32[1280,128]{1,0:T(8,128)S(1)}, f32[1280,128]{1,0:T(8,128)S(1)}, u32[]{:S(2)}, u32[]{:S(2)}) collective-permute-start(f32[1280,128]{1,0:T(8,128)S(1)} %maximum_select_fusion.1), channel_id=1, source_target_pairs={{0,4},{4,0},{8,12},{12,8},{1,5},{5,1},{9,13},{13,9},{2,6},{6,2},{1... | collective-permute-start | bytes 1966088 | tf_op jit(solution)/shard_map/ppermute | solution.py:200
  (52 shorter events, 15.2 us)
Async XLA Ops:
  0.6 1.5 %copy-start.5 = (f32[1,16,160,128]{3,2,1,0:T(8,128)S(1)}, f32[1,16,160,128]{3,2,1,0:T(8,128)}, u32[]{:S(2)}) copy-start(f32[1,16,160,128]{3,2,1,0:T(8,128)} %param.12) | copy-start | bytes 3932164
  3.4 7.7 %copy-start.12 = (f32[2]{0:T(128)S(1)}, f32[2]{0:T(128)}, u32[]{:S(2)}) copy-start(f32[2]{0:T(128)} %param.16) | copy-start | bytes 28
  3.4 8.3 %copy-start.10 = (s32[256]{0:T(256)S(1)}, s32[256]{0:T(256)}, u32[]{:S(2)}) copy-start(s32[256]{0:T(256)} %param.18) | copy-start | bytes 3076
  3.4 24.5 %collective-permute-start = (f32[12,160,128]{2,1,0:T(8,128)S(1)}, f32[12,160,128]{2,1,0:T(8,128)S(1)}, u32[]{:S(2)}, u32[]{:S(2)}) collective-permute-start(f32[12,160,128]{2,1,0:T(8,128)S(1)} %pad_maximum_fusion), channel_id=1, source_target_pairs={{0,1},{1,2},{2,3},{4,5},{5,6},{6,7},{8,9},{9,10},{10,11},{12,13},{... | collective-permute-start | bytes 2949128 | tf_op jit(solution)/shard_map/ppermute | solution.py:212
  7.6 24.4 %collective-permute-start.1 = (f32[12,160,128]{2,1,0:T(8,128)}, f32[12,160,128]{2,1,0:T(8,128)S(1)}, u32[]{:S(2)}, u32[]{:S(2)}) collective-permute-start(f32[12,160,128]{2,1,0:T(8,128)} %pad_maximum_fusion.1), channel_id=1, source_target_pairs={{1,0},{2,1},{3,2},{5,4},{6,5},{7,6},{9,8},{10,9},{11,10},{13,12},{... | collective-permute-start | bytes 2949128 | tf_op jit(solution)/shard_map/ppermute | solution.py:212
  27.9 4.1 %copy-start.3 = (f32[12,160,128]{2,1,0:T(8,128)}, f32[12,160,128]{2,1,0:T(8,128)S(1)}, u32[]{:S(2)}) copy-start(f32[12,160,128]{2,1,0:T(8,128)S(1)} %collective-permute-done.lo_ref.refs_0_) | copy-start | bytes 2949124
  32.0 1.0 copy-start.4
  51.7 19.3 %collective-permute-start.2 = (f32[4,160,128]{2,1,0:T(8,128)}, f32[4,160,128]{2,1,0:T(8,128)S(1)}, u32[]{:S(2)}, u32[]{:S(2)}) collective-permute-start(f32[4,160,128]{2,1,0:T(8,128)} %get-tuple-element.18), channel_id=1, source_target_pairs={{0,1},{1,2},{2,3},{4,5},{5,6},{6,7},{8,9},{9,10},{10,11},{12,13},{... | collective-permute-start | bytes 983048 | tf_op jit(solution)/shard_map/ppermute | solution.py:219
  54.9 16.1 %collective-permute-start.3 = (f32[4,160,128]{2,1,0:T(8,128)}, f32[4,160,128]{2,1,0:T(8,128)S(1)}, u32[]{:S(2)}, u32[]{:S(2)}) collective-permute-start(f32[4,160,128]{2,1,0:T(8,128)} %get-tuple-element.19), channel_id=1, source_target_pairs={{1,0},{2,1},{3,2},{5,4},{6,5},{7,6},{9,8},{10,9},{11,10},{13,12},{... | collective-permute-start | bytes 983048 | tf_op jit(solution)/shard_map/ppermute | solution.py:219
  71.0 0.8 copy-start.8
  71.0 0.9 copy-start.9
  71.9 14.8 %copy-start.11 = (f32[2,256]{1,0:T(2,128)S(1)}, f32[2,256]{1,0:T(2,128)}, u32[]{:S(2)}) copy-start(f32[2,256]{1,0:T(2,128)} %param.19) | copy-start | bytes 6148
  71.9 14.9 %copy-start = (f32[16,160,128]{2,1,0:T(8,128)S(1)}, f32[16,160,128]{2,1,0:T(8,128)}, u32[]{:S(2)}) copy-start(f32[16,160,128]{2,1,0:T(8,128)} %get-tuple-element.16) | copy-start | bytes 3932164
  89.2 17.3 %copy-start.1 = (f32[327680]{0:T(1024)}, f32[327680]{0:T(1024)S(1)}, u32[]{:S(2)}) copy-start(f32[327680]{0:T(1024)S(1)} %scatter_fusion) | copy-start | bytes 3932164
  89.3 12.1 %collective-permute-start.4 = (f32[4,160,128]{2,1,0:T(8,128)S(1)}, f32[4,160,128]{2,1,0:T(8,128)S(1)}, u32[]{:S(2)}, u32[]{:S(2)}) collective-permute-start(f32[4,160,128]{2,1,0:T(8,128)S(1)} %bitcast.51), channel_id=1, source_target_pairs={{0,1},{1,2},{2,3},{4,5},{5,6},{6,7},{8,9},{9,10},{10,11},{12,13},{... | collective-permute-start | bytes 983048 | tf_op jit(solution)/shard_map/ppermute | solution.py:212
  94.6 11.9 %collective-permute-start.5 = (f32[4,160,128]{2,1,0:T(8,128)S(1)}, f32[4,160,128]{2,1,0:T(8,128)S(1)}, u32[]{:S(2)}, u32[]{:S(2)}) collective-permute-start(f32[4,160,128]{2,1,0:T(8,128)S(1)} %bitcast.50), channel_id=1, source_target_pairs={{1,0},{2,1},{3,2},{5,4},{6,5},{7,6},{9,8},{10,9},{11,10},{13,12},{... | collective-permute-start | bytes 983048 | tf_op jit(solution)/shard_map/ppermute | solution.py:212
  101.4 5.2 %copy-start.6 = (f32[4,160,128]{2,1,0:T(8,128)}, f32[4,160,128]{2,1,0:T(8,128)S(1)}, u32[]{:S(2)}) copy-start(f32[4,160,128]{2,1,0:T(8,128)S(1)} %collective-permute-done.4.refs_0_) | copy-start | bytes 983044
  106.6 0.7 copy-start.7
  115.5 4.4 %copy-start.2 = (f32[327680]{0:T(1024)S(1)}, f32[327680]{0:T(1024)}, u32[]{:S(2)}) copy-start(f32[327680]{0:T(1024)} %copy-done.1) | copy-start | bytes 3932164
  122.4 4.9 %collective-permute-start.6 = (f32[1280,128]{1,0:T(8,128)S(1)}, f32[1280,128]{1,0:T(8,128)S(1)}, u32[]{:S(2)}, u32[]{:S(2)}) collective-permute-start(f32[1280,128]{1,0:T(8,128)S(1)} %constant_dynamic-slice_fusion.1), channel_id=1, source_target_pairs={{0,4},{4,0},{8,12},{12,8},{1,5},{5,1},{9,13},{13,9},{2,6},{6,2},{1... | collective-permute-start | bytes 1966088 | tf_op jit(solution)/shard_map/ppermute | solution.py:194
  127.4 9.0 %collective-permute-start.7 = (f32[640,128]{1,0:T(8,128)S(1)}, f32[640,128]{1,0:T(8,128)S(1)}, u32[]{:S(2)}, u32[]{:S(2)}) collective-permute-start(f32[640,128]{1,0:T(8,128)S(1)} %constant_dynamic-slice_fusion), channel_id=1, source_target_pairs={{0,8},{4,12},{8,0},{12,4},{1,9},{5,13},{9,1},{13,5},{2,10},{6,14},... | collective-permute-start | bytes 983048 | tf_op jit(solution)/shard_map/ppermute | solution.py:194
  136.4 8.1 %collective-permute-start.8 = (f32[640,128]{1,0:T(8,128)S(1)}, f32[640,128]{1,0:T(8,128)S(1)}, u32[]{:S(2)}, u32[]{:S(2)}) collective-permute-start(f32[640,128]{1,0:T(8,128)S(1)} %add_multiply_fusion), channel_id=1, source_target_pairs={{0,8},{4,12},{8,0},{12,4},{1,9},{5,13},{9,1},{13,5},{2,10},{6,14},... | collective-permute-start | bytes 983048 | tf_op jit(solution)/shard_map/ppermute | solution.py:200
  144.5 3.9 %collective-permute-start.9 = (f32[1280,128]{1,0:T(8,128)S(1)}, f32[1280,128]{1,0:T(8,128)S(1)}, u32[]{:S(2)}, u32[]{:S(2)}) collective-permute-start(f32[1280,128]{1,0:T(8,128)S(1)} %maximum_select_fusion.1), channel_id=1, source_target_pairs={{0,4},{4,0},{8,12},{12,8},{1,5},{5,1},{9,13},{13,9},{2,6},{6,2},{1... | collective-permute-start | bytes 1966088 | tf_op jit(solution)/shard_map/ppermute | solution.py:200

commit v4 on v2

--- a/solution.py
+++ b/solution.py
@@ -52,16 +52,24 @@
     return centre, lap, grads
 
 
-def step_kernel(lo_ref, mid_ref, hi_ref, b_ref, g0_ref, g1_ref, g2_ref, c_ref, old_ref,
-                force_ref, new_ref, pad_ref, *, block, rows):
+def step_kernel(*refs, block, rows, track):
+    lo_ref, mid_ref, hi_ref, b_ref, g0_ref, g1_ref, g2_ref, c_ref, old_ref = refs[:9]
+    if track:
+        where_ref, amount_ref, rec_ref = refs[9:12]
+        force_ref, new_ref, edge_lo_ref, edge_hi_ref, sample_ref, pad_ref, keep_ref = refs[12:]
+    else:
+        force_ref, new_ref, pad_ref = refs[9:]
     i = pl.program_id(0)
 
     @pl.when(i == 0)
     def _():
         fill_padded(pad_ref, lo_ref, mid_ref, hi_ref)
 
+    planes = mid_ref.shape[0]
     height = b_ref.shape[1]
-    lane = lax.broadcasted_iota(jnp.int32, (rows, b_ref.shape[2]), 1)
+    depth = b_ref.shape[2]
+    lane = lax.broadcasted_iota(jnp.int32, (rows, depth), 1)
+    row = lax.broadcasted_iota(jnp.int32, (rows, depth), 0)
     for p in range(block):
         plane = i * block + p + HALO
         for y0 in range(0, height, rows):
@@ -69,7 +77,30 @@
             centre, lap, grads = taps(pad_ref, plane, y0, rows, lane)
             force = b_ref[sl] * lap + (g0_ref[sl] * grads[0] + g1_ref[sl] * grads[1] + g2_ref[sl] * grads[2])
             force_ref[sl] = force
-            new_ref[sl] = 2.0 * centre - old_ref[sl] + c_ref[sl] * force
+            newer = 2.0 * centre - old_ref[sl] + c_ref[sl] * force
+            if track:
+                hit = (where_ref[3] == 1) & (where_ref[0] == plane - HALO)
+                mask = hit & (row == where_ref[1] - y0) & (lane == where_ref[2])
+                newer = jnp.where(mask, newer + amount_ref[0], newer)
+                keep_ref[plane - HALO, pl.ds(y0, rows), :] = newer
+            new_ref[sl] = newer
+
+    if track:
+        @pl.when(i == pl.num_programs(0) - 1)
+        def _():
+            edge_lo_ref[...] = keep_ref[0:HALO]
+            edge_hi_ref[...] = keep_ref[planes - HALO:planes]
+            one_lane = lax.broadcasted_iota(jnp.int32, (1, depth), 1)
+
+            def sample(r, carry):
+                x = rec_ref[0, r]
+                y = rec_ref[1, r]
+                z = rec_ref[2, r]
+                line = keep_ref[x, pl.ds(y, 1), :]
+                sample_ref[pl.ds(r, 1), :] = jnp.where(one_lane == z, line, 0.0)
+                return carry
+
+            lax.fori_loop(0, sample_ref.shape[0], sample, 0, unroll=8)
 
 
 def grad_kernel(lo_ref, mid_ref, hi_ref, g0_ref, g1_ref, g2_ref, pad_ref, *, block, rows):
@@ -104,20 +135,35 @@
     return full, blk
 
 
-def apply_step(lo, mid, hi, b, g, c, old, rows=40):
+def apply_step(lo, mid, hi, b, g, c, old, track=None, rows=40):
     planes, height, depth = mid.shape
     block = pick_block(planes)
     full, blk = specs(mid.shape, block)
     out = jax.ShapeDtypeStruct(mid.shape, jnp.float32)
+    in_specs = [full(lo.shape), full(mid.shape), full(hi.shape)] + [blk] * 6
+    args = [lo, mid, hi, b, g[0], g[1], g[2], c, old]
+    out_specs = [blk, blk]
+    out_shape = [out, out]
+    scratch = [pltpu.VMEM((planes + 2 * HALO, height + 2 * PADY, depth), jnp.float32)]
+    if track is not None:
+        smem = pl.BlockSpec(memory_space=pltpu.SMEM)
+        in_specs += [smem, smem, smem]
+        args += list(track)
+        count = track[2].shape[1]
+        edge = jax.ShapeDtypeStruct((HALO, height, depth), jnp.float32)
+        lines = jax.ShapeDtypeStruct((count, depth), jnp.float32)
+        out_specs += [full(edge.shape), full(edge.shape), pl.BlockSpec((count, depth), lambda i: (0, 0))]
+        out_shape += [edge, edge, lines]
+        scratch.append(pltpu.VMEM(mid.shape, jnp.float32))
     return pl.pallas_call(
-        functools.partial(step_kernel, block=block, rows=rows),
+        functools.partial(step_kernel, block=block, rows=rows, track=track is not None),
         grid=(planes // block,),
-        in_specs=[full(lo.shape), full(mid.shape), full(hi.shape)] + [blk] * 6,
-        out_specs=[blk, blk],
-        out_shape=[out, out],
-        scratch_shapes=[pltpu.VMEM((planes + 2 * HALO, height + 2 * PADY, depth), jnp.float32)],
+        in_specs=in_specs,
+        out_specs=out_specs,
+        out_shape=out_shape,
+        scratch_shapes=scratch,
         compiler_params=pltpu.CompilerParams(dimension_semantics=("arbitrary",)),
-    )(lo, mid, hi, b, g[0], g[1], g[2], c, old)
+    )(*args)
 
 
 def apply_grad(lo, mid, hi, rows=40):
@@ -171,6 +217,13 @@
     return low, high
 
 
+def edge_halos(low_edge, high_edge, axis):
+    count = lax.axis_size(axis)
+    forward = [(i, i + 1) for i in range(count - 1)]
+    backward = [(target, source) for source, target in forward]
+    return lax.ppermute(high_edge, axis, forward), lax.ppermute(low_edge, axis, backward)
+
+
 def inject(field, where, valid, values):
     flat = field.reshape(-1).at[where].add(jnp.where(valid, values, 0.0))
     return flat.reshape(field.shape)
@@ -203,14 +256,22 @@
     rec_local, rec_valid = locate(rec_cell)
     b_lo, b_hi = halos(buoyancy, "tile")
     grad_b = apply_grad(b_lo, buoyancy, b_hi)
+
+    def spread(cells):
+        return jnp.stack([cells // (height * depth), (cells // depth) % height, cells % depth])
+
+    where = jnp.concatenate([spread(src_local)[:, 0], src_valid.astype(jnp.int32)])
+    receivers = spread(rec_local)
     older, now = (prev_field[0], cur_field[0])
+    lo, hi = halos(now, "tile")
     forces = []
     samples = []
     for k in range(steps):
-        lo, hi = halos(now, "tile")
-        force, newer = apply_step(lo, now, hi, buoyancy, grad_b, speed, older)
-        newer = inject(newer, src_local, src_valid, jnp.full((1,), wavelet[k], jnp.float32))
-        samples.append(jnp.where(rec_valid, newer.reshape(-1)[rec_local], 0.0))
+        track = (where, wavelet[k:k + 1], receivers)
+        force, newer, edge_lo, edge_hi, lines = apply_step(lo, now, hi, buoyancy, grad_b, speed, older, track)
+        if k + 1 < steps:
+            lo, hi = edge_halos(edge_lo, edge_hi, "tile")
+        samples.append(jnp.sum(lines, axis=1))
         forces.append(force)
         older, now = (now, newer)
     residual = jnp.where(rec_valid, jnp.stack(samples) - observed, 0.0)

time: 136 us -> 127 us (0.934)
  local copies, waits for them, and re-layouts: 14.6 us -> 5.35 us
  Pallas kernels: 39.3 us -> 43.9 us
  waiting for transfers between devices: 26.5 us -> 24.3 us
  other arithmetic: 16.1 us -> 14.1 us
    gather x2 -> x0, local copies, waits for them, and re-layouts: 7.72 us -> none  [shards(): samples.append(jnp.where(rec_valid, newer.reshape(-1)[rec_local], 0.0))]
    scatter-add x4 -> x2, other arithmetic: 12.3 us -> 6.83 us  [inject(): flat = field.reshape(-1).at[where].add(jnp.where(valid, values, 0.0))]
    ppermute x0 -> x2, starting transfers between devices: none -> 5.3 us  [the longest x1 3.38 us: edge_halos(): lax.ppermute(high_edge, axis, forward)]
    pallas_call x4, Pallas kernels: 33 us -> 37.6 us  [apply_step(): pl.pallas_call(functools.partial(step_kernel, block=block, rows=rows, tra...]
    ppermute x5 -> x4, starting transfers between devices: 17.3 us -> 13.5 us  [halos(): low = lax.ppermute(block[planes - HALO:], axis, forward)]
    ppermute x5 -> x4, waiting for transfers between devices: 5.74 us -> 3.12 us  [halos(): high = lax.ppermute(block[:HALO], axis, backward)]
    slice x5 -> x4, local copies, waits for them, and re-layouts: 3.48 us -> 1.4 us  [halos(): high = lax.ppermute(block[:HALO], axis, backward)]
    reduce_sum x0 -> x2, other arithmetic: none -> 2.03 us  [shards(): samples.append(jnp.sum(lines, axis=1))]
  transfers between devices with their start and end apart: 14 -> 14, of which waited for: 6 -> 6; matrix products, arithmetic and copies ran while one was open for 5% -> 2% of each run, Pallas kernels for 17% -> 20%
where the time goes in v4:
time: 127 us; the launch traced here: 125 us
  Pallas kernels  43.9 us (35%)
  starting transfers between devices  35.5 us (28%)
  waiting for transfers between devices  24.3 us (19%)
  other arithmetic  14.1 us (11%)
  local copies, waits for them, and re-layouts  5.35 us (4%)
  between operations  1.76 us (1%)
    pallas_call x4, Pallas kernels, apply_step(): pl.pallas_call(functools.partial(step_kernel, block=block, rows=rows, tra...  37.6 us
    ppermute x4, starting transfers between devices, halos(): low = lax.ppermute(block[planes - HALO:], axis, forward)  13.5 us
    ppermute x2, waiting for transfers between devices, reduce_members(): rows = keep + lax.ppermute(give, axis, pairs)  9.44 us
    ppermute x2, waiting for transfers between devices, reduce_members(): other = lax.ppermute(rows, axis, pairs)  8.52 us
    ppermute x4, starting transfers between devices, halos(): high = lax.ppermute(block[:HALO], axis, backward)  8.03 us
    scatter-add x2, other arithmetic, inject(): flat = field.reshape(-1).at[where].add(jnp.where(valid, values, 0.0))  6.83 us
    pallas_call x1, Pallas kernels, apply_grad(): pl.pallas_call(functools.partial(grad_kernel, block=block, rows=rows), gr...  6.33 us
    ppermute x2, starting transfers between devices, reduce_members(): rows = keep + lax.ppermute(give, axis, pairs)  5.18 us
  transfers between devices with their start and end apart: 14, of which 6 were waited for; matrix products, arithmetic and copies ran while one was open for 2% of the time, Pallas kernels for 20%

profile of v4, /device:TPU:9, one launch (start us, length us, event | category | flops | bytes accessed | tf_op | source)
XLA Modules:
  0.0 124.8 jit_solution(16248870974884290916)
XLA Ops:
  1.9 3.2 %collective-permute-start.2 = (f32[4,160,128]{2,1,0:T(8,128)S(1)}, f32[4,160,128]{2,1,0:T(8,128)S(1)}, u32[]{:S(2)}, u32[]{:S(2)}) collective-permute-start(f32[4,160,128]{2,1,0:T(8,128)S(1)} %get-tuple-element.31), channel_id=1, source_target_pairs={{0,1},{1,2},{2,3},{4,5},{5,6},{6,7},{8,9},{9,10},{10,11},{12,13},{... | collective-permute-start | bytes 983048 | tf_op jit(solution)/shard_map/ppermute | solution.py:215
  5.2 2.1 %collective-permute-start.3 = (f32[4,160,128]{2,1,0:T(8,128)S(1)}, f32[4,160,128]{2,1,0:T(8,128)}, u32[]{:S(2)}, u32[]{:S(2)}) collective-permute-start(f32[4,160,128]{2,1,0:T(8,128)S(1)} %get-tuple-element.30), channel_id=1, source_target_pairs={{1,0},{2,1},{3,2},{5,4},{6,5},{7,6},{9,8},{10,9},{11,10},{13,12},{... | collective-permute-start | bytes 983048 | tf_op jit(solution)/shard_map/ppermute | solution.py:216
  7.3 3.2 %collective-permute-start.4 = (f32[4,160,128]{2,1,0:T(8,128)S(1)}, f32[4,160,128]{2,1,0:T(8,128)S(1)}, u32[]{:S(2)}, u32[]{:S(2)}) collective-permute-start(f32[4,160,128]{2,1,0:T(8,128)S(1)} %get-tuple-element.29), channel_id=1, source_target_pairs={{0,1},{1,2},{2,3},{4,5},{5,6},{6,7},{8,9},{9,10},{10,11},{12,13},{... | collective-permute-start | bytes 983048 | tf_op jit(solution)/shard_map/ppermute | solution.py:215
  10.5 2.1 %collective-permute-start.5 = (f32[4,160,128]{2,1,0:T(8,128)S(1)}, f32[4,160,128]{2,1,0:T(8,128)S(1)}, u32[]{:S(2)}, u32[]{:S(2)}) collective-permute-start(f32[4,160,128]{2,1,0:T(8,128)S(1)} %get-tuple-element.28), channel_id=1, source_target_pairs={{1,0},{2,1},{3,2},{5,4},{6,5},{7,6},{9,8},{10,9},{11,10},{13,12},{... | collective-permute-start | bytes 983048 | tf_op jit(solution)/shard_map/ppermute | solution.py:216
  12.7 3.7 %collective-permute-start = (f32[4,160,128]{2,1,0:T(8,128)S(1)}, f32[4,160,128]{2,1,0:T(8,128)S(1)}, u32[]{:S(2)}, u32[]{:S(2)}) collective-permute-start(f32[4,160,128]{2,1,0:T(8,128)S(1)} %get-tuple-element.33), channel_id=1, source_target_pairs={{0,1},{1,2},{2,3},{4,5},{5,6},{6,7},{8,9},{9,10},{10,11},{12,13},{... | collective-permute-start | bytes 983048 | tf_op jit(solution)/shard_map/ppermute | solution.py:215
  19.1 1.9 %collective-permute-start.1 = (f32[4,160,128]{2,1,0:T(8,128)S(1)}, f32[4,160,128]{2,1,0:T(8,128)S(1)}, u32[]{:S(2)}, u32[]{:S(2)}) collective-permute-start(f32[4,160,128]{2,1,0:T(8,128)S(1)} %get-tuple-element.32), channel_id=1, source_target_pairs={{1,0},{2,1},{3,2},{5,4},{6,5},{7,6},{9,8},{10,9},{11,10},{13,12},{... | collective-permute-start | bytes 983048 | tf_op jit(solution)/shard_map/ppermute | solution.py:216
  21.1 6.3 %shard_map.113 = (f32[16,160,128]{2,1,0:T(8,128)}, f32[16,160,128]{2,1,0:T(8,128)}, f32[16,160,128]{2,1,0:T(8,128)}) custom-call(f32[4,160,128]{2,1,0:T(8,128)} %copy-done.13, f32[16,160,128]{2,1,0:T(8,128)} %refs_3_.7, f32[4,160,128]{2,1,0:T(8,128)} %collective-permute-done.3.hi_ref), custom_call_target="tpu_custom_call" | custom-call | tf_op jit(solution)/shard_map/pallas_call | solution.py:174
  28.2 10.6 %shard_map.115 = (f32[16,160,128]{2,1,0:T(8,128)}, f32[16,160,128]{2,1,0:T(8,128)}, f32[4,160,128]{2,1,0:T(8,128)}, f32[4,160,128]{2,1,0:T(8,128)}, f32[256,128]{1,0:T(8,128)}) custom-call(f32[4,160,128]{2,1,0:T(8,128)} %copy-done.6, f32[16,160,128]{2,1,0:T(8,128)} %bitcast.42, f32[4,160,128]{2,1,0:T(8,128)} %copy-done.7, f32[16,160,128]{2,1,0:T(8,128)} %refs_3_.7, ...), custom_call_target="tpu_custom_call" | custom-call | tf_op jit(solution)/shard_map/pallas_call | solution.py:158
  38.8 3.4 %collective-permute-start.6 = (f32[4,160,128]{2,1,0:T(8,128)}, f32[4,160,128]{2,1,0:T(8,128)S(1)}, u32[]{:S(2)}, u32[]{:S(2)}) collective-permute-start(f32[4,160,128]{2,1,0:T(8,128)} %get-tuple-element.19), channel_id=1, source_target_pairs={{0,1},{1,2},{2,3},{4,5},{5,6},{6,7},{8,9},{9,10},{10,11},{12,13},{... | collective-permute-start | bytes 983048 | tf_op jit(solution)/shard_map/ppermute | solution.py:224
  42.2 1.9 %collective-permute-start.7 = (f32[4,160,128]{2,1,0:T(8,128)}, f32[4,160,128]{2,1,0:T(8,128)S(1)}, u32[]{:S(2)}, u32[]{:S(2)}) collective-permute-start(f32[4,160,128]{2,1,0:T(8,128)} %get-tuple-element.21), channel_id=1, source_target_pairs={{1,0},{2,1},{3,2},{5,4},{6,5},{7,6},{9,8},{10,9},{11,10},{13,12},{... | collective-permute-start | bytes 983048 | tf_op jit(solution)/shard_map/ppermute | solution.py:224
  46.0 8.2 %shard_map.114 = (f32[16,160,128]{2,1,0:T(8,128)}, f32[16,160,128]{2,1,0:T(8,128)}) custom-call(f32[4,160,128]{2,1,0:T(8,128)} %copy-done.5, f32[16,160,128]{2,1,0:T(8,128)} %bitcast.44, f32[4,160,128]{2,1,0:T(8,128)} %copy-done.9, f32[16,160,128]{2,1,0:T(8,128)} %refs_3_.7, f32[16,160,128]{2,1,0:T(8,128)} %get-tuple-element.14.refs_4_, ...), custom_call_target="tpu_custom_call" | custom-call | tf_op jit(solution)/shard_map/pallas_call | solution.py:158
  55.2 10.6 %shard_map.116 = (f32[16,160,128]{2,1,0:T(8,128)}, f32[16,160,128]{2,1,0:T(8,128)}, f32[4,160,128]{2,1,0:T(8,128)}, f32[4,160,128]{2,1,0:T(8,128)}, f32[256,128]{1,0:T(8,128)}) custom-call(f32[4,160,128]{2,1,0:T(8,128)} %copy-done.11, f32[16,160,128]{2,1,0:T(8,128)} %get-tuple-element.20.refs_1_, f32[4,160,128]{2,1,0:T(8,128)} %copy-done.12, ...), custom_call_target="tpu_custom_call" | custom-call | tf_op jit(solution)/shard_map/pallas_call | solution.py:158
  66.8 2.4 %scatter_fusion = f32[327680]{0:T(1024)S(1)} fusion(f32[327680]{0:T(1024)S(1)} %bitcast.39, s32[256]{0:T(256)S(1)} %get-tuple-element.37, f32[256]{0:T(256)S(1)} %get-tuple-element.41), kind=kCustom, calls=%fused_computation | custom fusion | flops 256 | bytes 4096 | tf_op jit(solution)/shard_map/scatter-add | solution.py:228
  69.3 3.4 %collective-permute-start.8 = (f32[4,160,128]{2,1,0:T(8,128)S(1)}, f32[4,160,128]{2,1,0:T(8,128)S(1)}, u32[]{:S(2)}, u32[]{:S(2)}) collective-permute-start(f32[4,160,128]{2,1,0:T(8,128)S(1)} %bitcast.55), channel_id=1, source_target_pairs={{0,1},{1,2},{2,3},{4,5},{5,6},{6,7},{8,9},{9,10},{10,11},{12,13},{... | collective-permute-start | bytes 983048 | tf_op jit(solution)/shard_map/ppermute | solution.py:215
  72.7 1.9 %collective-permute-start.9 = (f32[4,160,128]{2,1,0:T(8,128)S(1)}, f32[4,160,128]{2,1,0:T(8,128)S(1)}, u32[]{:S(2)}, u32[]{:S(2)}) collective-permute-start(f32[4,160,128]{2,1,0:T(8,128)S(1)} %bitcast.54), channel_id=1, source_target_pairs={{1,0},{2,1},{3,2},{5,4},{6,5},{7,6},{9,8},{10,9},{11,10},{13,12},{... | collective-permute-start | bytes 983048 | tf_op jit(solution)/shard_map/ppermute | solution.py:216
  74.7 3.2 %collective-permute-done.8.refs_0_ = f32[4,160,128]{2,1,0:T(8,128)S(1)} collective-permute-done((f32[4,160,128]{2,1,0:T(8,128)S(1)}, f32[4,160,128]{2,1,0:T(8,128)S(1)}, u32[]{:S(2)}, u32[]{:S(2)}) %collective-permute-start.8) | collective-permute-done | bytes 327712 | tf_op jit(solution)/shard_map/ppermute | solution.py:215
  77.9 3.1 %collective-permute-done.9.refs_2_ = f32[4,160,128]{2,1,0:T(8,128)S(1)} collective-permute-done((f32[4,160,128]{2,1,0:T(8,128)S(1)}, f32[4,160,128]{2,1,0:T(8,128)S(1)}, u32[]{:S(2)}, u32[]{:S(2)}) %collective-permute-start.9) | collective-permute-done | bytes 327712 | tf_op jit(solution)/shard_map/ppermute | solution.py:216
  81.7 8.2 %shard_map.117 = (f32[16,160,128]{2,1,0:T(8,128)}, f32[16,160,128]{2,1,0:T(8,128)}) custom-call(f32[4,160,128]{2,1,0:T(8,128)} %copy-done.8, f32[16,160,128]{2,1,0:T(8,128)} %bitcast.40, f32[4,160,128]{2,1,0:T(8,128)} %copy-done.10, f32[16,160,128]{2,1,0:T(8,128)} %refs_3_.7, f32[16,160,128]{2,1,0:T(8,128)} %get-tuple-element.14.refs_4_, ...), custom_call_target="tpu_custom_call" | custom-call | tf_op jit(solution)/shard_map/pallas_call | solution.py:158
  89.9 4.4 %scatter_fusion.1 = f32[327680]{0:T(1024)} fusion(f32[327680]{0:T(1024)} %bitcast.48, s32[256]{0:T(256)S(1)} %get-tuple-element.37, f32[256]{0:T(256)S(1)} %get-tuple-element.40), kind=kCustom, calls=%fused_computation.1 | custom fusion | flops 256 | bytes 4096 | tf_op jit(solution)/shard_map/scatter-add | solution.py:228
  94.3 2.5 %multiply_add_fusion = f32[16,160,128]{2,1,0:T(8,128)S(1)} fusion(f32[16,160,128]{2,1,0:T(8,128)} %bitcast.49, f32[16,160,128]{2,1,0:T(8,128)} %get-tuple-element.25, f32[16,160,128]{2,1,0:T(8,128)S(1)} %bitcast.41, f32[16,160,128]{2,1,0:T(8,128)} %get-tuple-element.23), kind=kLoop, calls=%fused_computation.3 | loop fusion | flops 983040 | bytes 6553600 | tf_op jit(solution)/shard_map/add | solution.py:284
  96.9 3.9 %collective-permute-start.10 = (f32[1280,128]{1,0:T(8,128)S(1)}, f32[1280,128]{1,0:T(8,128)S(1)}, u32[]{:S(2)}, u32[]{:S(2)}) collective-permute-start(f32[1280,128]{1,0:T(8,128)S(1)} %constant_dynamic-slice_fusion.1), channel_id=1, source_target_pairs={{0,4},{4,0},{8,12},{12,8},{1,5},{5,1},{9,13},{13,9},{2,6},{6,2},{1... | collective-permute-start | bytes 1966088 | tf_op jit(solution)/shard_map/ppermute | solution.py:199
  103.9 7.7 %collective-permute-done.11 = f32[640,128]{1,0:T(8,128)S(1)} collective-permute-done((f32[640,128]{1,0:T(8,128)S(1)}, f32[640,128]{1,0:T(8,128)S(1)}, u32[]{:S(2)}, u32[]{:S(2)}) %collective-permute-start.11) | collective-permute-done | bytes 327712 | tf_op jit(solution)/shard_map/ppermute | solution.py:199
  112.9 6.8 %collective-permute-done.12 = f32[640,128]{1,0:T(8,128)S(1)} collective-permute-done((f32[640,128]{1,0:T(8,128)S(1)}, f32[640,128]{1,0:T(8,128)S(1)}, u32[]{:S(2)}, u32[]{:S(2)}) %collective-permute-start.12) | collective-permute-done | bytes 327712 | tf_op jit(solution)/shard_map/ppermute | solution.py:205
  119.7 2.2 %collective-permute-start.13 = (f32[1280,128]{1,0:T(8,128)S(1)}, f32[1280,128]{1,0:T(8,128)S(1)}, u32[]{:S(2)}, u32[]{:S(2)}) collective-permute-start(f32[1280,128]{1,0:T(8,128)S(1)} %maximum_select_fusion.1), channel_id=1, source_target_pairs={{0,4},{4,0},{8,12},{12,8},{1,5},{5,1},{9,13},{13,9},{2,6},{6,2},{1... | collective-permute-start | bytes 1966088 | tf_op jit(solution)/shard_map/ppermute | solution.py:205
  (67 shorter events, 16.1 us)
Async XLA Ops:
  0.6 6.6 %copy-start.3 = (f32[1,16,160,128]{3,2,1,0:T(8,128)S(1)}, f32[1,16,160,128]{3,2,1,0:T(8,128)}, u32[]{:S(2)}) copy-start(f32[1,16,160,128]{3,2,1,0:T(8,128)} %param.12) | copy-start | bytes 3932164
  0.6 12.0 %copy-start.4 = (f32[1,16,160,128]{3,2,1,0:T(8,128)S(1)}, f32[1,16,160,128]{3,2,1,0:T(8,128)}, u32[]{:S(2)}) copy-start(f32[1,16,160,128]{3,2,1,0:T(8,128)} %param.14) | copy-start | bytes 3932164
  1.9 17.2 %collective-permute-start.2 = (f32[4,160,128]{2,1,0:T(8,128)S(1)}, f32[4,160,128]{2,1,0:T(8,128)S(1)}, u32[]{:S(2)}, u32[]{:S(2)}) collective-permute-start(f32[4,160,128]{2,1,0:T(8,128)S(1)} %get-tuple-element.31), channel_id=1, source_target_pairs={{0,1},{1,2},{2,3},{4,5},{5,6},{6,7},{8,9},{9,10},{10,11},{12,13},{... | collective-permute-start | bytes 983048 | tf_op jit(solution)/shard_map/ppermute | solution.py:215
  5.1 12.0 %copy-start.14 = (s32[256]{0:T(256)S(1)}, s32[256]{0:T(256)}, u32[]{:S(2)}) copy-start(s32[256]{0:T(256)} %param.18) | copy-start | bytes 3076
  5.2 13.4 %copy-start.16 = (f32[2]{0:T(128)S(1)}, f32[2]{0:T(128)}, u32[]{:S(2)}) copy-start(f32[2]{0:T(128)} %param.16) | copy-start | bytes 28
  5.2 15.9 %collective-permute-start.3 = (f32[4,160,128]{2,1,0:T(8,128)S(1)}, f32[4,160,128]{2,1,0:T(8,128)}, u32[]{:S(2)}, u32[]{:S(2)}) collective-permute-start(f32[4,160,128]{2,1,0:T(8,128)S(1)} %get-tuple-element.30), channel_id=1, source_target_pairs={{1,0},{2,1},{3,2},{5,4},{6,5},{7,6},{9,8},{10,9},{11,10},{13,12},{... | collective-permute-start | bytes 983048 | tf_op jit(solution)/shard_map/ppermute | solution.py:216
  7.3 20.1 %collective-permute-start.4 = (f32[4,160,128]{2,1,0:T(8,128)S(1)}, f32[4,160,128]{2,1,0:T(8,128)S(1)}, u32[]{:S(2)}, u32[]{:S(2)}) collective-permute-start(f32[4,160,128]{2,1,0:T(8,128)S(1)} %get-tuple-element.29), channel_id=1, source_target_pairs={{0,1},{1,2},{2,3},{4,5},{5,6},{6,7},{8,9},{9,10},{10,11},{12,13},{... | collective-permute-start | bytes 983048 | tf_op jit(solution)/shard_map/ppermute | solution.py:215
  10.5 16.9 %collective-permute-start.5 = (f32[4,160,128]{2,1,0:T(8,128)S(1)}, f32[4,160,128]{2,1,0:T(8,128)S(1)}, u32[]{:S(2)}, u32[]{:S(2)}) collective-permute-start(f32[4,160,128]{2,1,0:T(8,128)S(1)} %get-tuple-element.28), channel_id=1, source_target_pairs={{1,0},{2,1},{3,2},{5,4},{6,5},{7,6},{9,8},{10,9},{11,10},{13,12},{... | collective-permute-start | bytes 983048 | tf_op jit(solution)/shard_map/ppermute | solution.py:216
  12.7 32.5 %collective-permute-start = (f32[4,160,128]{2,1,0:T(8,128)S(1)}, f32[4,160,128]{2,1,0:T(8,128)S(1)}, u32[]{:S(2)}, u32[]{:S(2)}) collective-permute-start(f32[4,160,128]{2,1,0:T(8,128)S(1)} %get-tuple-element.33), channel_id=1, source_target_pairs={{0,1},{1,2},{2,3},{4,5},{5,6},{6,7},{8,9},{9,10},{10,11},{12,13},{... | collective-permute-start | bytes 983048 | tf_op jit(solution)/shard_map/ppermute | solution.py:215
  19.1 1.9 %copy-start.13 = (f32[4,160,128]{2,1,0:T(8,128)}, f32[4,160,128]{2,1,0:T(8,128)S(1)}, u32[]{:S(2)}) copy-start(f32[4,160,128]{2,1,0:T(8,128)S(1)} %collective-permute-done.2.lo_ref) | copy-start | bytes 983044
  19.1 26.1 %collective-permute-start.1 = (f32[4,160,128]{2,1,0:T(8,128)S(1)}, f32[4,160,128]{2,1,0:T(8,128)S(1)}, u32[]{:S(2)}, u32[]{:S(2)}) collective-permute-start(f32[4,160,128]{2,1,0:T(8,128)S(1)} %get-tuple-element.32), channel_id=1, source_target_pairs={{1,0},{2,1},{3,2},{5,4},{6,5},{7,6},{9,8},{10,9},{11,10},{13,12},{... | collective-permute-start | bytes 983048 | tf_op jit(solution)/shard_map/ppermute | solution.py:216
  38.8 15.4 %collective-permute-start.6 = (f32[4,160,128]{2,1,0:T(8,128)}, f32[4,160,128]{2,1,0:T(8,128)S(1)}, u32[]{:S(2)}, u32[]{:S(2)}) collective-permute-start(f32[4,160,128]{2,1,0:T(8,128)} %get-tuple-element.19), channel_id=1, source_target_pairs={{0,1},{1,2},{2,3},{4,5},{5,6},{6,7},{8,9},{9,10},{10,11},{12,13},{... | collective-permute-start | bytes 983048 | tf_op jit(solution)/shard_map/ppermute | solution.py:224
  42.2 12.1 %collective-permute-start.7 = (f32[4,160,128]{2,1,0:T(8,128)}, f32[4,160,128]{2,1,0:T(8,128)S(1)}, u32[]{:S(2)}, u32[]{:S(2)}) collective-permute-start(f32[4,160,128]{2,1,0:T(8,128)} %get-tuple-element.21), channel_id=1, source_target_pairs={{1,0},{2,1},{3,2},{5,4},{6,5},{7,6},{9,8},{10,9},{11,10},{13,12},{... | collective-permute-start | bytes 983048 | tf_op jit(solution)/shard_map/ppermute | solution.py:224
  55.2 11.6 %copy-start.15 = (f32[2,256]{1,0:T(2,128)S(1)}, f32[2,256]{1,0:T(2,128)}, u32[]{:S(2)}) copy-start(f32[2,256]{1,0:T(2,128)} %param.19) | copy-start | bytes 6148
  55.2 11.7 %copy-start = (f32[16,160,128]{2,1,0:T(8,128)S(1)}, f32[16,160,128]{2,1,0:T(8,128)}, u32[]{:S(2)}) copy-start(f32[16,160,128]{2,1,0:T(8,128)} %get-tuple-element.17) | copy-start | bytes 3932164
  69.3 11.7 %copy-start.1 = (f32[327680]{0:T(1024)}, f32[327680]{0:T(1024)S(1)}, u32[]{:S(2)}) copy-start(f32[327680]{0:T(1024)S(1)} %scatter_fusion) | copy-start | bytes 3932164
  69.3 8.5 %collective-permute-start.8 = (f32[4,160,128]{2,1,0:T(8,128)S(1)}, f32[4,160,128]{2,1,0:T(8,128)S(1)}, u32[]{:S(2)}, u32[]{:S(2)}) collective-permute-start(f32[4,160,128]{2,1,0:T(8,128)S(1)} %bitcast.55), channel_id=1, source_target_pairs={{0,1},{1,2},{2,3},{4,5},{5,6},{6,7},{8,9},{9,10},{10,11},{12,13},{... | collective-permute-start | bytes 983048 | tf_op jit(solution)/shard_map/ppermute | solution.py:215
  72.7 8.3 %collective-permute-start.9 = (f32[4,160,128]{2,1,0:T(8,128)S(1)}, f32[4,160,128]{2,1,0:T(8,128)S(1)}, u32[]{:S(2)}, u32[]{:S(2)}) collective-permute-start(f32[4,160,128]{2,1,0:T(8,128)S(1)} %bitcast.54), channel_id=1, source_target_pairs={{1,0},{2,1},{3,2},{5,4},{6,5},{7,6},{9,8},{10,9},{11,10},{13,12},{... | collective-permute-start | bytes 983048 | tf_op jit(solution)/shard_map/ppermute | solution.py:216
  77.9 3.1 %copy-start.8 = (f32[4,160,128]{2,1,0:T(8,128)}, f32[4,160,128]{2,1,0:T(8,128)S(1)}, u32[]{:S(2)}) copy-start(f32[4,160,128]{2,1,0:T(8,128)S(1)} %collective-permute-done.8.refs_0_) | copy-start | bytes 983044
  89.9 4.4 %copy-start.2 = (f32[327680]{0:T(1024)S(1)}, f32[327680]{0:T(1024)}, u32[]{:S(2)}) copy-start(f32[327680]{0:T(1024)} %copy-done.1) | copy-start | bytes 3932164
  96.9 5.6 %collective-permute-start.10 = (f32[1280,128]{1,0:T(8,128)S(1)}, f32[1280,128]{1,0:T(8,128)S(1)}, u32[]{:S(2)}, u32[]{:S(2)}) collective-permute-start(f32[1280,128]{1,0:T(8,128)S(1)} %constant_dynamic-slice_fusion.1), channel_id=1, source_target_pairs={{0,4},{4,0},{8,12},{12,8},{1,5},{5,1},{9,13},{13,9},{2,6},{6,2},{1... | collective-permute-start | bytes 1966088 | tf_op jit(solution)/shard_map/ppermute | solution.py:199
  102.6 9.0 %collective-permute-start.11 = (f32[640,128]{1,0:T(8,128)S(1)}, f32[640,128]{1,0:T(8,128)S(1)}, u32[]{:S(2)}, u32[]{:S(2)}) collective-permute-start(f32[640,128]{1,0:T(8,128)S(1)} %constant_dynamic-slice_fusion), channel_id=1, source_target_pairs={{0,8},{4,12},{8,0},{12,4},{1,9},{5,13},{9,1},{13,5},{2,10},{6,14},... | collective-permute-start | bytes 983048 | tf_op jit(solution)/shard_map/ppermute | solution.py:199
  111.6 8.1 %collective-permute-start.12 = (f32[640,128]{1,0:T(8,128)S(1)}, f32[640,128]{1,0:T(8,128)S(1)}, u32[]{:S(2)}, u32[]{:S(2)}) collective-permute-start(f32[640,128]{1,0:T(8,128)S(1)} %add_multiply_fusion), channel_id=1, source_target_pairs={{0,8},{4,12},{8,0},{12,4},{1,9},{5,13},{9,1},{13,5},{2,10},{6,14},... | collective-permute-start | bytes 983048 | tf_op jit(solution)/shard_map/ppermute | solution.py:205
  119.7 3.9 %collective-permute-start.13 = (f32[1280,128]{1,0:T(8,128)S(1)}, f32[1280,128]{1,0:T(8,128)S(1)}, u32[]{:S(2)}, u32[]{:S(2)}) collective-permute-start(f32[1280,128]{1,0:T(8,128)S(1)} %maximum_select_fusion.1), channel_id=1, source_target_pairs={{0,4},{4,0},{8,12},{12,8},{1,5},{5,1},{9,13},{13,9},{2,6},{6,2},{1... | collective-permute-start | bytes 1966088 | tf_op jit(solution)/shard_map/ppermute | solution.py:205
  (7 other events, 5.4 us)

commit v5 on v4

--- a/solution.py
+++ b/solution.py
@@ -52,22 +52,39 @@
     return centre, lap, grads
 
 
-def step_kernel(*refs, block, rows, track):
-    lo_ref, mid_ref, hi_ref, b_ref, g0_ref, g1_ref, g2_ref, c_ref, old_ref = refs[:9]
+def step_kernel(*refs, block, rows, track, own_grad, want_force):
+    refs = list(refs)
+    take = lambda n: [refs.pop(0) for _ in range(n)]
+    lo_ref, mid_ref, hi_ref = take(3)
+    if own_grad:
+        b_lo_ref, b_mid_ref, b_hi_ref = take(3)
+    else:
+        b_ref, g0_ref, g1_ref, g2_ref = take(4)
+    c_ref, old_ref = take(2)
     if track:
-        where_ref, amount_ref, rec_ref = refs[9:12]
-        force_ref, new_ref, edge_lo_ref, edge_hi_ref, sample_ref, pad_ref, keep_ref = refs[12:]
-    else:
-        force_ref, new_ref, pad_ref = refs[9:]
+        where_ref, amount_ref, rec_ref = take(3)
+    force_ref = take(1)[0] if want_force else None
+    (new_ref,) = take(1)
+    if own_grad:
+        g_out = take(3)
+    if track:
+        edge_lo_ref, edge_hi_ref, sample_ref = take(3)
+    (pad_ref,) = take(1)
+    if own_grad:
+        (b_pad_ref,) = take(1)
+    if track:
+        (keep_ref,) = take(1)
     i = pl.program_id(0)
 
     @pl.when(i == 0)
     def _():
         fill_padded(pad_ref, lo_ref, mid_ref, hi_ref)
+        if own_grad:
+            fill_padded(b_pad_ref, b_lo_ref, b_mid_ref, b_hi_ref)
 
     planes = mid_ref.shape[0]
-    height = b_ref.shape[1]
-    depth = b_ref.shape[2]
+    height = c_ref.shape[1]
+    depth = c_ref.shape[2]
     lane = lax.broadcasted_iota(jnp.int32, (rows, depth), 1)
     row = lax.broadcasted_iota(jnp.int32, (rows, depth), 0)
     for p in range(block):
@@ -75,8 +92,16 @@
         for y0 in range(0, height, rows):
             sl = (p, pl.ds(y0, rows), slice(None))
             centre, lap, grads = taps(pad_ref, plane, y0, rows, lane)
-            force = b_ref[sl] * lap + (g0_ref[sl] * grads[0] + g1_ref[sl] * grads[1] + g2_ref[sl] * grads[2])
-            force_ref[sl] = force
+            if own_grad:
+                bvals, _, gb = taps(b_pad_ref, plane, y0, rows, lane)
+                for out_ref, value in zip(g_out, gb):
+                    out_ref[sl] = value
+            else:
+                bvals = b_ref[sl]
+                gb = [g0_ref[sl], g1_ref[sl], g2_ref[sl]]
+            force = bvals * lap + (gb[0] * grads[0] + gb[1] * grads[1] + gb[2] * grads[2])
+            if want_force:
+                force_ref[sl] = force
             newer = 2.0 * centre - old_ref[sl] + c_ref[sl] * force
             if track:
                 hit = (where_ref[3] == 1) & (where_ref[0] == plane - HALO)
@@ -135,16 +160,32 @@
     return full, blk
 
 
-def apply_step(lo, mid, hi, b, g, c, old, track=None, rows=40):
+def apply_step(lo, mid, hi, b, g, c, old, track=None, rows=40, want_force=True):
     planes, height, depth = mid.shape
     block = pick_block(planes)
     full, blk = specs(mid.shape, block)
     out = jax.ShapeDtypeStruct(mid.shape, jnp.float32)
-    in_specs = [full(lo.shape), full(mid.shape), full(hi.shape)] + [blk] * 6
-    args = [lo, mid, hi, b, g[0], g[1], g[2], c, old]
-    out_specs = [blk, blk]
-    out_shape = [out, out]
+    own_grad = g is None
+    in_specs = [full(lo.shape), full(mid.shape), full(hi.shape)]
+    args = [lo, mid, hi]
+    if own_grad:
+        in_specs += [full(b[0].shape), full(b[1].shape), full(b[2].shape)]
+        args += list(b)
+    else:
+        in_specs += [blk] * 4
+        args += [b, g[0], g[1], g[2]]
+    in_specs += [blk, blk]
+    args += [c, old]
+    out_specs = [blk] if want_force else []
+    out_shape = [out] if want_force else []
+    out_specs.append(blk)
+    out_shape.append(out)
+    if own_grad:
+        out_specs += [blk] * 3
+        out_shape += [out] * 3
     scratch = [pltpu.VMEM((planes + 2 * HALO, height + 2 * PADY, depth), jnp.float32)]
+    if own_grad:
+        scratch.append(pltpu.VMEM((planes + 2 * HALO, height + 2 * PADY, depth), jnp.float32))
     if track is not None:
         smem = pl.BlockSpec(memory_space=pltpu.SMEM)
         in_specs += [smem, smem, smem]
@@ -155,8 +196,11 @@
         out_specs += [full(edge.shape), full(edge.shape), pl.BlockSpec((count, depth), lambda i: (0, 0))]
         out_shape += [edge, edge, lines]
         scratch.append(pltpu.VMEM(mid.shape, jnp.float32))
+    kernel = functools.partial(
+        step_kernel, block=block, rows=rows, track=track is not None, own_grad=own_grad, want_force=want_force
+    )
     return pl.pallas_call(
-        functools.partial(step_kernel, block=block, rows=rows, track=track is not None),
+        kernel,
         grid=(planes // block,),
         in_specs=in_specs,
         out_specs=out_specs,
@@ -255,7 +299,6 @@
     src_local, src_valid = locate(src_cell)
     rec_local, rec_valid = locate(rec_cell)
     b_lo, b_hi = halos(buoyancy, "tile")
-    grad_b = apply_grad(b_lo, buoyancy, b_hi)
 
     def spread(cells):
         return jnp.stack([cells // (height * depth), (cells // depth) % height, cells % depth])
@@ -266,9 +309,16 @@
     lo, hi = halos(now, "tile")
     forces = []
     samples = []
+    grad_b = None
     for k in range(steps):
         track = (where, wavelet[k:k + 1], receivers)
-        force, newer, edge_lo, edge_hi, lines = apply_step(lo, now, hi, buoyancy, grad_b, speed, older, track)
+        if grad_b is None:
+            outs = apply_step(lo, now, hi, (b_lo, buoyancy, b_hi), None, speed, older, track)
+            force, newer = outs[:2]
+            grad_b = outs[2:5]
+            edge_lo, edge_hi, lines = outs[5:]
+        else:
+            force, newer, edge_lo, edge_hi, lines = apply_step(lo, now, hi, buoyancy, grad_b, speed, older, track)
         if k + 1 < steps:
             lo, hi = edge_halos(edge_lo, edge_hi, "tile")
         samples.append(jnp.sum(lines, axis=1))
@@ -279,7 +329,7 @@
     image_part = jnp.zeros(buoyancy.shape, jnp.float32)
     for j in range(steps):
         lo, hi = halos(now, "tile")
-        _, newer = apply_step(lo, now, hi, buoyancy, grad_b, speed, older)
+        (newer,) = apply_step(lo, now, hi, buoyancy, grad_b, speed, older, want_force=False)
         newer = inject(newer, rec_local, rec_valid, residual[steps - 1 - j])
         image_part = image_part + newer * forces[steps - 1 - j]
         older, now = (now, newer)

time: 127 us -> 123 us (0.969)
  Pallas kernels: 43.9 us -> 39.1 us
  waiting for transfers between devices: 24.3 us -> 25.9 us
    pallas_call x5 -> x4, Pallas kernels: 43.9 us -> 39.1 us  [apply_step(): pl.pallas_call(kernel, grid=(planes // block,), in_specs=in_specs, out_sp...]
    unnamed x34 -> x36, local copies, waits for them, and re-layouts: 3.28 us -> 3.18 us
  transfers between devices with their start and end apart: 14 -> 14, of which waited for: 6 -> 7; matrix products, arithmetic and copies ran while one was open for 2% -> 3% of each run, Pallas kernels for 20% -> 17%
where the time goes in v5:
time: 123 us; the launch traced here: 121 us
  Pallas kernels  39.1 us (32%)
  starting transfers between devices  34.5 us (28%)
  waiting for transfers between devices  25.9 us (21%)
  other arithmetic  14 us (11%)
  local copies, waits for them, and re-layouts  6.01 us (5%)
  between operations  1.75 us (1%)
    pallas_call x4, Pallas kernels, apply_step(): pl.pallas_call(kernel, grid=(planes // block,), in_specs=in_specs, out_sp...  39.1 us
    ppermute x4, starting transfers between devices, halos(): low = lax.ppermute(block[planes - HALO:], axis, forward)  12.7 us
    ppermute x2, waiting for transfers between devices, reduce_members(): rows = keep + lax.ppermute(give, axis, pairs)  9.44 us
    ppermute x2, waiting for transfers between devices, reduce_members(): other = lax.ppermute(rows, axis, pairs)  8.52 us
    ppermute x4, starting transfers between devices, halos(): high = lax.ppermute(block[:HALO], axis, backward)  8.44 us
    scatter-add x2, other arithmetic, inject(): flat = field.reshape(-1).at[where].add(jnp.where(valid, values, 0.0))  6.83 us
    ppermute x2, starting transfers between devices, reduce_members(): rows = keep + lax.ppermute(give, axis, pairs)  4.61 us
    ppermute x4, waiting for transfers between devices, halos(): high = lax.ppermute(block[:HALO], axis, backward)  4.19 us
  transfers between devices with their start and end apart: 14, of which 7 were waited for; matrix products, arithmetic and copies ran while one was open for 3% of the time, Pallas kernels for 17%

profile of v5, /device:TPU:9, one launch (start us, length us, event | category | flops | bytes accessed | tf_op | source)
XLA Modules:
  0.0 121.2 jit_solution(3955980253524187343)
XLA Ops:
  1.9 3.2 %collective-permute-start.2 = (f32[4,160,128]{2,1,0:T(8,128)S(1)}, f32[4,160,128]{2,1,0:T(8,128)S(1)}, u32[]{:S(2)}, u32[]{:S(2)}) collective-permute-start(f32[4,160,128]{2,1,0:T(8,128)S(1)} %get-tuple-element.27), channel_id=1, source_target_pairs={{0,1},{1,2},{2,3},{4,5},{5,6},{6,7},{8,9},{9,10},{10,11},{12,13},{... | collective-permute-start | bytes 983048 | tf_op jit(solution)/shard_map/ppermute | solution.py:259
  5.2 2.1 %collective-permute-start.3 = (f32[4,160,128]{2,1,0:T(8,128)S(1)}, f32[4,160,128]{2,1,0:T(8,128)S(1)}, u32[]{:S(2)}, u32[]{:S(2)}) collective-permute-start(f32[4,160,128]{2,1,0:T(8,128)S(1)} %get-tuple-element.26), channel_id=1, source_target_pairs={{1,0},{2,1},{3,2},{5,4},{6,5},{7,6},{9,8},{10,9},{11,10},{13,12},{... | collective-permute-start | bytes 983048 | tf_op jit(solution)/shard_map/ppermute | solution.py:260
  8.0 3.2 %collective-permute-start.4 = (f32[4,160,128]{2,1,0:T(8,128)}, f32[4,160,128]{2,1,0:T(8,128)S(1)}, u32[]{:S(2)}, u32[]{:S(2)}) collective-permute-start(f32[4,160,128]{2,1,0:T(8,128)} %get-tuple-element.25), channel_id=1, source_target_pairs={{0,1},{1,2},{2,3},{4,5},{5,6},{6,7},{8,9},{9,10},{10,11},{12,13},{... | collective-permute-start | bytes 983048 | tf_op jit(solution)/shard_map/ppermute | solution.py:259
  11.2 2.1 %collective-permute-start.5 = (f32[4,160,128]{2,1,0:T(8,128)S(1)}, f32[4,160,128]{2,1,0:T(8,128)S(1)}, u32[]{:S(2)}, u32[]{:S(2)}) collective-permute-start(f32[4,160,128]{2,1,0:T(8,128)S(1)} %get-tuple-element.24), channel_id=1, source_target_pairs={{1,0},{2,1},{3,2},{5,4},{6,5},{7,6},{9,8},{10,9},{11,10},{13,12},{... | collective-permute-start | bytes 983048 | tf_op jit(solution)/shard_map/ppermute | solution.py:260
  13.4 3.2 %collective-permute-start = (f32[4,160,128]{2,1,0:T(8,128)S(1)}, f32[4,160,128]{2,1,0:T(8,128)S(1)}, u32[]{:S(2)}, u32[]{:S(2)}) collective-permute-start(f32[4,160,128]{2,1,0:T(8,128)S(1)} %get-tuple-element.29), channel_id=1, source_target_pairs={{0,1},{1,2},{2,3},{4,5},{5,6},{6,7},{8,9},{9,10},{10,11},{12,13},{... | collective-permute-start | bytes 983048 | tf_op jit(solution)/shard_map/ppermute | solution.py:259
  19.3 2.1 %collective-permute-start.1 = (f32[4,160,128]{2,1,0:T(8,128)S(1)}, f32[4,160,128]{2,1,0:T(8,128)S(1)}, u32[]{:S(2)}, u32[]{:S(2)}) collective-permute-start(f32[4,160,128]{2,1,0:T(8,128)S(1)} %get-tuple-element.28), channel_id=1, source_target_pairs={{1,0},{2,1},{3,2},{5,4},{6,5},{7,6},{9,8},{10,9},{11,10},{13,12},{... | collective-permute-start | bytes 983048 | tf_op jit(solution)/shard_map/ppermute | solution.py:260
  23.5 12.5 %shard_map.113 = (f32[16,160,128]{2,1,0:T(8,128)}, f32[16,160,128]{2,1,0:T(8,128)}, f32[16,160,128]{2,1,0:T(8,128)}, f32[16,160,128]{2,1,0:T(8,128)}, f32[16,160...) custom-call(f32[4,160,128]{2,1,0:T(8,128)} %copy-done.6, ...), custom_call_target="tpu_custom_call" | custom-call | tf_op jit(solution)/shard_map/pallas_call | solution.py:202
  35.9 3.2 %collective-permute-start.6 = (f32[4,160,128]{2,1,0:T(8,128)}, f32[4,160,128]{2,1,0:T(8,128)S(1)}, u32[]{:S(2)}, u32[]{:S(2)}) collective-permute-start(f32[4,160,128]{2,1,0:T(8,128)} %get-tuple-element.16), channel_id=1, source_target_pairs={{0,1},{1,2},{2,3},{4,5},{5,6},{6,7},{8,9},{9,10},{10,11},{12,13},{... | collective-permute-start | bytes 983048 | tf_op jit(solution)/shard_map/ppermute | solution.py:268
  39.1 2.1 %collective-permute-start.7 = (f32[4,160,128]{2,1,0:T(8,128)}, f32[4,160,128]{2,1,0:T(8,128)S(1)}, u32[]{:S(2)}, u32[]{:S(2)}) collective-permute-start(f32[4,160,128]{2,1,0:T(8,128)} %get-tuple-element.18), channel_id=1, source_target_pairs={{1,0},{2,1},{3,2},{5,4},{6,5},{7,6},{9,8},{10,9},{11,10},{13,12},{... | collective-permute-start | bytes 983048 | tf_op jit(solution)/shard_map/ppermute | solution.py:268
  43.1 8.0 %shard_map.114 = f32[16,160,128]{2,1,0:T(8,128)} custom-call(f32[4,160,128]{2,1,0:T(8,128)} %copy-done.5, f32[16,160,128]{2,1,0:T(8,128)} %bitcast.47, f32[4,160,128]{2,1,0:T(8,128)} %copy-done.12, f32[16,160,128]{2,1,0:T(8,128)} %refs_3_.5, f32[16,160,128]{2,1,0:T(8,128)} %get-tuple-element.12.refs_4_, f32[16,160,128]{2,1,0:T(8,128)} %get-tuple-element.13.refs_5_, ...), custom_call_target="tpu_custom_call" | custom-call | tf_op jit(solution)/shard_map/pallas_call | solution.py:202
  52.0 10.7 %shard_map.115 = (f32[16,160,128]{2,1,0:T(8,128)}, f32[16,160,128]{2,1,0:T(8,128)}, f32[4,160,128]{2,1,0:T(8,128)}, f32[4,160,128]{2,1,0:T(8,128)}, f32[256,128]{1,0:T(8,128)}) custom-call(f32[4,160,128]{2,1,0:T(8,128)} %copy-done.13, f32[16,160,128]{2,1,0:T(8,128)} %get-tuple-element.17.refs_1_, f32[4,160,128]{2,1,0:T(8,128)} %copy-done.14, ...), custom_call_target="tpu_custom_call" | custom-call | tf_op jit(solution)/shard_map/pallas_call | solution.py:202
  63.8 2.4 %scatter_fusion = f32[327680]{0:T(1024)S(1)} fusion(f32[327680]{0:T(1024)S(1)} %bitcast.35, s32[256]{0:T(256)S(1)} %get-tuple-element.32, f32[256]{0:T(256)S(1)} %get-tuple-element.37), kind=kCustom, calls=%fused_computation | custom fusion | flops 256 | bytes 4096 | tf_op jit(solution)/shard_map/scatter-add | solution.py:272
  66.3 3.2 %collective-permute-start.8 = (f32[4,160,128]{2,1,0:T(8,128)S(1)}, f32[4,160,128]{2,1,0:T(8,128)S(1)}, u32[]{:S(2)}, u32[]{:S(2)}) collective-permute-start(f32[4,160,128]{2,1,0:T(8,128)S(1)} %bitcast.55), channel_id=1, source_target_pairs={{0,1},{1,2},{2,3},{4,5},{5,6},{6,7},{8,9},{9,10},{10,11},{12,13},{... | collective-permute-start | bytes 983048 | tf_op jit(solution)/shard_map/ppermute | solution.py:259
  69.5 2.1 %collective-permute-start.9 = (f32[4,160,128]{2,1,0:T(8,128)S(1)}, f32[4,160,128]{2,1,0:T(8,128)S(1)}, u32[]{:S(2)}, u32[]{:S(2)}) collective-permute-start(f32[4,160,128]{2,1,0:T(8,128)S(1)} %bitcast.54), channel_id=1, source_target_pairs={{1,0},{2,1},{3,2},{5,4},{6,5},{7,6},{9,8},{10,9},{11,10},{13,12},{... | collective-permute-start | bytes 983048 | tf_op jit(solution)/shard_map/ppermute | solution.py:260
  71.6 3.7 %collective-permute-done.8.refs_0_ = f32[4,160,128]{2,1,0:T(8,128)S(1)} collective-permute-done((f32[4,160,128]{2,1,0:T(8,128)S(1)}, f32[4,160,128]{2,1,0:T(8,128)S(1)}, u32[]{:S(2)}, u32[]{:S(2)}) %collective-permute-start.8) | collective-permute-done | bytes 327712 | tf_op jit(solution)/shard_map/ppermute | solution.py:259
  75.4 2.9 %collective-permute-done.9.refs_2_ = f32[4,160,128]{2,1,0:T(8,128)S(1)} collective-permute-done((f32[4,160,128]{2,1,0:T(8,128)S(1)}, f32[4,160,128]{2,1,0:T(8,128)S(1)}, u32[]{:S(2)}, u32[]{:S(2)}) %collective-permute-start.9) | collective-permute-done | bytes 327712 | tf_op jit(solution)/shard_map/ppermute | solution.py:260
  79.0 7.9 %shard_map.116 = f32[16,160,128]{2,1,0:T(8,128)} custom-call(f32[4,160,128]{2,1,0:T(8,128)} %copy-done.10, f32[16,160,128]{2,1,0:T(8,128)} %bitcast.36, f32[4,160,128]{2,1,0:T(8,128)} %copy-done.11, f32[16,160,128]{2,1,0:T(8,128)} %refs_3_.5, f32[16,160,128]{2,1,0:T(8,128)} %get-tuple-element.12.refs_4_, f32[16,160,128]{2,1,0:T(8,128)} %get-tuple-element.13.refs_5_, ...), custom_call_target="tpu_custom_call" | custom-call | tf_op jit(solution)/shard_map/pallas_call | solution.py:202
  86.9 4.4 %scatter_fusion.1 = f32[327680]{0:T(1024)} fusion(f32[327680]{0:T(1024)} %bitcast.42, s32[256]{0:T(256)S(1)} %get-tuple-element.32, f32[256]{0:T(256)S(1)} %get-tuple-element.36), kind=kCustom, calls=%fused_computation.1 | custom fusion | flops 256 | bytes 4096 | tf_op jit(solution)/shard_map/scatter-add | solution.py:272
  91.3 2.5 %multiply_add_fusion = f32[16,160,128]{2,1,0:T(8,128)S(1)} fusion(f32[16,160,128]{2,1,0:T(8,128)} %bitcast.43, f32[16,160,128]{2,1,0:T(8,128)} %get-tuple-element.21, f32[16,160,128]{2,1,0:T(8,128)S(1)} %bitcast.37, f32[16,160,128]{2,1,0:T(8,128)} %get-tuple-element.20), kind=kLoop, calls=%fused_computation.3 | loop fusion | flops 983040 | bytes 6553600 | tf_op jit(solution)/shard_map/add | solution.py:334
  93.8 3.3 %collective-permute-start.10 = (f32[1280,128]{1,0:T(8,128)S(1)}, f32[1280,128]{1,0:T(8,128)S(1)}, u32[]{:S(2)}, u32[]{:S(2)}) collective-permute-start(f32[1280,128]{1,0:T(8,128)S(1)} %constant_dynamic-slice_fusion.1), channel_id=1, source_target_pairs={{0,4},{4,0},{8,12},{12,8},{1,5},{5,1},{9,13},{13,9},{2,6},{6,2},{1... | collective-permute-start | bytes 1966088 | tf_op jit(solution)/shard_map/ppermute | solution.py:243
  100.2 7.7 %collective-permute-done.11 = f32[640,128]{1,0:T(8,128)S(1)} collective-permute-done((f32[640,128]{1,0:T(8,128)S(1)}, f32[640,128]{1,0:T(8,128)S(1)}, u32[]{:S(2)}, u32[]{:S(2)}) %collective-permute-start.11) | collective-permute-done | bytes 327712 | tf_op jit(solution)/shard_map/ppermute | solution.py:243
  109.3 6.8 %collective-permute-done.12 = f32[640,128]{1,0:T(8,128)S(1)} collective-permute-done((f32[640,128]{1,0:T(8,128)S(1)}, f32[640,128]{1,0:T(8,128)S(1)}, u32[]{:S(2)}, u32[]{:S(2)}) %collective-permute-start.12) | collective-permute-done | bytes 327712 | tf_op jit(solution)/shard_map/ppermute | solution.py:249
  116.1 2.2 %collective-permute-start.13 = (f32[1280,128]{1,0:T(8,128)S(1)}, f32[1280,128]{1,0:T(8,128)S(1)}, u32[]{:S(2)}, u32[]{:S(2)}) collective-permute-start(f32[1280,128]{1,0:T(8,128)S(1)} %maximum_select_fusion.1), channel_id=1, source_target_pairs={{0,4},{4,0},{8,12},{12,8},{1,5},{5,1},{9,13},{13,9},{2,6},{6,2},{1... | collective-permute-start | bytes 1966088 | tf_op jit(solution)/shard_map/ppermute | solution.py:249
  118.3 1.7 %collective-permute-done.13 = f32[1280,128]{1,0:T(8,128)S(1)} collective-permute-done((f32[1280,128]{1,0:T(8,128)S(1)}, f32[1280,128]{1,0:T(8,128)S(1)}, u32[]{:S(2)}, u32[]{:S(2)}) %collective-permute-start.13) | collective-permute-done | bytes 655392 | tf_op jit(solution)/shard_map/ppermute | solution.py:249
  (68 shorter events, 16.3 us)
Async XLA Ops:
  0.6 6.6 %copy-start = (f32[16,160,128]{2,1,0:T(8,128)S(1)}, f32[16,160,128]{2,1,0:T(8,128)}, u32[]{:S(2)}) copy-start(f32[16,160,128]{2,1,0:T(8,128)} %refs_3_.5) | copy-start | bytes 3932164
  0.6 12.7 %copy-start.4 = (f32[1,16,160,128]{3,2,1,0:T(8,128)S(1)}, f32[1,16,160,128]{3,2,1,0:T(8,128)}, u32[]{:S(2)}) copy-start(f32[1,16,160,128]{3,2,1,0:T(8,128)} %param.14) | copy-start | bytes 3932164
  1.9 17.3 %collective-permute-start.2 = (f32[4,160,128]{2,1,0:T(8,128)S(1)}, f32[4,160,128]{2,1,0:T(8,128)S(1)}, u32[]{:S(2)}, u32[]{:S(2)}) collective-permute-start(f32[4,160,128]{2,1,0:T(8,128)S(1)} %get-tuple-element.27), channel_id=1, source_target_pairs={{0,1},{1,2},{2,3},{4,5},{5,6},{6,7},{8,9},{9,10},{10,11},{12,13},{... | collective-permute-start | bytes 983048 | tf_op jit(solution)/shard_map/ppermute | solution.py:259
  5.1 12.2 %copy-start.15 = (s32[256]{0:T(256)S(1)}, s32[256]{0:T(256)}, u32[]{:S(2)}) copy-start(s32[256]{0:T(256)} %param.18) | copy-start | bytes 3076
  5.2 13.5 %copy-start.17 = (f32[2]{0:T(128)S(1)}, f32[2]{0:T(128)}, u32[]{:S(2)}) copy-start(f32[2]{0:T(128)} %param.16) | copy-start | bytes 28
  5.2 16.2 %collective-permute-start.3 = (f32[4,160,128]{2,1,0:T(8,128)S(1)}, f32[4,160,128]{2,1,0:T(8,128)S(1)}, u32[]{:S(2)}, u32[]{:S(2)}) collective-permute-start(f32[4,160,128]{2,1,0:T(8,128)S(1)} %get-tuple-element.26), channel_id=1, source_target_pairs={{1,0},{2,1},{3,2},{5,4},{6,5},{7,6},{9,8},{10,9},{11,10},{13,12},{... | collective-permute-start | bytes 983048 | tf_op jit(solution)/shard_map/ppermute | solution.py:260
  8.0 13.4 %collective-permute-start.4 = (f32[4,160,128]{2,1,0:T(8,128)}, f32[4,160,128]{2,1,0:T(8,128)S(1)}, u32[]{:S(2)}, u32[]{:S(2)}) collective-permute-start(f32[4,160,128]{2,1,0:T(8,128)} %get-tuple-element.25), channel_id=1, source_target_pairs={{0,1},{1,2},{2,3},{4,5},{5,6},{6,7},{8,9},{9,10},{10,11},{12,13},{... | collective-permute-start | bytes 983048 | tf_op jit(solution)/shard_map/ppermute | solution.py:259
  11.2 11.5 %collective-permute-start.5 = (f32[4,160,128]{2,1,0:T(8,128)S(1)}, f32[4,160,128]{2,1,0:T(8,128)S(1)}, u32[]{:S(2)}, u32[]{:S(2)}) collective-permute-start(f32[4,160,128]{2,1,0:T(8,128)S(1)} %get-tuple-element.24), channel_id=1, source_target_pairs={{1,0},{2,1},{3,2},{5,4},{6,5},{7,6},{9,8},{10,9},{11,10},{13,12},{... | collective-permute-start | bytes 983048 | tf_op jit(solution)/shard_map/ppermute | solution.py:260
  13.4 28.9 %collective-permute-start = (f32[4,160,128]{2,1,0:T(8,128)S(1)}, f32[4,160,128]{2,1,0:T(8,128)S(1)}, u32[]{:S(2)}, u32[]{:S(2)}) collective-permute-start(f32[4,160,128]{2,1,0:T(8,128)S(1)} %get-tuple-element.29), channel_id=1, source_target_pairs={{0,1},{1,2},{2,3},{4,5},{5,6},{6,7},{8,9},{9,10},{10,11},{12,13},{... | collective-permute-start | bytes 983048 | tf_op jit(solution)/shard_map/ppermute | solution.py:259
  19.3 3.5 %copy-start.6 = (f32[4,160,128]{2,1,0:T(8,128)}, f32[4,160,128]{2,1,0:T(8,128)S(1)}, u32[]{:S(2)}) copy-start(f32[4,160,128]{2,1,0:T(8,128)S(1)} %collective-permute-done.2.refs_0_) | copy-start | bytes 983044
  19.3 23.1 %collective-permute-start.1 = (f32[4,160,128]{2,1,0:T(8,128)S(1)}, f32[4,160,128]{2,1,0:T(8,128)S(1)}, u32[]{:S(2)}, u32[]{:S(2)}) collective-permute-start(f32[4,160,128]{2,1,0:T(8,128)S(1)} %get-tuple-element.28), channel_id=1, source_target_pairs={{1,0},{2,1},{3,2},{5,4},{6,5},{7,6},{9,8},{10,9},{11,10},{13,12},{... | collective-permute-start | bytes 983048 | tf_op jit(solution)/shard_map/ppermute | solution.py:260
  35.9 15.2 %collective-permute-start.6 = (f32[4,160,128]{2,1,0:T(8,128)}, f32[4,160,128]{2,1,0:T(8,128)S(1)}, u32[]{:S(2)}, u32[]{:S(2)}) collective-permute-start(f32[4,160,128]{2,1,0:T(8,128)} %get-tuple-element.16), channel_id=1, source_target_pairs={{0,1},{1,2},{2,3},{4,5},{5,6},{6,7},{8,9},{9,10},{10,11},{12,13},{... | collective-permute-start | bytes 983048 | tf_op jit(solution)/shard_map/ppermute | solution.py:268
  39.1 12.0 %collective-permute-start.7 = (f32[4,160,128]{2,1,0:T(8,128)}, f32[4,160,128]{2,1,0:T(8,128)S(1)}, u32[]{:S(2)}, u32[]{:S(2)}) collective-permute-start(f32[4,160,128]{2,1,0:T(8,128)} %get-tuple-element.18), channel_id=1, source_target_pairs={{1,0},{2,1},{3,2},{5,4},{6,5},{7,6},{9,8},{10,9},{11,10},{13,12},{... | collective-permute-start | bytes 983048 | tf_op jit(solution)/shard_map/ppermute | solution.py:268
  52.0 11.7 %copy-start.16 = (f32[2,256]{1,0:T(2,128)S(1)}, f32[2,256]{1,0:T(2,128)}, u32[]{:S(2)}) copy-start(f32[2,256]{1,0:T(2,128)} %param.19) | copy-start | bytes 6148
  52.0 11.8 %copy-start.1 = (f32[16,160,128]{2,1,0:T(8,128)S(1)}, f32[16,160,128]{2,1,0:T(8,128)}, u32[]{:S(2)}) copy-start(f32[16,160,128]{2,1,0:T(8,128)} %shard_map.114) | copy-start | bytes 3932164
  66.2 12.0 %copy-start.2 = (f32[327680]{0:T(1024)}, f32[327680]{0:T(1024)S(1)}, u32[]{:S(2)}) copy-start(f32[327680]{0:T(1024)S(1)} %scatter_fusion) | copy-start | bytes 3932164
  66.3 9.1 %collective-permute-start.8 = (f32[4,160,128]{2,1,0:T(8,128)S(1)}, f32[4,160,128]{2,1,0:T(8,128)S(1)}, u32[]{:S(2)}, u32[]{:S(2)}) collective-permute-start(f32[4,160,128]{2,1,0:T(8,128)S(1)} %bitcast.55), channel_id=1, source_target_pairs={{0,1},{1,2},{2,3},{4,5},{5,6},{6,7},{8,9},{9,10},{10,11},{12,13},{... | collective-permute-start | bytes 983048 | tf_op jit(solution)/shard_map/ppermute | solution.py:259
  69.5 8.8 %collective-permute-start.9 = (f32[4,160,128]{2,1,0:T(8,128)S(1)}, f32[4,160,128]{2,1,0:T(8,128)S(1)}, u32[]{:S(2)}, u32[]{:S(2)}) collective-permute-start(f32[4,160,128]{2,1,0:T(8,128)S(1)} %bitcast.54), channel_id=1, source_target_pairs={{1,0},{2,1},{3,2},{5,4},{6,5},{7,6},{9,8},{10,9},{11,10},{13,12},{... | collective-permute-start | bytes 983048 | tf_op jit(solution)/shard_map/ppermute | solution.py:260
  75.4 2.9 %copy-start.10 = (f32[4,160,128]{2,1,0:T(8,128)}, f32[4,160,128]{2,1,0:T(8,128)S(1)}, u32[]{:S(2)}) copy-start(f32[4,160,128]{2,1,0:T(8,128)S(1)} %collective-permute-done.8.refs_0_) | copy-start | bytes 983044
  86.9 4.4 %copy-start.3 = (f32[327680]{0:T(1024)S(1)}, f32[327680]{0:T(1024)}, u32[]{:S(2)}) copy-start(f32[327680]{0:T(1024)} %copy-done.2) | copy-start | bytes 3932164
  93.8 5.1 %collective-permute-start.10 = (f32[1280,128]{1,0:T(8,128)S(1)}, f32[1280,128]{1,0:T(8,128)S(1)}, u32[]{:S(2)}, u32[]{:S(2)}) collective-permute-start(f32[1280,128]{1,0:T(8,128)S(1)} %constant_dynamic-slice_fusion.1), channel_id=1, source_target_pairs={{0,4},{4,0},{8,12},{12,8},{1,5},{5,1},{9,13},{13,9},{2,6},{6,2},{1... | collective-permute-start | bytes 1966088 | tf_op jit(solution)/shard_map/ppermute | solution.py:243
  99.0 9.0 %collective-permute-start.11 = (f32[640,128]{1,0:T(8,128)S(1)}, f32[640,128]{1,0:T(8,128)S(1)}, u32[]{:S(2)}, u32[]{:S(2)}) collective-permute-start(f32[640,128]{1,0:T(8,128)S(1)} %constant_dynamic-slice_fusion), channel_id=1, source_target_pairs={{0,8},{4,12},{8,0},{12,4},{1,9},{5,13},{9,1},{13,5},{2,10},{6,14},... | collective-permute-start | bytes 983048 | tf_op jit(solution)/shard_map/ppermute | solution.py:243
  108.0 8.1 %collective-permute-start.12 = (f32[640,128]{1,0:T(8,128)S(1)}, f32[640,128]{1,0:T(8,128)S(1)}, u32[]{:S(2)}, u32[]{:S(2)}) collective-permute-start(f32[640,128]{1,0:T(8,128)S(1)} %add_multiply_fusion), channel_id=1, source_target_pairs={{0,8},{4,12},{8,0},{12,4},{1,9},{5,13},{9,1},{13,5},{2,10},{6,14},... | collective-permute-start | bytes 983048 | tf_op jit(solution)/shard_map/ppermute | solution.py:249
  116.1 3.9 %collective-permute-start.13 = (f32[1280,128]{1,0:T(8,128)S(1)}, f32[1280,128]{1,0:T(8,128)S(1)}, u32[]{:S(2)}, u32[]{:S(2)}) collective-permute-start(f32[1280,128]{1,0:T(8,128)S(1)} %maximum_select_fusion.1), channel_id=1, source_target_pairs={{0,4},{4,0},{8,12},{12,8},{1,5},{5,1},{9,13},{13,9},{2,6},{6,2},{1... | collective-permute-start | bytes 1966088 | tf_op jit(solution)/shard_map/ppermute | solution.py:249
  (8 other events, 7.3 us)

commit v6 on v5

--- a/solution.py
+++ b/solution.py
@@ -166,11 +166,18 @@
     full, blk = specs(mid.shape, block)
     out = jax.ShapeDtypeStruct(mid.shape, jnp.float32)
     own_grad = g is None
-    in_specs = [full(lo.shape), full(mid.shape), full(hi.shape)]
+
+    def halo(pair):
+        array, at = pair if isinstance(pair, tuple) else (pair, 0)
+        return array, pl.BlockSpec((HALO, height, depth), lambda i: (at, 0, 0))
+
+    (lo, lo_spec), (hi, hi_spec) = halo(lo), halo(hi)
+    in_specs = [lo_spec, full(mid.shape), hi_spec]
     args = [lo, mid, hi]
     if own_grad:
-        in_specs += [full(b[0].shape), full(b[1].shape), full(b[2].shape)]
-        args += list(b)
+        (b_lo, b_lo_spec), (b_hi, b_hi_spec) = halo(b[0]), halo(b[2])
+        in_specs += [b_lo_spec, full(b[1].shape), b_hi_spec]
+        args += [b_lo, b[1], b_hi]
     else:
         in_specs += [blk] * 4
         args += [b, g[0], g[1], g[2]]
@@ -251,14 +258,14 @@
     return rows.reshape(part.shape)
 
 
-def halos(block, axis):
+def halos(blocks, axis):
     count = lax.axis_size(axis)
     forward = [(i, i + 1) for i in range(count - 1)]
     backward = [(target, source) for source, target in forward]
-    planes = block.shape[0]
-    low = lax.ppermute(block[planes - HALO:], axis, forward)
-    high = lax.ppermute(block[:HALO], axis, backward)
-    return low, high
+    planes = blocks[0].shape[0]
+    tops = jnp.concatenate([block[planes - HALO:] for block in blocks])
+    bottoms = jnp.concatenate([block[:HALO] for block in blocks])
+    return lax.ppermute(tops, axis, forward), lax.ppermute(bottoms, axis, backward)
 
 
 def edge_halos(low_edge, high_edge, axis):
@@ -298,7 +305,7 @@
 
     src_local, src_valid = locate(src_cell)
     rec_local, rec_valid = locate(rec_cell)
-    b_lo, b_hi = halos(buoyancy, "tile")
+    first_lo, first_hi = halos([buoyancy, cur_field[0]], "tile")
 
     def spread(cells):
         return jnp.stack([cells // (height * depth), (cells // depth) % height, cells % depth])
@@ -306,14 +313,14 @@
     where = jnp.concatenate([spread(src_local)[:, 0], src_valid.astype(jnp.int32)])
     receivers = spread(rec_local)
     older, now = (prev_field[0], cur_field[0])
-    lo, hi = halos(now, "tile")
+    lo, hi = (first_lo, 1), (first_hi, 1)
     forces = []
     samples = []
     grad_b = None
     for k in range(steps):
         track = (where, wavelet[k:k + 1], receivers)
         if grad_b is None:
-            outs = apply_step(lo, now, hi, (b_lo, buoyancy, b_hi), None, speed, older, track)
+            outs = apply_step(lo, now, hi, ((first_lo, 0), buoyancy, (first_hi, 0)), None, speed, older, track)
             force, newer = outs[:2]
             grad_b = outs[2:5]
             edge_lo, edge_hi, lines = outs[5:]
@@ -328,7 +335,7 @@
     older, now = (adj_prev[0], adj_cur[0])
     image_part = jnp.zeros(buoyancy.shape, jnp.float32)
     for j in range(steps):
-        lo, hi = halos(now, "tile")
+        lo, hi = halos([now], "tile")
         (newer,) = apply_step(lo, now, hi, buoyancy, grad_b, speed, older, want_force=False)
         newer = inject(newer, rec_local, rec_valid, residual[steps - 1 - j])
         image_part = image_part + newer * forces[steps - 1 - j]

time: 123 us -> 125 us (1.016)
  waiting for transfers between devices: 25.9 us -> 30.2 us
  starting transfers between devices: 34.5 us -> 31.2 us
    ppermute x8 -> x6, starting transfers between devices: 21.2 us -> 16 us  [the longest x3 9.68 us: halos(): lax.ppermute(tops, axis, forward)]
    ppermute x8 -> x6, waiting for transfers between devices: 7.92 us -> 12.2 us  [the longest x3 6.46 us: halos(): lax.ppermute(bottoms, axis, backward)]
    ppermute x2, starting transfers between devices: 4.61 us -> 6.37 us  [reduce_members(): rows = keep + lax.ppermute(give, axis, pairs)]
    unnamed x36 -> x32, local copies, waits for them, and re-layouts: 3.18 us -> 3.61 us
  transfers between devices with their start and end apart: 14 -> 12, of which waited for: 7 -> 8; matrix products, arithmetic and copies ran while one was open for 3% -> 3% of each run, Pallas kernels for 17% -> 17%
where the time goes in v6:
time: 125 us; the launch traced here: 123 us
  Pallas kernels  39.1 us (31%)
  starting transfers between devices  31.2 us (25%)
  waiting for transfers between devices  30.2 us (24%)
  other arithmetic  14.1 us (11%)
  local copies, waits for them, and re-layouts  6.51 us (5%)
  between operations  1.68 us (1%)
    pallas_call x4, Pallas kernels, apply_step(): pl.pallas_call(kernel, grid=(planes // block,), in_specs=in_specs, out_sp...  39.1 us
    ppermute x3, starting transfers between devices, halos(): lax.ppermute(tops, axis, forward)  9.68 us
    ppermute x2, waiting for transfers between devices, reduce_members(): rows = keep + lax.ppermute(give, axis, pairs)  9.44 us
    ppermute x2, waiting for transfers between devices, reduce_members(): other = lax.ppermute(rows, axis, pairs)  8.52 us
    scatter-add x2, other arithmetic, inject(): flat = field.reshape(-1).at[where].add(jnp.where(valid, values, 0.0))  6.84 us
    ppermute x3, waiting for transfers between devices, halos(): lax.ppermute(bottoms, axis, backward)  6.46 us
    ppermute x2, starting transfers between devices, reduce_members(): rows = keep + lax.ppermute(give, axis, pairs)  6.37 us
    ppermute x3, starting transfers between devices, halos(): lax.ppermute(bottoms, axis, backward)  6.36 us
  transfers between devices with their start and end apart: 12, of which 8 were waited for; matrix products, arithmetic and copies ran while one was open for 3% of the time, Pallas kernels for 17%

profile of v6, /device:TPU:9, one launch (start us, length us, event | category | flops | bytes accessed | tf_op | source)
XLA Modules:
  0.0 122.7 jit_solution(3235331683784147338)
XLA Ops:
  2.3 3.3 %collective-permute-start.2 = (f32[8,160,128]{2,1,0:T(8,128)S(1)}, f32[8,160,128]{2,1,0:T(8,128)S(1)}, u32[]{:S(2)}, u32[]{:S(2)}) collective-permute-start(f32[8,160,128]{2,1,0:T(8,128)S(1)} %pad_maximum_fusion), channel_id=1, source_target_pairs={{0,1},{1,2},{2,3},{4,5},{5,6},{6,7},{8,9},{9,10},{10,11},{12,13},{... | collective-permute-start | bytes 1966088 | tf_op jit(solution)/shard_map/ppermute | solution.py:268
  5.7 2.1 %collective-permute-start.3 = (f32[8,160,128]{2,1,0:T(8,128)S(1)}, f32[8,160,128]{2,1,0:T(8,128)S(1)}, u32[]{:S(2)}, u32[]{:S(2)}) collective-permute-start(f32[8,160,128]{2,1,0:T(8,128)S(1)} %pad_maximum_fusion.1), channel_id=1, source_target_pairs={{1,0},{2,1},{3,2},{5,4},{6,5},{7,6},{9,8},{10,9},{11,10},{13,12},{... | collective-permute-start | bytes 1966088 | tf_op jit(solution)/shard_map/ppermute | solution.py:268
  8.7 3.2 %collective-permute-start = (f32[4,160,128]{2,1,0:T(8,128)}, f32[4,160,128]{2,1,0:T(8,128)S(1)}, u32[]{:S(2)}, u32[]{:S(2)}) collective-permute-start(f32[4,160,128]{2,1,0:T(8,128)} %get-tuple-element.29), channel_id=1, source_target_pairs={{0,1},{1,2},{2,3},{4,5},{5,6},{6,7},{8,9},{9,10},{10,11},{12,13},{... | collective-permute-start | bytes 983048 | tf_op jit(solution)/shard_map/ppermute | solution.py:268
  11.9 2.1 %collective-permute-start.1 = (f32[4,160,128]{2,1,0:T(8,128)}, f32[4,160,128]{2,1,0:T(8,128)S(1)}, u32[]{:S(2)}, u32[]{:S(2)}) collective-permute-start(f32[4,160,128]{2,1,0:T(8,128)} %get-tuple-element.28), channel_id=1, source_target_pairs={{1,0},{2,1},{3,2},{5,4},{6,5},{7,6},{9,8},{10,9},{11,10},{13,12},{... | collective-permute-start | bytes 983048 | tf_op jit(solution)/shard_map/ppermute | solution.py:268
  16.6 3.3 %collective-permute-done.2.refs_0_.refs_3_ = f32[8,160,128]{2,1,0:T(8,128)S(1)} collective-permute-done((f32[8,160,128]{2,1,0:T(8,128)S(1)}, f32[8,160,128]{2,1,0:T(8,128)S(1)}, u32[]{:S(2)}, u32[]{:S(2)}) %collective-permute-start.2) | collective-permute-done | bytes 655392 | tf_op jit(solution)/shard_map/ppermute | solution.py:268
  19.9 3.0 %collective-permute-done.3.refs_2_.refs_5_ = f32[8,160,128]{2,1,0:T(8,128)S(1)} collective-permute-done((f32[8,160,128]{2,1,0:T(8,128)S(1)}, f32[8,160,128]{2,1,0:T(8,128)S(1)}, u32[]{:S(2)}, u32[]{:S(2)}) %collective-permute-start.3) | collective-permute-done | bytes 655392 | tf_op jit(solution)/shard_map/ppermute | solution.py:268
  23.7 12.6 %shard_map.113 = (f32[16,160,128]{2,1,0:T(8,128)}, f32[16,160,128]{2,1,0:T(8,128)}, f32[16,160,128]{2,1,0:T(8,128)}, f32[16,160,128]{2,1,0:T(8,128)}, f32[16,160...) custom-call(f32[8,160,128]{2,1,0:T(8,128)} %copy-done.5, ...), custom_call_target="tpu_custom_call" | custom-call | tf_op jit(solution)/shard_map/pallas_call | solution.py:209
  36.3 3.2 %collective-permute-start.4 = (f32[4,160,128]{2,1,0:T(8,128)}, f32[4,160,128]{2,1,0:T(8,128)S(1)}, u32[]{:S(2)}, u32[]{:S(2)}) collective-permute-start(f32[4,160,128]{2,1,0:T(8,128)} %get-tuple-element.16), channel_id=1, source_target_pairs={{0,1},{1,2},{2,3},{4,5},{5,6},{6,7},{8,9},{9,10},{10,11},{12,13},{... | collective-permute-start | bytes 983048 | tf_op jit(solution)/shard_map/ppermute | solution.py:275
  39.5 2.1 %collective-permute-start.5 = (f32[4,160,128]{2,1,0:T(8,128)}, f32[4,160,128]{2,1,0:T(8,128)S(1)}, u32[]{:S(2)}, u32[]{:S(2)}) collective-permute-start(f32[4,160,128]{2,1,0:T(8,128)} %get-tuple-element.18), channel_id=1, source_target_pairs={{1,0},{2,1},{3,2},{5,4},{6,5},{7,6},{9,8},{10,9},{11,10},{13,12},{... | collective-permute-start | bytes 983048 | tf_op jit(solution)/shard_map/ppermute | solution.py:275
  43.5 8.0 %shard_map.114 = f32[16,160,128]{2,1,0:T(8,128)} custom-call(f32[4,160,128]{2,1,0:T(8,128)} %copy-done.7, f32[16,160,128]{2,1,0:T(8,128)} %bitcast.47, f32[4,160,128]{2,1,0:T(8,128)} %copy-done.8, f32[16,160,128]{2,1,0:T(8,128)} %refs_3_.5, f32[16,160,128]{2,1,0:T(8,128)} %get-tuple-element.12.refs_4_, f32[16,160,128]{2,1,0:T(8,128)} %get-tuple-element.13.refs_5_, ...), custom_call_target="tpu_custom_call" | custom-call | tf_op jit(solution)/shard_map/pallas_call | solution.py:209
  52.4 10.7 %shard_map.115 = (f32[16,160,128]{2,1,0:T(8,128)}, f32[16,160,128]{2,1,0:T(8,128)}, f32[4,160,128]{2,1,0:T(8,128)}, f32[4,160,128]{2,1,0:T(8,128)}, f32[256,128]{1,0:T(8,128)}) custom-call(f32[4,160,128]{2,1,0:T(8,128)} %copy-done.11, f32[16,160,128]{2,1,0:T(8,128)} %get-tuple-element.17.refs_1_, f32[4,160,128]{2,1,0:T(8,128)} %copy-done.12, ...), custom_call_target="tpu_custom_call" | custom-call | tf_op jit(solution)/shard_map/pallas_call | solution.py:209
  64.1 2.5 %scatter_fusion = f32[327680]{0:T(1024)S(1)} fusion(f32[327680]{0:T(1024)S(1)} %bitcast.35, s32[256]{0:T(256)S(1)} %get-tuple-element.32, f32[256]{0:T(256)S(1)} %get-tuple-element.37), kind=kCustom, calls=%fused_computation | custom fusion | flops 256 | bytes 4096 | tf_op jit(solution)/shard_map/scatter-add | solution.py:279
  66.7 3.2 %collective-permute-start.6 = (f32[4,160,128]{2,1,0:T(8,128)S(1)}, f32[4,160,128]{2,1,0:T(8,128)S(1)}, u32[]{:S(2)}, u32[]{:S(2)}) collective-permute-start(f32[4,160,128]{2,1,0:T(8,128)S(1)} %bitcast.55), channel_id=1, source_target_pairs={{0,1},{1,2},{2,3},{4,5},{5,6},{6,7},{8,9},{9,10},{10,11},{12,13},{... | collective-permute-start | bytes 983048 | tf_op jit(solution)/shard_map/ppermute | solution.py:268
  69.9 2.1 %collective-permute-start.7 = (f32[4,160,128]{2,1,0:T(8,128)S(1)}, f32[4,160,128]{2,1,0:T(8,128)S(1)}, u32[]{:S(2)}, u32[]{:S(2)}) collective-permute-start(f32[4,160,128]{2,1,0:T(8,128)S(1)} %bitcast.54), channel_id=1, source_target_pairs={{1,0},{2,1},{3,2},{5,4},{6,5},{7,6},{9,8},{10,9},{11,10},{13,12},{... | collective-permute-start | bytes 983048 | tf_op jit(solution)/shard_map/ppermute | solution.py:268
  72.0 2.5 %collective-permute-done.6.refs_0_ = f32[4,160,128]{2,1,0:T(8,128)S(1)} collective-permute-done((f32[4,160,128]{2,1,0:T(8,128)S(1)}, f32[4,160,128]{2,1,0:T(8,128)S(1)}, u32[]{:S(2)}, u32[]{:S(2)}) %collective-permute-start.6) | collective-permute-done | bytes 327712 | tf_op jit(solution)/shard_map/ppermute | solution.py:268
  74.5 3.5 %collective-permute-done.7.refs_2_ = f32[4,160,128]{2,1,0:T(8,128)S(1)} collective-permute-done((f32[4,160,128]{2,1,0:T(8,128)S(1)}, f32[4,160,128]{2,1,0:T(8,128)S(1)}, u32[]{:S(2)}, u32[]{:S(2)}) %collective-permute-start.7) | collective-permute-done | bytes 327712 | tf_op jit(solution)/shard_map/ppermute | solution.py:268
  78.7 7.9 %shard_map.116 = f32[16,160,128]{2,1,0:T(8,128)} custom-call(f32[4,160,128]{2,1,0:T(8,128)} %copy-done.9, f32[16,160,128]{2,1,0:T(8,128)} %bitcast.36, f32[4,160,128]{2,1,0:T(8,128)} %copy-done.10, f32[16,160,128]{2,1,0:T(8,128)} %refs_3_.5, f32[16,160,128]{2,1,0:T(8,128)} %get-tuple-element.12.refs_4_, f32[16,160,128]{2,1,0:T(8,128)} %get-tuple-element.13.refs_5_, ...), custom_call_target="tpu_custom_call" | custom-call | tf_op jit(solution)/shard_map/pallas_call | solution.py:209
  86.6 4.4 %scatter_fusion.1 = f32[327680]{0:T(1024)} fusion(f32[327680]{0:T(1024)} %bitcast.42, s32[256]{0:T(256)S(1)} %get-tuple-element.32, f32[256]{0:T(256)S(1)} %get-tuple-element.36), kind=kCustom, calls=%fused_computation.1 | custom fusion | flops 256 | bytes 4096 | tf_op jit(solution)/shard_map/scatter-add | solution.py:279
  91.0 2.5 %multiply_add_fusion = f32[16,160,128]{2,1,0:T(8,128)S(1)} fusion(f32[16,160,128]{2,1,0:T(8,128)} %bitcast.43, f32[16,160,128]{2,1,0:T(8,128)} %get-tuple-element.21, f32[16,160,128]{2,1,0:T(8,128)S(1)} %bitcast.37, f32[16,160,128]{2,1,0:T(8,128)} %get-tuple-element.20), kind=kLoop, calls=%fused_computation.3 | loop fusion | flops 983040 | bytes 6553600 | tf_op jit(solution)/shard_map/add | solution.py:341
  93.5 5.1 %collective-permute-start.8 = (f32[1280,128]{1,0:T(8,128)S(1)}, f32[1280,128]{1,0:T(8,128)S(1)}, u32[]{:S(2)}, u32[]{:S(2)}) collective-permute-start(f32[1280,128]{1,0:T(8,128)S(1)} %constant_dynamic-slice_fusion.1), channel_id=1, source_target_pairs={{0,4},{4,0},{8,12},{12,8},{1,5},{5,1},{9,13},{13,9},{2,6},{6,2},{1... | collective-permute-start | bytes 1966088 | tf_op jit(solution)/shard_map/ppermute | solution.py:250
  98.6 1.7 %collective-permute-done.8 = f32[1280,128]{1,0:T(8,128)S(1)} collective-permute-done((f32[1280,128]{1,0:T(8,128)S(1)}, f32[1280,128]{1,0:T(8,128)S(1)}, u32[]{:S(2)}, u32[]{:S(2)}) %collective-permute-start.8) | collective-permute-done | bytes 655392 | tf_op jit(solution)/shard_map/ppermute | solution.py:250
  101.7 7.7 %collective-permute-done.9 = f32[640,128]{1,0:T(8,128)S(1)} collective-permute-done((f32[640,128]{1,0:T(8,128)S(1)}, f32[640,128]{1,0:T(8,128)S(1)}, u32[]{:S(2)}, u32[]{:S(2)}) %collective-permute-start.9) | collective-permute-done | bytes 327712 | tf_op jit(solution)/shard_map/ppermute | solution.py:250
  110.8 6.8 %collective-permute-done.10 = f32[640,128]{1,0:T(8,128)S(1)} collective-permute-done((f32[640,128]{1,0:T(8,128)S(1)}, f32[640,128]{1,0:T(8,128)S(1)}, u32[]{:S(2)}, u32[]{:S(2)}) %collective-permute-start.10) | collective-permute-done | bytes 327712 | tf_op jit(solution)/shard_map/ppermute | solution.py:256
  117.6 2.2 %collective-permute-start.11 = (f32[1280,128]{1,0:T(8,128)S(1)}, f32[1280,128]{1,0:T(8,128)S(1)}, u32[]{:S(2)}, u32[]{:S(2)}) collective-permute-start(f32[1280,128]{1,0:T(8,128)S(1)} %maximum_select_fusion.1), channel_id=1, source_target_pairs={{0,4},{4,0},{8,12},{12,8},{1,5},{5,1},{9,13},{13,9},{2,6},{6,2},{1... | collective-permute-start | bytes 1966088 | tf_op jit(solution)/shard_map/ppermute | solution.py:256
  (62 shorter events, 15.6 us)
Async XLA Ops:
  0.6 1.5 %copy-start.3 = (f32[1,16,160,128]{3,2,1,0:T(8,128)S(1)}, f32[1,16,160,128]{3,2,1,0:T(8,128)}, u32[]{:S(2)}) copy-start(f32[1,16,160,128]{3,2,1,0:T(8,128)} %param.12) | copy-start | bytes 3932164
  2.2 5.6 %copy-start.4 = (f32[1,16,160,128]{3,2,1,0:T(8,128)S(1)}, f32[1,16,160,128]{3,2,1,0:T(8,128)}, u32[]{:S(2)}) copy-start(f32[1,16,160,128]{3,2,1,0:T(8,128)} %param.14) | copy-start | bytes 3932164
  2.3 17.6 %collective-permute-start.2 = (f32[8,160,128]{2,1,0:T(8,128)S(1)}, f32[8,160,128]{2,1,0:T(8,128)S(1)}, u32[]{:S(2)}, u32[]{:S(2)}) collective-permute-start(f32[8,160,128]{2,1,0:T(8,128)S(1)} %pad_maximum_fusion), channel_id=1, source_target_pairs={{0,1},{1,2},{2,3},{4,5},{5,6},{6,7},{8,9},{9,10},{10,11},{12,13},{... | collective-permute-start | bytes 1966088 | tf_op jit(solution)/shard_map/ppermute | solution.py:268
  5.6 9.8 %copy-start.13 = (s32[256]{0:T(256)S(1)}, s32[256]{0:T(256)}, u32[]{:S(2)}) copy-start(s32[256]{0:T(256)} %param.18) | copy-start | bytes 3076
  5.6 10.4 %copy-start.15 = (f32[2]{0:T(128)S(1)}, f32[2]{0:T(128)}, u32[]{:S(2)}) copy-start(f32[2]{0:T(128)} %param.16) | copy-start | bytes 28
  5.7 17.2 %collective-permute-start.3 = (f32[8,160,128]{2,1,0:T(8,128)S(1)}, f32[8,160,128]{2,1,0:T(8,128)S(1)}, u32[]{:S(2)}, u32[]{:S(2)}) collective-permute-start(f32[8,160,128]{2,1,0:T(8,128)S(1)} %pad_maximum_fusion.1), channel_id=1, source_target_pairs={{1,0},{2,1},{3,2},{5,4},{6,5},{7,6},{9,8},{10,9},{11,10},{13,12},{... | collective-permute-start | bytes 1966088 | tf_op jit(solution)/shard_map/ppermute | solution.py:268
  8.7 33.9 %collective-permute-start = (f32[4,160,128]{2,1,0:T(8,128)}, f32[4,160,128]{2,1,0:T(8,128)S(1)}, u32[]{:S(2)}, u32[]{:S(2)}) collective-permute-start(f32[4,160,128]{2,1,0:T(8,128)} %get-tuple-element.29), channel_id=1, source_target_pairs={{0,1},{1,2},{2,3},{4,5},{5,6},{6,7},{8,9},{9,10},{10,11},{12,13},{... | collective-permute-start | bytes 983048 | tf_op jit(solution)/shard_map/ppermute | solution.py:268
  11.9 30.8 %collective-permute-start.1 = (f32[4,160,128]{2,1,0:T(8,128)}, f32[4,160,128]{2,1,0:T(8,128)S(1)}, u32[]{:S(2)}, u32[]{:S(2)}) collective-permute-start(f32[4,160,128]{2,1,0:T(8,128)} %get-tuple-element.28), channel_id=1, source_target_pairs={{1,0},{2,1},{3,2},{5,4},{6,5},{7,6},{9,8},{10,9},{11,10},{13,12},{... | collective-permute-start | bytes 983048 | tf_op jit(solution)/shard_map/ppermute | solution.py:268
  19.9 3.0 %copy-start.5 = (f32[8,160,128]{2,1,0:T(8,128)}, f32[8,160,128]{2,1,0:T(8,128)S(1)}, u32[]{:S(2)}) copy-start(f32[8,160,128]{2,1,0:T(8,128)S(1)} %collective-permute-done.2.refs_0_.refs_3_) | copy-start | bytes 1966084
  22.9 0.9 copy-start.6
  36.3 15.2 %collective-permute-start.4 = (f32[4,160,128]{2,1,0:T(8,128)}, f32[4,160,128]{2,1,0:T(8,128)S(1)}, u32[]{:S(2)}, u32[]{:S(2)}) collective-permute-start(f32[4,160,128]{2,1,0:T(8,128)} %get-tuple-element.16), channel_id=1, source_target_pairs={{0,1},{1,2},{2,3},{4,5},{5,6},{6,7},{8,9},{9,10},{10,11},{12,13},{... | collective-permute-start | bytes 983048 | tf_op jit(solution)/shard_map/ppermute | solution.py:275
  39.5 12.0 %collective-permute-start.5 = (f32[4,160,128]{2,1,0:T(8,128)}, f32[4,160,128]{2,1,0:T(8,128)S(1)}, u32[]{:S(2)}, u32[]{:S(2)}) collective-permute-start(f32[4,160,128]{2,1,0:T(8,128)} %get-tuple-element.18), channel_id=1, source_target_pairs={{1,0},{2,1},{3,2},{5,4},{6,5},{7,6},{9,8},{10,9},{11,10},{13,12},{... | collective-permute-start | bytes 983048 | tf_op jit(solution)/shard_map/ppermute | solution.py:275
  51.5 0.9 copy-start.12
  52.4 11.7 %copy-start.14 = (f32[2,256]{1,0:T(2,128)S(1)}, f32[2,256]{1,0:T(2,128)}, u32[]{:S(2)}) copy-start(f32[2,256]{1,0:T(2,128)} %param.19) | copy-start | bytes 6148
  52.4 11.8 %copy-start = (f32[16,160,128]{2,1,0:T(8,128)S(1)}, f32[16,160,128]{2,1,0:T(8,128)}, u32[]{:S(2)}) copy-start(f32[16,160,128]{2,1,0:T(8,128)} %shard_map.114) | copy-start | bytes 3932164
  66.6 11.4 %copy-start.1 = (f32[327680]{0:T(1024)}, f32[327680]{0:T(1024)S(1)}, u32[]{:S(2)}) copy-start(f32[327680]{0:T(1024)S(1)} %scatter_fusion) | copy-start | bytes 3932164
  66.7 7.8 %collective-permute-start.6 = (f32[4,160,128]{2,1,0:T(8,128)S(1)}, f32[4,160,128]{2,1,0:T(8,128)S(1)}, u32[]{:S(2)}, u32[]{:S(2)}) collective-permute-start(f32[4,160,128]{2,1,0:T(8,128)S(1)} %bitcast.55), channel_id=1, source_target_pairs={{0,1},{1,2},{2,3},{4,5},{5,6},{6,7},{8,9},{9,10},{10,11},{12,13},{... | collective-permute-start | bytes 983048 | tf_op jit(solution)/shard_map/ppermute | solution.py:268
  69.9 8.1 %collective-permute-start.7 = (f32[4,160,128]{2,1,0:T(8,128)S(1)}, f32[4,160,128]{2,1,0:T(8,128)S(1)}, u32[]{:S(2)}, u32[]{:S(2)}) collective-permute-start(f32[4,160,128]{2,1,0:T(8,128)S(1)} %bitcast.54), channel_id=1, source_target_pairs={{1,0},{2,1},{3,2},{5,4},{6,5},{7,6},{9,8},{10,9},{11,10},{13,12},{... | collective-permute-start | bytes 983048 | tf_op jit(solution)/shard_map/ppermute | solution.py:268
  74.5 3.5 %copy-start.9 = (f32[4,160,128]{2,1,0:T(8,128)}, f32[4,160,128]{2,1,0:T(8,128)S(1)}, u32[]{:S(2)}) copy-start(f32[4,160,128]{2,1,0:T(8,128)S(1)} %collective-permute-done.6.refs_0_) | copy-start | bytes 983044
  86.6 4.4 %copy-start.2 = (f32[327680]{0:T(1024)S(1)}, f32[327680]{0:T(1024)}, u32[]{:S(2)}) copy-start(f32[327680]{0:T(1024)} %copy-done.1) | copy-start | bytes 3932164
  93.5 6.8 %collective-permute-start.8 = (f32[1280,128]{1,0:T(8,128)S(1)}, f32[1280,128]{1,0:T(8,128)S(1)}, u32[]{:S(2)}, u32[]{:S(2)}) collective-permute-start(f32[1280,128]{1,0:T(8,128)S(1)} %constant_dynamic-slice_fusion.1), channel_id=1, source_target_pairs={{0,4},{4,0},{8,12},{12,8},{1,5},{5,1},{9,13},{13,9},{2,6},{6,2},{1... | collective-permute-start | bytes 1966088 | tf_op jit(solution)/shard_map/ppermute | solution.py:250
  100.5 9.0 %collective-permute-start.9 = (f32[640,128]{1,0:T(8,128)S(1)}, f32[640,128]{1,0:T(8,128)S(1)}, u32[]{:S(2)}, u32[]{:S(2)}) collective-permute-start(f32[640,128]{1,0:T(8,128)S(1)} %constant_dynamic-slice_fusion), channel_id=1, source_target_pairs={{0,8},{4,12},{8,0},{12,4},{1,9},{5,13},{9,1},{13,5},{2,10},{6,14},... | collective-permute-start | bytes 983048 | tf_op jit(solution)/shard_map/ppermute | solution.py:250
  109.5 8.1 %collective-permute-start.10 = (f32[640,128]{1,0:T(8,128)S(1)}, f32[640,128]{1,0:T(8,128)S(1)}, u32[]{:S(2)}, u32[]{:S(2)}) collective-permute-start(f32[640,128]{1,0:T(8,128)S(1)} %add_multiply_fusion), channel_id=1, source_target_pairs={{0,8},{4,12},{8,0},{12,4},{1,9},{5,13},{9,1},{13,5},{2,10},{6,14},... | collective-permute-start | bytes 983048 | tf_op jit(solution)/shard_map/ppermute | solution.py:256
  117.6 3.9 %collective-permute-start.11 = (f32[1280,128]{1,0:T(8,128)S(1)}, f32[1280,128]{1,0:T(8,128)S(1)}, u32[]{:S(2)}, u32[]{:S(2)}) collective-permute-start(f32[1280,128]{1,0:T(8,128)S(1)} %maximum_select_fusion.1), channel_id=1, source_target_pairs={{0,4},{4,0},{8,12},{12,8},{1,5},{5,1},{9,13},{13,9},{2,6},{6,2},{1... | collective-permute-start | bytes 1966088 | tf_op jit(solution)/shard_map/ppermute | solution.py:256
  (4 other events, 3.0 us)

commit v7 on v5

--- a/solution.py
+++ b/solution.py
@@ -21,12 +21,20 @@
     return jnp.where(lane >= -k, rolled, 0.0)
 
 
-def fill_padded(pad_ref, lo_ref, mid_ref, hi_ref):
+def fill_padded(pad_ref, lo_ref, mid_ref, hi_ref, sem):
     planes, height, depth = mid_ref.shape
-    pad_ref[...] = jnp.zeros(pad_ref.shape, jnp.float32)
-    pad_ref[0:HALO, PADY:PADY + height, :] = lo_ref[...]
-    pad_ref[HALO:HALO + planes, PADY:PADY + height, :] = mid_ref[...]
-    pad_ref[HALO + planes:, PADY:PADY + height, :] = hi_ref[...]
+    rows = pl.ds(PADY, height)
+    copies = [
+        pltpu.make_async_copy(lo_ref, pad_ref.at[pl.ds(0, HALO), rows, :], sem.at[0]),
+        pltpu.make_async_copy(mid_ref, pad_ref.at[pl.ds(HALO, planes), rows, :], sem.at[1]),
+        pltpu.make_async_copy(hi_ref, pad_ref.at[pl.ds(HALO + planes, HALO), rows, :], sem.at[2]),
+    ]
+    for copy in copies:
+        copy.start()
+    pad_ref[:, 0:PADY, :] = jnp.zeros((planes + 2 * HALO, PADY, depth), jnp.float32)
+    pad_ref[:, PADY + height:, :] = jnp.zeros((planes + 2 * HALO, PADY, depth), jnp.float32)
+    for copy in copies:
+        copy.wait()
 
 
 def taps(pad_ref, plane, y0, rows, lane):
@@ -69,18 +77,18 @@
         g_out = take(3)
     if track:
         edge_lo_ref, edge_hi_ref, sample_ref = take(3)
-    (pad_ref,) = take(1)
-    if own_grad:
-        (b_pad_ref,) = take(1)
+    pad_ref, sem = take(2)
+    if own_grad:
+        b_pad_ref, b_sem = take(2)
     if track:
         (keep_ref,) = take(1)
     i = pl.program_id(0)
 
     @pl.when(i == 0)
     def _():
-        fill_padded(pad_ref, lo_ref, mid_ref, hi_ref)
+        fill_padded(pad_ref, lo_ref, mid_ref, hi_ref, sem)
         if own_grad:
-            fill_padded(b_pad_ref, b_lo_ref, b_mid_ref, b_hi_ref)
+            fill_padded(b_pad_ref, b_lo_ref, b_mid_ref, b_hi_ref, b_sem)
 
     planes = mid_ref.shape[0]
     height = c_ref.shape[1]
@@ -128,25 +136,6 @@
             lax.fori_loop(0, sample_ref.shape[0], sample, 0, unroll=8)
 
 
-def grad_kernel(lo_ref, mid_ref, hi_ref, g0_ref, g1_ref, g2_ref, pad_ref, *, block, rows):
-    i = pl.program_id(0)
-
-    @pl.when(i == 0)
-    def _():
-        fill_padded(pad_ref, lo_ref, mid_ref, hi_ref)
-
-    height = mid_ref.shape[1]
-    lane = lax.broadcasted_iota(jnp.int32, (rows, mid_ref.shape[2]), 1)
-    for p in range(block):
-        plane = i * block + p + HALO
-        for y0 in range(0, height, rows):
-            sl = (p, pl.ds(y0, rows), slice(None))
-            _, _, grads = taps(pad_ref, plane, y0, rows, lane)
-            g0_ref[sl] = grads[0]
-            g1_ref[sl] = grads[1]
-            g2_ref[sl] = grads[2]
-
-
 def pick_block(planes):
     for b in (4, 2, 1):
         if planes % b == 0:
@@ -166,10 +155,11 @@
     full, blk = specs(mid.shape, block)
     out = jax.ShapeDtypeStruct(mid.shape, jnp.float32)
     own_grad = g is None
-    in_specs = [full(lo.shape), full(mid.shape), full(hi.shape)]
+    anywhere = pl.BlockSpec(memory_space=pl.ANY)
+    in_specs = [anywhere] * 3
     args = [lo, mid, hi]
     if own_grad:
-        in_specs += [full(b[0].shape), full(b[1].shape), full(b[2].shape)]
+        in_specs += [anywhere] * 3
         args += list(b)
     else:
         in_specs += [blk] * 4
@@ -183,9 +173,10 @@
     if own_grad:
         out_specs += [blk] * 3
         out_shape += [out] * 3
-    scratch = [pltpu.VMEM((planes + 2 * HALO, height + 2 * PADY, depth), jnp.float32)]
-    if own_grad:
-        scratch.append(pltpu.VMEM((planes + 2 * HALO, height + 2 * PADY, depth), jnp.float32))
+    padded = pltpu.VMEM((planes + 2 * HALO, height + 2 * PADY, depth), jnp.float32)
+    scratch = [padded, pltpu.SemaphoreType.DMA((3,))]
+    if own_grad:
+        scratch += [padded, pltpu.SemaphoreType.DMA((3,))]
     if track is not None:
         smem = pl.BlockSpec(memory_space=pltpu.SMEM)
         in_specs += [smem, smem, smem]
@@ -208,22 +199,6 @@
         scratch_shapes=scratch,
         compiler_params=pltpu.CompilerParams(dimension_semantics=("arbitrary",)),
     )(*args)
-
-
-def apply_grad(lo, mid, hi, rows=40):
-    planes, height, depth = mid.shape
-    block = pick_block(planes)
-    full, blk = specs(mid.shape, block)
-    out = jax.ShapeDtypeStruct(mid.shape, jnp.float32)
-    return pl.pallas_call(
-        functools.partial(grad_kernel, block=block, rows=rows),
-        grid=(planes // block,),
-        in_specs=[full(lo.shape), full(mid.shape), full(hi.shape)],
-        out_specs=[blk, blk, blk],
-        out_shape=[out, out, out],
-        scratch_shapes=[pltpu.VMEM((planes + 2 * HALO, height + 2 * PADY, depth), jnp.float32)],
-        compiler_params=pltpu.CompilerParams(dimension_semantics=("arbitrary",)),
-    )(lo, mid, hi)
 
 
 def reduce_members(part, axis):

time: 123 us -> 127 us (1.033)
  Pallas kernels: 39.1 us -> 42.6 us
    pallas_call x4, Pallas kernels: 39.1 us -> 42.6 us  [apply_step(): pl.pallas_call(kernel, grid=(planes // block,), in_specs=in_specs, out_sp...]
  transfers between devices with their start and end apart: 14 -> 14, of which waited for: 7 -> 7; matrix products, arithmetic and copies ran while one was open for 3% -> 3% of each run, Pallas kernels for 17% -> 18%
where the time goes in v7:
time: 127 us; the launch traced here: 125 us
  Pallas kernels  42.6 us (34%)
  starting transfers between devices  34.5 us (27%)
  waiting for transfers between devices  25.9 us (20%)
  other arithmetic  14 us (11%)
  local copies, waits for them, and re-layouts  6.01 us (5%)
  between operations  1.78 us (1%)
    pallas_call x4, Pallas kernels, apply_step(): pl.pallas_call(kernel, grid=(planes // block,), in_specs=in_specs, out_sp...  42.6 us
    ppermute x4, starting transfers between devices, halos(): low = lax.ppermute(block[planes - HALO:], axis, forward)  12.7 us
    ppermute x2, waiting for transfers between devices, reduce_members(): rows = keep + lax.ppermute(give, axis, pairs)  9.44 us
    ppermute x2, waiting for transfers between devices, reduce_members(): other = lax.ppermute(rows, axis, pairs)  8.52 us
    ppermute x4, starting transfers between devices, halos(): high = lax.ppermute(block[:HALO], axis, backward)  8.45 us
    scatter-add x2, other arithmetic, inject(): flat = field.reshape(-1).at[where].add(jnp.where(valid, values, 0.0))  6.84 us
    ppermute x2, starting transfers between devices, reduce_members(): rows = keep + lax.ppermute(give, axis, pairs)  4.61 us
    ppermute x4, waiting for transfers between devices, halos(): high = lax.ppermute(block[:HALO], axis, backward)  4.18 us
  transfers between devices with their start and end apart: 14, of which 7 were waited for; matrix products, arithmetic and copies ran while one was open for 3% of the time, Pallas kernels for 18%

profile of v7, /device:TPU:9, one launch (start us, length us, event | category | flops | bytes accessed | tf_op | source)
XLA Modules:
  0.0 124.8 jit_solution(13122089050908116460)
XLA Ops:
  1.9 3.2 %collective-permute-start.2 = (f32[4,160,128]{2,1,0:T(8,128)S(1)}, f32[4,160,128]{2,1,0:T(8,128)S(1)}, u32[]{:S(2)}, u32[]{:S(2)}) collective-permute-start(f32[4,160,128]{2,1,0:T(8,128)S(1)} %get-tuple-element.27), channel_id=1, source_target_pairs={{0,1},{1,2},{2,3},{4,5},{5,6},{6,7},{8,9},{9,10},{10,11},{12,13},{... | collective-permute-start | bytes 983048 | tf_op jit(solution)/shard_map/ppermute | solution.py:234
  5.2 2.1 %collective-permute-start.3 = (f32[4,160,128]{2,1,0:T(8,128)S(1)}, f32[4,160,128]{2,1,0:T(8,128)S(1)}, u32[]{:S(2)}, u32[]{:S(2)}) collective-permute-start(f32[4,160,128]{2,1,0:T(8,128)S(1)} %get-tuple-element.26), channel_id=1, source_target_pairs={{1,0},{2,1},{3,2},{5,4},{6,5},{7,6},{9,8},{10,9},{11,10},{13,12},{... | collective-permute-start | bytes 983048 | tf_op jit(solution)/shard_map/ppermute | solution.py:235
  8.0 3.2 %collective-permute-start.4 = (f32[4,160,128]{2,1,0:T(8,128)}, f32[4,160,128]{2,1,0:T(8,128)S(1)}, u32[]{:S(2)}, u32[]{:S(2)}) collective-permute-start(f32[4,160,128]{2,1,0:T(8,128)} %get-tuple-element.25), channel_id=1, source_target_pairs={{0,1},{1,2},{2,3},{4,5},{5,6},{6,7},{8,9},{9,10},{10,11},{12,13},{... | collective-permute-start | bytes 983048 | tf_op jit(solution)/shard_map/ppermute | solution.py:234
  11.2 2.1 %collective-permute-start.5 = (f32[4,160,128]{2,1,0:T(8,128)S(1)}, f32[4,160,128]{2,1,0:T(8,128)S(1)}, u32[]{:S(2)}, u32[]{:S(2)}) collective-permute-start(f32[4,160,128]{2,1,0:T(8,128)S(1)} %get-tuple-element.24), channel_id=1, source_target_pairs={{1,0},{2,1},{3,2},{5,4},{6,5},{7,6},{9,8},{10,9},{11,10},{13,12},{... | collective-permute-start | bytes 983048 | tf_op jit(solution)/shard_map/ppermute | solution.py:235
  13.4 3.2 %collective-permute-start = (f32[4,160,128]{2,1,0:T(8,128)S(1)}, f32[4,160,128]{2,1,0:T(8,128)S(1)}, u32[]{:S(2)}, u32[]{:S(2)}) collective-permute-start(f32[4,160,128]{2,1,0:T(8,128)S(1)} %get-tuple-element.29), channel_id=1, source_target_pairs={{0,1},{1,2},{2,3},{4,5},{5,6},{6,7},{8,9},{9,10},{10,11},{12,13},{... | collective-permute-start | bytes 983048 | tf_op jit(solution)/shard_map/ppermute | solution.py:234
  19.3 2.1 %collective-permute-start.1 = (f32[4,160,128]{2,1,0:T(8,128)S(1)}, f32[4,160,128]{2,1,0:T(8,128)S(1)}, u32[]{:S(2)}, u32[]{:S(2)}) collective-permute-start(f32[4,160,128]{2,1,0:T(8,128)S(1)} %get-tuple-element.28), channel_id=1, source_target_pairs={{1,0},{2,1},{3,2},{5,4},{6,5},{7,6},{9,8},{10,9},{11,10},{13,12},{... | collective-permute-start | bytes 983048 | tf_op jit(solution)/shard_map/ppermute | solution.py:235
  23.5 14.0 %shard_map.113 = (f32[16,160,128]{2,1,0:T(8,128)}, f32[16,160,128]{2,1,0:T(8,128)}, f32[16,160,128]{2,1,0:T(8,128)}, f32[16,160,128]{2,1,0:T(8,128)}, f32[16,160...) custom-call(f32[4,160,128]{2,1,0:T(8,128)} %copy-done.6, ...), custom_call_target="tpu_custom_call" | custom-call | tf_op jit(solution)/shard_map/pallas_call | solution.py:193
  37.4 3.2 %collective-permute-start.6 = (f32[4,160,128]{2,1,0:T(8,128)}, f32[4,160,128]{2,1,0:T(8,128)S(1)}, u32[]{:S(2)}, u32[]{:S(2)}) collective-permute-start(f32[4,160,128]{2,1,0:T(8,128)} %get-tuple-element.16), channel_id=1, source_target_pairs={{0,1},{1,2},{2,3},{4,5},{5,6},{6,7},{8,9},{9,10},{10,11},{12,13},{... | collective-permute-start | bytes 983048 | tf_op jit(solution)/shard_map/ppermute | solution.py:243
  40.6 2.1 %collective-permute-start.7 = (f32[4,160,128]{2,1,0:T(8,128)}, f32[4,160,128]{2,1,0:T(8,128)S(1)}, u32[]{:S(2)}, u32[]{:S(2)}) collective-permute-start(f32[4,160,128]{2,1,0:T(8,128)} %get-tuple-element.18), channel_id=1, source_target_pairs={{1,0},{2,1},{3,2},{5,4},{6,5},{7,6},{9,8},{10,9},{11,10},{13,12},{... | collective-permute-start | bytes 983048 | tf_op jit(solution)/shard_map/ppermute | solution.py:243
  44.6 8.6 %shard_map.114 = f32[16,160,128]{2,1,0:T(8,128)} custom-call(f32[4,160,128]{2,1,0:T(8,128)} %copy-done.5, f32[16,160,128]{2,1,0:T(8,128)} %bitcast.47, f32[4,160,128]{2,1,0:T(8,128)} %copy-done.12, f32[16,160,128]{2,1,0:T(8,128)} %refs_3_.5, f32[16,160,128]{2,1,0:T(8,128)} %get-tuple-element.12.refs_4_, f32[16,160,128]{2,1,0:T(8,128)} %get-tuple-element.13.refs_5_, ...), custom_call_target="tpu_custom_call" | custom-call | tf_op jit(solution)/shard_map/pallas_call | solution.py:193
  54.2 11.4 %shard_map.115 = (f32[16,160,128]{2,1,0:T(8,128)}, f32[16,160,128]{2,1,0:T(8,128)}, f32[4,160,128]{2,1,0:T(8,128)}, f32[4,160,128]{2,1,0:T(8,128)}, f32[256,128]{1,0:T(8,128)}) custom-call(f32[4,160,128]{2,1,0:T(8,128)} %copy-done.13, f32[16,160,128]{2,1,0:T(8,128)} %get-tuple-element.17.refs_1_, f32[4,160,128]{2,1,0:T(8,128)} %copy-done.14, ...), custom_call_target="tpu_custom_call" | custom-call | tf_op jit(solution)/shard_map/pallas_call | solution.py:193
  66.7 2.5 %scatter_fusion = f32[327680]{0:T(1024)S(1)} fusion(f32[327680]{0:T(1024)S(1)} %bitcast.35, s32[256]{0:T(256)S(1)} %get-tuple-element.32, f32[256]{0:T(256)S(1)} %get-tuple-element.37), kind=kCustom, calls=%fused_computation | custom fusion | flops 256 | bytes 4096 | tf_op jit(solution)/shard_map/scatter-add | solution.py:247
  69.2 3.2 %collective-permute-start.8 = (f32[4,160,128]{2,1,0:T(8,128)S(1)}, f32[4,160,128]{2,1,0:T(8,128)S(1)}, u32[]{:S(2)}, u32[]{:S(2)}) collective-permute-start(f32[4,160,128]{2,1,0:T(8,128)S(1)} %bitcast.55), channel_id=1, source_target_pairs={{0,1},{1,2},{2,3},{4,5},{5,6},{6,7},{8,9},{9,10},{10,11},{12,13},{... | collective-permute-start | bytes 983048 | tf_op jit(solution)/shard_map/ppermute | solution.py:234
  72.4 2.1 %collective-permute-start.9 = (f32[4,160,128]{2,1,0:T(8,128)S(1)}, f32[4,160,128]{2,1,0:T(8,128)S(1)}, u32[]{:S(2)}, u32[]{:S(2)}) collective-permute-start(f32[4,160,128]{2,1,0:T(8,128)S(1)} %bitcast.54), channel_id=1, source_target_pairs={{1,0},{2,1},{3,2},{5,4},{6,5},{7,6},{9,8},{10,9},{11,10},{13,12},{... | collective-permute-start | bytes 983048 | tf_op jit(solution)/shard_map/ppermute | solution.py:235
  74.5 3.7 %collective-permute-done.8.refs_0_ = f32[4,160,128]{2,1,0:T(8,128)S(1)} collective-permute-done((f32[4,160,128]{2,1,0:T(8,128)S(1)}, f32[4,160,128]{2,1,0:T(8,128)S(1)}, u32[]{:S(2)}, u32[]{:S(2)}) %collective-permute-start.8) | collective-permute-done | bytes 327712 | tf_op jit(solution)/shard_map/ppermute | solution.py:234
  78.3 2.9 %collective-permute-done.9.refs_2_ = f32[4,160,128]{2,1,0:T(8,128)S(1)} collective-permute-done((f32[4,160,128]{2,1,0:T(8,128)S(1)}, f32[4,160,128]{2,1,0:T(8,128)S(1)}, u32[]{:S(2)}, u32[]{:S(2)}) %collective-permute-start.9) | collective-permute-done | bytes 327712 | tf_op jit(solution)/shard_map/ppermute | solution.py:235
  81.8 8.6 %shard_map.116 = f32[16,160,128]{2,1,0:T(8,128)} custom-call(f32[4,160,128]{2,1,0:T(8,128)} %copy-done.10, f32[16,160,128]{2,1,0:T(8,128)} %bitcast.36, f32[4,160,128]{2,1,0:T(8,128)} %copy-done.11, f32[16,160,128]{2,1,0:T(8,128)} %refs_3_.5, f32[16,160,128]{2,1,0:T(8,128)} %get-tuple-element.12.refs_4_, f32[16,160,128]{2,1,0:T(8,128)} %get-tuple-element.13.refs_5_, ...), custom_call_target="tpu_custom_call" | custom-call | tf_op jit(solution)/shard_map/pallas_call | solution.py:193
  90.5 4.4 %scatter_fusion.1 = f32[327680]{0:T(1024)} fusion(f32[327680]{0:T(1024)} %bitcast.42, s32[256]{0:T(256)S(1)} %get-tuple-element.32, f32[256]{0:T(256)S(1)} %get-tuple-element.36), kind=kCustom, calls=%fused_computation.1 | custom fusion | flops 256 | bytes 4096 | tf_op jit(solution)/shard_map/scatter-add | solution.py:247
  94.9 2.5 %multiply_add_fusion = f32[16,160,128]{2,1,0:T(8,128)S(1)} fusion(f32[16,160,128]{2,1,0:T(8,128)} %bitcast.43, f32[16,160,128]{2,1,0:T(8,128)} %get-tuple-element.21, f32[16,160,128]{2,1,0:T(8,128)S(1)} %bitcast.37, f32[16,160,128]{2,1,0:T(8,128)} %get-tuple-element.20), kind=kLoop, calls=%fused_computation.3 | loop fusion | flops 983040 | bytes 6553600 | tf_op jit(solution)/shard_map/add | solution.py:309
  97.4 3.3 %collective-permute-start.10 = (f32[1280,128]{1,0:T(8,128)S(1)}, f32[1280,128]{1,0:T(8,128)S(1)}, u32[]{:S(2)}, u32[]{:S(2)}) collective-permute-start(f32[1280,128]{1,0:T(8,128)S(1)} %constant_dynamic-slice_fusion.1), channel_id=1, source_target_pairs={{0,4},{4,0},{8,12},{12,8},{1,5},{5,1},{9,13},{13,9},{2,6},{6,2},{1... | collective-permute-start | bytes 1966088 | tf_op jit(solution)/shard_map/ppermute | solution.py:218
  100.7 1.7 %collective-permute-done.10 = f32[1280,128]{1,0:T(8,128)S(1)} collective-permute-done((f32[1280,128]{1,0:T(8,128)S(1)}, f32[1280,128]{1,0:T(8,128)S(1)}, u32[]{:S(2)}, u32[]{:S(2)}) %collective-permute-start.10) | collective-permute-done | bytes 655392 | tf_op jit(solution)/shard_map/ppermute | solution.py:218
  103.8 7.7 %collective-permute-done.11 = f32[640,128]{1,0:T(8,128)S(1)} collective-permute-done((f32[640,128]{1,0:T(8,128)S(1)}, f32[640,128]{1,0:T(8,128)S(1)}, u32[]{:S(2)}, u32[]{:S(2)}) %collective-permute-start.11) | collective-permute-done | bytes 327712 | tf_op jit(solution)/shard_map/ppermute | solution.py:218
  112.9 6.8 %collective-permute-done.12 = f32[640,128]{1,0:T(8,128)S(1)} collective-permute-done((f32[640,128]{1,0:T(8,128)S(1)}, f32[640,128]{1,0:T(8,128)S(1)}, u32[]{:S(2)}, u32[]{:S(2)}) %collective-permute-start.12) | collective-permute-done | bytes 327712 | tf_op jit(solution)/shard_map/ppermute | solution.py:224
  119.7 2.2 %collective-permute-start.13 = (f32[1280,128]{1,0:T(8,128)S(1)}, f32[1280,128]{1,0:T(8,128)S(1)}, u32[]{:S(2)}, u32[]{:S(2)}) collective-permute-start(f32[1280,128]{1,0:T(8,128)S(1)} %maximum_select_fusion.1), channel_id=1, source_target_pairs={{0,4},{4,0},{8,12},{12,8},{1,5},{5,1},{9,13},{13,9},{2,6},{6,2},{1... | collective-permute-start | bytes 1966088 | tf_op jit(solution)/shard_map/ppermute | solution.py:224
  (68 shorter events, 16.3 us)
Async XLA Ops:
  0.6 6.6 %copy-start = (f32[16,160,128]{2,1,0:T(8,128)S(1)}, f32[16,160,128]{2,1,0:T(8,128)}, u32[]{:S(2)}) copy-start(f32[16,160,128]{2,1,0:T(8,128)} %refs_3_.5) | copy-start | bytes 3932164
  0.6 12.7 %copy-start.4 = (f32[1,16,160,128]{3,2,1,0:T(8,128)S(1)}, f32[1,16,160,128]{3,2,1,0:T(8,128)}, u32[]{:S(2)}) copy-start(f32[1,16,160,128]{3,2,1,0:T(8,128)} %param.14) | copy-start | bytes 3932164
  1.9 17.3 %collective-permute-start.2 = (f32[4,160,128]{2,1,0:T(8,128)S(1)}, f32[4,160,128]{2,1,0:T(8,128)S(1)}, u32[]{:S(2)}, u32[]{:S(2)}) collective-permute-start(f32[4,160,128]{2,1,0:T(8,128)S(1)} %get-tuple-element.27), channel_id=1, source_target_pairs={{0,1},{1,2},{2,3},{4,5},{5,6},{6,7},{8,9},{9,10},{10,11},{12,13},{... | collective-permute-start | bytes 983048 | tf_op jit(solution)/shard_map/ppermute | solution.py:234
  5.1 12.2 %copy-start.15 = (s32[256]{0:T(256)S(1)}, s32[256]{0:T(256)}, u32[]{:S(2)}) copy-start(s32[256]{0:T(256)} %param.18) | copy-start | bytes 3076
  5.2 13.5 %copy-start.17 = (f32[2]{0:T(128)S(1)}, f32[2]{0:T(128)}, u32[]{:S(2)}) copy-start(f32[2]{0:T(128)} %param.16) | copy-start | bytes 28
  5.2 16.2 %collective-permute-start.3 = (f32[4,160,128]{2,1,0:T(8,128)S(1)}, f32[4,160,128]{2,1,0:T(8,128)S(1)}, u32[]{:S(2)}, u32[]{:S(2)}) collective-permute-start(f32[4,160,128]{2,1,0:T(8,128)S(1)} %get-tuple-element.26), channel_id=1, source_target_pairs={{1,0},{2,1},{3,2},{5,4},{6,5},{7,6},{9,8},{10,9},{11,10},{13,12},{... | collective-permute-start | bytes 983048 | tf_op jit(solution)/shard_map/ppermute | solution.py:235
  8.0 13.4 %collective-permute-start.4 = (f32[4,160,128]{2,1,0:T(8,128)}, f32[4,160,128]{2,1,0:T(8,128)S(1)}, u32[]{:S(2)}, u32[]{:S(2)}) collective-permute-start(f32[4,160,128]{2,1,0:T(8,128)} %get-tuple-element.25), channel_id=1, source_target_pairs={{0,1},{1,2},{2,3},{4,5},{5,6},{6,7},{8,9},{9,10},{10,11},{12,13},{... | collective-permute-start | bytes 983048 | tf_op jit(solution)/shard_map/ppermute | solution.py:234
  11.2 11.5 %collective-permute-start.5 = (f32[4,160,128]{2,1,0:T(8,128)S(1)}, f32[4,160,128]{2,1,0:T(8,128)S(1)}, u32[]{:S(2)}, u32[]{:S(2)}) collective-permute-start(f32[4,160,128]{2,1,0:T(8,128)S(1)} %get-tuple-element.24), channel_id=1, source_target_pairs={{1,0},{2,1},{3,2},{5,4},{6,5},{7,6},{9,8},{10,9},{11,10},{13,12},{... | collective-permute-start | bytes 983048 | tf_op jit(solution)/shard_map/ppermute | solution.py:235
  13.4 30.4 %collective-permute-start = (f32[4,160,128]{2,1,0:T(8,128)S(1)}, f32[4,160,128]{2,1,0:T(8,128)S(1)}, u32[]{:S(2)}, u32[]{:S(2)}) collective-permute-start(f32[4,160,128]{2,1,0:T(8,128)S(1)} %get-tuple-element.29), channel_id=1, source_target_pairs={{0,1},{1,2},{2,3},{4,5},{5,6},{6,7},{8,9},{9,10},{10,11},{12,13},{... | collective-permute-start | bytes 983048 | tf_op jit(solution)/shard_map/ppermute | solution.py:234
  19.3 3.5 %copy-start.6 = (f32[4,160,128]{2,1,0:T(8,128)}, f32[4,160,128]{2,1,0:T(8,128)S(1)}, u32[]{:S(2)}) copy-start(f32[4,160,128]{2,1,0:T(8,128)S(1)} %collective-permute-done.2.refs_0_) | copy-start | bytes 983044
  19.3 24.6 %collective-permute-start.1 = (f32[4,160,128]{2,1,0:T(8,128)S(1)}, f32[4,160,128]{2,1,0:T(8,128)S(1)}, u32[]{:S(2)}, u32[]{:S(2)}) collective-permute-start(f32[4,160,128]{2,1,0:T(8,128)S(1)} %get-tuple-element.28), channel_id=1, source_target_pairs={{1,0},{2,1},{3,2},{5,4},{6,5},{7,6},{9,8},{10,9},{11,10},{13,12},{... | collective-permute-start | bytes 983048 | tf_op jit(solution)/shard_map/ppermute | solution.py:235
  37.4 15.9 %collective-permute-start.6 = (f32[4,160,128]{2,1,0:T(8,128)}, f32[4,160,128]{2,1,0:T(8,128)S(1)}, u32[]{:S(2)}, u32[]{:S(2)}) collective-permute-start(f32[4,160,128]{2,1,0:T(8,128)} %get-tuple-element.16), channel_id=1, source_target_pairs={{0,1},{1,2},{2,3},{4,5},{5,6},{6,7},{8,9},{9,10},{10,11},{12,13},{... | collective-permute-start | bytes 983048 | tf_op jit(solution)/shard_map/ppermute | solution.py:243
  40.6 12.7 %collective-permute-start.7 = (f32[4,160,128]{2,1,0:T(8,128)}, f32[4,160,128]{2,1,0:T(8,128)S(1)}, u32[]{:S(2)}, u32[]{:S(2)}) collective-permute-start(f32[4,160,128]{2,1,0:T(8,128)} %get-tuple-element.18), channel_id=1, source_target_pairs={{1,0},{2,1},{3,2},{5,4},{6,5},{7,6},{9,8},{10,9},{11,10},{13,12},{... | collective-permute-start | bytes 983048 | tf_op jit(solution)/shard_map/ppermute | solution.py:243
  54.2 12.4 %copy-start.16 = (f32[2,256]{1,0:T(2,128)S(1)}, f32[2,256]{1,0:T(2,128)}, u32[]{:S(2)}) copy-start(f32[2,256]{1,0:T(2,128)} %param.19) | copy-start | bytes 6148
  54.2 12.5 %copy-start.1 = (f32[16,160,128]{2,1,0:T(8,128)S(1)}, f32[16,160,128]{2,1,0:T(8,128)}, u32[]{:S(2)}) copy-start(f32[16,160,128]{2,1,0:T(8,128)} %shard_map.114) | copy-start | bytes 3932164
  69.1 12.0 %copy-start.2 = (f32[327680]{0:T(1024)}, f32[327680]{0:T(1024)S(1)}, u32[]{:S(2)}) copy-start(f32[327680]{0:T(1024)S(1)} %scatter_fusion) | copy-start | bytes 3932164
  69.2 9.1 %collective-permute-start.8 = (f32[4,160,128]{2,1,0:T(8,128)S(1)}, f32[4,160,128]{2,1,0:T(8,128)S(1)}, u32[]{:S(2)}, u32[]{:S(2)}) collective-permute-start(f32[4,160,128]{2,1,0:T(8,128)S(1)} %bitcast.55), channel_id=1, source_target_pairs={{0,1},{1,2},{2,3},{4,5},{5,6},{6,7},{8,9},{9,10},{10,11},{12,13},{... | collective-permute-start | bytes 983048 | tf_op jit(solution)/shard_map/ppermute | solution.py:234
  72.4 8.8 %collective-permute-start.9 = (f32[4,160,128]{2,1,0:T(8,128)S(1)}, f32[4,160,128]{2,1,0:T(8,128)S(1)}, u32[]{:S(2)}, u32[]{:S(2)}) collective-permute-start(f32[4,160,128]{2,1,0:T(8,128)S(1)} %bitcast.54), channel_id=1, source_target_pairs={{1,0},{2,1},{3,2},{5,4},{6,5},{7,6},{9,8},{10,9},{11,10},{13,12},{... | collective-permute-start | bytes 983048 | tf_op jit(solution)/shard_map/ppermute | solution.py:235
  78.3 2.9 %copy-start.10 = (f32[4,160,128]{2,1,0:T(8,128)}, f32[4,160,128]{2,1,0:T(8,128)S(1)}, u32[]{:S(2)}) copy-start(f32[4,160,128]{2,1,0:T(8,128)S(1)} %collective-permute-done.8.refs_0_) | copy-start | bytes 983044
  90.5 4.4 %copy-start.3 = (f32[327680]{0:T(1024)S(1)}, f32[327680]{0:T(1024)}, u32[]{:S(2)}) copy-start(f32[327680]{0:T(1024)} %copy-done.2) | copy-start | bytes 3932164
  97.4 5.1 %collective-permute-start.10 = (f32[1280,128]{1,0:T(8,128)S(1)}, f32[1280,128]{1,0:T(8,128)S(1)}, u32[]{:S(2)}, u32[]{:S(2)}) collective-permute-start(f32[1280,128]{1,0:T(8,128)S(1)} %constant_dynamic-slice_fusion.1), channel_id=1, source_target_pairs={{0,4},{4,0},{8,12},{12,8},{1,5},{5,1},{9,13},{13,9},{2,6},{6,2},{1... | collective-permute-start | bytes 1966088 | tf_op jit(solution)/shard_map/ppermute | solution.py:218
  102.6 9.0 %collective-permute-start.11 = (f32[640,128]{1,0:T(8,128)S(1)}, f32[640,128]{1,0:T(8,128)S(1)}, u32[]{:S(2)}, u32[]{:S(2)}) collective-permute-start(f32[640,128]{1,0:T(8,128)S(1)} %constant_dynamic-slice_fusion), channel_id=1, source_target_pairs={{0,8},{4,12},{8,0},{12,4},{1,9},{5,13},{9,1},{13,5},{2,10},{6,14},... | collective-permute-start | bytes 983048 | tf_op jit(solution)/shard_map/ppermute | solution.py:218
  111.6 8.1 %collective-permute-start.12 = (f32[640,128]{1,0:T(8,128)S(1)}, f32[640,128]{1,0:T(8,128)S(1)}, u32[]{:S(2)}, u32[]{:S(2)}) collective-permute-start(f32[640,128]{1,0:T(8,128)S(1)} %add_multiply_fusion), channel_id=1, source_target_pairs={{0,8},{4,12},{8,0},{12,4},{1,9},{5,13},{9,1},{13,5},{2,10},{6,14},... | collective-permute-start | bytes 983048 | tf_op jit(solution)/shard_map/ppermute | solution.py:224
  119.7 3.9 %collective-permute-start.13 = (f32[1280,128]{1,0:T(8,128)S(1)}, f32[1280,128]{1,0:T(8,128)S(1)}, u32[]{:S(2)}, u32[]{:S(2)}) collective-permute-start(f32[1280,128]{1,0:T(8,128)S(1)} %maximum_select_fusion.1), channel_id=1, source_target_pairs={{0,4},{4,0},{8,12},{12,8},{1,5},{5,1},{9,13},{13,9},{2,6},{6,2},{1... | collective-permute-start | bytes 1966088 | tf_op jit(solution)/shard_map/ppermute | solution.py:224
  (8 other events, 7.3 us)

commit v8 on v5

--- a/solution.py
+++ b/solution.py
@@ -327,10 +327,27 @@
     residual = jnp.where(rec_valid, jnp.stack(samples) - observed, 0.0)
     older, now = (adj_prev[0], adj_cur[0])
     image_part = jnp.zeros(buoyancy.shape, jnp.float32)
+    edge = HALO * height * depth
+    count = lax.axis_size("tile")
+    forward = [(i, i + 1) for i in range(count - 1)]
+    backward = [(target, source) for source, target in forward]
+
+    def near(start):
+        local = rec_cell - start
+        valid = (local >= 0) & (local < edge)
+        return jnp.clip(local, 0, edge - 1), valid
+
+    below_local, below_valid = near(offset - edge)
+    above_local, above_valid = near(offset + volume)
+    lo, hi = halos(now, "tile")
     for j in range(steps):
-        lo, hi = halos(now, "tile")
         (newer,) = apply_step(lo, now, hi, buoyancy, grad_b, speed, older, want_force=False)
-        newer = inject(newer, rec_local, rec_valid, residual[steps - 1 - j])
+        values = residual[steps - 1 - j]
+        if j + 1 < steps:
+            lo, hi = edge_halos(newer[:HALO], newer[planes - HALO:], "tile")
+            lo = inject(lo, below_local, below_valid, lax.ppermute(values, "tile", forward))
+            hi = inject(hi, above_local, above_valid, lax.ppermute(values, "tile", backward))
+        newer = inject(newer, rec_local, rec_valid, values)
         image_part = image_part + newer * forces[steps - 1 - j]
         older, now = (now, newer)
     image = reduce_members(image_part, "real")

time: 123 us -> 129 us (1.049)
  waiting for transfers between devices: 25.9 us -> 19.4 us
  starting transfers between devices: 34.5 us -> 40.2 us
  other arithmetic: 14 us -> 17.7 us
  Pallas kernels: 39.1 us -> 40.6 us
    ppermute x0 -> x2, starting transfers between devices: none -> 5.28 us  [the longest x1 3.35 us: shards(): lax.ppermute(values, 'tile', forward)]
    scatter-add x2 -> x4, other arithmetic: 6.83 us -> 11.3 us  [inject(): flat = field.reshape(-1).at[where].add(jnp.where(valid, values, 0.0))]
    ppermute x4 -> x3, waiting for transfers between devices: 3.73 us -> 0.01 us  [halos(): low = lax.ppermute(block[planes - HALO:], axis, forward)]
    ppermute x1 -> x2, starting transfers between devices: 3.19 us -> 6.55 us  [edge_halos(): lax.ppermute(high_edge, axis, forward)]
    ppermute x4 -> x3, starting transfers between devices: 12.7 us -> 9.55 us  [halos(): low = lax.ppermute(block[planes - HALO:], axis, forward)]
    ppermute x4 -> x3, waiting for transfers between devices: 4.19 us -> 1.38 us  [halos(): high = lax.ppermute(block[:HALO], axis, backward)]
    ppermute x4 -> x3, starting transfers between devices: 8.44 us -> 6.32 us  [halos(): high = lax.ppermute(block[:HALO], axis, backward)]
    ppermute x1 -> x2, starting transfers between devices: 2.11 us -> 4.03 us  [edge_halos(): lax.ppermute(low_edge, axis, backward)]
  transfers between devices with their start and end apart: 14 -> 16, of which waited for: 7 -> 5; matrix products, arithmetic and copies ran while one was open for 3% -> 8% of each run, Pallas kernels for 17% -> 25%
where the time goes in v8:
time: 129 us; the launch traced here: 127 us
  Pallas kernels  40.6 us (31%)
  starting transfers between devices  40.2 us (31%)
  waiting for transfers between devices  19.4 us (15%)
  other arithmetic  17.7 us (14%)
  local copies, waits for them, and re-layouts  7.1 us (6%)
  between operations  1.83 us (1%)
    pallas_call x4, Pallas kernels, apply_step(): pl.pallas_call(kernel, grid=(planes // block,), in_specs=in_specs, out_sp...  40.6 us
    scatter-add x4, other arithmetic, inject(): flat = field.reshape(-1).at[where].add(jnp.where(valid, values, 0.0))  11.3 us
    ppermute x3, starting transfers between devices, halos(): low = lax.ppermute(block[planes - HALO:], axis, forward)  9.55 us
    ppermute x2, waiting for transfers between devices, reduce_members(): rows = keep + lax.ppermute(give, axis, pairs)  9.44 us
    ppermute x2, waiting for transfers between devices, reduce_members(): other = lax.ppermute(rows, axis, pairs)  8.52 us
    ppermute x2, starting transfers between devices, edge_halos(): lax.ppermute(high_edge, axis, forward)  6.55 us
    ppermute x3, starting transfers between devices, halos(): high = lax.ppermute(block[:HALO], axis, backward)  6.32 us
    ppermute x2, starting transfers between devices, reduce_members(): rows = keep + lax.ppermute(give, axis, pairs)  5.05 us
  transfers between devices with their start and end apart: 16, of which 5 were waited for; matrix products, arithmetic and copies ran while one was open for 8% of the time, Pallas kernels for 25%

profile of v8, /device:TPU:9, one launch (start us, length us, event | category | flops | bytes accessed | tf_op | source)
XLA Modules:
  0.0 126.8 jit_solution(14298345793741563080)
XLA Ops:
  1.9 3.2 %collective-permute-start.2 = (f32[4,160,128]{2,1,0:T(8,128)S(1)}, f32[4,160,128]{2,1,0:T(8,128)S(1)}, u32[]{:S(2)}, u32[]{:S(2)}) collective-permute-start(f32[4,160,128]{2,1,0:T(8,128)S(1)} %get-tuple-element.27), channel_id=1, source_target_pairs={{0,1},{1,2},{2,3},{4,5},{5,6},{6,7},{8,9},{9,10},{10,11},{12,13},{... | collective-permute-start | bytes 983048 | tf_op jit(solution)/shard_map/ppermute | solution.py:259
  5.2 2.1 %collective-permute-start.3 = (f32[4,160,128]{2,1,0:T(8,128)S(1)}, f32[4,160,128]{2,1,0:T(8,128)S(1)}, u32[]{:S(2)}, u32[]{:S(2)}) collective-permute-start(f32[4,160,128]{2,1,0:T(8,128)S(1)} %get-tuple-element.26), channel_id=1, source_target_pairs={{1,0},{2,1},{3,2},{5,4},{6,5},{7,6},{9,8},{10,9},{11,10},{13,12},{... | collective-permute-start | bytes 983048 | tf_op jit(solution)/shard_map/ppermute | solution.py:260
  8.0 3.2 %collective-permute-start.4 = (f32[4,160,128]{2,1,0:T(8,128)}, f32[4,160,128]{2,1,0:T(8,128)S(1)}, u32[]{:S(2)}, u32[]{:S(2)}) collective-permute-start(f32[4,160,128]{2,1,0:T(8,128)} %get-tuple-element.25), channel_id=1, source_target_pairs={{0,1},{1,2},{2,3},{4,5},{5,6},{6,7},{8,9},{9,10},{10,11},{12,13},{... | collective-permute-start | bytes 983048 | tf_op jit(solution)/shard_map/ppermute | solution.py:259
  11.2 2.1 %collective-permute-start.5 = (f32[4,160,128]{2,1,0:T(8,128)S(1)}, f32[4,160,128]{2,1,0:T(8,128)S(1)}, u32[]{:S(2)}, u32[]{:S(2)}) collective-permute-start(f32[4,160,128]{2,1,0:T(8,128)S(1)} %get-tuple-element.24), channel_id=1, source_target_pairs={{1,0},{2,1},{3,2},{5,4},{6,5},{7,6},{9,8},{10,9},{11,10},{13,12},{... | collective-permute-start | bytes 983048 | tf_op jit(solution)/shard_map/ppermute | solution.py:260
  13.4 3.2 %collective-permute-start = (f32[4,160,128]{2,1,0:T(8,128)S(1)}, f32[4,160,128]{2,1,0:T(8,128)S(1)}, u32[]{:S(2)}, u32[]{:S(2)}) collective-permute-start(f32[4,160,128]{2,1,0:T(8,128)S(1)} %get-tuple-element.29), channel_id=1, source_target_pairs={{0,1},{1,2},{2,3},{4,5},{5,6},{6,7},{8,9},{9,10},{10,11},{12,13},{... | collective-permute-start | bytes 983048 | tf_op jit(solution)/shard_map/ppermute | solution.py:259
  18.6 2.1 %collective-permute-start.1 = (f32[4,160,128]{2,1,0:T(8,128)S(1)}, f32[4,160,128]{2,1,0:T(8,128)S(1)}, u32[]{:S(2)}, u32[]{:S(2)}) collective-permute-start(f32[4,160,128]{2,1,0:T(8,128)S(1)} %get-tuple-element.28), channel_id=1, source_target_pairs={{1,0},{2,1},{3,2},{5,4},{6,5},{7,6},{9,8},{10,9},{11,10},{13,12},{... | collective-permute-start | bytes 983048 | tf_op jit(solution)/shard_map/ppermute | solution.py:260
  23.5 13.1 %shard_map.113 = (f32[16,160,128]{2,1,0:T(8,128)}, f32[16,160,128]{2,1,0:T(8,128)}, f32[16,160,128]{2,1,0:T(8,128)}, f32[16,160,128]{2,1,0:T(8,128)}, f32[16,160...) custom-call(f32[4,160,128]{2,1,0:T(8,128)} %copy-done.8, ...), custom_call_target="tpu_custom_call" | custom-call | tf_op jit(solution)/shard_map/pallas_call | solution.py:202
  36.5 3.2 %collective-permute-start.6 = (f32[4,160,128]{2,1,0:T(8,128)}, f32[4,160,128]{2,1,0:T(8,128)S(1)}, u32[]{:S(2)}, u32[]{:S(2)}) collective-permute-start(f32[4,160,128]{2,1,0:T(8,128)} %get-tuple-element.16), channel_id=1, source_target_pairs={{0,1},{1,2},{2,3},{4,5},{5,6},{6,7},{8,9},{9,10},{10,11},{12,13},{... | collective-permute-start | bytes 983048 | tf_op jit(solution)/shard_map/ppermute | solution.py:268
  39.7 2.1 %collective-permute-start.7 = (f32[4,160,128]{2,1,0:T(8,128)}, f32[4,160,128]{2,1,0:T(8,128)S(1)}, u32[]{:S(2)}, u32[]{:S(2)}) collective-permute-start(f32[4,160,128]{2,1,0:T(8,128)} %get-tuple-element.18), channel_id=1, source_target_pairs={{1,0},{2,1},{3,2},{5,4},{6,5},{7,6},{9,8},{10,9},{11,10},{13,12},{... | collective-permute-start | bytes 983048 | tf_op jit(solution)/shard_map/ppermute | solution.py:268
  42.8 8.3 %shard_map.114 = f32[16,160,128]{2,1,0:T(8,128)} custom-call(f32[4,160,128]{2,1,0:T(8,128)} %copy-done.7, f32[16,160,128]{2,1,0:T(8,128)} %bitcast.49, f32[4,160,128]{2,1,0:T(8,128)} %copy-done.13, f32[16,160,128]{2,1,0:T(8,128)} %refs_3_.5, f32[16,160,128]{2,1,0:T(8,128)} %get-tuple-element.12.refs_4_, f32[16,160,128]{2,1,0:T(8,128)} %get-tuple-element.13.refs_5_, ...), custom_call_target="tpu_custom_call" | custom-call | tf_op jit(solution)/shard_map/pallas_call | solution.py:202
  54.1 3.4 %collective-permute-start.8 = (f32[4,160,128]{2,1,0:T(8,128)S(1)}, f32[4,160,128]{2,1,0:T(8,128)S(1)}, u32[]{:S(2)}, u32[]{:S(2)}) collective-permute-start(f32[4,160,128]{2,1,0:T(8,128)S(1)} %get-tuple-element.23), channel_id=1, source_target_pairs={{0,1},{1,2},{2,3},{4,5},{5,6},{6,7},{8,9},{9,10},{10,11},{12,13},{... | collective-permute-start | bytes 983048 | tf_op jit(solution)/shard_map/ppermute | solution.py:268
  58.6 11.0 %shard_map.115 = (f32[16,160,128]{2,1,0:T(8,128)}, f32[16,160,128]{2,1,0:T(8,128)}, f32[4,160,128]{2,1,0:T(8,128)}, f32[4,160,128]{2,1,0:T(8,128)}, f32[256,128]{1,0:T(8,128)}) custom-call(f32[4,160,128]{2,1,0:T(8,128)} %copy-done.12, f32[16,160,128]{2,1,0:T(8,128)} %get-tuple-element.17.refs_1_, f32[4,160,128]{2,1,0:T(8,128)} %copy-done.14, ...), custom_call_target="tpu_custom_call" | custom-call | tf_op jit(solution)/shard_map/pallas_call | solution.py:202
  70.6 1.9 %collective-permute-start.11 = (f32[256]{0:T(256)S(1)}, f32[256]{0:T(256)S(1)}, u32[]{:S(2)}, u32[]{:S(2)}) collective-permute-start(f32[256]{0:T(256)S(1)} %bitcast.65), channel_id=1, source_target_pairs={{1,0},{2,1},{3,2},{5,4},{6,5},{7,6},{9,8},{10,9},{11,10},{13,12},{... | collective-permute-start | bytes 3080 | tf_op jit(solution)/shard_map/ppermute | solution.py:349
  72.5 3.3 %collective-permute-start.9 = (f32[256]{0:T(256)S(1)}, f32[256]{0:T(256)S(1)}, u32[]{:S(2)}, u32[]{:S(2)}) collective-permute-start(f32[256]{0:T(256)S(1)} %bitcast.66), channel_id=1, source_target_pairs={{0,1},{1,2},{2,3},{4,5},{5,6},{6,7},{8,9},{9,10},{10,11},{12,13},{... | collective-permute-start | bytes 3080 | tf_op jit(solution)/shard_map/ppermute | solution.py:348
  75.9 2.4 %scatter_fusion = f32[327680]{0:T(1024)S(1)} fusion(f32[327680]{0:T(1024)S(1)} %bitcast.37, s32[256]{0:T(256)S(1)} %get-tuple-element.35, f32[256]{0:T(256)S(1)} %get-tuple-element.41), kind=kCustom, calls=%fused_computation | custom fusion | flops 256 | bytes 4096 | tf_op jit(solution)/shard_map/scatter-add | solution.py:272
  78.4 2.1 %scatter_fusion.2 = f32[81920]{0:T(1024)S(1)} fusion(f32[81920]{0:T(1024)S(1)} %bitcast.53, s32[256]{0:T(256)S(1)} %get-tuple-element.34, f32[256]{0:T(256)S(1)} %get-tuple-element.32), kind=kCustom, calls=%fused_computation.2 | custom fusion | flops 256 | bytes 4096 | tf_op jit(solution)/shard_map/scatter-add | solution.py:272
  80.5 2.4 %scatter_fusion.1 = f32[81920]{0:T(1024)S(1)} fusion(f32[81920]{0:T(1024)S(1)} %bitcast.51, s32[256]{0:T(256)S(1)} %get-tuple-element.39, f32[256]{0:T(256)S(1)} %get-tuple-element.33), kind=kCustom, calls=%fused_computation.1 | custom fusion | flops 256 | bytes 4096 | tf_op jit(solution)/shard_map/scatter-add | solution.py:272
  83.6 8.3 %shard_map.116 = f32[16,160,128]{2,1,0:T(8,128)} custom-call(f32[4,160,128]{2,1,0:T(8,128)} %bitcast.52, f32[16,160,128]{2,1,0:T(8,128)} %bitcast.38, f32[4,160,128]{2,1,0:T(8,128)} %bitcast.54, f32[16,160,128]{2,1,0:T(8,128)} %refs_3_.5, f32[16,160,128]{2,1,0:T(8,128)} %get-tuple-element.12.refs_4_, f32[16,160,128]{2,1,0:T(8,128)} %get-tuple-element.13.refs_5_, ...), custom_call_target="tpu_custom_call" | custom-call | tf_op jit(solution)/shard_map/pallas_call | solution.py:202
  91.9 4.4 %scatter_fusion.3 = f32[327680]{0:T(1024)} fusion(f32[327680]{0:T(1024)} %bitcast.44, s32[256]{0:T(256)S(1)} %get-tuple-element.35, f32[256]{0:T(256)S(1)} %get-tuple-element.40), kind=kCustom, calls=%fused_computation.3 | custom fusion | flops 256 | bytes 4096 | tf_op jit(solution)/shard_map/scatter-add | solution.py:272
  96.3 2.6 %multiply_add_fusion = f32[16,160,128]{2,1,0:T(8,128)S(1)} fusion(f32[16,160,128]{2,1,0:T(8,128)} %bitcast.45, f32[16,160,128]{2,1,0:T(8,128)} %get-tuple-element.21, f32[16,160,128]{2,1,0:T(8,128)S(1)} %bitcast.39, f32[16,160,128]{2,1,0:T(8,128)} %get-tuple-element.20), kind=kLoop, calls=%fused_computation.5 | loop fusion | flops 983040 | bytes 6553600 | tf_op jit(solution)/shard_map/add | solution.py:351
  99.0 3.8 %collective-permute-start.12 = (f32[1280,128]{1,0:T(8,128)S(1)}, f32[1280,128]{1,0:T(8,128)S(1)}, u32[]{:S(2)}, u32[]{:S(2)}) collective-permute-start(f32[1280,128]{1,0:T(8,128)S(1)} %constant_dynamic-slice_fusion.1), channel_id=1, source_target_pairs={{0,4},{4,0},{8,12},{12,8},{1,5},{5,1},{9,13},{13,9},{2,6},{6,2},{1... | collective-permute-start | bytes 1966088 | tf_op jit(solution)/shard_map/ppermute | solution.py:243
  105.8 7.7 %collective-permute-done.13 = f32[640,128]{1,0:T(8,128)S(1)} collective-permute-done((f32[640,128]{1,0:T(8,128)S(1)}, f32[640,128]{1,0:T(8,128)S(1)}, u32[]{:S(2)}, u32[]{:S(2)}) %collective-permute-start.13) | collective-permute-done | bytes 327712 | tf_op jit(solution)/shard_map/ppermute | solution.py:243
  114.9 6.8 %collective-permute-done.14 = f32[640,128]{1,0:T(8,128)S(1)} collective-permute-done((f32[640,128]{1,0:T(8,128)S(1)}, f32[640,128]{1,0:T(8,128)S(1)}, u32[]{:S(2)}, u32[]{:S(2)}) %collective-permute-start.14) | collective-permute-done | bytes 327712 | tf_op jit(solution)/shard_map/ppermute | solution.py:249
  121.7 2.2 %collective-permute-start.15 = (f32[1280,128]{1,0:T(8,128)S(1)}, f32[1280,128]{1,0:T(8,128)S(1)}, u32[]{:S(2)}, u32[]{:S(2)}) collective-permute-start(f32[1280,128]{1,0:T(8,128)S(1)} %maximum_select_fusion.1), channel_id=1, source_target_pairs={{0,4},{4,0},{8,12},{12,8},{1,5},{5,1},{9,13},{13,9},{2,6},{6,2},{1... | collective-permute-start | bytes 1966088 | tf_op jit(solution)/shard_map/ppermute | solution.py:249
  (77 shorter events, 20.2 us)
Async XLA Ops:
  0.6 6.6 %copy-start = (f32[16,160,128]{2,1,0:T(8,128)S(1)}, f32[16,160,128]{2,1,0:T(8,128)}, u32[]{:S(2)}) copy-start(f32[16,160,128]{2,1,0:T(8,128)} %refs_3_.5) | copy-start | bytes 3932164
  0.6 12.7 %copy-start.4 = (f32[1,16,160,128]{3,2,1,0:T(8,128)S(1)}, f32[1,16,160,128]{3,2,1,0:T(8,128)}, u32[]{:S(2)}) copy-start(f32[1,16,160,128]{3,2,1,0:T(8,128)} %param.14) | copy-start | bytes 3932164
  1.9 16.7 %collective-permute-start.2 = (f32[4,160,128]{2,1,0:T(8,128)S(1)}, f32[4,160,128]{2,1,0:T(8,128)S(1)}, u32[]{:S(2)}, u32[]{:S(2)}) collective-permute-start(f32[4,160,128]{2,1,0:T(8,128)S(1)} %get-tuple-element.27), channel_id=1, source_target_pairs={{0,1},{1,2},{2,3},{4,5},{5,6},{6,7},{8,9},{9,10},{10,11},{12,13},{... | collective-permute-start | bytes 983048 | tf_op jit(solution)/shard_map/ppermute | solution.py:259
  5.1 12.2 %copy-start.16 = (s32[256]{0:T(256)S(1)}, s32[256]{0:T(256)}, u32[]{:S(2)}) copy-start(s32[256]{0:T(256)} %param.18) | copy-start | bytes 3076
  5.2 12.9 %copy-start.18 = (f32[2]{0:T(128)S(1)}, f32[2]{0:T(128)}, u32[]{:S(2)}) copy-start(f32[2]{0:T(128)} %param.16) | copy-start | bytes 28
  5.2 16.2 %collective-permute-start.3 = (f32[4,160,128]{2,1,0:T(8,128)S(1)}, f32[4,160,128]{2,1,0:T(8,128)S(1)}, u32[]{:S(2)}, u32[]{:S(2)}) collective-permute-start(f32[4,160,128]{2,1,0:T(8,128)S(1)} %get-tuple-element.26), channel_id=1, source_target_pairs={{1,0},{2,1},{3,2},{5,4},{6,5},{7,6},{9,8},{10,9},{11,10},{13,12},{... | collective-permute-start | bytes 983048 | tf_op jit(solution)/shard_map/ppermute | solution.py:260
  8.0 13.3 %collective-permute-start.4 = (f32[4,160,128]{2,1,0:T(8,128)}, f32[4,160,128]{2,1,0:T(8,128)S(1)}, u32[]{:S(2)}, u32[]{:S(2)}) collective-permute-start(f32[4,160,128]{2,1,0:T(8,128)} %get-tuple-element.25), channel_id=1, source_target_pairs={{0,1},{1,2},{2,3},{4,5},{5,6},{6,7},{8,9},{9,10},{10,11},{12,13},{... | collective-permute-start | bytes 983048 | tf_op jit(solution)/shard_map/ppermute | solution.py:259
  11.2 11.5 %collective-permute-start.5 = (f32[4,160,128]{2,1,0:T(8,128)S(1)}, f32[4,160,128]{2,1,0:T(8,128)S(1)}, u32[]{:S(2)}, u32[]{:S(2)}) collective-permute-start(f32[4,160,128]{2,1,0:T(8,128)S(1)} %get-tuple-element.24), channel_id=1, source_target_pairs={{1,0},{2,1},{3,2},{5,4},{6,5},{7,6},{9,8},{10,9},{11,10},{13,12},{... | collective-permute-start | bytes 983048 | tf_op jit(solution)/shard_map/ppermute | solution.py:260
  13.4 28.5 %collective-permute-start = (f32[4,160,128]{2,1,0:T(8,128)S(1)}, f32[4,160,128]{2,1,0:T(8,128)S(1)}, u32[]{:S(2)}, u32[]{:S(2)}) collective-permute-start(f32[4,160,128]{2,1,0:T(8,128)S(1)} %get-tuple-element.29), channel_id=1, source_target_pairs={{0,1},{1,2},{2,3},{4,5},{5,6},{6,7},{8,9},{9,10},{10,11},{12,13},{... | collective-permute-start | bytes 983048 | tf_op jit(solution)/shard_map/ppermute | solution.py:259
  18.6 23.3 %collective-permute-start.1 = (f32[4,160,128]{2,1,0:T(8,128)S(1)}, f32[4,160,128]{2,1,0:T(8,128)S(1)}, u32[]{:S(2)}, u32[]{:S(2)}) collective-permute-start(f32[4,160,128]{2,1,0:T(8,128)S(1)} %get-tuple-element.28), channel_id=1, source_target_pairs={{1,0},{2,1},{3,2},{5,4},{6,5},{7,6},{9,8},{10,9},{11,10},{13,12},{... | collective-permute-start | bytes 983048 | tf_op jit(solution)/shard_map/ppermute | solution.py:260
  36.5 21.1 %collective-permute-start.6 = (f32[4,160,128]{2,1,0:T(8,128)}, f32[4,160,128]{2,1,0:T(8,128)S(1)}, u32[]{:S(2)}, u32[]{:S(2)}) collective-permute-start(f32[4,160,128]{2,1,0:T(8,128)} %get-tuple-element.16), channel_id=1, source_target_pairs={{0,1},{1,2},{2,3},{4,5},{5,6},{6,7},{8,9},{9,10},{10,11},{12,13},{... | collective-permute-start | bytes 983048 | tf_op jit(solution)/shard_map/ppermute | solution.py:268
  39.7 17.9 %collective-permute-start.7 = (f32[4,160,128]{2,1,0:T(8,128)}, f32[4,160,128]{2,1,0:T(8,128)S(1)}, u32[]{:S(2)}, u32[]{:S(2)}) collective-permute-start(f32[4,160,128]{2,1,0:T(8,128)} %get-tuple-element.18), channel_id=1, source_target_pairs={{1,0},{2,1},{3,2},{5,4},{6,5},{7,6},{9,8},{10,9},{11,10},{13,12},{... | collective-permute-start | bytes 983048 | tf_op jit(solution)/shard_map/ppermute | solution.py:268
  51.1 6.5 %copy-start.15 = (f32[256,128]{1,0:T(8,128)S(1)}, f32[256,128]{1,0:T(8,128)}, u32[]{:S(2)}) copy-start(f32[256,128]{1,0:T(8,128)} %get-tuple-element.15) | copy-start | bytes 393220
  52.2 26.2 %collective-permute-start.10 = (f32[4,160,128]{2,1,0:T(8,128)S(1)}, f32[4,160,128]{2,1,0:T(8,128)S(1)}, u32[]{:S(2)}, u32[]{:S(2)}) collective-permute-start(f32[4,160,128]{2,1,0:T(8,128)S(1)} %get-tuple-element.22), channel_id=1, source_target_pairs={{1,0},{2,1},{3,2},{5,4},{6,5},{7,6},{9,8},{10,9},{11,10},{13,12},{... | collective-permute-start | bytes 983048 | tf_op jit(solution)/shard_map/ppermute | solution.py:268
  54.1 26.4 %collective-permute-start.8 = (f32[4,160,128]{2,1,0:T(8,128)S(1)}, f32[4,160,128]{2,1,0:T(8,128)S(1)}, u32[]{:S(2)}, u32[]{:S(2)}) collective-permute-start(f32[4,160,128]{2,1,0:T(8,128)S(1)} %get-tuple-element.23), channel_id=1, source_target_pairs={{0,1},{1,2},{2,3},{4,5},{5,6},{6,7},{8,9},{9,10},{10,11},{12,13},{... | collective-permute-start | bytes 983048 | tf_op jit(solution)/shard_map/ppermute | solution.py:268
  58.5 12.0 %copy-start.17 = (f32[2,256]{1,0:T(2,128)S(1)}, f32[2,256]{1,0:T(2,128)}, u32[]{:S(2)}) copy-start(f32[2,256]{1,0:T(2,128)} %param.19) | copy-start | bytes 6148
  58.6 17.3 %copy-start.1 = (f32[16,160,128]{2,1,0:T(8,128)S(1)}, f32[16,160,128]{2,1,0:T(8,128)}, u32[]{:S(2)}) copy-start(f32[16,160,128]{2,1,0:T(8,128)} %shard_map.114) | copy-start | bytes 3932164
  70.6 7.8 %collective-permute-start.11 = (f32[256]{0:T(256)S(1)}, f32[256]{0:T(256)S(1)}, u32[]{:S(2)}, u32[]{:S(2)}) collective-permute-start(f32[256]{0:T(256)S(1)} %bitcast.65), channel_id=1, source_target_pairs={{1,0},{2,1},{3,2},{5,4},{6,5},{7,6},{9,8},{10,9},{11,10},{13,12},{... | collective-permute-start | bytes 3080 | tf_op jit(solution)/shard_map/ppermute | solution.py:349
  72.5 5.9 %collective-permute-start.9 = (f32[256]{0:T(256)S(1)}, f32[256]{0:T(256)S(1)}, u32[]{:S(2)}, u32[]{:S(2)}) collective-permute-start(f32[256]{0:T(256)S(1)} %bitcast.66), channel_id=1, source_target_pairs={{0,1},{1,2},{2,3},{4,5},{5,6},{6,7},{8,9},{9,10},{10,11},{12,13},{... | collective-permute-start | bytes 3080 | tf_op jit(solution)/shard_map/ppermute | solution.py:348
  78.3 4.6 %copy-start.2 = (f32[327680]{0:T(1024)}, f32[327680]{0:T(1024)S(1)}, u32[]{:S(2)}) copy-start(f32[327680]{0:T(1024)S(1)} %scatter_fusion) | copy-start | bytes 3932164
  99.0 5.5 %collective-permute-start.12 = (f32[1280,128]{1,0:T(8,128)S(1)}, f32[1280,128]{1,0:T(8,128)S(1)}, u32[]{:S(2)}, u32[]{:S(2)}) collective-permute-start(f32[1280,128]{1,0:T(8,128)S(1)} %constant_dynamic-slice_fusion.1), channel_id=1, source_target_pairs={{0,4},{4,0},{8,12},{12,8},{1,5},{5,1},{9,13},{13,9},{2,6},{6,2},{1... | collective-permute-start | bytes 1966088 | tf_op jit(solution)/shard_map/ppermute | solution.py:243
  104.6 9.0 %collective-permute-start.13 = (f32[640,128]{1,0:T(8,128)S(1)}, f32[640,128]{1,0:T(8,128)S(1)}, u32[]{:S(2)}, u32[]{:S(2)}) collective-permute-start(f32[640,128]{1,0:T(8,128)S(1)} %constant_dynamic-slice_fusion), channel_id=1, source_target_pairs={{0,8},{4,12},{8,0},{12,4},{1,9},{5,13},{9,1},{13,5},{2,10},{6,14},... | collective-permute-start | bytes 983048 | tf_op jit(solution)/shard_map/ppermute | solution.py:243
  113.6 8.1 %collective-permute-start.14 = (f32[640,128]{1,0:T(8,128)S(1)}, f32[640,128]{1,0:T(8,128)S(1)}, u32[]{:S(2)}, u32[]{:S(2)}) collective-permute-start(f32[640,128]{1,0:T(8,128)S(1)} %add_multiply_fusion), channel_id=1, source_target_pairs={{0,8},{4,12},{8,0},{12,4},{1,9},{5,13},{9,1},{13,5},{2,10},{6,14},... | collective-permute-start | bytes 983048 | tf_op jit(solution)/shard_map/ppermute | solution.py:249
  121.7 3.9 %collective-permute-start.15 = (f32[1280,128]{1,0:T(8,128)S(1)}, f32[1280,128]{1,0:T(8,128)S(1)}, u32[]{:S(2)}, u32[]{:S(2)}) collective-permute-start(f32[1280,128]{1,0:T(8,128)S(1)} %maximum_select_fusion.1), channel_id=1, source_target_pairs={{0,4},{4,0},{8,12},{12,8},{1,5},{5,1},{9,13},{13,9},{2,6},{6,2},{1... | collective-permute-start | bytes 1966088 | tf_op jit(solution)/shard_map/ppermute | solution.py:249
  (11 other events, 18.4 us)

commit v9 on v5

--- a/solution.py
+++ b/solution.py
@@ -251,21 +251,23 @@
     return rows.reshape(part.shape)
 
 
+def swap_halos(bottom, top, axis):
+    count = lax.axis_size(axis)
+    odd = lax.axis_index(axis) % 2 == 1
+    first = [(i, i ^ 1) for i in range(count) if i ^ 1 < count]
+    second = [(i, i + 1) for i in range(1, count - 1, 2)] + [(i + 1, i) for i in range(1, count - 1, 2)]
+    got_first = lax.ppermute(jnp.where(odd, bottom, top), axis, first)
+    got_second = lax.ppermute(jnp.where(odd, top, bottom), axis, second)
+    return jnp.where(odd, got_first, got_second), jnp.where(odd, got_second, got_first)
+
+
 def halos(block, axis):
-    count = lax.axis_size(axis)
-    forward = [(i, i + 1) for i in range(count - 1)]
-    backward = [(target, source) for source, target in forward]
     planes = block.shape[0]
-    low = lax.ppermute(block[planes - HALO:], axis, forward)
-    high = lax.ppermute(block[:HALO], axis, backward)
-    return low, high
+    return swap_halos(block[:HALO], block[planes - HALO:], axis)
 
 
 def edge_halos(low_edge, high_edge, axis):
-    count = lax.axis_size(axis)
-    forward = [(i, i + 1) for i in range(count - 1)]
-    backward = [(target, source) for source, target in forward]
-    return lax.ppermute(high_edge, axis, forward), lax.ppermute(low_edge, axis, backward)
+    return swap_halos(low_edge, high_edge, axis)
 
 
 def inject(field, where, valid, values):

time: 123 us -> 118 us (0.959)
  starting transfers between devices: 34.5 us -> 24.7 us
  other arithmetic: 14 us -> 21.9 us
  local copies, waits for them, and re-layouts: 6.01 us -> 0.72 us
  waiting for transfers between devices: 25.9 us -> 28.8 us
    ppermute x10, starting transfers between devices: 26.5 us -> 15.5 us  [the longest x5 15 us: swap_halos(): got_second = lax.ppermute(jnp.where(odd, top, bottom), axis, second)]
    select_n x0 -> x10, other arithmetic: none -> 8.82 us  [the longest x5 5.52 us: swap_halos(): jnp.where(odd, got_second, got_first)]
    unnamed x36 -> x18, local copies, waits for them, and re-layouts: 3.18 us -> 0.04 us
    ppermute x10, waiting for transfers between devices: 7.92 us -> 10.8 us  [the longest x5 5.67 us: swap_halos(): got_first = lax.ppermute(jnp.where(odd, bottom, top), axis, first)]
    slice x4 -> x0, local copies, waits for them, and re-layouts: 2.13 us -> none  [halos(): high = lax.ppermute(block[:HALO], axis, backward)]
  transfers between devices with their start and end apart: 14 -> 14, of which waited for: 7 -> 8; matrix products, arithmetic and copies ran while one was open for 3% -> 6% of each run, Pallas kernels for 17% -> 18%
where the time goes in v9:
time: 118 us; the launch traced here: 117 us
  Pallas kernels  39.2 us (33%)
  waiting for transfers between devices  28.8 us (24%)
  starting transfers between devices  24.7 us (21%)
  other arithmetic  21.9 us (19%)
  between operations  1.7 us (1%)
    pallas_call x4, Pallas kernels, apply_step(): pl.pallas_call(kernel, grid=(planes // block,), in_specs=in_specs, out_sp...  39.2 us
    ppermute x5, starting transfers between devices, swap_halos(): got_second = lax.ppermute(jnp.where(odd, top, bottom), axis, second)  15 us
    ppermute x2, waiting for transfers between devices, reduce_members(): rows = keep + lax.ppermute(give, axis, pairs)  9.44 us
    ppermute x2, waiting for transfers between devices, reduce_members(): other = lax.ppermute(rows, axis, pairs)  8.52 us
    scatter-add x2, other arithmetic, inject(): flat = field.reshape(-1).at[where].add(jnp.where(valid, values, 0.0))  6.84 us
    ppermute x2, starting transfers between devices, reduce_members(): rows = keep + lax.ppermute(give, axis, pairs)  5.81 us
    ppermute x5, waiting for transfers between devices, swap_halos(): got_first = lax.ppermute(jnp.where(odd, bottom, top), axis, first)  5.67 us
    select_n x5, other arithmetic, swap_halos(): jnp.where(odd, got_second, got_first)  5.52 us
  transfers between devices with their start and end apart: 14, of which 8 were waited for; matrix products, arithmetic and copies ran while one was open for 6% of the time, Pallas kernels for 18%

profile of v9, /device:TPU:9, one launch (start us, length us, event | category | flops | bytes accessed | tf_op | source)
XLA Modules:
  0.0 117.1 jit_solution(3500912541342666986)
XLA Ops:
  0.7 2.0 %slice_select_fusion.2 = (f32[4,160,128]{2,1,0:T(8,128)S(1)}, f32[4,160,128]{2,1,0:T(8,128)}) fusion(f32[16,160,128]{2,1,0:T(8,128)} %refs_3_.5, pred[]{:T(512)S(6)} %eq.31), kind=kLoop, calls=%fused_computation.13 | loop fusion | flops 163840 | bytes 1310721 | tf_op jit(solution)/shard_map/jit(_where)/select_n | solution.py:260
  2.7 4.6 %collective-permute-start.5 = (f32[4,160,128]{2,1,0:T(8,128)S(1)}, f32[4,160,128]{2,1,0:T(8,128)S(1)}, u32[]{:S(2)}, u32[]{:S(2)}) collective-permute-start(f32[4,160,128]{2,1,0:T(8,128)S(1)} %get-tuple-element.24), channel_id=1, source_target_pairs={{1,2},{2,1},{5,6},{6,5},{9,10},{10,9},{13,14},{14,13},{17,18},{18,... | collective-permute-start | bytes 983048 | tf_op jit(solution)/shard_map/ppermute | solution.py:260
  7.4 1.9 %collective-permute-start.3 = (f32[4,160,128]{2,1,0:T(8,128)S(1)}, f32[4,160,128]{2,1,0:T(8,128)S(1)}, u32[]{:S(2)}, u32[]{:S(2)}) collective-permute-start(f32[4,160,128]{2,1,0:T(8,128)S(1)} %get-tuple-element.26), channel_id=1, source_target_pairs={{1,2},{2,1},{5,6},{6,5},{9,10},{10,9},{13,14},{14,13},{17,18},{18,... | collective-permute-start | bytes 983048 | tf_op jit(solution)/shard_map/ppermute | solution.py:260
  12.4 3.2 %collective-permute-start.1 = (f32[4,160,128]{2,1,0:T(8,128)S(1)}, f32[4,160,128]{2,1,0:T(8,128)}, u32[]{:S(2)}, u32[]{:S(2)}) collective-permute-start(f32[4,160,128]{2,1,0:T(8,128)S(1)} %get-tuple-element.28), channel_id=1, source_target_pairs={{1,2},{2,1},{5,6},{6,5},{9,10},{10,9},{13,14},{14,13},{17,18},{18,... | collective-permute-start | bytes 983048 | tf_op jit(solution)/shard_map/ppermute | solution.py:260
  16.5 2.0 %collective-permute-done.2 = f32[4,160,128]{2,1,0:T(8,128)S(1)} collective-permute-done((f32[4,160,128]{2,1,0:T(8,128)S(1)}, f32[4,160,128]{2,1,0:T(8,128)S(1)}, u32[]{:S(2)}, u32[]{:S(2)}) %collective-permute-start.2) | collective-permute-done | bytes 327712 | tf_op jit(solution)/shard_map/ppermute | solution.py:259
  18.5 2.9 %collective-permute-done.3 = f32[4,160,128]{2,1,0:T(8,128)S(1)} collective-permute-done((f32[4,160,128]{2,1,0:T(8,128)S(1)}, f32[4,160,128]{2,1,0:T(8,128)S(1)}, u32[]{:S(2)}, u32[]{:S(2)}) %collective-permute-start.3) | collective-permute-done | bytes 327712 | tf_op jit(solution)/shard_map/ppermute | solution.py:260
  22.3 12.6 %shard_map.113 = (f32[16,160,128]{2,1,0:T(8,128)}, f32[16,160,128]{2,1,0:T(8,128)}, f32[16,160,128]{2,1,0:T(8,128)}, f32[16,160,128]{2,1,0:T(8,128)}, f32[16,160...) custom-call(f32[4,160,128]{2,1,0:T(8,128)} %get-tuple-element.39.refs_0_, ...), custom_call_target="tpu_custom_call" | custom-call | tf_op jit(solution)/shard_map/pallas_call | solution.py:202
  36.2 3.0 %collective-permute-start.7 = (f32[4,160,128]{2,1,0:T(8,128)S(1)}, f32[4,160,128]{2,1,0:T(8,128)S(1)}, u32[]{:S(2)}, u32[]{:S(2)}) collective-permute-start(f32[4,160,128]{2,1,0:T(8,128)S(1)} %get-tuple-element.34), channel_id=1, source_target_pairs={{1,2},{2,1},{5,6},{6,5},{9,10},{10,9},{13,14},{14,13},{17,18},{18,... | collective-permute-start | bytes 983048 | tf_op jit(solution)/shard_map/ppermute | solution.py:260
  39.4 1.9 %broadcast_select_fusion.10 = (f32[4,160,128]{2,1,0:T(8,128)}, f32[4,160,128]{2,1,0:T(8,128)}) fusion(f32[4,160,128]{2,1,0:T(8,128)} %collective-permute-done.1, f32[4,160,128]{2,1,0:T(8,128)S(1)} %collective-permute-done, pred[]{:T(512)S(6)} %eq.31), kind=kLoop, calls=%fused_computation.25 | loop fusion | flops 163840 | bytes 1310721 | tf_op jit(solution)/shard_map/jit(_where)/select_n | solution.py:261
  41.3 7.9 %shard_map.114 = f32[16,160,128]{2,1,0:T(8,128)} custom-call(f32[4,160,128]{2,1,0:T(8,128)} %get-tuple-element.41.refs_0_, f32[16,160,128]{2,1,0:T(8,128)} %bitcast.47, f32[4,160,128]{2,1,0:T(8,128)} %get-tuple-element.40.refs_2_, f32[16,160,128]{2,1,0:T(8,128)} %refs_3_.5, f32[16,160,128]{2,1,0:T(8,128)} %get-tuple-element.12.refs_4_, ...), custom_call_target="tpu_custom_call" | custom-call | tf_op jit(solution)/shard_map/pallas_call | solution.py:202
  50.2 10.7 %shard_map.115 = (f32[16,160,128]{2,1,0:T(8,128)}, f32[16,160,128]{2,1,0:T(8,128)}, f32[4,160,128]{2,1,0:T(8,128)}, f32[4,160,128]{2,1,0:T(8,128)}, f32[256,128]{1,0:T(8,128)}) custom-call(f32[4,160,128]{2,1,0:T(8,128)} %get-tuple-element.33.refs_0_, f32[16,160,128]{2,1,0:T(8,128)} %get-tuple-element.18.refs_1_, f32[4,160,128]{2,1,0:T(8,128)} %get-tuple-element.32.refs_2_, ...), custom_call_target="tpu_custom_call" | custom-call | tf_op jit(solution)/shard_map/pallas_call | solution.py:202
  62.0 2.5 %scatter_fusion = f32[327680]{0:T(1024)S(1)} fusion(f32[327680]{0:T(1024)S(1)} %bitcast.35, s32[256]{0:T(256)S(1)} %get-tuple-element.44, f32[256]{0:T(256)S(1)} %get-tuple-element.49), kind=kCustom, calls=%fused_computation | custom fusion | flops 256 | bytes 4096 | tf_op jit(solution)/shard_map/scatter-add | solution.py:274
  64.6 2.2 %collective-permute-start.9 = (f32[4,160,128]{2,1,0:T(8,128)S(1)}, f32[4,160,128]{2,1,0:T(8,128)S(1)}, u32[]{:S(2)}, u32[]{:S(2)}) collective-permute-start(f32[4,160,128]{2,1,0:T(8,128)S(1)} %bitcast.54), channel_id=1, source_target_pairs={{1,2},{2,1},{5,6},{6,5},{9,10},{10,9},{13,14},{14,13},{17,18},{18,... | collective-permute-start | bytes 983048 | tf_op jit(solution)/shard_map/ppermute | solution.py:260
  66.9 3.7 %collective-permute-done.8 = f32[4,160,128]{2,1,0:T(8,128)S(1)} collective-permute-done((f32[4,160,128]{2,1,0:T(8,128)S(1)}, f32[4,160,128]{2,1,0:T(8,128)S(1)}, u32[]{:S(2)}, u32[]{:S(2)}) %collective-permute-start.8) | collective-permute-done | bytes 327712 | tf_op jit(solution)/shard_map/ppermute | solution.py:259
  70.5 2.2 %collective-permute-done.9 = f32[4,160,128]{2,1,0:T(8,128)S(1)} collective-permute-done((f32[4,160,128]{2,1,0:T(8,128)S(1)}, f32[4,160,128]{2,1,0:T(8,128)S(1)}, u32[]{:S(2)}, u32[]{:S(2)}) %collective-permute-start.9) | collective-permute-done | bytes 327712 | tf_op jit(solution)/shard_map/ppermute | solution.py:260
  73.6 8.0 %shard_map.116 = f32[16,160,128]{2,1,0:T(8,128)} custom-call(f32[4,160,128]{2,1,0:T(8,128)} %get-tuple-element.31.refs_0_, f32[16,160,128]{2,1,0:T(8,128)} %bitcast.36, f32[4,160,128]{2,1,0:T(8,128)} %get-tuple-element.30.refs_2_, f32[16,160,128]{2,1,0:T(8,128)} %refs_3_.5, f32[16,160,128]{2,1,0:T(8,128)} %get-tuple-element.12.refs_4_, ...), custom_call_target="tpu_custom_call" | custom-call | tf_op jit(solution)/shard_map/pallas_call | solution.py:202
  81.5 4.4 %scatter_fusion.1 = f32[327680]{0:T(1024)} fusion(f32[327680]{0:T(1024)} %bitcast.42, s32[256]{0:T(256)S(1)} %get-tuple-element.44, f32[256]{0:T(256)S(1)} %get-tuple-element.48), kind=kCustom, calls=%fused_computation.1 | custom fusion | flops 256 | bytes 4096 | tf_op jit(solution)/shard_map/scatter-add | solution.py:274
  85.9 2.5 %multiply_add_fusion = f32[16,160,128]{2,1,0:T(8,128)S(1)} fusion(f32[16,160,128]{2,1,0:T(8,128)} %bitcast.43, f32[16,160,128]{2,1,0:T(8,128)} %get-tuple-element.21, f32[16,160,128]{2,1,0:T(8,128)S(1)} %bitcast.37, f32[16,160,128]{2,1,0:T(8,128)} %get-tuple-element.20), kind=kLoop, calls=%fused_computation.3 | loop fusion | flops 983040 | bytes 6553600 | tf_op jit(solution)/shard_map/add | solution.py:336
  88.4 4.5 %collective-permute-start.10 = (f32[1280,128]{1,0:T(8,128)S(1)}, f32[1280,128]{1,0:T(8,128)S(1)}, u32[]{:S(2)}, u32[]{:S(2)}) collective-permute-start(f32[1280,128]{1,0:T(8,128)S(1)} %constant_dynamic-slice_fusion.1), channel_id=1, source_target_pairs={{0,4},{4,0},{8,12},{12,8},{1,5},{5,1},{9,13},{13,9},{2,6},{6,2},{1... | collective-permute-start | bytes 1966088 | tf_op jit(solution)/shard_map/ppermute | solution.py:243
  93.0 1.7 %collective-permute-done.10 = f32[1280,128]{1,0:T(8,128)S(1)} collective-permute-done((f32[1280,128]{1,0:T(8,128)S(1)}, f32[1280,128]{1,0:T(8,128)S(1)}, u32[]{:S(2)}, u32[]{:S(2)}) %collective-permute-start.10) | collective-permute-done | bytes 655392 | tf_op jit(solution)/shard_map/ppermute | solution.py:243
  96.1 7.7 %collective-permute-done.11 = f32[640,128]{1,0:T(8,128)S(1)} collective-permute-done((f32[640,128]{1,0:T(8,128)S(1)}, f32[640,128]{1,0:T(8,128)S(1)}, u32[]{:S(2)}, u32[]{:S(2)}) %collective-permute-start.11) | collective-permute-done | bytes 327712 | tf_op jit(solution)/shard_map/ppermute | solution.py:243
  105.1 6.8 %collective-permute-done.12 = f32[640,128]{1,0:T(8,128)S(1)} collective-permute-done((f32[640,128]{1,0:T(8,128)S(1)}, f32[640,128]{1,0:T(8,128)S(1)}, u32[]{:S(2)}, u32[]{:S(2)}) %collective-permute-start.12) | collective-permute-done | bytes 327712 | tf_op jit(solution)/shard_map/ppermute | solution.py:249
  112.0 2.2 %collective-permute-start.13 = (f32[1280,128]{1,0:T(8,128)S(1)}, f32[1280,128]{1,0:T(8,128)S(1)}, u32[]{:S(2)}, u32[]{:S(2)}) collective-permute-start(f32[1280,128]{1,0:T(8,128)S(1)} %maximum_select_fusion.1), channel_id=1, source_target_pairs={{0,4},{4,0},{8,12},{12,8},{1,5},{5,1},{9,13},{13,9},{2,6},{6,2},{1... | collective-permute-start | bytes 1966088 | tf_op jit(solution)/shard_map/ppermute | solution.py:249
  114.1 1.7 %collective-permute-done.13 = f32[1280,128]{1,0:T(8,128)S(1)} collective-permute-done((f32[1280,128]{1,0:T(8,128)S(1)}, f32[1280,128]{1,0:T(8,128)S(1)}, u32[]{:S(2)}, u32[]{:S(2)}) %collective-permute-start.13) | collective-permute-done | bytes 655392 | tf_op jit(solution)/shard_map/ppermute | solution.py:249
  (56 shorter events, 12.5 us)
Async XLA Ops:
  0.6 6.7 %copy-start.3 = (f32[1,16,160,128]{3,2,1,0:T(8,128)S(1)}, f32[1,16,160,128]{3,2,1,0:T(8,128)}, u32[]{:S(2)}) copy-start(f32[1,16,160,128]{3,2,1,0:T(8,128)} %param.12) | copy-start | bytes 3932164
  0.7 8.7 %copy-start.4 = (f32[1,16,160,128]{3,2,1,0:T(8,128)S(1)}, f32[1,16,160,128]{3,2,1,0:T(8,128)}, u32[]{:S(2)}) copy-start(f32[1,16,160,128]{3,2,1,0:T(8,128)} %param.14) | copy-start | bytes 3932164
  2.7 9.7 %collective-permute-start.4 = (f32[4,160,128]{2,1,0:T(8,128)}, f32[4,160,128]{2,1,0:T(8,128)S(1)}, u32[]{:S(2)}, u32[]{:S(2)}) collective-permute-start(f32[4,160,128]{2,1,0:T(8,128)} %get-tuple-element.25), channel_id=1, source_target_pairs={{0,1},{1,0},{2,3},{3,2},{4,5},{5,4},{6,7},{7,6},{8,9},{9,8},{10,11... | collective-permute-start | bytes 983048 | tf_op jit(solution)/shard_map/ppermute | solution.py:259
  2.7 7.7 %copy-start.6 = (s32[256]{0:T(256)S(1)}, s32[256]{0:T(256)}, u32[]{:S(2)}) copy-start(s32[256]{0:T(256)} %param.18) | copy-start | bytes 3076
  2.7 8.5 %copy-start.8 = (f32[2]{0:T(128)S(1)}, f32[2]{0:T(128)}, u32[]{:S(2)}) copy-start(f32[2]{0:T(128)} %param.16) | copy-start | bytes 28
  2.7 12.9 %collective-permute-start.5 = (f32[4,160,128]{2,1,0:T(8,128)S(1)}, f32[4,160,128]{2,1,0:T(8,128)S(1)}, u32[]{:S(2)}, u32[]{:S(2)}) collective-permute-start(f32[4,160,128]{2,1,0:T(8,128)S(1)} %get-tuple-element.24), channel_id=1, source_target_pairs={{1,2},{2,1},{5,6},{6,5},{9,10},{10,9},{13,14},{14,13},{17,18},{18,... | collective-permute-start | bytes 983048 | tf_op jit(solution)/shard_map/ppermute | solution.py:260
  7.4 11.1 %collective-permute-start.2 = (f32[4,160,128]{2,1,0:T(8,128)S(1)}, f32[4,160,128]{2,1,0:T(8,128)S(1)}, u32[]{:S(2)}, u32[]{:S(2)}) collective-permute-start(f32[4,160,128]{2,1,0:T(8,128)S(1)} %get-tuple-element.27), channel_id=1, source_target_pairs={{0,1},{1,0},{2,3},{3,2},{4,5},{5,4},{6,7},{7,6},{8,9},{9,8},{10,11... | collective-permute-start | bytes 983048 | tf_op jit(solution)/shard_map/ppermute | solution.py:259
  7.4 14.0 %collective-permute-start.3 = (f32[4,160,128]{2,1,0:T(8,128)S(1)}, f32[4,160,128]{2,1,0:T(8,128)S(1)}, u32[]{:S(2)}, u32[]{:S(2)}) collective-permute-start(f32[4,160,128]{2,1,0:T(8,128)S(1)} %get-tuple-element.26), channel_id=1, source_target_pairs={{1,2},{2,1},{5,6},{6,5},{9,10},{10,9},{13,14},{14,13},{17,18},{18,... | collective-permute-start | bytes 983048 | tf_op jit(solution)/shard_map/ppermute | solution.py:260
  9.4 30.0 %collective-permute-start = (f32[4,160,128]{2,1,0:T(8,128)S(1)}, f32[4,160,128]{2,1,0:T(8,128)S(1)}, u32[]{:S(2)}, u32[]{:S(2)}) collective-permute-start(f32[4,160,128]{2,1,0:T(8,128)S(1)} %get-tuple-element.29), channel_id=1, source_target_pairs={{0,1},{1,0},{2,3},{3,2},{4,5},{5,4},{6,7},{7,6},{8,9},{9,8},{10,11... | collective-permute-start | bytes 983048 | tf_op jit(solution)/shard_map/ppermute | solution.py:259
  12.4 27.1 %collective-permute-start.1 = (f32[4,160,128]{2,1,0:T(8,128)S(1)}, f32[4,160,128]{2,1,0:T(8,128)}, u32[]{:S(2)}, u32[]{:S(2)}) collective-permute-start(f32[4,160,128]{2,1,0:T(8,128)S(1)} %get-tuple-element.28), channel_id=1, source_target_pairs={{1,2},{2,1},{5,6},{6,5},{9,10},{10,9},{13,14},{14,13},{17,18},{18,... | collective-permute-start | bytes 983048 | tf_op jit(solution)/shard_map/ppermute | solution.py:260
  35.0 4.3 %copy-start.5 = (f32[256,128]{1,0:T(8,128)S(1)}, f32[256,128]{1,0:T(8,128)}, u32[]{:S(2)}) copy-start(f32[256,128]{1,0:T(8,128)} %get-tuple-element.15) | copy-start | bytes 393220
  36.1 13.1 %collective-permute-start.6 = (f32[4,160,128]{2,1,0:T(8,128)S(1)}, f32[4,160,128]{2,1,0:T(8,128)S(1)}, u32[]{:S(2)}, u32[]{:S(2)}) collective-permute-start(f32[4,160,128]{2,1,0:T(8,128)S(1)} %get-tuple-element.35), channel_id=1, source_target_pairs={{0,1},{1,0},{2,3},{3,2},{4,5},{5,4},{6,7},{7,6},{8,9},{9,8},{10,11... | collective-permute-start | bytes 983048 | tf_op jit(solution)/shard_map/ppermute | solution.py:259
  36.2 13.0 %collective-permute-start.7 = (f32[4,160,128]{2,1,0:T(8,128)S(1)}, f32[4,160,128]{2,1,0:T(8,128)S(1)}, u32[]{:S(2)}, u32[]{:S(2)}) collective-permute-start(f32[4,160,128]{2,1,0:T(8,128)S(1)} %get-tuple-element.34), channel_id=1, source_target_pairs={{1,2},{2,1},{5,6},{6,5},{9,10},{10,9},{13,14},{14,13},{17,18},{18,... | collective-permute-start | bytes 983048 | tf_op jit(solution)/shard_map/ppermute | solution.py:260
  50.2 11.7 %copy-start.7 = (f32[2,256]{1,0:T(2,128)S(1)}, f32[2,256]{1,0:T(2,128)}, u32[]{:S(2)}) copy-start(f32[2,256]{1,0:T(2,128)} %param.19) | copy-start | bytes 6148
  50.2 11.8 %copy-start = (f32[16,160,128]{2,1,0:T(8,128)S(1)}, f32[16,160,128]{2,1,0:T(8,128)}, u32[]{:S(2)}) copy-start(f32[16,160,128]{2,1,0:T(8,128)} %shard_map.114) | copy-start | bytes 3932164
  64.4 9.1 %copy-start.1 = (f32[327680]{0:T(1024)}, f32[327680]{0:T(1024)S(1)}, u32[]{:S(2)}) copy-start(f32[327680]{0:T(1024)S(1)} %scatter_fusion) | copy-start | bytes 3932164
  64.5 6.0 %collective-permute-start.8 = (f32[4,160,128]{2,1,0:T(8,128)S(1)}, f32[4,160,128]{2,1,0:T(8,128)S(1)}, u32[]{:S(2)}, u32[]{:S(2)}) collective-permute-start(f32[4,160,128]{2,1,0:T(8,128)S(1)} %bitcast.55), channel_id=1, source_target_pairs={{0,1},{1,0},{2,3},{3,2},{4,5},{5,4},{6,7},{7,6},{8,9},{9,8},{10,11... | collective-permute-start | bytes 983048 | tf_op jit(solution)/shard_map/ppermute | solution.py:259
  64.6 8.1 %collective-permute-start.9 = (f32[4,160,128]{2,1,0:T(8,128)S(1)}, f32[4,160,128]{2,1,0:T(8,128)S(1)}, u32[]{:S(2)}, u32[]{:S(2)}) collective-permute-start(f32[4,160,128]{2,1,0:T(8,128)S(1)} %bitcast.54), channel_id=1, source_target_pairs={{1,2},{2,1},{5,6},{6,5},{9,10},{10,9},{13,14},{14,13},{17,18},{18,... | collective-permute-start | bytes 983048 | tf_op jit(solution)/shard_map/ppermute | solution.py:260
  81.5 4.4 %copy-start.2 = (f32[327680]{0:T(1024)S(1)}, f32[327680]{0:T(1024)}, u32[]{:S(2)}) copy-start(f32[327680]{0:T(1024)} %copy-done.1) | copy-start | bytes 3932164
  88.4 6.3 %collective-permute-start.10 = (f32[1280,128]{1,0:T(8,128)S(1)}, f32[1280,128]{1,0:T(8,128)S(1)}, u32[]{:S(2)}, u32[]{:S(2)}) collective-permute-start(f32[1280,128]{1,0:T(8,128)S(1)} %constant_dynamic-slice_fusion.1), channel_id=1, source_target_pairs={{0,4},{4,0},{8,12},{12,8},{1,5},{5,1},{9,13},{13,9},{2,6},{6,2},{1... | collective-permute-start | bytes 1966088 | tf_op jit(solution)/shard_map/ppermute | solution.py:243
  94.8 9.0 %collective-permute-start.11 = (f32[640,128]{1,0:T(8,128)S(1)}, f32[640,128]{1,0:T(8,128)S(1)}, u32[]{:S(2)}, u32[]{:S(2)}) collective-permute-start(f32[640,128]{1,0:T(8,128)S(1)} %constant_dynamic-slice_fusion), channel_id=1, source_target_pairs={{0,8},{4,12},{8,0},{12,4},{1,9},{5,13},{9,1},{13,5},{2,10},{6,14},... | collective-permute-start | bytes 983048 | tf_op jit(solution)/shard_map/ppermute | solution.py:243
  103.8 8.1 %collective-permute-start.12 = (f32[640,128]{1,0:T(8,128)S(1)}, f32[640,128]{1,0:T(8,128)S(1)}, u32[]{:S(2)}, u32[]{:S(2)}) collective-permute-start(f32[640,128]{1,0:T(8,128)S(1)} %add_multiply_fusion), channel_id=1, source_target_pairs={{0,8},{4,12},{8,0},{12,4},{1,9},{5,13},{9,1},{13,5},{2,10},{6,14},... | collective-permute-start | bytes 983048 | tf_op jit(solution)/shard_map/ppermute | solution.py:249
  112.0 3.9 %collective-permute-start.13 = (f32[1280,128]{1,0:T(8,128)S(1)}, f32[1280,128]{1,0:T(8,128)S(1)}, u32[]{:S(2)}, u32[]{:S(2)}) collective-permute-start(f32[1280,128]{1,0:T(8,128)S(1)} %maximum_select_fusion.1), channel_id=1, source_target_pairs={{0,4},{4,0},{8,12},{12,8},{1,5},{5,1},{9,13},{13,9},{2,6},{6,2},{1... | collective-permute-start | bytes 1966088 | tf_op jit(solution)/shard_map/ppermute | solution.py:249

commit v10 on v9

--- a/solution.py
+++ b/solution.py
@@ -21,12 +21,14 @@
     return jnp.where(lane >= -k, rolled, 0.0)
 
 
-def fill_padded(pad_ref, lo_ref, mid_ref, hi_ref):
+def fill_padded(pad_ref, first_ref, mid_ref, second_ref, odd):
     planes, height, depth = mid_ref.shape
     pad_ref[...] = jnp.zeros(pad_ref.shape, jnp.float32)
-    pad_ref[0:HALO, PADY:PADY + height, :] = lo_ref[...]
+    first = first_ref[...]
+    second = second_ref[...]
+    pad_ref[0:HALO, PADY:PADY + height, :] = jnp.where(odd, first, second)
     pad_ref[HALO:HALO + planes, PADY:PADY + height, :] = mid_ref[...]
-    pad_ref[HALO + planes:, PADY:PADY + height, :] = hi_ref[...]
+    pad_ref[HALO + planes:, PADY:PADY + height, :] = jnp.where(odd, second, first)
 
 
 def taps(pad_ref, plane, y0, rows, lane):
@@ -55,6 +57,7 @@
 def step_kernel(*refs, block, rows, track, own_grad, want_force):
     refs = list(refs)
     take = lambda n: [refs.pop(0) for _ in range(n)]
+    (parity_ref,) = take(1)
     lo_ref, mid_ref, hi_ref = take(3)
     if own_grad:
         b_lo_ref, b_mid_ref, b_hi_ref = take(3)
@@ -76,11 +79,13 @@
         (keep_ref,) = take(1)
     i = pl.program_id(0)
 
+    odd = parity_ref[0] == 1
+
     @pl.when(i == 0)
     def _():
-        fill_padded(pad_ref, lo_ref, mid_ref, hi_ref)
+        fill_padded(pad_ref, lo_ref, mid_ref, hi_ref, odd)
         if own_grad:
-            fill_padded(b_pad_ref, b_lo_ref, b_mid_ref, b_hi_ref)
+            fill_padded(b_pad_ref, b_lo_ref, b_mid_ref, b_hi_ref, odd)
 
     planes = mid_ref.shape[0]
     height = c_ref.shape[1]
@@ -113,8 +118,10 @@
     if track:
         @pl.when(i == pl.num_programs(0) - 1)
         def _():
-            edge_lo_ref[...] = keep_ref[0:HALO]
-            edge_hi_ref[...] = keep_ref[planes - HALO:planes]
+            bottom = keep_ref[0:HALO]
+            top = keep_ref[planes - HALO:planes]
+            edge_lo_ref[...] = jnp.where(odd, bottom, top)
+            edge_hi_ref[...] = jnp.where(odd, top, bottom)
             one_lane = lax.broadcasted_iota(jnp.int32, (1, depth), 1)
 
             def sample(r, carry):
@@ -160,14 +167,14 @@
     return full, blk
 
 
-def apply_step(lo, mid, hi, b, g, c, old, track=None, rows=40, want_force=True):
+def apply_step(parity, lo, mid, hi, b, g, c, old, track=None, rows=40, want_force=True):
     planes, height, depth = mid.shape
     block = pick_block(planes)
     full, blk = specs(mid.shape, block)
     out = jax.ShapeDtypeStruct(mid.shape, jnp.float32)
     own_grad = g is None
-    in_specs = [full(lo.shape), full(mid.shape), full(hi.shape)]
-    args = [lo, mid, hi]
+    in_specs = [pl.BlockSpec(memory_space=pltpu.SMEM), full(lo.shape), full(mid.shape), full(hi.shape)]
+    args = [parity, lo, mid, hi]
     if own_grad:
         in_specs += [full(b[0].shape), full(b[1].shape), full(b[2].shape)]
         args += list(b)
@@ -251,23 +258,19 @@
     return rows.reshape(part.shape)
 
 
-def swap_halos(bottom, top, axis):
+def swap_halos(sends, axis):
     count = lax.axis_size(axis)
-    odd = lax.axis_index(axis) % 2 == 1
     first = [(i, i ^ 1) for i in range(count) if i ^ 1 < count]
     second = [(i, i + 1) for i in range(1, count - 1, 2)] + [(i + 1, i) for i in range(1, count - 1, 2)]
-    got_first = lax.ppermute(jnp.where(odd, bottom, top), axis, first)
-    got_second = lax.ppermute(jnp.where(odd, top, bottom), axis, second)
-    return jnp.where(odd, got_first, got_second), jnp.where(odd, got_second, got_first)
+    return lax.ppermute(sends[0], axis, first), lax.ppermute(sends[1], axis, second)
 
 
 def halos(block, axis):
     planes = block.shape[0]
-    return swap_halos(block[:HALO], block[planes - HALO:], axis)
-
-
-def edge_halos(low_edge, high_edge, axis):
-    return swap_halos(low_edge, high_edge, axis)
+    odd = lax.axis_index(axis) % 2
+    near = lax.dynamic_slice_in_dim(block, (1 - odd) * (planes - HALO), HALO, 0)
+    far = lax.dynamic_slice_in_dim(block, odd * (planes - HALO), HALO, 0)
+    return swap_halos((near, far), axis)
 
 
 def inject(field, where, valid, values):
@@ -300,6 +303,7 @@
 
     src_local, src_valid = locate(src_cell)
     rec_local, rec_valid = locate(rec_cell)
+    parity = (lax.axis_index("tile") % 2).astype(jnp.int32).reshape(1)
     b_lo, b_hi = halos(buoyancy, "tile")
 
     def spread(cells):
@@ -315,14 +319,14 @@
     for k in range(steps):
         track = (where, wavelet[k:k + 1], receivers)
         if grad_b is None:
-            outs = apply_step(lo, now, hi, (b_lo, buoyancy, b_hi), None, speed, older, track)
+            outs = apply_step(parity, lo, now, hi, (b_lo, buoyancy, b_hi), None, speed, older, track)
             force, newer = outs[:2]
             grad_b = outs[2:5]
             edge_lo, edge_hi, lines = outs[5:]
         else:
-            force, newer, edge_lo, edge_hi, lines = apply_step(lo, now, hi, buoyancy, grad_b, speed, older, track)
+            force, newer, edge_lo, edge_hi, lines = apply_step(parity, lo, now, hi, buoyancy, grad_b, speed, older, track)
         if k + 1 < steps:
-            lo, hi = edge_halos(edge_lo, edge_hi, "tile")
+            lo, hi = swap_halos((edge_lo, edge_hi), "tile")
         samples.append(jnp.sum(lines, axis=1))
         forces.append(force)
         older, now = (now, newer)
@@ -331,7 +335,7 @@
     image_part = jnp.zeros(buoyancy.shape, jnp.float32)
     for j in range(steps):
         lo, hi = halos(now, "tile")
-        (newer,) = apply_step(lo, now, hi, buoyancy, grad_b, speed, older, want_force=False)
+        (newer,) = apply_step(parity, lo, now, hi, buoyancy, grad_b, speed, older, want_force=False)
         newer = inject(newer, rec_local, rec_valid, residual[steps - 1 - j])
         image_part = image_part + newer * forces[steps - 1 - j]
         older, now = (now, newer)

time: 118 us -> 116 us (0.983)
  other arithmetic: 21.9 us -> 14 us
  local copies, waits for them, and re-layouts: 0.72 us -> 6.81 us
    select_n x10 -> x0, other arithmetic: 8.82 us -> none  [the longest x5 5.52 us: swap_halos(): jnp.where(odd, got_second, got_first)]
    unnamed x18 -> x36, local copies, waits for them, and re-layouts: 0.04 us -> 3.18 us
    dynamic_slice x0 -> x4, local copies, waits for them, and re-layouts: none -> 2.88 us  [halos(): far = lax.dynamic_slice_in_dim(block, odd * (planes - HALO), HALO, 0)]
  transfers between devices with their start and end apart: 14 -> 14, of which waited for: 8 -> 8; matrix products, arithmetic and copies ran while one was open for 6% -> 3% of each run, Pallas kernels for 18% -> 18%
where the time goes in v10:
time: 116 us; the launch traced here: 115 us
  Pallas kernels  39.2 us (34%)
  waiting for transfers between devices  29 us (25%)
  starting transfers between devices  24.7 us (21%)
  other arithmetic  14 us (12%)
  local copies, waits for them, and re-layouts  6.81 us (6%)
  between operations  1.71 us (1%)
    pallas_call x4, Pallas kernels, apply_step(): pl.pallas_call(kernel, grid=(planes // block,), in_specs=in_specs, out_sp...  39.2 us
    ppermute x5, starting transfers between devices, swap_halos(): lax.ppermute(sends[1], axis, second)  15 us
    ppermute x2, waiting for transfers between devices, reduce_members(): rows = keep + lax.ppermute(give, axis, pairs)  9.44 us
    ppermute x2, waiting for transfers between devices, reduce_members(): other = lax.ppermute(rows, axis, pairs)  8.52 us
    scatter-add x2, other arithmetic, inject(): flat = field.reshape(-1).at[where].add(jnp.where(valid, values, 0.0))  6.83 us
    ppermute x5, waiting for transfers between devices, swap_halos(): lax.ppermute(sends[0], axis, first)  5.87 us
    ppermute x2, starting transfers between devices, reduce_members(): rows = keep + lax.ppermute(give, axis, pairs)  5.81 us
    ppermute x5, waiting for transfers between devices, swap_halos(): lax.ppermute(sends[1], axis, second)  5.15 us
  transfers between devices with their start and end apart: 14, of which 8 were waited for; matrix products, arithmetic and copies ran while one was open for 3% of the time, Pallas kernels for 18%

profile of v10, /device:TPU:9, one launch (start us, length us, event | category | flops | bytes accessed | tf_op | source)
XLA Modules:
  0.0 115.4 jit_solution(739876407552611664)
XLA Ops:
  0.7 2.0 %dynamic-slice_bitcast_fusion = (f32[4,160,128]{2,1,0:T(8,128)S(1)}, f32[4,160,128]{2,1,0:T(8,128)}) fusion(f32[1,16,160,128]{3,2,1,0:T(8,128)} %param.12, s32[]{:T(128)S(6)} %select_n.136, s32[]{:T(128)S(6)} %select_n.135), kind=kLoop, calls=%fused_computation.7 | loop fusion | bytes 1310728 | tf_op jit(solution)/shard_map/dynamic_slice | solution.py:272
  2.7 4.6 %collective-permute-start.3 = (f32[4,160,128]{2,1,0:T(8,128)S(1)}, f32[4,160,128]{2,1,0:T(8,128)S(1)}, u32[]{:S(2)}, u32[]{:S(2)}) collective-permute-start(f32[4,160,128]{2,1,0:T(8,128)S(1)} %get-tuple-element.26), channel_id=1, source_target_pairs={{1,2},{2,1},{5,6},{6,5},{9,10},{10,9},{13,14},{14,13},{17,18},{18,... | collective-permute-start | bytes 983048 | tf_op jit(solution)/shard_map/ppermute | solution.py:265
  8.1 1.9 %collective-permute-start.5 = (f32[4,160,128]{2,1,0:T(8,128)S(1)}, f32[4,160,128]{2,1,0:T(8,128)S(1)}, u32[]{:S(2)}, u32[]{:S(2)}) collective-permute-start(f32[4,160,128]{2,1,0:T(8,128)S(1)} %get-tuple-element.24), channel_id=1, source_target_pairs={{1,2},{2,1},{5,6},{6,5},{9,10},{10,9},{13,14},{14,13},{17,18},{18,... | collective-permute-start | bytes 983048 | tf_op jit(solution)/shard_map/ppermute | solution.py:265
  13.1 3.1 %collective-permute-start.1 = (f32[4,160,128]{2,1,0:T(8,128)S(1)}, f32[4,160,128]{2,1,0:T(8,128)S(1)}, u32[]{:S(2)}, u32[]{:S(2)}) collective-permute-start(f32[4,160,128]{2,1,0:T(8,128)S(1)} %get-tuple-element.28), channel_id=1, source_target_pairs={{1,2},{2,1},{5,6},{6,5},{9,10},{10,9},{13,14},{14,13},{17,18},{18,... | collective-permute-start | bytes 983048 | tf_op jit(solution)/shard_map/ppermute | solution.py:265
  16.3 2.2 %collective-permute-done.4.refs_4_ = f32[4,160,128]{2,1,0:T(8,128)S(1)} collective-permute-done((f32[4,160,128]{2,1,0:T(8,128)}, f32[4,160,128]{2,1,0:T(8,128)S(1)}, u32[]{:S(2)}, u32[]{:S(2)}) %collective-permute-start.4) | collective-permute-done | bytes 327712 | tf_op jit(solution)/shard_map/ppermute | solution.py:265
  18.5 2.9 %collective-permute-done.5.refs_6_ = f32[4,160,128]{2,1,0:T(8,128)S(1)} collective-permute-done((f32[4,160,128]{2,1,0:T(8,128)S(1)}, f32[4,160,128]{2,1,0:T(8,128)S(1)}, u32[]{:S(2)}, u32[]{:S(2)}) %collective-permute-start.5) | collective-permute-done | bytes 327712 | tf_op jit(solution)/shard_map/ppermute | solution.py:265
  22.2 12.5 %shard_map.113 = (f32[16,160,128]{2,1,0:T(8,128)}, f32[16,160,128]{2,1,0:T(8,128)}, f32[16,160,128]{2,1,0:T(8,128)}, f32[16,160,128]{2,1,0:T(8,128)}, f32[16,160...) custom-call(s32[1]{0:T(128)} %bitcast.refs_0_, ...), custom_call_target="tpu_custom_call" | custom-call | tf_op jit(solution)/shard_map/pallas_call | solution.py:209
  34.8 3.0 %collective-permute-start.7 = (f32[4,160,128]{2,1,0:T(8,128)}, f32[4,160,128]{2,1,0:T(8,128)S(1)}, u32[]{:S(2)}, u32[]{:S(2)}) collective-permute-start(f32[4,160,128]{2,1,0:T(8,128)} %get-tuple-element.18), channel_id=1, source_target_pairs={{1,2},{2,1},{5,6},{6,5},{9,10},{10,9},{13,14},{14,13},{17,18},{18,... | collective-permute-start | bytes 983048 | tf_op jit(solution)/shard_map/ppermute | solution.py:265
  39.7 8.0 %shard_map.114 = f32[16,160,128]{2,1,0:T(8,128)} custom-call(s32[1]{0:T(128)} %bitcast.refs_0_, f32[4,160,128]{2,1,0:T(8,128)} %copy-done.5, f32[16,160,128]{2,1,0:T(8,128)} %bitcast.47, f32[4,160,128]{2,1,0:T(8,128)} %copy-done.12, f32[16,160,128]{2,1,0:T(8,128)} %refs_4_.5, f32[16,160,128]{2,1,0:T(8,128)} %get-tuple-element.12.refs_5_, ...), custom_call_target="tpu_custom_call" | custom-call | tf_op jit(solution)/shard_map/pallas_call | solution.py:209
  48.6 10.8 %shard_map.115 = (f32[16,160,128]{2,1,0:T(8,128)}, f32[16,160,128]{2,1,0:T(8,128)}, f32[4,160,128]{2,1,0:T(8,128)}, f32[4,160,128]{2,1,0:T(8,128)}, f32[256,128]{1,0:T(8,128)}) custom-call(s32[1]{0:T(128)} %bitcast.refs_0_, f32[4,160,128]{2,1,0:T(8,128)} %copy-done.13, f32[16,160,128]{2,1,0:T(8,128)} %get-tuple-element.17.refs_2_, ...), custom_call_target="tpu_custom_call" | custom-call | tf_op jit(solution)/shard_map/pallas_call | solution.py:209
  60.4 2.4 %scatter_fusion = f32[327680]{0:T(1024)S(1)} fusion(f32[327680]{0:T(1024)S(1)} %bitcast.34, s32[256]{0:T(256)S(1)} %get-tuple-element.32, f32[256]{0:T(256)S(1)} %get-tuple-element.37), kind=kCustom, calls=%fused_computation | custom fusion | flops 256 | bytes 4096 | tf_op jit(solution)/shard_map/scatter-add | solution.py:277
  63.0 2.2 %collective-permute-start.9 = (f32[4,160,128]{2,1,0:T(8,128)S(1)}, f32[4,160,128]{2,1,0:T(8,128)S(1)}, u32[]{:S(2)}, u32[]{:S(2)}) collective-permute-start(f32[4,160,128]{2,1,0:T(8,128)S(1)} %get-tuple-element.22), channel_id=1, source_target_pairs={{1,2},{2,1},{5,6},{6,5},{9,10},{10,9},{13,14},{14,13},{17,18},{18,... | collective-permute-start | bytes 983048 | tf_op jit(solution)/shard_map/ppermute | solution.py:265
  65.3 3.6 %collective-permute-done.8.refs_1_ = f32[4,160,128]{2,1,0:T(8,128)S(1)} collective-permute-done((f32[4,160,128]{2,1,0:T(8,128)S(1)}, f32[4,160,128]{2,1,0:T(8,128)S(1)}, u32[]{:S(2)}, u32[]{:S(2)}) %collective-permute-start.8) | collective-permute-done | bytes 327712 | tf_op jit(solution)/shard_map/ppermute | solution.py:265
  69.0 2.2 %collective-permute-done.9.refs_3_ = f32[4,160,128]{2,1,0:T(8,128)S(1)} collective-permute-done((f32[4,160,128]{2,1,0:T(8,128)S(1)}, f32[4,160,128]{2,1,0:T(8,128)S(1)}, u32[]{:S(2)}, u32[]{:S(2)}) %collective-permute-start.9) | collective-permute-done | bytes 327712 | tf_op jit(solution)/shard_map/ppermute | solution.py:265
  71.9 8.0 %shard_map.116 = f32[16,160,128]{2,1,0:T(8,128)} custom-call(s32[1]{0:T(128)} %bitcast.refs_0_, f32[4,160,128]{2,1,0:T(8,128)} %copy-done.10, f32[16,160,128]{2,1,0:T(8,128)} %bitcast.36, f32[4,160,128]{2,1,0:T(8,128)} %copy-done.11, f32[16,160,128]{2,1,0:T(8,128)} %refs_4_.5, f32[16,160,128]{2,1,0:T(8,128)} %get-tuple-element.12.refs_5_, ...), custom_call_target="tpu_custom_call" | custom-call | tf_op jit(solution)/shard_map/pallas_call | solution.py:209
  79.8 4.4 %scatter_fusion.1 = f32[327680]{0:T(1024)} fusion(f32[327680]{0:T(1024)} %bitcast.42, s32[256]{0:T(256)S(1)} %get-tuple-element.32, f32[256]{0:T(256)S(1)} %get-tuple-element.36), kind=kCustom, calls=%fused_computation.1 | custom fusion | flops 256 | bytes 4096 | tf_op jit(solution)/shard_map/scatter-add | solution.py:277
  84.2 2.5 %multiply_add_fusion = f32[16,160,128]{2,1,0:T(8,128)S(1)} fusion(f32[16,160,128]{2,1,0:T(8,128)} %bitcast.43, f32[16,160,128]{2,1,0:T(8,128)} %get-tuple-element.21, f32[16,160,128]{2,1,0:T(8,128)S(1)} %bitcast.37, f32[16,160,128]{2,1,0:T(8,128)} %get-tuple-element.20), kind=kLoop, calls=%fused_computation.3 | loop fusion | flops 983040 | bytes 6553600 | tf_op jit(solution)/shard_map/add | solution.py:340
  86.7 4.5 %collective-permute-start.10 = (f32[1280,128]{1,0:T(8,128)S(1)}, f32[1280,128]{1,0:T(8,128)S(1)}, u32[]{:S(2)}, u32[]{:S(2)}) collective-permute-start(f32[1280,128]{1,0:T(8,128)S(1)} %constant_dynamic-slice_fusion.1), channel_id=1, source_target_pairs={{0,4},{4,0},{8,12},{12,8},{1,5},{5,1},{9,13},{13,9},{2,6},{6,2},{1... | collective-permute-start | bytes 1966088 | tf_op jit(solution)/shard_map/ppermute | solution.py:250
  91.3 1.7 %collective-permute-done.10 = f32[1280,128]{1,0:T(8,128)S(1)} collective-permute-done((f32[1280,128]{1,0:T(8,128)S(1)}, f32[1280,128]{1,0:T(8,128)S(1)}, u32[]{:S(2)}, u32[]{:S(2)}) %collective-permute-start.10) | collective-permute-done | bytes 655392 | tf_op jit(solution)/shard_map/ppermute | solution.py:250
  93.1 1.3 %collective-permute-start.11 = (f32[640,128]{1,0:T(8,128)S(1)}, f32[640,128]{1,0:T(8,128)S(1)}, u32[]{:S(2)}, u32[]{:S(2)}) collective-permute-start(f32[640,128]{1,0:T(8,128)S(1)} %constant_dynamic-slice_fusion), channel_id=1, source_target_pairs={{0,8},{4,12},{8,0},{12,4},{1,9},{5,13},{9,1},{13,5},{2,10},{6,14},... | collective-permute-start | bytes 983048 | tf_op jit(solution)/shard_map/ppermute | solution.py:250
  94.4 7.7 %collective-permute-done.11 = f32[640,128]{1,0:T(8,128)S(1)} collective-permute-done((f32[640,128]{1,0:T(8,128)S(1)}, f32[640,128]{1,0:T(8,128)S(1)}, u32[]{:S(2)}, u32[]{:S(2)}) %collective-permute-start.11) | collective-permute-done | bytes 327712 | tf_op jit(solution)/shard_map/ppermute | solution.py:250
  103.4 6.8 %collective-permute-done.12 = f32[640,128]{1,0:T(8,128)S(1)} collective-permute-done((f32[640,128]{1,0:T(8,128)S(1)}, f32[640,128]{1,0:T(8,128)S(1)}, u32[]{:S(2)}, u32[]{:S(2)}) %collective-permute-start.12) | collective-permute-done | bytes 327712 | tf_op jit(solution)/shard_map/ppermute | solution.py:256
  110.2 2.2 %collective-permute-start.13 = (f32[1280,128]{1,0:T(8,128)S(1)}, f32[1280,128]{1,0:T(8,128)S(1)}, u32[]{:S(2)}, u32[]{:S(2)}) collective-permute-start(f32[1280,128]{1,0:T(8,128)S(1)} %maximum_select_fusion.1), channel_id=1, source_target_pairs={{0,4},{4,0},{8,12},{12,8},{1,5},{5,1},{9,13},{13,9},{2,6},{6,2},{1... | collective-permute-start | bytes 1966088 | tf_op jit(solution)/shard_map/ppermute | solution.py:256
  112.4 1.7 %collective-permute-done.13 = f32[1280,128]{1,0:T(8,128)S(1)} collective-permute-done((f32[1280,128]{1,0:T(8,128)S(1)}, f32[1280,128]{1,0:T(8,128)S(1)}, u32[]{:S(2)}, u32[]{:S(2)}) %collective-permute-start.13) | collective-permute-done | bytes 655392 | tf_op jit(solution)/shard_map/ppermute | solution.py:256
  (68 shorter events, 11.3 us)
Async XLA Ops:
  0.6 6.7 %copy-start = (f32[16,160,128]{2,1,0:T(8,128)S(1)}, f32[16,160,128]{2,1,0:T(8,128)}, u32[]{:S(2)}) copy-start(f32[16,160,128]{2,1,0:T(8,128)} %refs_4_.5) | copy-start | bytes 3932164
  0.7 9.4 %copy-start.4 = (f32[1,16,160,128]{3,2,1,0:T(8,128)S(1)}, f32[1,16,160,128]{3,2,1,0:T(8,128)}, u32[]{:S(2)}) copy-start(f32[1,16,160,128]{3,2,1,0:T(8,128)} %param.14) | copy-start | bytes 3932164
  2.7 10.4 %collective-permute-start.2 = (f32[4,160,128]{2,1,0:T(8,128)}, f32[4,160,128]{2,1,0:T(8,128)S(1)}, u32[]{:S(2)}, u32[]{:S(2)}) collective-permute-start(f32[4,160,128]{2,1,0:T(8,128)} %get-tuple-element.27), channel_id=1, source_target_pairs={{0,1},{1,0},{2,3},{3,2},{4,5},{5,4},{6,7},{7,6},{8,9},{9,8},{10,11... | collective-permute-start | bytes 983048 | tf_op jit(solution)/shard_map/ppermute | solution.py:265
  2.7 8.4 %copy-start.15 = (s32[256]{0:T(256)S(1)}, s32[256]{0:T(256)}, u32[]{:S(2)}) copy-start(s32[256]{0:T(256)} %param.18) | copy-start | bytes 3076
  2.7 9.7 %copy-start.17 = (f32[2]{0:T(128)S(1)}, f32[2]{0:T(128)}, u32[]{:S(2)}) copy-start(f32[2]{0:T(128)} %param.16) | copy-start | bytes 28
  2.7 13.6 %collective-permute-start.3 = (f32[4,160,128]{2,1,0:T(8,128)S(1)}, f32[4,160,128]{2,1,0:T(8,128)S(1)}, u32[]{:S(2)}, u32[]{:S(2)}) collective-permute-start(f32[4,160,128]{2,1,0:T(8,128)S(1)} %get-tuple-element.26), channel_id=1, source_target_pairs={{1,2},{2,1},{5,6},{6,5},{9,10},{10,9},{13,14},{14,13},{17,18},{18,... | collective-permute-start | bytes 983048 | tf_op jit(solution)/shard_map/ppermute | solution.py:265
  8.1 10.4 %collective-permute-start.4 = (f32[4,160,128]{2,1,0:T(8,128)}, f32[4,160,128]{2,1,0:T(8,128)S(1)}, u32[]{:S(2)}, u32[]{:S(2)}) collective-permute-start(f32[4,160,128]{2,1,0:T(8,128)} %get-tuple-element.25), channel_id=1, source_target_pairs={{0,1},{1,0},{2,3},{3,2},{4,5},{5,4},{6,7},{7,6},{8,9},{9,8},{10,11... | collective-permute-start | bytes 983048 | tf_op jit(solution)/shard_map/ppermute | solution.py:265
  8.1 13.3 %collective-permute-start.5 = (f32[4,160,128]{2,1,0:T(8,128)S(1)}, f32[4,160,128]{2,1,0:T(8,128)S(1)}, u32[]{:S(2)}, u32[]{:S(2)}) collective-permute-start(f32[4,160,128]{2,1,0:T(8,128)S(1)} %get-tuple-element.24), channel_id=1, source_target_pairs={{1,2},{2,1},{5,6},{6,5},{9,10},{10,9},{13,14},{14,13},{17,18},{18,... | collective-permute-start | bytes 983048 | tf_op jit(solution)/shard_map/ppermute | solution.py:265
  10.1 28.8 %collective-permute-start = (f32[4,160,128]{2,1,0:T(8,128)S(1)}, f32[4,160,128]{2,1,0:T(8,128)S(1)}, u32[]{:S(2)}, u32[]{:S(2)}) collective-permute-start(f32[4,160,128]{2,1,0:T(8,128)S(1)} %get-tuple-element.29), channel_id=1, source_target_pairs={{0,1},{1,0},{2,3},{3,2},{4,5},{5,4},{6,7},{7,6},{8,9},{9,8},{10,11... | collective-permute-start | bytes 983048 | tf_op jit(solution)/shard_map/ppermute | solution.py:265
  13.1 8.3 %copy-start.6 = (f32[4,160,128]{2,1,0:T(8,128)}, f32[4,160,128]{2,1,0:T(8,128)S(1)}, u32[]{:S(2)}) copy-start(f32[4,160,128]{2,1,0:T(8,128)S(1)} %collective-permute-done.2.refs_1_) | copy-start | bytes 983044
  13.1 25.8 %collective-permute-start.1 = (f32[4,160,128]{2,1,0:T(8,128)S(1)}, f32[4,160,128]{2,1,0:T(8,128)S(1)}, u32[]{:S(2)}, u32[]{:S(2)}) collective-permute-start(f32[4,160,128]{2,1,0:T(8,128)S(1)} %get-tuple-element.28), channel_id=1, source_target_pairs={{1,2},{2,1},{5,6},{6,5},{9,10},{10,9},{13,14},{14,13},{17,18},{18,... | collective-permute-start | bytes 983048 | tf_op jit(solution)/shard_map/ppermute | solution.py:265
  16.3 5.2 %copy-start.7 = (f32[4,160,128]{2,1,0:T(8,128)}, f32[4,160,128]{2,1,0:T(8,128)S(1)}, u32[]{:S(2)}) copy-start(f32[4,160,128]{2,1,0:T(8,128)S(1)} %collective-permute-done.3.refs_3_) | copy-start | bytes 983044
  34.7 13.0 %collective-permute-start.6 = (f32[4,160,128]{2,1,0:T(8,128)}, f32[4,160,128]{2,1,0:T(8,128)S(1)}, u32[]{:S(2)}, u32[]{:S(2)}) collective-permute-start(f32[4,160,128]{2,1,0:T(8,128)} %get-tuple-element.16), channel_id=1, source_target_pairs={{0,1},{1,0},{2,3},{3,2},{4,5},{5,4},{6,7},{7,6},{8,9},{9,8},{10,11... | collective-permute-start | bytes 983048 | tf_op jit(solution)/shard_map/ppermute | solution.py:265
  34.8 12.9 %collective-permute-start.7 = (f32[4,160,128]{2,1,0:T(8,128)}, f32[4,160,128]{2,1,0:T(8,128)S(1)}, u32[]{:S(2)}, u32[]{:S(2)}) collective-permute-start(f32[4,160,128]{2,1,0:T(8,128)} %get-tuple-element.18), channel_id=1, source_target_pairs={{1,2},{2,1},{5,6},{6,5},{9,10},{10,9},{13,14},{14,13},{17,18},{18,... | collective-permute-start | bytes 983048 | tf_op jit(solution)/shard_map/ppermute | solution.py:265
  48.6 11.8 %copy-start.16 = (f32[2,256]{1,0:T(2,128)S(1)}, f32[2,256]{1,0:T(2,128)}, u32[]{:S(2)}) copy-start(f32[2,256]{1,0:T(2,128)} %param.19) | copy-start | bytes 6148
  48.6 11.9 %copy-start.1 = (f32[16,160,128]{2,1,0:T(8,128)S(1)}, f32[16,160,128]{2,1,0:T(8,128)}, u32[]{:S(2)}) copy-start(f32[16,160,128]{2,1,0:T(8,128)} %shard_map.114) | copy-start | bytes 3932164
  62.9 8.3 %copy-start.2 = (f32[327680]{0:T(1024)}, f32[327680]{0:T(1024)S(1)}, u32[]{:S(2)}) copy-start(f32[327680]{0:T(1024)S(1)} %scatter_fusion) | copy-start | bytes 3932164
  63.0 6.0 %collective-permute-start.8 = (f32[4,160,128]{2,1,0:T(8,128)S(1)}, f32[4,160,128]{2,1,0:T(8,128)S(1)}, u32[]{:S(2)}, u32[]{:S(2)}) collective-permute-start(f32[4,160,128]{2,1,0:T(8,128)S(1)} %get-tuple-element.23), channel_id=1, source_target_pairs={{0,1},{1,0},{2,3},{3,2},{4,5},{5,4},{6,7},{7,6},{8,9},{9,8},{10,11... | collective-permute-start | bytes 983048 | tf_op jit(solution)/shard_map/ppermute | solution.py:265
  63.0 8.1 %collective-permute-start.9 = (f32[4,160,128]{2,1,0:T(8,128)S(1)}, f32[4,160,128]{2,1,0:T(8,128)S(1)}, u32[]{:S(2)}, u32[]{:S(2)}) collective-permute-start(f32[4,160,128]{2,1,0:T(8,128)S(1)} %get-tuple-element.22), channel_id=1, source_target_pairs={{1,2},{2,1},{5,6},{6,5},{9,10},{10,9},{13,14},{14,13},{17,18},{18,... | collective-permute-start | bytes 983048 | tf_op jit(solution)/shard_map/ppermute | solution.py:265
  79.8 4.4 %copy-start.3 = (f32[327680]{0:T(1024)S(1)}, f32[327680]{0:T(1024)}, u32[]{:S(2)}) copy-start(f32[327680]{0:T(1024)} %copy-done.2) | copy-start | bytes 3932164
  86.7 6.3 %collective-permute-start.10 = (f32[1280,128]{1,0:T(8,128)S(1)}, f32[1280,128]{1,0:T(8,128)S(1)}, u32[]{:S(2)}, u32[]{:S(2)}) collective-permute-start(f32[1280,128]{1,0:T(8,128)S(1)} %constant_dynamic-slice_fusion.1), channel_id=1, source_target_pairs={{0,4},{4,0},{8,12},{12,8},{1,5},{5,1},{9,13},{13,9},{2,6},{6,2},{1... | collective-permute-start | bytes 1966088 | tf_op jit(solution)/shard_map/ppermute | solution.py:250
  93.1 9.0 %collective-permute-start.11 = (f32[640,128]{1,0:T(8,128)S(1)}, f32[640,128]{1,0:T(8,128)S(1)}, u32[]{:S(2)}, u32[]{:S(2)}) collective-permute-start(f32[640,128]{1,0:T(8,128)S(1)} %constant_dynamic-slice_fusion), channel_id=1, source_target_pairs={{0,8},{4,12},{8,0},{12,4},{1,9},{5,13},{9,1},{13,5},{2,10},{6,14},... | collective-permute-start | bytes 983048 | tf_op jit(solution)/shard_map/ppermute | solution.py:250
  102.1 8.1 %collective-permute-start.12 = (f32[640,128]{1,0:T(8,128)S(1)}, f32[640,128]{1,0:T(8,128)S(1)}, u32[]{:S(2)}, u32[]{:S(2)}) collective-permute-start(f32[640,128]{1,0:T(8,128)S(1)} %add_multiply_fusion), channel_id=1, source_target_pairs={{0,8},{4,12},{8,0},{12,4},{1,9},{5,13},{9,1},{13,5},{2,10},{6,14},... | collective-permute-start | bytes 983048 | tf_op jit(solution)/shard_map/ppermute | solution.py:256
  110.2 3.9 %collective-permute-start.13 = (f32[1280,128]{1,0:T(8,128)S(1)}, f32[1280,128]{1,0:T(8,128)S(1)}, u32[]{:S(2)}, u32[]{:S(2)}) collective-permute-start(f32[1280,128]{1,0:T(8,128)S(1)} %maximum_select_fusion.1), channel_id=1, source_target_pairs={{0,4},{4,0},{8,12},{12,8},{1,5},{5,1},{9,13},{13,9},{2,6},{6,2},{1... | collective-permute-start | bytes 1966088 | tf_op jit(solution)/shard_map/ppermute | solution.py:256
  (8 other events, 9.8 us)

commit v11 on v10

--- a/solution.py
+++ b/solution.py
@@ -154,6 +154,60 @@
             g2_ref[sl] = grads[2]
 
 
+def final_kernel(parity_ref, lo_ref, mid_ref, hi_ref, b_ref, g0_ref, g1_ref, g2_ref, c_ref, old_ref,
+                 rec_ref, valid_ref, amount_ref, part_ref, force_ref, new_ref, image_ref, pad_ref, *, block, rows):
+    i = pl.program_id(0)
+    odd = parity_ref[0] == 1
+
+    @pl.when(i == 0)
+    def _():
+        fill_padded(pad_ref, lo_ref, mid_ref, hi_ref, odd)
+
+    planes, height, depth = mid_ref.shape
+    lane = lax.broadcasted_iota(jnp.int32, (rows, depth), 1)
+    for p in range(block):
+        plane = i * block + p + HALO
+        for y0 in range(0, height, rows):
+            sl = (p, pl.ds(y0, rows), slice(None))
+            centre, lap, grads = taps(pad_ref, plane, y0, rows, lane)
+            force = b_ref[sl] * lap + (g0_ref[sl] * grads[0] + g1_ref[sl] * grads[1] + g2_ref[sl] * grads[2])
+            new_ref[plane - HALO, pl.ds(y0, rows), :] = 2.0 * centre - old_ref[sl] + c_ref[sl] * force
+
+    @pl.when(i == pl.num_programs(0) - 1)
+    def _():
+        one_lane = lax.broadcasted_iota(jnp.int32, (1, depth), 1)
+
+        def add(r, carry):
+            x = rec_ref[0, r]
+            y = rec_ref[1, r]
+            hit = (one_lane == rec_ref[2, r]) & (valid_ref[r] == 1)
+            line = new_ref[x, pl.ds(y, 1), :]
+            new_ref[x, pl.ds(y, 1), :] = jnp.where(hit, line + amount_ref[r], line)
+            return carry
+
+        lax.fori_loop(0, amount_ref.shape[0], add, 0)
+        for q in range(planes):
+            image_ref[q] = part_ref[q] + new_ref[q] * force_ref[q]
+
+
+def apply_final(parity, lo, mid, hi, b, g, c, old, receivers, valid, amount, part, force, rows=40):
+    planes, height, depth = mid.shape
+    block = pick_block(planes)
+    full, blk = specs(mid.shape, block)
+    out = jax.ShapeDtypeStruct(mid.shape, jnp.float32)
+    smem = pl.BlockSpec(memory_space=pltpu.SMEM)
+    return pl.pallas_call(
+        functools.partial(final_kernel, block=block, rows=rows),
+        grid=(planes // block,),
+        in_specs=[smem, full(lo.shape), full(mid.shape), full(hi.shape)] + [blk] * 6
+        + [smem, smem, smem, full(mid.shape), full(mid.shape)],
+        out_specs=[full(mid.shape), full(mid.shape)],
+        out_shape=[out, out],
+        scratch_shapes=[pltpu.VMEM((planes + 2 * HALO, height + 2 * PADY, depth), jnp.float32)],
+        compiler_params=pltpu.CompilerParams(dimension_semantics=("arbitrary",)),
+    )(parity, lo, mid, hi, b, g[0], g[1], g[2], c, old, receivers, valid, amount, part, force)
+
+
 def pick_block(planes):
     for b in (4, 2, 1):
         if planes % b == 0:
@@ -335,9 +389,16 @@
     image_part = jnp.zeros(buoyancy.shape, jnp.float32)
     for j in range(steps):
         lo, hi = halos(now, "tile")
-        (newer,) = apply_step(parity, lo, now, hi, buoyancy, grad_b, speed, older, want_force=False)
-        newer = inject(newer, rec_local, rec_valid, residual[steps - 1 - j])
-        image_part = image_part + newer * forces[steps - 1 - j]
+        m = steps - 1 - j
+        if j + 1 < steps:
+            (newer,) = apply_step(parity, lo, now, hi, buoyancy, grad_b, speed, older, want_force=False)
+            newer = inject(newer, rec_local, rec_valid, residual[m])
+            image_part = image_part + newer * forces[m]
+        else:
+            valid = rec_valid.astype(jnp.int32)
+            newer, image_part = apply_final(
+                parity, lo, now, hi, buoyancy, grad_b, speed, older, receivers, valid, residual[m], image_part, forces[m]
+            )
         older, now = (now, newer)
     image = reduce_members(image_part, "real")
     return (image, now[None])

time: 116 us -> 117 us (level)
  other arithmetic: 14 us -> 8.94 us
  Pallas kernels: 39.2 us -> 43.7 us
  local copies, waits for them, and re-layouts: 6.81 us -> 9.56 us
    pallas_call x0 -> x1, Pallas kernels: none -> 12.5 us  [apply_final(): pl.pallas_call(functools.partial(final_kernel, block=block, rows=rows), g...]
    pallas_call x4 -> x3, Pallas kernels: 39.2 us -> 31.2 us  [apply_step(): pl.pallas_call(kernel, grid=(planes // block,), in_specs=in_specs, out_sp...]
    scatter-add x2 -> x1, other arithmetic: 6.83 us -> 2.44 us  [inject(): flat = field.reshape(-1).at[where].add(jnp.where(valid, values, 0.0))]
    add x1 -> x0, other arithmetic: 2.45 us -> none  [shards(): image_part = image_part + newer * forces[steps - 1 - j]]
    mul x0 -> x1, other arithmetic: none -> 1.2 us  [shards(): image_part = image_part + newer * forces[m]]
    dynamic_slice x2, local copies, waits for them, and re-layouts: 0.08 us -> 1.27 us  [reduce_members(): give = lax.dynamic_slice_in_dim(rows, (1 - upper) * half, half, 0)]
    unnamed x36 -> x38, local copies, waits for them, and re-layouts: 3.18 us -> 3.2 us
  transfers between devices with their start and end apart: 14 -> 14, of which waited for: 8 -> 8; matrix products, arithmetic and copies ran while one was open for 3% -> 5% of each run, Pallas kernels for 18% -> 18%
where the time goes in v11:
time: 117 us; the launch traced here: 116 us
  Pallas kernels  43.7 us (37%)
  waiting for transfers between devices  27.9 us (24%)
  starting transfers between devices  24.6 us (21%)
  local copies, waits for them, and re-layouts  9.56 us (8%)
  other arithmetic  8.94 us (8%)
  between operations  1.68 us (1%)
    pallas_call x3, Pallas kernels, apply_step(): pl.pallas_call(kernel, grid=(planes // block,), in_specs=in_specs, out_sp...  31.2 us
    ppermute x5, starting transfers between devices, swap_halos(): lax.ppermute(sends[1], axis, second)  14.9 us
    pallas_call x1, Pallas kernels, apply_final(): pl.pallas_call(functools.partial(final_kernel, block=block, rows=rows), g...  12.5 us
    ppermute x2, waiting for transfers between devices, reduce_members(): rows = keep + lax.ppermute(give, axis, pairs)  9.44 us
    ppermute x2, waiting for transfers between devices, reduce_members(): other = lax.ppermute(rows, axis, pairs)  8.52 us
    ppermute x2, starting transfers between devices, reduce_members(): rows = keep + lax.ppermute(give, axis, pairs)  5.81 us
    ppermute x5, waiting for transfers between devices, swap_halos(): lax.ppermute(sends[1], axis, second)  5.13 us
    ppermute x5, waiting for transfers between devices, swap_halos(): lax.ppermute(sends[0], axis, first)  4.85 us
  transfers between devices with their start and end apart: 14, of which 8 were waited for; matrix products, arithmetic and copies ran while one was open for 5% of the time, Pallas kernels for 18%

profile of v11, /device:TPU:9, one launch (start us, length us, event | category | flops | bytes accessed | tf_op | source)
XLA Modules:
  0.0 116.4 jit_solution(391710482592771150)
XLA Ops:
  0.7 2.0 %dynamic-slice_bitcast_fusion = (f32[4,160,128]{2,1,0:T(8,128)S(1)}, f32[4,160,128]{2,1,0:T(8,128)}) fusion(f32[1,16,160,128]{3,2,1,0:T(8,128)} %param.12, s32[]{:T(128)S(6)} %select_n.132, s32[]{:T(128)S(6)} %select_n.131), kind=kLoop, calls=%fused_computation.5 | loop fusion | bytes 1310728 | tf_op jit(solution)/shard_map/dynamic_slice | solution.py:326
  2.7 4.6 %collective-permute-start.3 = (f32[4,160,128]{2,1,0:T(8,128)S(1)}, f32[4,160,128]{2,1,0:T(8,128)S(1)}, u32[]{:S(2)}, u32[]{:S(2)}) collective-permute-start(f32[4,160,128]{2,1,0:T(8,128)S(1)} %get-tuple-element.32), channel_id=1, source_target_pairs={{1,2},{2,1},{5,6},{6,5},{9,10},{10,9},{13,14},{14,13},{17,18},{18,... | collective-permute-start | bytes 983048 | tf_op jit(solution)/shard_map/ppermute | solution.py:319
  8.2 1.9 %collective-permute-start.5 = (f32[4,160,128]{2,1,0:T(8,128)}, f32[4,160,128]{2,1,0:T(8,128)S(1)}, u32[]{:S(2)}, u32[]{:S(2)}) collective-permute-start(f32[4,160,128]{2,1,0:T(8,128)} %get-tuple-element.30), channel_id=1, source_target_pairs={{1,2},{2,1},{5,6},{6,5},{9,10},{10,9},{13,14},{14,13},{17,18},{18,... | collective-permute-start | bytes 983048 | tf_op jit(solution)/shard_map/ppermute | solution.py:319
  13.1 3.1 %collective-permute-start.1 = (f32[4,160,128]{2,1,0:T(8,128)S(1)}, f32[4,160,128]{2,1,0:T(8,128)S(1)}, u32[]{:S(2)}, u32[]{:S(2)}) collective-permute-start(f32[4,160,128]{2,1,0:T(8,128)S(1)} %get-tuple-element.34), channel_id=1, source_target_pairs={{1,2},{2,1},{5,6},{6,5},{9,10},{10,9},{13,14},{14,13},{17,18},{18,... | collective-permute-start | bytes 983048 | tf_op jit(solution)/shard_map/ppermute | solution.py:319
  16.3 2.2 %collective-permute-done.4.refs_4_ = f32[4,160,128]{2,1,0:T(8,128)S(1)} collective-permute-done((f32[4,160,128]{2,1,0:T(8,128)}, f32[4,160,128]{2,1,0:T(8,128)S(1)}, u32[]{:S(2)}, u32[]{:S(2)}) %collective-permute-start.4) | collective-permute-done | bytes 327712 | tf_op jit(solution)/shard_map/ppermute | solution.py:319
  18.5 2.9 %collective-permute-done.5.refs_6_ = f32[4,160,128]{2,1,0:T(8,128)S(1)} collective-permute-done((f32[4,160,128]{2,1,0:T(8,128)}, f32[4,160,128]{2,1,0:T(8,128)S(1)}, u32[]{:S(2)}, u32[]{:S(2)}) %collective-permute-start.5) | collective-permute-done | bytes 327712 | tf_op jit(solution)/shard_map/ppermute | solution.py:319
  22.2 12.6 %shard_map.113 = (f32[16,160,128]{2,1,0:T(8,128)}, f32[16,160,128]{2,1,0:T(8,128)}, f32[16,160,128]{2,1,0:T(8,128)}, f32[16,160,128]{2,1,0:T(8,128)}, f32[16,160...) custom-call(s32[1]{0:T(128)} %bitcast.refs_0_.parity_ref, ...), custom_call_target="tpu_custom_call" | custom-call | tf_op jit(solution)/shard_map/pallas_call | solution.py:263
  34.9 3.0 %collective-permute-start.7 = (f32[4,160,128]{2,1,0:T(8,128)}, f32[4,160,128]{2,1,0:T(8,128)S(1)}, u32[]{:S(2)}, u32[]{:S(2)}) collective-permute-start(f32[4,160,128]{2,1,0:T(8,128)} %get-tuple-element.20), channel_id=1, source_target_pairs={{1,2},{2,1},{5,6},{6,5},{9,10},{10,9},{13,14},{14,13},{17,18},{18,... | collective-permute-start | bytes 983048 | tf_op jit(solution)/shard_map/ppermute | solution.py:319
  40.4 8.0 %shard_map.114 = f32[16,160,128]{2,1,0:T(8,128)} custom-call(s32[1]{0:T(128)} %bitcast.refs_0_.parity_ref, f32[4,160,128]{2,1,0:T(8,128)} %copy-done.6, f32[16,160,128]{2,1,0:T(8,128)} %bitcast.42, f32[4,160,128]{2,1,0:T(8,128)} %copy-done.13, f32[16,160,128]{2,1,0:T(8,128)} %b_ref.1, f32[16,160,128]{2,1,0:T(8,128)} %get-tuple-element.14.refs_5_.g0_ref, ...), custom_call_target="tpu_custom_call" | custom-call | tf_op jit(solution)/shard_map/pallas_call | solution.py:263
  49.3 10.7 %shard_map.115 = (f32[16,160,128]{2,1,0:T(8,128)}, f32[16,160,128]{2,1,0:T(8,128)}, f32[4,160,128]{2,1,0:T(8,128)}, f32[4,160,128]{2,1,0:T(8,128)}, f32[256,128]{1,0:T(8,128)}) custom-call(s32[1]{0:T(128)} %bitcast.refs_0_.parity_ref, f32[4,160,128]{2,1,0:T(8,128)} %copy-done.14, f32[16,160,128]{2,1,0:T(8,128)} %get-tuple-element.19.refs_2_, ...), custom_call_target="tpu_custom_call" | custom-call | tf_op jit(solution)/shard_map/pallas_call | solution.py:263
  61.6 2.4 %scatter_fusion = f32[327680]{0:T(1024)S(1)} fusion(f32[327680]{0:T(1024)S(1)} %bitcast.32, s32[256]{0:T(256)S(1)} %get-tuple-element.38, f32[256]{0:T(256)S(1)} %broadcast_select_fusion), kind=kCustom, calls=%fused_computation | custom fusion | flops 256 | bytes 4096 | tf_op jit(solution)/shard_map/scatter-add | solution.py:331
  65.0 2.2 %collective-permute-start.9 = (f32[4,160,128]{2,1,0:T(8,128)}, f32[4,160,128]{2,1,0:T(8,128)S(1)}, u32[]{:S(2)}, u32[]{:S(2)}) collective-permute-start(f32[4,160,128]{2,1,0:T(8,128)} %get-tuple-element.28), channel_id=1, source_target_pairs={{1,2},{2,1},{5,6},{6,5},{9,10},{10,9},{13,14},{14,13},{17,18},{18,... | collective-permute-start | bytes 983048 | tf_op jit(solution)/shard_map/ppermute | solution.py:319
  68.5 2.7 %collective-permute-done.8.lo_ref = f32[4,160,128]{2,1,0:T(8,128)S(1)} collective-permute-done((f32[4,160,128]{2,1,0:T(8,128)}, f32[4,160,128]{2,1,0:T(8,128)S(1)}, u32[]{:S(2)}, u32[]{:S(2)}) %collective-permute-start.8) | collective-permute-done | bytes 327712 | tf_op jit(solution)/shard_map/ppermute | solution.py:319
  71.1 2.2 %collective-permute-done.9.hi_ref = f32[4,160,128]{2,1,0:T(8,128)S(1)} collective-permute-done((f32[4,160,128]{2,1,0:T(8,128)}, f32[4,160,128]{2,1,0:T(8,128)S(1)}, u32[]{:S(2)}, u32[]{:S(2)}) %collective-permute-start.9) | collective-permute-done | bytes 327712 | tf_op jit(solution)/shard_map/ppermute | solution.py:319
  74.1 12.5 %shard_map.116 = (f32[16,160,128]{2,1,0:T(8,128)}, f32[16,160,128]{2,1,0:T(8,128)}) custom-call(s32[1]{0:T(128)} %bitcast.refs_0_.parity_ref, f32[4,160,128]{2,1,0:T(8,128)} %copy-done.11, f32[16,160,128]{2,1,0:T(8,128)} %bitcast.35, f32[4,160,128]{2,1,0:T(8,128)} %copy-done.12, f32[16,160,128]{2,1,0:T(8,128)} %b_ref.1, ...), custom_call_target="tpu_custom_call" | custom-call | tf_op jit(solution)/shard_map/pallas_call | solution.py:199
  86.6 1.2 %constant_dynamic-slice_fusion.1 = f32[1280,128]{1,0:T(8,128)S(1)} fusion(f32[2560,128]{1,0:T(8,128)} %bitcast.45, s32[]{:T(128)S(6)} %select_n.145), kind=kLoop, calls=%fused_computation.11 | loop fusion | bytes 1310724 | tf_op jit(solution)/shard_map/dynamic_slice | solution.py:302
  87.8 4.5 %collective-permute-start.10 = (f32[1280,128]{1,0:T(8,128)S(1)}, f32[1280,128]{1,0:T(8,128)S(1)}, u32[]{:S(2)}, u32[]{:S(2)}) collective-permute-start(f32[1280,128]{1,0:T(8,128)S(1)} %constant_dynamic-slice_fusion.1), channel_id=1, source_target_pairs={{0,4},{4,0},{8,12},{12,8},{1,5},{5,1},{9,13},{13,9},{2,6},{6,2},{1... | collective-permute-start | bytes 1966088 | tf_op jit(solution)/shard_map/ppermute | solution.py:304
  92.3 1.7 %collective-permute-done.10 = f32[1280,128]{1,0:T(8,128)S(1)} collective-permute-done((f32[1280,128]{1,0:T(8,128)S(1)}, f32[1280,128]{1,0:T(8,128)S(1)}, u32[]{:S(2)}, u32[]{:S(2)}) %collective-permute-start.10) | collective-permute-done | bytes 655392 | tf_op jit(solution)/shard_map/ppermute | solution.py:304
  94.2 1.3 %collective-permute-start.11 = (f32[640,128]{1,0:T(8,128)S(1)}, f32[640,128]{1,0:T(8,128)S(1)}, u32[]{:S(2)}, u32[]{:S(2)}) collective-permute-start(f32[640,128]{1,0:T(8,128)S(1)} %constant_dynamic-slice_fusion), channel_id=1, source_target_pairs={{0,8},{4,12},{8,0},{12,4},{1,9},{5,13},{9,1},{13,5},{2,10},{6,14},... | collective-permute-start | bytes 983048 | tf_op jit(solution)/shard_map/ppermute | solution.py:304
  95.5 7.7 %collective-permute-done.11 = f32[640,128]{1,0:T(8,128)S(1)} collective-permute-done((f32[640,128]{1,0:T(8,128)S(1)}, f32[640,128]{1,0:T(8,128)S(1)}, u32[]{:S(2)}, u32[]{:S(2)}) %collective-permute-start.11) | collective-permute-done | bytes 327712 | tf_op jit(solution)/shard_map/ppermute | solution.py:304
  103.2 1.3 %collective-permute-start.12 = (f32[640,128]{1,0:T(8,128)S(1)}, f32[640,128]{1,0:T(8,128)S(1)}, u32[]{:S(2)}, u32[]{:S(2)}) collective-permute-start(f32[640,128]{1,0:T(8,128)S(1)} %add_multiply_fusion), channel_id=1, source_target_pairs={{0,8},{4,12},{8,0},{12,4},{1,9},{5,13},{9,1},{13,5},{2,10},{6,14},... | collective-permute-start | bytes 983048 | tf_op jit(solution)/shard_map/ppermute | solution.py:310
  104.5 6.8 %collective-permute-done.12 = f32[640,128]{1,0:T(8,128)S(1)} collective-permute-done((f32[640,128]{1,0:T(8,128)S(1)}, f32[640,128]{1,0:T(8,128)S(1)}, u32[]{:S(2)}, u32[]{:S(2)}) %collective-permute-start.12) | collective-permute-done | bytes 327712 | tf_op jit(solution)/shard_map/ppermute | solution.py:310
  111.3 2.2 %collective-permute-start.13 = (f32[1280,128]{1,0:T(8,128)S(1)}, f32[1280,128]{1,0:T(8,128)S(1)}, u32[]{:S(2)}, u32[]{:S(2)}) collective-permute-start(f32[1280,128]{1,0:T(8,128)S(1)} %maximum_select_fusion.1), channel_id=1, source_target_pairs={{0,4},{4,0},{8,12},{12,8},{1,5},{5,1},{9,13},{13,9},{2,6},{6,2},{1... | collective-permute-start | bytes 1966088 | tf_op jit(solution)/shard_map/ppermute | solution.py:310
  113.5 1.7 %collective-permute-done.13 = f32[1280,128]{1,0:T(8,128)S(1)} collective-permute-done((f32[1280,128]{1,0:T(8,128)S(1)}, f32[1280,128]{1,0:T(8,128)S(1)}, u32[]{:S(2)}, u32[]{:S(2)}) %collective-permute-start.13) | collective-permute-done | bytes 655392 | tf_op jit(solution)/shard_map/ppermute | solution.py:310
  (69 shorter events, 13.2 us)
Async XLA Ops:
  0.6 6.7 %copy-start = (f32[16,160,128]{2,1,0:T(8,128)S(1)}, f32[16,160,128]{2,1,0:T(8,128)}, u32[]{:S(2)}) copy-start(f32[16,160,128]{2,1,0:T(8,128)} %b_ref.1) | copy-start | bytes 3932164
  0.7 9.5 %copy-start.3 = (f32[1,16,160,128]{3,2,1,0:T(8,128)S(1)}, f32[1,16,160,128]{3,2,1,0:T(8,128)}, u32[]{:S(2)}) copy-start(f32[1,16,160,128]{3,2,1,0:T(8,128)} %param.14) | copy-start | bytes 3932164
  2.7 10.5 %collective-permute-start.2 = (f32[4,160,128]{2,1,0:T(8,128)}, f32[4,160,128]{2,1,0:T(8,128)S(1)}, u32[]{:S(2)}, u32[]{:S(2)}) collective-permute-start(f32[4,160,128]{2,1,0:T(8,128)} %get-tuple-element.33), channel_id=1, source_target_pairs={{0,1},{1,0},{2,3},{3,2},{4,5},{5,4},{6,7},{7,6},{8,9},{9,8},{10,11... | collective-permute-start | bytes 983048 | tf_op jit(solution)/shard_map/ppermute | solution.py:319
  2.7 8.5 %copy-start.16 = (s32[256]{0:T(256)S(1)}, s32[256]{0:T(256)}, u32[]{:S(2)}) copy-start(s32[256]{0:T(256)} %param.18) | copy-start | bytes 3076
  2.7 9.9 %copy-start.18 = (f32[2]{0:T(128)S(1)}, f32[2]{0:T(128)}, u32[]{:S(2)}) copy-start(f32[2]{0:T(128)} %param.16) | copy-start | bytes 28
  2.7 13.6 %collective-permute-start.3 = (f32[4,160,128]{2,1,0:T(8,128)S(1)}, f32[4,160,128]{2,1,0:T(8,128)S(1)}, u32[]{:S(2)}, u32[]{:S(2)}) collective-permute-start(f32[4,160,128]{2,1,0:T(8,128)S(1)} %get-tuple-element.32), channel_id=1, source_target_pairs={{1,2},{2,1},{5,6},{6,5},{9,10},{10,9},{13,14},{14,13},{17,18},{18,... | collective-permute-start | bytes 983048 | tf_op jit(solution)/shard_map/ppermute | solution.py:319
  8.2 10.3 %collective-permute-start.4 = (f32[4,160,128]{2,1,0:T(8,128)}, f32[4,160,128]{2,1,0:T(8,128)S(1)}, u32[]{:S(2)}, u32[]{:S(2)}) collective-permute-start(f32[4,160,128]{2,1,0:T(8,128)} %get-tuple-element.31), channel_id=1, source_target_pairs={{0,1},{1,0},{2,3},{3,2},{4,5},{5,4},{6,7},{7,6},{8,9},{9,8},{10,11... | collective-permute-start | bytes 983048 | tf_op jit(solution)/shard_map/ppermute | solution.py:319
  8.2 13.2 %collective-permute-start.5 = (f32[4,160,128]{2,1,0:T(8,128)}, f32[4,160,128]{2,1,0:T(8,128)S(1)}, u32[]{:S(2)}, u32[]{:S(2)}) collective-permute-start(f32[4,160,128]{2,1,0:T(8,128)} %get-tuple-element.30), channel_id=1, source_target_pairs={{1,2},{2,1},{5,6},{6,5},{9,10},{10,9},{13,14},{14,13},{17,18},{18,... | collective-permute-start | bytes 983048 | tf_op jit(solution)/shard_map/ppermute | solution.py:319
  10.2 29.3 %collective-permute-start = (f32[4,160,128]{2,1,0:T(8,128)S(1)}, f32[4,160,128]{2,1,0:T(8,128)S(1)}, u32[]{:S(2)}, u32[]{:S(2)}) collective-permute-start(f32[4,160,128]{2,1,0:T(8,128)S(1)} %get-tuple-element.35), channel_id=1, source_target_pairs={{0,1},{1,0},{2,3},{3,2},{4,5},{5,4},{6,7},{7,6},{8,9},{9,8},{10,11... | collective-permute-start | bytes 983048 | tf_op jit(solution)/shard_map/ppermute | solution.py:319
  13.1 8.3 %copy-start.7 = (f32[4,160,128]{2,1,0:T(8,128)}, f32[4,160,128]{2,1,0:T(8,128)S(1)}, u32[]{:S(2)}) copy-start(f32[4,160,128]{2,1,0:T(8,128)S(1)} %collective-permute-done.2.refs_1_) | copy-start | bytes 983044
  13.1 26.4 %collective-permute-start.1 = (f32[4,160,128]{2,1,0:T(8,128)S(1)}, f32[4,160,128]{2,1,0:T(8,128)S(1)}, u32[]{:S(2)}, u32[]{:S(2)}) collective-permute-start(f32[4,160,128]{2,1,0:T(8,128)S(1)} %get-tuple-element.34), channel_id=1, source_target_pairs={{1,2},{2,1},{5,6},{6,5},{9,10},{10,9},{13,14},{14,13},{17,18},{18,... | collective-permute-start | bytes 983048 | tf_op jit(solution)/shard_map/ppermute | solution.py:319
  16.3 5.1 %copy-start.8 = (f32[4,160,128]{2,1,0:T(8,128)}, f32[4,160,128]{2,1,0:T(8,128)S(1)}, u32[]{:S(2)}) copy-start(f32[4,160,128]{2,1,0:T(8,128)S(1)} %collective-permute-done.3.refs_3_) | copy-start | bytes 983044
  34.8 13.6 %collective-permute-start.6 = (f32[4,160,128]{2,1,0:T(8,128)}, f32[4,160,128]{2,1,0:T(8,128)S(1)}, u32[]{:S(2)}, u32[]{:S(2)}) collective-permute-start(f32[4,160,128]{2,1,0:T(8,128)} %get-tuple-element.18), channel_id=1, source_target_pairs={{0,1},{1,0},{2,3},{3,2},{4,5},{5,4},{6,7},{7,6},{8,9},{9,8},{10,11... | collective-permute-start | bytes 983048 | tf_op jit(solution)/shard_map/ppermute | solution.py:319
  34.9 13.5 %collective-permute-start.7 = (f32[4,160,128]{2,1,0:T(8,128)}, f32[4,160,128]{2,1,0:T(8,128)S(1)}, u32[]{:S(2)}, u32[]{:S(2)}) collective-permute-start(f32[4,160,128]{2,1,0:T(8,128)} %get-tuple-element.20), channel_id=1, source_target_pairs={{1,2},{2,1},{5,6},{6,5},{9,10},{10,9},{13,14},{14,13},{17,18},{18,... | collective-permute-start | bytes 983048 | tf_op jit(solution)/shard_map/ppermute | solution.py:319
  49.3 11.7 %copy-start.17 = (f32[2,256]{1,0:T(2,128)S(1)}, f32[2,256]{1,0:T(2,128)}, u32[]{:S(2)}) copy-start(f32[2,256]{1,0:T(2,128)} %param.19) | copy-start | bytes 6148
  49.3 12.3 %copy-start.1 = (f32[16,160,128]{2,1,0:T(8,128)S(1)}, f32[16,160,128]{2,1,0:T(8,128)}, u32[]{:S(2)}) copy-start(f32[16,160,128]{2,1,0:T(8,128)} %shard_map.114) | copy-start | bytes 3932164
  61.6 5.7 %copy-start.5 = (f32[16,160,128]{2,1,0:T(8,128)S(1)}, f32[16,160,128]{2,1,0:T(8,128)}, u32[]{:S(2)}) copy-start(f32[16,160,128]{2,1,0:T(8,128)} %get-tuple-element.22) | copy-start | bytes 3932164
  65.0 6.1 %collective-permute-start.8 = (f32[4,160,128]{2,1,0:T(8,128)}, f32[4,160,128]{2,1,0:T(8,128)S(1)}, u32[]{:S(2)}, u32[]{:S(2)}) collective-permute-start(f32[4,160,128]{2,1,0:T(8,128)} %get-tuple-element.29), channel_id=1, source_target_pairs={{0,1},{1,0},{2,3},{3,2},{4,5},{5,4},{6,7},{7,6},{8,9},{9,8},{10,11... | collective-permute-start | bytes 983048 | tf_op jit(solution)/shard_map/ppermute | solution.py:319
  65.0 8.3 %collective-permute-start.9 = (f32[4,160,128]{2,1,0:T(8,128)}, f32[4,160,128]{2,1,0:T(8,128)S(1)}, u32[]{:S(2)}, u32[]{:S(2)}) collective-permute-start(f32[4,160,128]{2,1,0:T(8,128)} %get-tuple-element.28), channel_id=1, source_target_pairs={{1,2},{2,1},{5,6},{6,5},{9,10},{10,9},{13,14},{14,13},{17,18},{18,... | collective-permute-start | bytes 983048 | tf_op jit(solution)/shard_map/ppermute | solution.py:319
  86.6 7.5 %copy-start.4 = (f32[16,160,128]{2,1,0:T(8,128)S(1)}, f32[16,160,128]{2,1,0:T(8,128)}, u32[]{:S(2)}) copy-start(f32[16,160,128]{2,1,0:T(8,128)} %get-tuple-element.24) | copy-start | bytes 3932164
  87.8 6.3 %collective-permute-start.10 = (f32[1280,128]{1,0:T(8,128)S(1)}, f32[1280,128]{1,0:T(8,128)S(1)}, u32[]{:S(2)}, u32[]{:S(2)}) collective-permute-start(f32[1280,128]{1,0:T(8,128)S(1)} %constant_dynamic-slice_fusion.1), channel_id=1, source_target_pairs={{0,4},{4,0},{8,12},{12,8},{1,5},{5,1},{9,13},{13,9},{2,6},{6,2},{1... | collective-permute-start | bytes 1966088 | tf_op jit(solution)/shard_map/ppermute | solution.py:304
  94.2 9.0 %collective-permute-start.11 = (f32[640,128]{1,0:T(8,128)S(1)}, f32[640,128]{1,0:T(8,128)S(1)}, u32[]{:S(2)}, u32[]{:S(2)}) collective-permute-start(f32[640,128]{1,0:T(8,128)S(1)} %constant_dynamic-slice_fusion), channel_id=1, source_target_pairs={{0,8},{4,12},{8,0},{12,4},{1,9},{5,13},{9,1},{13,5},{2,10},{6,14},... | collective-permute-start | bytes 983048 | tf_op jit(solution)/shard_map/ppermute | solution.py:304
  103.2 8.1 %collective-permute-start.12 = (f32[640,128]{1,0:T(8,128)S(1)}, f32[640,128]{1,0:T(8,128)S(1)}, u32[]{:S(2)}, u32[]{:S(2)}) collective-permute-start(f32[640,128]{1,0:T(8,128)S(1)} %add_multiply_fusion), channel_id=1, source_target_pairs={{0,8},{4,12},{8,0},{12,4},{1,9},{5,13},{9,1},{13,5},{2,10},{6,14},... | collective-permute-start | bytes 983048 | tf_op jit(solution)/shard_map/ppermute | solution.py:310
  111.3 3.9 %collective-permute-start.13 = (f32[1280,128]{1,0:T(8,128)S(1)}, f32[1280,128]{1,0:T(8,128)S(1)}, u32[]{:S(2)}, u32[]{:S(2)}) collective-permute-start(f32[1280,128]{1,0:T(8,128)S(1)} %maximum_select_fusion.1), channel_id=1, source_target_pairs={{0,4},{4,0},{8,12},{12,8},{1,5},{5,1},{9,13},{13,9},{2,6},{6,2},{1... | collective-permute-start | bytes 1966088 | tf_op jit(solution)/shard_map/ppermute | solution.py:310
  (9 other events, 14.3 us)

commit v12 on v10

--- a/solution.py
+++ b/solution.py
@@ -54,7 +54,7 @@
     return centre, lap, grads
 
 
-def step_kernel(*refs, block, rows, track, own_grad, want_force):
+def step_kernel(*refs, block, rows, track, own_grad, want_force, edges):
     refs = list(refs)
     take = lambda n: [refs.pop(0) for _ in range(n)]
     (parity_ref,) = take(1)
@@ -70,8 +70,10 @@
     (new_ref,) = take(1)
     if own_grad:
         g_out = take(3)
+    if track and edges:
+        edge_lo_ref, edge_hi_ref = take(2)
     if track:
-        edge_lo_ref, edge_hi_ref, sample_ref = take(3)
+        (sample_ref,) = take(1)
     (pad_ref,) = take(1)
     if own_grad:
         (b_pad_ref,) = take(1)
@@ -112,24 +114,23 @@
                 hit = (where_ref[3] == 1) & (where_ref[0] == plane - HALO)
                 mask = hit & (row == where_ref[1] - y0) & (lane == where_ref[2])
                 newer = jnp.where(mask, newer + amount_ref[0], newer)
-                keep_ref[plane - HALO, pl.ds(y0, rows), :] = newer
+                keep_ref[pl.ds(pl.multiple_of((plane - HALO) * height + y0, 8), rows), :] = newer
             new_ref[sl] = newer
 
     if track:
         @pl.when(i == pl.num_programs(0) - 1)
         def _():
-            bottom = keep_ref[0:HALO]
-            top = keep_ref[planes - HALO:planes]
-            edge_lo_ref[...] = jnp.where(odd, bottom, top)
-            edge_hi_ref[...] = jnp.where(odd, top, bottom)
+            if edges:
+                for q in range(HALO):
+                    bottom = keep_ref[q * height:(q + 1) * height, :]
+                    top = keep_ref[(planes - HALO + q) * height:(planes - HALO + q + 1) * height, :]
+                    edge_lo_ref[q] = jnp.where(odd, bottom, top)
+                    edge_hi_ref[q] = jnp.where(odd, top, bottom)
             one_lane = lax.broadcasted_iota(jnp.int32, (1, depth), 1)
 
             def sample(r, carry):
-                x = rec_ref[0, r]
-                y = rec_ref[1, r]
-                z = rec_ref[2, r]
-                line = keep_ref[x, pl.ds(y, 1), :]
-                sample_ref[pl.ds(r, 1), :] = jnp.where(one_lane == z, line, 0.0)
+                line = keep_ref[pl.ds(rec_ref[0, r], 1), :]
+                sample_ref[pl.ds(r, 1), :] = jnp.where(one_lane == rec_ref[1, r], line, 0.0)
                 return carry
 
             lax.fori_loop(0, sample_ref.shape[0], sample, 0, unroll=8)
@@ -167,7 +168,7 @@
     return full, blk
 
 
-def apply_step(parity, lo, mid, hi, b, g, c, old, track=None, rows=40, want_force=True):
+def apply_step(parity, lo, mid, hi, b, g, c, old, track=None, rows=40, want_force=True, edges=True):
     planes, height, depth = mid.shape
     block = pick_block(planes)
     full, blk = specs(mid.shape, block)
@@ -200,11 +201,15 @@
         count = track[2].shape[1]
         edge = jax.ShapeDtypeStruct((HALO, height, depth), jnp.float32)
         lines = jax.ShapeDtypeStruct((count, depth), jnp.float32)
-        out_specs += [full(edge.shape), full(edge.shape), pl.BlockSpec((count, depth), lambda i: (0, 0))]
-        out_shape += [edge, edge, lines]
-        scratch.append(pltpu.VMEM(mid.shape, jnp.float32))
+        if edges:
+            out_specs += [full(edge.shape), full(edge.shape)]
+            out_shape += [edge, edge]
+        out_specs.append(pl.BlockSpec((count, depth), lambda i: (0, 0)))
+        out_shape.append(lines)
+        scratch.append(pltpu.VMEM((planes * height, depth), jnp.float32))
     kernel = functools.partial(
-        step_kernel, block=block, rows=rows, track=track is not None, own_grad=own_grad, want_force=want_force
+        step_kernel, block=block, rows=rows, track=track is not None, own_grad=own_grad, want_force=want_force,
+        edges=edges,
     )
     return pl.pallas_call(
         kernel,
@@ -310,7 +315,7 @@
         return jnp.stack([cells // (height * depth), (cells // depth) % height, cells % depth])
 
     where = jnp.concatenate([spread(src_local)[:, 0], src_valid.astype(jnp.int32)])
-    receivers = spread(rec_local)
+    receivers = jnp.stack([rec_local // depth, rec_local % depth])
     older, now = (prev_field[0], cur_field[0])
     lo, hi = halos(now, "tile")
     forces = []
@@ -324,7 +329,9 @@
             grad_b = outs[2:5]
             edge_lo, edge_hi, lines = outs[5:]
         else:
-            force, newer, edge_lo, edge_hi, lines = apply_step(parity, lo, now, hi, buoyancy, grad_b, speed, older, track)
+            outs = apply_step(parity, lo, now, hi, buoyancy, grad_b, speed, older, track, edges=k + 1 < steps)
+            force, newer, lines = outs[0], outs[1], outs[-1]
+            edge_lo, edge_hi = (outs[2], outs[3]) if k + 1 < steps else (None, None)
         if k + 1 < steps:
             lo, hi = swap_halos((edge_lo, edge_hi), "tile")
         samples.append(jnp.sum(lines, axis=1))

time: 116 us -> 114 us (0.983)
  local copies, waits for them, and re-layouts: 6.81 us -> 4.6 us
    dynamic_slice x4, local copies, waits for them, and re-layouts: 2.88 us -> 1.43 us  [halos(): far = lax.dynamic_slice_in_dim(block, odd * (planes - HALO), HALO, 0)]
    unnamed x36 -> x32, local copies, waits for them, and re-layouts: 3.18 us -> 2.47 us
where the time goes in v12:
time: 114 us; the launch traced here: 113 us
  Pallas kernels  38.2 us (34%)
  waiting for transfers between devices  29.8 us (26%)
  starting transfers between devices  24.8 us (22%)
  other arithmetic  14 us (12%)
  local copies, waits for them, and re-layouts  4.6 us (4%)
  between operations  1.75 us (2%)
    pallas_call x4, Pallas kernels, apply_step(): pl.pallas_call(kernel, grid=(planes // block,), in_specs=in_specs, out_sp...  38.2 us
    ppermute x5, starting transfers between devices, swap_halos(): lax.ppermute(sends[1], axis, second)  14.3 us
    ppermute x2, waiting for transfers between devices, reduce_members(): rows = keep + lax.ppermute(give, axis, pairs)  9.44 us
    ppermute x2, waiting for transfers between devices, reduce_members(): other = lax.ppermute(rows, axis, pairs)  8.52 us
    scatter-add x2, other arithmetic, inject(): flat = field.reshape(-1).at[where].add(jnp.where(valid, values, 0.0))  6.82 us
    ppermute x5, waiting for transfers between devices, swap_halos(): lax.ppermute(sends[0], axis, first)  6.48 us
    ppermute x2, starting transfers between devices, reduce_members(): rows = keep + lax.ppermute(give, axis, pairs)  5.81 us
    ppermute x5, waiting for transfers between devices, swap_halos(): lax.ppermute(sends[1], axis, second)  5.36 us
  transfers between devices with their start and end apart: 14, of which 8 were waited for; matrix products, arithmetic and copies ran while one was open for 3% of the time, Pallas kernels for 18%

profile of v12, /device:TPU:9, one launch (start us, length us, event | category | flops | bytes accessed | tf_op | source)
XLA Modules:
  0.0 113.1 jit_solution(1036529960962348206)
XLA Ops:
  2.1 4.6 %collective-permute-start.3 = (f32[4,160,128]{2,1,0:T(8,128)S(1)}, f32[4,160,128]{2,1,0:T(8,128)S(1)}, u32[]{:S(2)}, u32[]{:S(2)}) collective-permute-start(f32[4,160,128]{2,1,0:T(8,128)S(1)} %get-tuple-element.26), channel_id=1, source_target_pairs={{1,2},{2,1},{5,6},{6,5},{9,10},{10,9},{13,14},{14,13},{17,18},{18,... | collective-permute-start | bytes 983048 | tf_op jit(solution)/shard_map/ppermute | solution.py:270
  6.8 1.9 %collective-permute-start.5 = (f32[4,160,128]{2,1,0:T(8,128)S(1)}, f32[4,160,128]{2,1,0:T(8,128)}, u32[]{:S(2)}, u32[]{:S(2)}) collective-permute-start(f32[4,160,128]{2,1,0:T(8,128)S(1)} %get-tuple-element.24), channel_id=1, source_target_pairs={{1,2},{2,1},{5,6},{6,5},{9,10},{10,9},{13,14},{14,13},{17,18},{18,... | collective-permute-start | bytes 983048 | tf_op jit(solution)/shard_map/ppermute | solution.py:270
  12.4 2.5 %collective-permute-start.1 = (f32[4,160,128]{2,1,0:T(8,128)S(1)}, f32[4,160,128]{2,1,0:T(8,128)S(1)}, u32[]{:S(2)}, u32[]{:S(2)}) collective-permute-start(f32[4,160,128]{2,1,0:T(8,128)S(1)} %get-tuple-element.28), channel_id=1, source_target_pairs={{1,2},{2,1},{5,6},{6,5},{9,10},{10,9},{13,14},{14,13},{17,18},{18,... | collective-permute-start | bytes 983048 | tf_op jit(solution)/shard_map/ppermute | solution.py:270
  14.9 2.8 %collective-permute-done.4.refs_4_ = f32[4,160,128]{2,1,0:T(8,128)} collective-permute-done((f32[4,160,128]{2,1,0:T(8,128)S(1)}, f32[4,160,128]{2,1,0:T(8,128)}, u32[]{:S(2)}, u32[]{:S(2)}) %collective-permute-start.4) | collective-permute-done | bytes 327712 | tf_op jit(solution)/shard_map/ppermute | solution.py:270
  17.7 3.2 %collective-permute-done.5.refs_6_ = f32[4,160,128]{2,1,0:T(8,128)} collective-permute-done((f32[4,160,128]{2,1,0:T(8,128)S(1)}, f32[4,160,128]{2,1,0:T(8,128)}, u32[]{:S(2)}, u32[]{:S(2)}) %collective-permute-start.5) | collective-permute-done | bytes 327712 | tf_op jit(solution)/shard_map/ppermute | solution.py:270
  20.9 12.2 %shard_map.113 = (f32[16,160,128]{2,1,0:T(8,128)}, f32[16,160,128]{2,1,0:T(8,128)}, f32[16,160,128]{2,1,0:T(8,128)}, f32[16,160,128]{2,1,0:T(8,128)}, f32[16,160...) custom-call(s32[1]{0:T(128)} %bitcast.refs_0_, ...), custom_call_target="tpu_custom_call" | custom-call | tf_op jit(solution)/shard_map/pallas_call | solution.py:214
  33.2 3.0 %collective-permute-start.7 = (f32[4,160,128]{2,1,0:T(8,128)}, f32[4,160,128]{2,1,0:T(8,128)S(1)}, u32[]{:S(2)}, u32[]{:S(2)}) collective-permute-start(f32[4,160,128]{2,1,0:T(8,128)} %get-tuple-element.18), channel_id=1, source_target_pairs={{1,2},{2,1},{5,6},{6,5},{9,10},{10,9},{13,14},{14,13},{17,18},{18,... | collective-permute-start | bytes 983048 | tf_op jit(solution)/shard_map/ppermute | solution.py:270
  38.1 7.9 %shard_map.114 = f32[16,160,128]{2,1,0:T(8,128)} custom-call(s32[1]{0:T(128)} %bitcast.refs_0_, f32[4,160,128]{2,1,0:T(8,128)} %copy-done.5, f32[16,160,128]{2,1,0:T(8,128)} %bitcast.46, f32[4,160,128]{2,1,0:T(8,128)} %copy-done.8, f32[16,160,128]{2,1,0:T(8,128)} %refs_4_.5, f32[16,160,128]{2,1,0:T(8,128)} %get-tuple-element.12.refs_5_, ...), custom_call_target="tpu_custom_call" | custom-call | tf_op jit(solution)/shard_map/pallas_call | solution.py:214
  47.0 10.1 %shard_map.115 = (f32[16,160,128]{2,1,0:T(8,128)}, f32[16,160,128]{2,1,0:T(8,128)}, f32[256,128]{1,0:T(8,128)}) custom-call(s32[1]{0:T(128)} %bitcast.refs_0_, f32[4,160,128]{2,1,0:T(8,128)} %copy-done.9, f32[16,160,128]{2,1,0:T(8,128)} %get-tuple-element.17.refs_2_, f32[4,160,128]{2,1,0:T(8,128)} %copy-done.10, f32[16,160,128]{2,1,0:T(8,128)} %refs_4_.5, ...), custom_call_target="tpu_custom_call" | custom-call | tf_op jit(solution)/shard_map/pallas_call | solution.py:214
  58.2 2.4 %scatter_fusion = f32[327680]{0:T(1024)S(1)} fusion(f32[327680]{0:T(1024)S(1)} %bitcast.33, s32[256]{0:T(256)S(1)} %get-tuple-element.32, f32[256]{0:T(256)S(1)} %get-tuple-element.36), kind=kCustom, calls=%fused_computation | custom fusion | flops 256 | bytes 4096 | tf_op jit(solution)/shard_map/scatter-add | solution.py:282
  60.8 2.2 %collective-permute-start.9 = (f32[4,160,128]{2,1,0:T(8,128)S(1)}, f32[4,160,128]{2,1,0:T(8,128)S(1)}, u32[]{:S(2)}, u32[]{:S(2)}) collective-permute-start(f32[4,160,128]{2,1,0:T(8,128)S(1)} %get-tuple-element.22), channel_id=1, source_target_pairs={{1,2},{2,1},{5,6},{6,5},{9,10},{10,9},{13,14},{14,13},{17,18},{18,... | collective-permute-start | bytes 983048 | tf_op jit(solution)/shard_map/ppermute | solution.py:270
  63.0 3.6 %collective-permute-done.8.refs_1_ = f32[4,160,128]{2,1,0:T(8,128)S(1)} collective-permute-done((f32[4,160,128]{2,1,0:T(8,128)S(1)}, f32[4,160,128]{2,1,0:T(8,128)S(1)}, u32[]{:S(2)}, u32[]{:S(2)}) %collective-permute-start.8) | collective-permute-done | bytes 327712 | tf_op jit(solution)/shard_map/ppermute | solution.py:270
  66.7 2.2 %collective-permute-done.9.refs_3_ = f32[4,160,128]{2,1,0:T(8,128)S(1)} collective-permute-done((f32[4,160,128]{2,1,0:T(8,128)S(1)}, f32[4,160,128]{2,1,0:T(8,128)S(1)}, u32[]{:S(2)}, u32[]{:S(2)}) %collective-permute-start.9) | collective-permute-done | bytes 327712 | tf_op jit(solution)/shard_map/ppermute | solution.py:270
  69.6 8.0 %shard_map.116 = f32[16,160,128]{2,1,0:T(8,128)} custom-call(s32[1]{0:T(128)} %bitcast.refs_0_, f32[4,160,128]{2,1,0:T(8,128)} %copy-done.6, f32[16,160,128]{2,1,0:T(8,128)} %bitcast.35, f32[4,160,128]{2,1,0:T(8,128)} %copy-done.7, f32[16,160,128]{2,1,0:T(8,128)} %refs_4_.5, f32[16,160,128]{2,1,0:T(8,128)} %get-tuple-element.12.refs_5_, ...), custom_call_target="tpu_custom_call" | custom-call | tf_op jit(solution)/shard_map/pallas_call | solution.py:214
  77.6 4.4 %scatter_fusion.1 = f32[327680]{0:T(1024)} fusion(f32[327680]{0:T(1024)} %bitcast.41, s32[256]{0:T(256)S(1)} %get-tuple-element.32, f32[256]{0:T(256)S(1)} %get-tuple-element.35), kind=kCustom, calls=%fused_computation.1 | custom fusion | flops 256 | bytes 4096 | tf_op jit(solution)/shard_map/scatter-add | solution.py:282
  82.0 2.5 %multiply_add_fusion = f32[16,160,128]{2,1,0:T(8,128)S(1)} fusion(f32[16,160,128]{2,1,0:T(8,128)} %bitcast.42, f32[16,160,128]{2,1,0:T(8,128)} %get-tuple-element.21, f32[16,160,128]{2,1,0:T(8,128)S(1)} %bitcast.36, f32[16,160,128]{2,1,0:T(8,128)} %get-tuple-element.20), kind=kLoop, calls=%fused_computation.3 | loop fusion | flops 983040 | bytes 6553600 | tf_op jit(solution)/shard_map/add | solution.py:347
  84.5 4.5 %collective-permute-start.10 = (f32[1280,128]{1,0:T(8,128)S(1)}, f32[1280,128]{1,0:T(8,128)S(1)}, u32[]{:S(2)}, u32[]{:S(2)}) collective-permute-start(f32[1280,128]{1,0:T(8,128)S(1)} %constant_dynamic-slice_fusion.1), channel_id=1, source_target_pairs={{0,4},{4,0},{8,12},{12,8},{1,5},{5,1},{9,13},{13,9},{2,6},{6,2},{1... | collective-permute-start | bytes 1966088 | tf_op jit(solution)/shard_map/ppermute | solution.py:255
  89.0 1.7 %collective-permute-done.10 = f32[1280,128]{1,0:T(8,128)S(1)} collective-permute-done((f32[1280,128]{1,0:T(8,128)S(1)}, f32[1280,128]{1,0:T(8,128)S(1)}, u32[]{:S(2)}, u32[]{:S(2)}) %collective-permute-start.10) | collective-permute-done | bytes 655392 | tf_op jit(solution)/shard_map/ppermute | solution.py:255
  90.8 1.3 %collective-permute-start.11 = (f32[640,128]{1,0:T(8,128)S(1)}, f32[640,128]{1,0:T(8,128)S(1)}, u32[]{:S(2)}, u32[]{:S(2)}) collective-permute-start(f32[640,128]{1,0:T(8,128)S(1)} %constant_dynamic-slice_fusion), channel_id=1, source_target_pairs={{0,8},{4,12},{8,0},{12,4},{1,9},{5,13},{9,1},{13,5},{2,10},{6,14},... | collective-permute-start | bytes 983048 | tf_op jit(solution)/shard_map/ppermute | solution.py:255
  92.1 7.7 %collective-permute-done.11 = f32[640,128]{1,0:T(8,128)S(1)} collective-permute-done((f32[640,128]{1,0:T(8,128)S(1)}, f32[640,128]{1,0:T(8,128)S(1)}, u32[]{:S(2)}, u32[]{:S(2)}) %collective-permute-start.11) | collective-permute-done | bytes 327712 | tf_op jit(solution)/shard_map/ppermute | solution.py:255
  99.9 1.3 %collective-permute-start.12 = (f32[640,128]{1,0:T(8,128)S(1)}, f32[640,128]{1,0:T(8,128)S(1)}, u32[]{:S(2)}, u32[]{:S(2)}) collective-permute-start(f32[640,128]{1,0:T(8,128)S(1)} %add_multiply_fusion), channel_id=1, source_target_pairs={{0,8},{4,12},{8,0},{12,4},{1,9},{5,13},{9,1},{13,5},{2,10},{6,14},... | collective-permute-start | bytes 983048 | tf_op jit(solution)/shard_map/ppermute | solution.py:261
  101.2 6.8 %collective-permute-done.12 = f32[640,128]{1,0:T(8,128)S(1)} collective-permute-done((f32[640,128]{1,0:T(8,128)S(1)}, f32[640,128]{1,0:T(8,128)S(1)}, u32[]{:S(2)}, u32[]{:S(2)}) %collective-permute-start.12) | collective-permute-done | bytes 327712 | tf_op jit(solution)/shard_map/ppermute | solution.py:261
  108.0 2.2 %collective-permute-start.13 = (f32[1280,128]{1,0:T(8,128)S(1)}, f32[1280,128]{1,0:T(8,128)S(1)}, u32[]{:S(2)}, u32[]{:S(2)}) collective-permute-start(f32[1280,128]{1,0:T(8,128)S(1)} %maximum_select_fusion.1), channel_id=1, source_target_pairs={{0,4},{4,0},{8,12},{12,8},{1,5},{5,1},{9,13},{13,9},{2,6},{6,2},{1... | collective-permute-start | bytes 1966088 | tf_op jit(solution)/shard_map/ppermute | solution.py:261
  110.2 1.7 %collective-permute-done.13 = f32[1280,128]{1,0:T(8,128)S(1)} collective-permute-done((f32[1280,128]{1,0:T(8,128)S(1)}, f32[1280,128]{1,0:T(8,128)S(1)}, u32[]{:S(2)}, u32[]{:S(2)}) %collective-permute-start.13) | collective-permute-done | bytes 655392 | tf_op jit(solution)/shard_map/ppermute | solution.py:261
  (64 shorter events, 10.6 us)
Async XLA Ops:
  0.6 6.0 %copy-start = (f32[16,160,128]{2,1,0:T(8,128)S(1)}, f32[16,160,128]{2,1,0:T(8,128)}, u32[]{:S(2)}) copy-start(f32[16,160,128]{2,1,0:T(8,128)} %refs_4_.5) | copy-start | bytes 3932164
  0.7 8.1 %copy-start.4 = (f32[1,16,160,128]{3,2,1,0:T(8,128)S(1)}, f32[1,16,160,128]{3,2,1,0:T(8,128)}, u32[]{:S(2)}) copy-start(f32[1,16,160,128]{3,2,1,0:T(8,128)} %param.14) | copy-start | bytes 3932164
  2.0 10.4 %collective-permute-start.2 = (f32[4,160,128]{2,1,0:T(8,128)S(1)}, f32[4,160,128]{2,1,0:T(8,128)S(1)}, u32[]{:S(2)}, u32[]{:S(2)}) collective-permute-start(f32[4,160,128]{2,1,0:T(8,128)S(1)} %get-tuple-element.27), channel_id=1, source_target_pairs={{0,1},{1,0},{2,3},{3,2},{4,5},{5,4},{6,7},{7,6},{8,9},{9,8},{10,11... | collective-permute-start | bytes 983048 | tf_op jit(solution)/shard_map/ppermute | solution.py:270
  2.0 8.4 %copy-start.13 = (s32[256]{0:T(256)S(1)}, s32[256]{0:T(256)}, u32[]{:S(2)}) copy-start(s32[256]{0:T(256)} %param.18) | copy-start | bytes 3076
  2.0 9.7 %copy-start.15 = (f32[2]{0:T(128)S(1)}, f32[2]{0:T(128)}, u32[]{:S(2)}) copy-start(f32[2]{0:T(128)} %param.16) | copy-start | bytes 28
  2.1 12.8 %collective-permute-start.3 = (f32[4,160,128]{2,1,0:T(8,128)S(1)}, f32[4,160,128]{2,1,0:T(8,128)S(1)}, u32[]{:S(2)}, u32[]{:S(2)}) collective-permute-start(f32[4,160,128]{2,1,0:T(8,128)S(1)} %get-tuple-element.26), channel_id=1, source_target_pairs={{1,2},{2,1},{5,6},{6,5},{9,10},{10,9},{13,14},{14,13},{17,18},{18,... | collective-permute-start | bytes 983048 | tf_op jit(solution)/shard_map/ppermute | solution.py:270
  6.7 11.0 %collective-permute-start.4 = (f32[4,160,128]{2,1,0:T(8,128)S(1)}, f32[4,160,128]{2,1,0:T(8,128)}, u32[]{:S(2)}, u32[]{:S(2)}) collective-permute-start(f32[4,160,128]{2,1,0:T(8,128)S(1)} %get-tuple-element.25), channel_id=1, source_target_pairs={{0,1},{1,0},{2,3},{3,2},{4,5},{5,4},{6,7},{7,6},{8,9},{9,8},{10,11... | collective-permute-start | bytes 983048 | tf_op jit(solution)/shard_map/ppermute | solution.py:270
  6.8 14.1 %collective-permute-start.5 = (f32[4,160,128]{2,1,0:T(8,128)S(1)}, f32[4,160,128]{2,1,0:T(8,128)}, u32[]{:S(2)}, u32[]{:S(2)}) collective-permute-start(f32[4,160,128]{2,1,0:T(8,128)S(1)} %get-tuple-element.24), channel_id=1, source_target_pairs={{1,2},{2,1},{5,6},{6,5},{9,10},{10,9},{13,14},{14,13},{17,18},{18,... | collective-permute-start | bytes 983048 | tf_op jit(solution)/shard_map/ppermute | solution.py:270
  8.8 28.5 %collective-permute-start = (f32[4,160,128]{2,1,0:T(8,128)S(1)}, f32[4,160,128]{2,1,0:T(8,128)S(1)}, u32[]{:S(2)}, u32[]{:S(2)}) collective-permute-start(f32[4,160,128]{2,1,0:T(8,128)S(1)} %get-tuple-element.29), channel_id=1, source_target_pairs={{0,1},{1,0},{2,3},{3,2},{4,5},{5,4},{6,7},{7,6},{8,9},{9,8},{10,11... | collective-permute-start | bytes 983048 | tf_op jit(solution)/shard_map/ppermute | solution.py:270
  12.4 8.5 %copy-start.11 = (f32[4,160,128]{2,1,0:T(8,128)}, f32[4,160,128]{2,1,0:T(8,128)S(1)}, u32[]{:S(2)}) copy-start(f32[4,160,128]{2,1,0:T(8,128)S(1)} %collective-permute-done.2.refs_1_) | copy-start | bytes 983044
  12.4 24.9 %collective-permute-start.1 = (f32[4,160,128]{2,1,0:T(8,128)S(1)}, f32[4,160,128]{2,1,0:T(8,128)S(1)}, u32[]{:S(2)}, u32[]{:S(2)}) collective-permute-start(f32[4,160,128]{2,1,0:T(8,128)S(1)} %get-tuple-element.28), channel_id=1, source_target_pairs={{1,2},{2,1},{5,6},{6,5},{9,10},{10,9},{13,14},{14,13},{17,18},{18,... | collective-permute-start | bytes 983048 | tf_op jit(solution)/shard_map/ppermute | solution.py:270
  14.9 6.0 %copy-start.12 = (f32[4,160,128]{2,1,0:T(8,128)}, f32[4,160,128]{2,1,0:T(8,128)S(1)}, u32[]{:S(2)}) copy-start(f32[4,160,128]{2,1,0:T(8,128)S(1)} %collective-permute-done.3.refs_3_) | copy-start | bytes 983044
  33.1 13.0 %collective-permute-start.6 = (f32[4,160,128]{2,1,0:T(8,128)}, f32[4,160,128]{2,1,0:T(8,128)S(1)}, u32[]{:S(2)}, u32[]{:S(2)}) collective-permute-start(f32[4,160,128]{2,1,0:T(8,128)} %get-tuple-element.16), channel_id=1, source_target_pairs={{0,1},{1,0},{2,3},{3,2},{4,5},{5,4},{6,7},{7,6},{8,9},{9,8},{10,11... | collective-permute-start | bytes 983048 | tf_op jit(solution)/shard_map/ppermute | solution.py:270
  33.2 12.9 %collective-permute-start.7 = (f32[4,160,128]{2,1,0:T(8,128)}, f32[4,160,128]{2,1,0:T(8,128)S(1)}, u32[]{:S(2)}, u32[]{:S(2)}) collective-permute-start(f32[4,160,128]{2,1,0:T(8,128)} %get-tuple-element.18), channel_id=1, source_target_pairs={{1,2},{2,1},{5,6},{6,5},{9,10},{10,9},{13,14},{14,13},{17,18},{18,... | collective-permute-start | bytes 983048 | tf_op jit(solution)/shard_map/ppermute | solution.py:270
  47.0 11.1 %copy-start.14 = (f32[2,256]{1,0:T(2,128)S(1)}, f32[2,256]{1,0:T(2,128)}, u32[]{:S(2)}) copy-start(f32[2,256]{1,0:T(2,128)} %param.19) | copy-start | bytes 6148
  47.0 11.2 %copy-start.1 = (f32[16,160,128]{2,1,0:T(8,128)S(1)}, f32[16,160,128]{2,1,0:T(8,128)}, u32[]{:S(2)}) copy-start(f32[16,160,128]{2,1,0:T(8,128)} %shard_map.114) | copy-start | bytes 3932164
  60.6 8.3 %copy-start.2 = (f32[327680]{0:T(1024)}, f32[327680]{0:T(1024)S(1)}, u32[]{:S(2)}) copy-start(f32[327680]{0:T(1024)S(1)} %scatter_fusion) | copy-start | bytes 3932164
  60.7 6.0 %collective-permute-start.8 = (f32[4,160,128]{2,1,0:T(8,128)S(1)}, f32[4,160,128]{2,1,0:T(8,128)S(1)}, u32[]{:S(2)}, u32[]{:S(2)}) collective-permute-start(f32[4,160,128]{2,1,0:T(8,128)S(1)} %get-tuple-element.23), channel_id=1, source_target_pairs={{0,1},{1,0},{2,3},{3,2},{4,5},{5,4},{6,7},{7,6},{8,9},{9,8},{10,11... | collective-permute-start | bytes 983048 | tf_op jit(solution)/shard_map/ppermute | solution.py:270
  60.8 8.1 %collective-permute-start.9 = (f32[4,160,128]{2,1,0:T(8,128)S(1)}, f32[4,160,128]{2,1,0:T(8,128)S(1)}, u32[]{:S(2)}, u32[]{:S(2)}) collective-permute-start(f32[4,160,128]{2,1,0:T(8,128)S(1)} %get-tuple-element.22), channel_id=1, source_target_pairs={{1,2},{2,1},{5,6},{6,5},{9,10},{10,9},{13,14},{14,13},{17,18},{18,... | collective-permute-start | bytes 983048 | tf_op jit(solution)/shard_map/ppermute | solution.py:270
  77.6 4.4 %copy-start.3 = (f32[327680]{0:T(1024)S(1)}, f32[327680]{0:T(1024)}, u32[]{:S(2)}) copy-start(f32[327680]{0:T(1024)} %copy-done.2) | copy-start | bytes 3932164
  84.5 6.3 %collective-permute-start.10 = (f32[1280,128]{1,0:T(8,128)S(1)}, f32[1280,128]{1,0:T(8,128)S(1)}, u32[]{:S(2)}, u32[]{:S(2)}) collective-permute-start(f32[1280,128]{1,0:T(8,128)S(1)} %constant_dynamic-slice_fusion.1), channel_id=1, source_target_pairs={{0,4},{4,0},{8,12},{12,8},{1,5},{5,1},{9,13},{13,9},{2,6},{6,2},{1... | collective-permute-start | bytes 1966088 | tf_op jit(solution)/shard_map/ppermute | solution.py:255
  90.8 9.0 %collective-permute-start.11 = (f32[640,128]{1,0:T(8,128)S(1)}, f32[640,128]{1,0:T(8,128)S(1)}, u32[]{:S(2)}, u32[]{:S(2)}) collective-permute-start(f32[640,128]{1,0:T(8,128)S(1)} %constant_dynamic-slice_fusion), channel_id=1, source_target_pairs={{0,8},{4,12},{8,0},{12,4},{1,9},{5,13},{9,1},{13,5},{2,10},{6,14},... | collective-permute-start | bytes 983048 | tf_op jit(solution)/shard_map/ppermute | solution.py:255
  99.9 8.1 %collective-permute-start.12 = (f32[640,128]{1,0:T(8,128)S(1)}, f32[640,128]{1,0:T(8,128)S(1)}, u32[]{:S(2)}, u32[]{:S(2)}) collective-permute-start(f32[640,128]{1,0:T(8,128)S(1)} %add_multiply_fusion), channel_id=1, source_target_pairs={{0,8},{4,12},{8,0},{12,4},{1,9},{5,13},{9,1},{13,5},{2,10},{6,14},... | collective-permute-start | bytes 983048 | tf_op jit(solution)/shard_map/ppermute | solution.py:261
  108.0 3.9 %collective-permute-start.13 = (f32[1280,128]{1,0:T(8,128)S(1)}, f32[1280,128]{1,0:T(8,128)S(1)}, u32[]{:S(2)}, u32[]{:S(2)}) collective-permute-start(f32[1280,128]{1,0:T(8,128)S(1)} %maximum_select_fusion.1), channel_id=1, source_target_pairs={{0,4},{4,0},{8,12},{12,8},{1,5},{5,1},{9,13},{13,9},{2,6},{6,2},{1... | collective-permute-start | bytes 1966088 | tf_op jit(solution)/shard_map/ppermute | solution.py:261
  (6 other events, 6.1 us)

commit v13 on v12

--- a/solution.py
+++ b/solution.py
@@ -238,9 +238,15 @@
     )(lo, mid, hi)
 
 
+def split_permute(block, axis, pairs, pieces):
+    size = block.shape[0] // pieces
+    parts = [lax.ppermute(block[p * size:(p + 1) * size], axis, pairs) for p in range(pieces)]
+    return parts[0] if pieces == 1 else jnp.concatenate(parts)
+
+
 def reduce_members(part, axis):
     members = lax.axis_size(axis)
-    if members & (members - 1) or part.size % (members * 1024):
+    if members & (members - 1) or part.size % (members * 2048):
         return lax.psum(part, axis) / members
     me = lax.axis_index(axis)
     rows = part.reshape(-1, 128)
@@ -252,13 +258,13 @@
         keep = lax.dynamic_slice_in_dim(rows, upper * half, half, 0)
         give = lax.dynamic_slice_in_dim(rows, (1 - upper) * half, half, 0)
         pairs = [(i, i ^ mask) for i in range(members)]
-        rows = keep + lax.ppermute(give, axis, pairs)
+        rows = keep + split_permute(give, axis, pairs, 2 if b else 1)
     rows = rows / members
     for b in reversed(range(bits)):
         mask = 1 << b
         upper = (me // mask) % 2
         pairs = [(i, i ^ mask) for i in range(members)]
-        other = lax.ppermute(rows, axis, pairs)
+        other = split_permute(rows, axis, pairs, 2 if b else 1)
         rows = jnp.where(upper == 1, jnp.concatenate([other, rows]), jnp.concatenate([rows, other]))
     return rows.reshape(part.shape)
 

time: 114 us -> 114 us (level)
    ppermute x4 -> x6, waiting for transfers between devices: 18 us -> 17.4 us  [split_permute(): lax.ppermute(block[p * size:(p + 1) * size], axis, pairs)]
    ppermute x4 -> x6, starting transfers between devices: 9.27 us -> 9.78 us  [split_permute(): lax.ppermute(block[p * size:(p + 1) * size], axis, pairs)]
  transfers between devices with their start and end apart: 14 -> 16, of which waited for: 8 -> 10; matrix products, arithmetic and copies ran while one was open for 3% -> 3% of each run, Pallas kernels for 18% -> 18%
where the time goes in v13:
time: 114 us; the launch traced here: 113 us
  Pallas kernels  38.3 us (34%)
  waiting for transfers between devices  29.4 us (26%)
  starting transfers between devices  25.3 us (22%)
  other arithmetic  13.9 us (12%)
  local copies, waits for them, and re-layouts  4.6 us (4%)
  between operations  1.76 us (2%)
    pallas_call x4, Pallas kernels, apply_step(): pl.pallas_call(kernel, grid=(planes // block,), in_specs=in_specs, out_sp...  38.3 us
    ppermute x6, waiting for transfers between devices, split_permute(): lax.ppermute(block[p * size:(p + 1) * size], axis, pairs)  17.4 us
    ppermute x5, starting transfers between devices, swap_halos(): lax.ppermute(sends[1], axis, second)  14.3 us
    ppermute x6, starting transfers between devices, split_permute(): lax.ppermute(block[p * size:(p + 1) * size], axis, pairs)  9.78 us
    scatter-add x2, other arithmetic, inject(): flat = field.reshape(-1).at[where].add(jnp.where(valid, values, 0.0))  6.83 us
    ppermute x5, waiting for transfers between devices, swap_halos(): lax.ppermute(sends[0], axis, first)  6.56 us
    ppermute x5, waiting for transfers between devices, swap_halos(): lax.ppermute(sends[1], axis, second)  5.36 us
    unnamed x32, local copies, waits for them, and re-layouts  2.46 us
  transfers between devices with their start and end apart: 16, of which 10 were waited for; matrix products, arithmetic and copies ran while one was open for 3% of the time, Pallas kernels for 18%

profile of v13, /device:TPU:9, one launch (start us, length us, event | category | flops | bytes accessed | tf_op | source)
XLA Modules:
  0.0 113.2 jit_solution(77233572463830574)
XLA Ops:
  2.1 4.6 %collective-permute-start.3 = (f32[4,160,128]{2,1,0:T(8,128)S(1)}, f32[4,160,128]{2,1,0:T(8,128)S(1)}, u32[]{:S(2)}, u32[]{:S(2)}) collective-permute-start(f32[4,160,128]{2,1,0:T(8,128)S(1)} %get-tuple-element.26), channel_id=1, source_target_pairs={{1,2},{2,1},{5,6},{6,5},{9,10},{10,9},{13,14},{14,13},{17,18},{18,... | collective-permute-start | bytes 983048 | tf_op jit(solution)/shard_map/ppermute | solution.py:276
  6.8 1.9 %collective-permute-start.5 = (f32[4,160,128]{2,1,0:T(8,128)S(1)}, f32[4,160,128]{2,1,0:T(8,128)}, u32[]{:S(2)}, u32[]{:S(2)}) collective-permute-start(f32[4,160,128]{2,1,0:T(8,128)S(1)} %get-tuple-element.24), channel_id=1, source_target_pairs={{1,2},{2,1},{5,6},{6,5},{9,10},{10,9},{13,14},{14,13},{17,18},{18,... | collective-permute-start | bytes 983048 | tf_op jit(solution)/shard_map/ppermute | solution.py:276
  12.3 2.5 %collective-permute-start.1 = (f32[4,160,128]{2,1,0:T(8,128)S(1)}, f32[4,160,128]{2,1,0:T(8,128)S(1)}, u32[]{:S(2)}, u32[]{:S(2)}) collective-permute-start(f32[4,160,128]{2,1,0:T(8,128)S(1)} %get-tuple-element.28), channel_id=1, source_target_pairs={{1,2},{2,1},{5,6},{6,5},{9,10},{10,9},{13,14},{14,13},{17,18},{18,... | collective-permute-start | bytes 983048 | tf_op jit(solution)/shard_map/ppermute | solution.py:276
  14.8 2.9 %collective-permute-done.4.refs_4_ = f32[4,160,128]{2,1,0:T(8,128)} collective-permute-done((f32[4,160,128]{2,1,0:T(8,128)S(1)}, f32[4,160,128]{2,1,0:T(8,128)}, u32[]{:S(2)}, u32[]{:S(2)}) %collective-permute-start.4) | collective-permute-done | bytes 327712 | tf_op jit(solution)/shard_map/ppermute | solution.py:276
  17.7 3.2 %collective-permute-done.5.refs_6_ = f32[4,160,128]{2,1,0:T(8,128)} collective-permute-done((f32[4,160,128]{2,1,0:T(8,128)S(1)}, f32[4,160,128]{2,1,0:T(8,128)}, u32[]{:S(2)}, u32[]{:S(2)}) %collective-permute-start.5) | collective-permute-done | bytes 327712 | tf_op jit(solution)/shard_map/ppermute | solution.py:276
  20.9 12.2 %shard_map.113 = (f32[16,160,128]{2,1,0:T(8,128)}, f32[16,160,128]{2,1,0:T(8,128)}, f32[16,160,128]{2,1,0:T(8,128)}, f32[16,160,128]{2,1,0:T(8,128)}, f32[16,160...) custom-call(s32[1]{0:T(128)} %bitcast.refs_0_, ...), custom_call_target="tpu_custom_call" | custom-call | tf_op jit(solution)/shard_map/pallas_call | solution.py:214
  33.2 3.0 %collective-permute-start.7 = (f32[4,160,128]{2,1,0:T(8,128)}, f32[4,160,128]{2,1,0:T(8,128)S(1)}, u32[]{:S(2)}, u32[]{:S(2)}) collective-permute-start(f32[4,160,128]{2,1,0:T(8,128)} %get-tuple-element.18), channel_id=1, source_target_pairs={{1,2},{2,1},{5,6},{6,5},{9,10},{10,9},{13,14},{14,13},{17,18},{18,... | collective-permute-start | bytes 983048 | tf_op jit(solution)/shard_map/ppermute | solution.py:276
  38.1 8.0 %shard_map.114 = f32[16,160,128]{2,1,0:T(8,128)} custom-call(s32[1]{0:T(128)} %bitcast.refs_0_, f32[4,160,128]{2,1,0:T(8,128)} %copy-done.5, f32[16,160,128]{2,1,0:T(8,128)} %bitcast.46, f32[4,160,128]{2,1,0:T(8,128)} %copy-done.8, f32[16,160,128]{2,1,0:T(8,128)} %refs_4_.5, f32[16,160,128]{2,1,0:T(8,128)} %get-tuple-element.12.refs_5_, ...), custom_call_target="tpu_custom_call" | custom-call | tf_op jit(solution)/shard_map/pallas_call | solution.py:214
  47.0 10.1 %shard_map.115 = (f32[16,160,128]{2,1,0:T(8,128)}, f32[16,160,128]{2,1,0:T(8,128)}, f32[256,128]{1,0:T(8,128)}) custom-call(s32[1]{0:T(128)} %bitcast.refs_0_, f32[4,160,128]{2,1,0:T(8,128)} %copy-done.9, f32[16,160,128]{2,1,0:T(8,128)} %get-tuple-element.17.refs_2_, f32[4,160,128]{2,1,0:T(8,128)} %copy-done.10, f32[16,160,128]{2,1,0:T(8,128)} %refs_4_.5, ...), custom_call_target="tpu_custom_call" | custom-call | tf_op jit(solution)/shard_map/pallas_call | solution.py:214
  58.2 2.4 %scatter_fusion = f32[327680]{0:T(1024)S(1)} fusion(f32[327680]{0:T(1024)S(1)} %bitcast.33, s32[256]{0:T(256)S(1)} %get-tuple-element.36, f32[256]{0:T(256)S(1)} %get-tuple-element.40), kind=kCustom, calls=%fused_computation | custom fusion | flops 256 | bytes 4096 | tf_op jit(solution)/shard_map/scatter-add | solution.py:288
  60.8 2.2 %collective-permute-start.9 = (f32[4,160,128]{2,1,0:T(8,128)S(1)}, f32[4,160,128]{2,1,0:T(8,128)S(1)}, u32[]{:S(2)}, u32[]{:S(2)}) collective-permute-start(f32[4,160,128]{2,1,0:T(8,128)S(1)} %get-tuple-element.22), channel_id=1, source_target_pairs={{1,2},{2,1},{5,6},{6,5},{9,10},{10,9},{13,14},{14,13},{17,18},{18,... | collective-permute-start | bytes 983048 | tf_op jit(solution)/shard_map/ppermute | solution.py:276
  63.1 3.6 %collective-permute-done.8.refs_1_ = f32[4,160,128]{2,1,0:T(8,128)S(1)} collective-permute-done((f32[4,160,128]{2,1,0:T(8,128)S(1)}, f32[4,160,128]{2,1,0:T(8,128)S(1)}, u32[]{:S(2)}, u32[]{:S(2)}) %collective-permute-start.8) | collective-permute-done | bytes 327712 | tf_op jit(solution)/shard_map/ppermute | solution.py:276
  66.7 2.2 %collective-permute-done.9.refs_3_ = f32[4,160,128]{2,1,0:T(8,128)S(1)} collective-permute-done((f32[4,160,128]{2,1,0:T(8,128)S(1)}, f32[4,160,128]{2,1,0:T(8,128)S(1)}, u32[]{:S(2)}, u32[]{:S(2)}) %collective-permute-start.9) | collective-permute-done | bytes 327712 | tf_op jit(solution)/shard_map/ppermute | solution.py:276
  69.7 8.0 %shard_map.116 = f32[16,160,128]{2,1,0:T(8,128)} custom-call(s32[1]{0:T(128)} %bitcast.refs_0_, f32[4,160,128]{2,1,0:T(8,128)} %copy-done.6, f32[16,160,128]{2,1,0:T(8,128)} %bitcast.35, f32[4,160,128]{2,1,0:T(8,128)} %copy-done.7, f32[16,160,128]{2,1,0:T(8,128)} %refs_4_.5, f32[16,160,128]{2,1,0:T(8,128)} %get-tuple-element.12.refs_5_, ...), custom_call_target="tpu_custom_call" | custom-call | tf_op jit(solution)/shard_map/pallas_call | solution.py:214
  77.6 4.4 %scatter_fusion.1 = f32[327680]{0:T(1024)} fusion(f32[327680]{0:T(1024)} %bitcast.41, s32[256]{0:T(256)S(1)} %get-tuple-element.36, f32[256]{0:T(256)S(1)} %get-tuple-element.39), kind=kCustom, calls=%fused_computation.1 | custom fusion | flops 256 | bytes 4096 | tf_op jit(solution)/shard_map/scatter-add | solution.py:288
  82.0 2.5 %multiply_add_fusion = f32[16,160,128]{2,1,0:T(8,128)S(1)} fusion(f32[16,160,128]{2,1,0:T(8,128)} %bitcast.42, f32[16,160,128]{2,1,0:T(8,128)} %get-tuple-element.21, f32[16,160,128]{2,1,0:T(8,128)S(1)} %bitcast.36, f32[16,160,128]{2,1,0:T(8,128)} %get-tuple-element.20), kind=kLoop, calls=%fused_computation.3 | loop fusion | flops 983040 | bytes 6553600 | tf_op jit(solution)/shard_map/add | solution.py:353
  84.5 4.5 %collective-permute-start.10 = (f32[1280,128]{1,0:T(8,128)S(1)}, f32[1280,128]{1,0:T(8,128)S(1)}, u32[]{:S(2)}, u32[]{:S(2)}) collective-permute-start(f32[1280,128]{1,0:T(8,128)S(1)} %constant_dynamic-slice_fusion.2), channel_id=1, source_target_pairs={{0,4},{4,0},{8,12},{12,8},{1,5},{5,1},{9,13},{13,9},{2,6},{6,2},{1... | collective-permute-start | bytes 1966088 | tf_op jit(solution)/shard_map/ppermute | solution.py:243
  89.1 1.7 %collective-permute-done.10 = f32[1280,128]{1,0:T(8,128)S(1)} collective-permute-done((f32[1280,128]{1,0:T(8,128)S(1)}, f32[1280,128]{1,0:T(8,128)S(1)}, u32[]{:S(2)}, u32[]{:S(2)}) %collective-permute-start.10) | collective-permute-done | bytes 655392 | tf_op jit(solution)/shard_map/ppermute | solution.py:243
  92.4 3.9 %collective-permute-done.11 = f32[320,128]{1,0:T(8,128)S(1)} collective-permute-done((f32[320,128]{1,0:T(8,128)S(1)}, f32[320,128]{1,0:T(8,128)S(1)}, u32[]{:S(2)}, u32[]{:S(2)}) %collective-permute-start.11) | collective-permute-done | bytes 163872 | tf_op jit(solution)/shard_map/ppermute | solution.py:243
  96.4 3.5 %collective-permute-done.12 = f32[320,128]{1,0:T(8,128)S(1)} collective-permute-done((f32[320,128]{1,0:T(8,128)S(1)}, f32[320,128]{1,0:T(8,128)S(1)}, u32[]{:S(2)}, u32[]{:S(2)}) %collective-permute-start.12) | collective-permute-done | bytes 163872 | tf_op jit(solution)/shard_map/ppermute | solution.py:243
  101.5 3.0 %collective-permute-done.13 = f32[320,128]{1,0:T(8,128)S(1)} collective-permute-done((f32[320,128]{1,0:T(8,128)S(1)}, f32[320,128]{1,0:T(8,128)S(1)}, u32[]{:S(2)}, u32[]{:S(2)}) %collective-permute-start.13) | collective-permute-done | bytes 163872 | tf_op jit(solution)/shard_map/ppermute | solution.py:243
  104.5 3.5 %collective-permute-done.14 = f32[320,128]{1,0:T(8,128)S(1)} collective-permute-done((f32[320,128]{1,0:T(8,128)S(1)}, f32[320,128]{1,0:T(8,128)S(1)}, u32[]{:S(2)}, u32[]{:S(2)}) %collective-permute-start.14) | collective-permute-done | bytes 163872 | tf_op jit(solution)/shard_map/ppermute | solution.py:243
  108.1 2.2 %collective-permute-start.15 = (f32[1280,128]{1,0:T(8,128)S(1)}, f32[1280,128]{1,0:T(8,128)S(1)}, u32[]{:S(2)}, u32[]{:S(2)}) collective-permute-start(f32[1280,128]{1,0:T(8,128)S(1)} %maximum_select_fusion.1), channel_id=1, source_target_pairs={{0,4},{4,0},{8,12},{12,8},{1,5},{5,1},{9,13},{13,9},{2,6},{6,2},{1... | collective-permute-start | bytes 1966088 | tf_op jit(solution)/shard_map/ppermute | solution.py:243
  110.3 1.7 %collective-permute-done.15 = f32[1280,128]{1,0:T(8,128)S(1)} collective-permute-done((f32[1280,128]{1,0:T(8,128)S(1)}, f32[1280,128]{1,0:T(8,128)S(1)}, u32[]{:S(2)}, u32[]{:S(2)}) %collective-permute-start.15) | collective-permute-done | bytes 655392 | tf_op jit(solution)/shard_map/ppermute | solution.py:243
  (69 shorter events, 13.5 us)
Async XLA Ops:
  0.7 8.1 %copy-start.4 = (f32[1,16,160,128]{3,2,1,0:T(8,128)S(1)}, f32[1,16,160,128]{3,2,1,0:T(8,128)}, u32[]{:S(2)}) copy-start(f32[1,16,160,128]{3,2,1,0:T(8,128)} %param.14) | copy-start | bytes 3932164
  2.0 10.4 %collective-permute-start.2 = (f32[4,160,128]{2,1,0:T(8,128)S(1)}, f32[4,160,128]{2,1,0:T(8,128)S(1)}, u32[]{:S(2)}, u32[]{:S(2)}) collective-permute-start(f32[4,160,128]{2,1,0:T(8,128)S(1)} %get-tuple-element.27), channel_id=1, source_target_pairs={{0,1},{1,0},{2,3},{3,2},{4,5},{5,4},{6,7},{7,6},{8,9},{9,8},{10,11... | collective-permute-start | bytes 983048 | tf_op jit(solution)/shard_map/ppermute | solution.py:276
  2.0 8.4 %copy-start.13 = (s32[256]{0:T(256)S(1)}, s32[256]{0:T(256)}, u32[]{:S(2)}) copy-start(s32[256]{0:T(256)} %param.18) | copy-start | bytes 3076
  2.0 9.7 %copy-start.15 = (f32[2]{0:T(128)S(1)}, f32[2]{0:T(128)}, u32[]{:S(2)}) copy-start(f32[2]{0:T(128)} %param.16) | copy-start | bytes 28
  2.1 12.7 %collective-permute-start.3 = (f32[4,160,128]{2,1,0:T(8,128)S(1)}, f32[4,160,128]{2,1,0:T(8,128)S(1)}, u32[]{:S(2)}, u32[]{:S(2)}) collective-permute-start(f32[4,160,128]{2,1,0:T(8,128)S(1)} %get-tuple-element.26), channel_id=1, source_target_pairs={{1,2},{2,1},{5,6},{6,5},{9,10},{10,9},{13,14},{14,13},{17,18},{18,... | collective-permute-start | bytes 983048 | tf_op jit(solution)/shard_map/ppermute | solution.py:276
  6.7 11.0 %collective-permute-start.4 = (f32[4,160,128]{2,1,0:T(8,128)S(1)}, f32[4,160,128]{2,1,0:T(8,128)}, u32[]{:S(2)}, u32[]{:S(2)}) collective-permute-start(f32[4,160,128]{2,1,0:T(8,128)S(1)} %get-tuple-element.25), channel_id=1, source_target_pairs={{0,1},{1,0},{2,3},{3,2},{4,5},{5,4},{6,7},{7,6},{8,9},{9,8},{10,11... | collective-permute-start | bytes 983048 | tf_op jit(solution)/shard_map/ppermute | solution.py:276
  6.8 14.1 %collective-permute-start.5 = (f32[4,160,128]{2,1,0:T(8,128)S(1)}, f32[4,160,128]{2,1,0:T(8,128)}, u32[]{:S(2)}, u32[]{:S(2)}) collective-permute-start(f32[4,160,128]{2,1,0:T(8,128)S(1)} %get-tuple-element.24), channel_id=1, source_target_pairs={{1,2},{2,1},{5,6},{6,5},{9,10},{10,9},{13,14},{14,13},{17,18},{18,... | collective-permute-start | bytes 983048 | tf_op jit(solution)/shard_map/ppermute | solution.py:276
  8.8 28.5 %collective-permute-start = (f32[4,160,128]{2,1,0:T(8,128)S(1)}, f32[4,160,128]{2,1,0:T(8,128)S(1)}, u32[]{:S(2)}, u32[]{:S(2)}) collective-permute-start(f32[4,160,128]{2,1,0:T(8,128)S(1)} %get-tuple-element.29), channel_id=1, source_target_pairs={{0,1},{1,0},{2,3},{3,2},{4,5},{5,4},{6,7},{7,6},{8,9},{9,8},{10,11... | collective-permute-start | bytes 983048 | tf_op jit(solution)/shard_map/ppermute | solution.py:276
  12.3 8.6 %copy-start.11 = (f32[4,160,128]{2,1,0:T(8,128)}, f32[4,160,128]{2,1,0:T(8,128)S(1)}, u32[]{:S(2)}) copy-start(f32[4,160,128]{2,1,0:T(8,128)S(1)} %collective-permute-done.2.refs_1_) | copy-start | bytes 983044
  12.3 25.0 %collective-permute-start.1 = (f32[4,160,128]{2,1,0:T(8,128)S(1)}, f32[4,160,128]{2,1,0:T(8,128)S(1)}, u32[]{:S(2)}, u32[]{:S(2)}) collective-permute-start(f32[4,160,128]{2,1,0:T(8,128)S(1)} %get-tuple-element.28), channel_id=1, source_target_pairs={{1,2},{2,1},{5,6},{6,5},{9,10},{10,9},{13,14},{14,13},{17,18},{18,... | collective-permute-start | bytes 983048 | tf_op jit(solution)/shard_map/ppermute | solution.py:276
  14.8 6.1 %copy-start.12 = (f32[4,160,128]{2,1,0:T(8,128)}, f32[4,160,128]{2,1,0:T(8,128)S(1)}, u32[]{:S(2)}) copy-start(f32[4,160,128]{2,1,0:T(8,128)S(1)} %collective-permute-done.3.refs_3_) | copy-start | bytes 983044
  33.1 13.0 %collective-permute-start.6 = (f32[4,160,128]{2,1,0:T(8,128)}, f32[4,160,128]{2,1,0:T(8,128)S(1)}, u32[]{:S(2)}, u32[]{:S(2)}) collective-permute-start(f32[4,160,128]{2,1,0:T(8,128)} %get-tuple-element.16), channel_id=1, source_target_pairs={{0,1},{1,0},{2,3},{3,2},{4,5},{5,4},{6,7},{7,6},{8,9},{9,8},{10,11... | collective-permute-start | bytes 983048 | tf_op jit(solution)/shard_map/ppermute | solution.py:276
  33.2 12.9 %collective-permute-start.7 = (f32[4,160,128]{2,1,0:T(8,128)}, f32[4,160,128]{2,1,0:T(8,128)S(1)}, u32[]{:S(2)}, u32[]{:S(2)}) collective-permute-start(f32[4,160,128]{2,1,0:T(8,128)} %get-tuple-element.18), channel_id=1, source_target_pairs={{1,2},{2,1},{5,6},{6,5},{9,10},{10,9},{13,14},{14,13},{17,18},{18,... | collective-permute-start | bytes 983048 | tf_op jit(solution)/shard_map/ppermute | solution.py:276
  47.0 11.2 %copy-start.14 = (f32[2,256]{1,0:T(2,128)S(1)}, f32[2,256]{1,0:T(2,128)}, u32[]{:S(2)}) copy-start(f32[2,256]{1,0:T(2,128)} %param.19) | copy-start | bytes 6148
  47.0 11.2 %copy-start.1 = (f32[16,160,128]{2,1,0:T(8,128)S(1)}, f32[16,160,128]{2,1,0:T(8,128)}, u32[]{:S(2)}) copy-start(f32[16,160,128]{2,1,0:T(8,128)} %shard_map.114) | copy-start | bytes 3932164
  60.7 8.3 %copy-start.2 = (f32[327680]{0:T(1024)}, f32[327680]{0:T(1024)S(1)}, u32[]{:S(2)}) copy-start(f32[327680]{0:T(1024)S(1)} %scatter_fusion) | copy-start | bytes 3932164
  60.7 6.0 %collective-permute-start.8 = (f32[4,160,128]{2,1,0:T(8,128)S(1)}, f32[4,160,128]{2,1,0:T(8,128)S(1)}, u32[]{:S(2)}, u32[]{:S(2)}) collective-permute-start(f32[4,160,128]{2,1,0:T(8,128)S(1)} %get-tuple-element.23), channel_id=1, source_target_pairs={{0,1},{1,0},{2,3},{3,2},{4,5},{5,4},{6,7},{7,6},{8,9},{9,8},{10,11... | collective-permute-start | bytes 983048 | tf_op jit(solution)/shard_map/ppermute | solution.py:276
  60.8 8.1 %collective-permute-start.9 = (f32[4,160,128]{2,1,0:T(8,128)S(1)}, f32[4,160,128]{2,1,0:T(8,128)S(1)}, u32[]{:S(2)}, u32[]{:S(2)}) collective-permute-start(f32[4,160,128]{2,1,0:T(8,128)S(1)} %get-tuple-element.22), channel_id=1, source_target_pairs={{1,2},{2,1},{5,6},{6,5},{9,10},{10,9},{13,14},{14,13},{17,18},{18,... | collective-permute-start | bytes 983048 | tf_op jit(solution)/shard_map/ppermute | solution.py:276
  84.5 6.3 %collective-permute-start.10 = (f32[1280,128]{1,0:T(8,128)S(1)}, f32[1280,128]{1,0:T(8,128)S(1)}, u32[]{:S(2)}, u32[]{:S(2)}) collective-permute-start(f32[1280,128]{1,0:T(8,128)S(1)} %constant_dynamic-slice_fusion.2), channel_id=1, source_target_pairs={{0,4},{4,0},{8,12},{12,8},{1,5},{5,1},{9,13},{13,9},{2,6},{6,2},{1... | collective-permute-start | bytes 1966088 | tf_op jit(solution)/shard_map/ppermute | solution.py:243
  90.9 5.5 %collective-permute-start.11 = (f32[320,128]{1,0:T(8,128)S(1)}, f32[320,128]{1,0:T(8,128)S(1)}, u32[]{:S(2)}, u32[]{:S(2)}) collective-permute-start(f32[320,128]{1,0:T(8,128)S(1)} %get-tuple-element.30), channel_id=1, source_target_pairs={{0,8},{4,12},{8,0},{12,4},{1,9},{5,13},{9,1},{13,5},{2,10},{6,14},... | collective-permute-start | bytes 491528 | tf_op jit(solution)/shard_map/ppermute | solution.py:243
  92.2 7.7 %collective-permute-start.12 = (f32[320,128]{1,0:T(8,128)S(1)}, f32[320,128]{1,0:T(8,128)S(1)}, u32[]{:S(2)}, u32[]{:S(2)}) collective-permute-start(f32[320,128]{1,0:T(8,128)S(1)} %get-tuple-element.31), channel_id=1, source_target_pairs={{0,8},{4,12},{8,0},{12,4},{1,9},{5,13},{9,1},{13,5},{2,10},{6,14},... | collective-permute-start | bytes 491528 | tf_op jit(solution)/shard_map/ppermute | solution.py:243
  100.0 4.6 %collective-permute-start.13 = (f32[320,128]{1,0:T(8,128)S(1)}, f32[320,128]{1,0:T(8,128)S(1)}, u32[]{:S(2)}, u32[]{:S(2)}) collective-permute-start(f32[320,128]{1,0:T(8,128)S(1)} %get-tuple-element.32), channel_id=1, source_target_pairs={{0,8},{4,12},{8,0},{12,4},{1,9},{5,13},{9,1},{13,5},{2,10},{6,14},... | collective-permute-start | bytes 491528 | tf_op jit(solution)/shard_map/ppermute | solution.py:243
  101.2 6.8 %collective-permute-start.14 = (f32[320,128]{1,0:T(8,128)S(1)}, f32[320,128]{1,0:T(8,128)S(1)}, u32[]{:S(2)}, u32[]{:S(2)}) collective-permute-start(f32[320,128]{1,0:T(8,128)S(1)} %get-tuple-element.33), channel_id=1, source_target_pairs={{0,8},{4,12},{8,0},{12,4},{1,9},{5,13},{9,1},{13,5},{2,10},{6,14},... | collective-permute-start | bytes 491528 | tf_op jit(solution)/shard_map/ppermute | solution.py:243
  108.1 3.9 %collective-permute-start.15 = (f32[1280,128]{1,0:T(8,128)S(1)}, f32[1280,128]{1,0:T(8,128)S(1)}, u32[]{:S(2)}, u32[]{:S(2)}) collective-permute-start(f32[1280,128]{1,0:T(8,128)S(1)} %maximum_select_fusion.1), channel_id=1, source_target_pairs={{0,4},{4,0},{8,12},{12,8},{1,5},{5,1},{9,13},{13,9},{2,6},{6,2},{1... | collective-permute-start | bytes 1966088 | tf_op jit(solution)/shard_map/ppermute | solution.py:243
  (8 other events, 16.6 us)

commit v14 on v12

--- a/solution.py
+++ b/solution.py
@@ -133,7 +133,7 @@
                 sample_ref[pl.ds(r, 1), :] = jnp.where(one_lane == rec_ref[1, r], line, 0.0)
                 return carry
 
-            lax.fori_loop(0, sample_ref.shape[0], sample, 0, unroll=8)
+            lax.fori_loop(0, sample_ref.shape[0], sample, 0, unroll=32)
 
 
 def grad_kernel(lo_ref, mid_ref, hi_ref, g0_ref, g1_ref, g2_ref, pad_ref, *, block, rows):

time: 114 us -> 113 us (level)
  no operation moved by 1% of the time
where the time goes in v14:
time: 113 us
  Pallas kernels  38 us (34%)
  waiting for transfers between devices  29.8 us (26%)
  starting transfers between devices  24.8 us (22%)
  other arithmetic  14 us (12%)
  local copies, waits for them, and re-layouts  4.6 us (4%)
  between operations  1.75 us (2%)
    pallas_call x4, Pallas kernels, apply_step(): pl.pallas_call(kernel, grid=(planes // block,), in_specs=in_specs, out_sp...  38 us
    ppermute x5, starting transfers between devices, swap_halos(): lax.ppermute(sends[1], axis, second)  14.3 us
    ppermute x2, waiting for transfers between devices, reduce_members(): rows = keep + lax.ppermute(give, axis, pairs)  9.44 us
    ppermute x2, waiting for transfers between devices, reduce_members(): other = lax.ppermute(rows, axis, pairs)  8.52 us
    scatter-add x2, other arithmetic, inject(): flat = field.reshape(-1).at[where].add(jnp.where(valid, values, 0.0))  6.83 us
    ppermute x5, waiting for transfers between devices, swap_halos(): lax.ppermute(sends[0], axis, first)  6.47 us
    ppermute x2, starting transfers between devices, reduce_members(): rows = keep + lax.ppermute(give, axis, pairs)  5.81 us
    ppermute x5, waiting for transfers between devices, swap_halos(): lax.ppermute(sends[1], axis, second)  5.36 us
  transfers between devices with their start and end apart: 14, of which 8 were waited for; matrix products, arithmetic and copies ran while one was open for 3% of the time, Pallas kernels for 18%

profile of v14, /device:TPU:9, one launch (start us, length us, event | category | flops | bytes accessed | tf_op | source)
XLA Modules:
  0.0 112.9 jit_solution(13764875556569679756)
XLA Ops:
  2.1 4.6 %collective-permute-start.3 = (f32[4,160,128]{2,1,0:T(8,128)S(1)}, f32[4,160,128]{2,1,0:T(8,128)S(1)}, u32[]{:S(2)}, u32[]{:S(2)}) collective-permute-start(f32[4,160,128]{2,1,0:T(8,128)S(1)} %get-tuple-element.26), channel_id=1, source_target_pairs={{1,2},{2,1},{5,6},{6,5},{9,10},{10,9},{13,14},{14,13},{17,18},{18,... | collective-permute-start | bytes 983048 | tf_op jit(solution)/shard_map/ppermute | solution.py:270
  6.8 1.9 %collective-permute-start.5 = (f32[4,160,128]{2,1,0:T(8,128)S(1)}, f32[4,160,128]{2,1,0:T(8,128)}, u32[]{:S(2)}, u32[]{:S(2)}) collective-permute-start(f32[4,160,128]{2,1,0:T(8,128)S(1)} %get-tuple-element.24), channel_id=1, source_target_pairs={{1,2},{2,1},{5,6},{6,5},{9,10},{10,9},{13,14},{14,13},{17,18},{18,... | collective-permute-start | bytes 983048 | tf_op jit(solution)/shard_map/ppermute | solution.py:270
  12.4 2.5 %collective-permute-start.1 = (f32[4,160,128]{2,1,0:T(8,128)S(1)}, f32[4,160,128]{2,1,0:T(8,128)S(1)}, u32[]{:S(2)}, u32[]{:S(2)}) collective-permute-start(f32[4,160,128]{2,1,0:T(8,128)S(1)} %get-tuple-element.28), channel_id=1, source_target_pairs={{1,2},{2,1},{5,6},{6,5},{9,10},{10,9},{13,14},{14,13},{17,18},{18,... | collective-permute-start | bytes 983048 | tf_op jit(solution)/shard_map/ppermute | solution.py:270
  14.9 2.8 %collective-permute-done.4.refs_4_ = f32[4,160,128]{2,1,0:T(8,128)} collective-permute-done((f32[4,160,128]{2,1,0:T(8,128)S(1)}, f32[4,160,128]{2,1,0:T(8,128)}, u32[]{:S(2)}, u32[]{:S(2)}) %collective-permute-start.4) | collective-permute-done | bytes 327712 | tf_op jit(solution)/shard_map/ppermute | solution.py:270
  17.7 3.2 %collective-permute-done.5.refs_6_ = f32[4,160,128]{2,1,0:T(8,128)} collective-permute-done((f32[4,160,128]{2,1,0:T(8,128)S(1)}, f32[4,160,128]{2,1,0:T(8,128)}, u32[]{:S(2)}, u32[]{:S(2)}) %collective-permute-start.5) | collective-permute-done | bytes 327712 | tf_op jit(solution)/shard_map/ppermute | solution.py:270
  20.9 12.1 %shard_map.113 = (f32[16,160,128]{2,1,0:T(8,128)}, f32[16,160,128]{2,1,0:T(8,128)}, f32[16,160,128]{2,1,0:T(8,128)}, f32[16,160,128]{2,1,0:T(8,128)}, f32[16,160...) custom-call(s32[1]{0:T(128)} %bitcast.refs_0_, ...), custom_call_target="tpu_custom_call" | custom-call | tf_op jit(solution)/shard_map/pallas_call | solution.py:214
  33.1 3.0 %collective-permute-start.7 = (f32[4,160,128]{2,1,0:T(8,128)}, f32[4,160,128]{2,1,0:T(8,128)S(1)}, u32[]{:S(2)}, u32[]{:S(2)}) collective-permute-start(f32[4,160,128]{2,1,0:T(8,128)} %get-tuple-element.18), channel_id=1, source_target_pairs={{1,2},{2,1},{5,6},{6,5},{9,10},{10,9},{13,14},{14,13},{17,18},{18,... | collective-permute-start | bytes 983048 | tf_op jit(solution)/shard_map/ppermute | solution.py:270
  38.0 7.9 %shard_map.114 = f32[16,160,128]{2,1,0:T(8,128)} custom-call(s32[1]{0:T(128)} %bitcast.refs_0_, f32[4,160,128]{2,1,0:T(8,128)} %copy-done.5, f32[16,160,128]{2,1,0:T(8,128)} %bitcast.46, f32[4,160,128]{2,1,0:T(8,128)} %copy-done.8, f32[16,160,128]{2,1,0:T(8,128)} %refs_4_.5, f32[16,160,128]{2,1,0:T(8,128)} %get-tuple-element.12.refs_5_, ...), custom_call_target="tpu_custom_call" | custom-call | tf_op jit(solution)/shard_map/pallas_call | solution.py:214
  46.9 10.0 %shard_map.115 = (f32[16,160,128]{2,1,0:T(8,128)}, f32[16,160,128]{2,1,0:T(8,128)}, f32[256,128]{1,0:T(8,128)}) custom-call(s32[1]{0:T(128)} %bitcast.refs_0_, f32[4,160,128]{2,1,0:T(8,128)} %copy-done.9, f32[16,160,128]{2,1,0:T(8,128)} %get-tuple-element.17.refs_2_, f32[4,160,128]{2,1,0:T(8,128)} %copy-done.10, f32[16,160,128]{2,1,0:T(8,128)} %refs_4_.5, ...), custom_call_target="tpu_custom_call" | custom-call | tf_op jit(solution)/shard_map/pallas_call | solution.py:214
  57.9 2.4 %scatter_fusion = f32[327680]{0:T(1024)S(1)} fusion(f32[327680]{0:T(1024)S(1)} %bitcast.33, s32[256]{0:T(256)S(1)} %get-tuple-element.32, f32[256]{0:T(256)S(1)} %get-tuple-element.36), kind=kCustom, calls=%fused_computation | custom fusion | flops 256 | bytes 4096 | tf_op jit(solution)/shard_map/scatter-add | solution.py:282
  60.5 2.2 %collective-permute-start.9 = (f32[4,160,128]{2,1,0:T(8,128)S(1)}, f32[4,160,128]{2,1,0:T(8,128)S(1)}, u32[]{:S(2)}, u32[]{:S(2)}) collective-permute-start(f32[4,160,128]{2,1,0:T(8,128)S(1)} %get-tuple-element.22), channel_id=1, source_target_pairs={{1,2},{2,1},{5,6},{6,5},{9,10},{10,9},{13,14},{14,13},{17,18},{18,... | collective-permute-start | bytes 983048 | tf_op jit(solution)/shard_map/ppermute | solution.py:270
  62.8 3.6 %collective-permute-done.8.refs_1_ = f32[4,160,128]{2,1,0:T(8,128)S(1)} collective-permute-done((f32[4,160,128]{2,1,0:T(8,128)S(1)}, f32[4,160,128]{2,1,0:T(8,128)S(1)}, u32[]{:S(2)}, u32[]{:S(2)}) %collective-permute-start.8) | collective-permute-done | bytes 327712 | tf_op jit(solution)/shard_map/ppermute | solution.py:270
  66.5 2.2 %collective-permute-done.9.refs_3_ = f32[4,160,128]{2,1,0:T(8,128)S(1)} collective-permute-done((f32[4,160,128]{2,1,0:T(8,128)S(1)}, f32[4,160,128]{2,1,0:T(8,128)S(1)}, u32[]{:S(2)}, u32[]{:S(2)}) %collective-permute-start.9) | collective-permute-done | bytes 327712 | tf_op jit(solution)/shard_map/ppermute | solution.py:270
  69.4 8.0 %shard_map.116 = f32[16,160,128]{2,1,0:T(8,128)} custom-call(s32[1]{0:T(128)} %bitcast.refs_0_, f32[4,160,128]{2,1,0:T(8,128)} %copy-done.6, f32[16,160,128]{2,1,0:T(8,128)} %bitcast.35, f32[4,160,128]{2,1,0:T(8,128)} %copy-done.7, f32[16,160,128]{2,1,0:T(8,128)} %refs_4_.5, f32[16,160,128]{2,1,0:T(8,128)} %get-tuple-element.12.refs_5_, ...), custom_call_target="tpu_custom_call" | custom-call | tf_op jit(solution)/shard_map/pallas_call | solution.py:214
  77.4 4.4 %scatter_fusion.1 = f32[327680]{0:T(1024)} fusion(f32[327680]{0:T(1024)} %bitcast.41, s32[256]{0:T(256)S(1)} %get-tuple-element.32, f32[256]{0:T(256)S(1)} %get-tuple-element.35), kind=kCustom, calls=%fused_computation.1 | custom fusion | flops 256 | bytes 4096 | tf_op jit(solution)/shard_map/scatter-add | solution.py:282
  81.7 2.5 %multiply_add_fusion = f32[16,160,128]{2,1,0:T(8,128)S(1)} fusion(f32[16,160,128]{2,1,0:T(8,128)} %bitcast.42, f32[16,160,128]{2,1,0:T(8,128)} %get-tuple-element.21, f32[16,160,128]{2,1,0:T(8,128)S(1)} %bitcast.36, f32[16,160,128]{2,1,0:T(8,128)} %get-tuple-element.20), kind=kLoop, calls=%fused_computation.3 | loop fusion | flops 983040 | bytes 6553600 | tf_op jit(solution)/shard_map/add | solution.py:347
  84.3 4.5 %collective-permute-start.10 = (f32[1280,128]{1,0:T(8,128)S(1)}, f32[1280,128]{1,0:T(8,128)S(1)}, u32[]{:S(2)}, u32[]{:S(2)}) collective-permute-start(f32[1280,128]{1,0:T(8,128)S(1)} %constant_dynamic-slice_fusion.1), channel_id=1, source_target_pairs={{0,4},{4,0},{8,12},{12,8},{1,5},{5,1},{9,13},{13,9},{2,6},{6,2},{1... | collective-permute-start | bytes 1966088 | tf_op jit(solution)/shard_map/ppermute | solution.py:255
  88.8 1.7 %collective-permute-done.10 = f32[1280,128]{1,0:T(8,128)S(1)} collective-permute-done((f32[1280,128]{1,0:T(8,128)S(1)}, f32[1280,128]{1,0:T(8,128)S(1)}, u32[]{:S(2)}, u32[]{:S(2)}) %collective-permute-start.10) | collective-permute-done | bytes 655392 | tf_op jit(solution)/shard_map/ppermute | solution.py:255
  90.6 1.3 %collective-permute-start.11 = (f32[640,128]{1,0:T(8,128)S(1)}, f32[640,128]{1,0:T(8,128)S(1)}, u32[]{:S(2)}, u32[]{:S(2)}) collective-permute-start(f32[640,128]{1,0:T(8,128)S(1)} %constant_dynamic-slice_fusion), channel_id=1, source_target_pairs={{0,8},{4,12},{8,0},{12,4},{1,9},{5,13},{9,1},{13,5},{2,10},{6,14},... | collective-permute-start | bytes 983048 | tf_op jit(solution)/shard_map/ppermute | solution.py:255
  91.9 7.7 %collective-permute-done.11 = f32[640,128]{1,0:T(8,128)S(1)} collective-permute-done((f32[640,128]{1,0:T(8,128)S(1)}, f32[640,128]{1,0:T(8,128)S(1)}, u32[]{:S(2)}, u32[]{:S(2)}) %collective-permute-start.11) | collective-permute-done | bytes 327712 | tf_op jit(solution)/shard_map/ppermute | solution.py:255
  99.6 1.3 %collective-permute-start.12 = (f32[640,128]{1,0:T(8,128)S(1)}, f32[640,128]{1,0:T(8,128)S(1)}, u32[]{:S(2)}, u32[]{:S(2)}) collective-permute-start(f32[640,128]{1,0:T(8,128)S(1)} %add_multiply_fusion), channel_id=1, source_target_pairs={{0,8},{4,12},{8,0},{12,4},{1,9},{5,13},{9,1},{13,5},{2,10},{6,14},... | collective-permute-start | bytes 983048 | tf_op jit(solution)/shard_map/ppermute | solution.py:261
  100.9 6.8 %collective-permute-done.12 = f32[640,128]{1,0:T(8,128)S(1)} collective-permute-done((f32[640,128]{1,0:T(8,128)S(1)}, f32[640,128]{1,0:T(8,128)S(1)}, u32[]{:S(2)}, u32[]{:S(2)}) %collective-permute-start.12) | collective-permute-done | bytes 327712 | tf_op jit(solution)/shard_map/ppermute | solution.py:261
  107.8 2.2 %collective-permute-start.13 = (f32[1280,128]{1,0:T(8,128)S(1)}, f32[1280,128]{1,0:T(8,128)S(1)}, u32[]{:S(2)}, u32[]{:S(2)}) collective-permute-start(f32[1280,128]{1,0:T(8,128)S(1)} %maximum_select_fusion.1), channel_id=1, source_target_pairs={{0,4},{4,0},{8,12},{12,8},{1,5},{5,1},{9,13},{13,9},{2,6},{6,2},{1... | collective-permute-start | bytes 1966088 | tf_op jit(solution)/shard_map/ppermute | solution.py:261
  110.0 1.7 %collective-permute-done.13 = f32[1280,128]{1,0:T(8,128)S(1)} collective-permute-done((f32[1280,128]{1,0:T(8,128)S(1)}, f32[1280,128]{1,0:T(8,128)S(1)}, u32[]{:S(2)}, u32[]{:S(2)}) %collective-permute-start.13) | collective-permute-done | bytes 655392 | tf_op jit(solution)/shard_map/ppermute | solution.py:261
  (64 shorter events, 10.5 us)
Async XLA Ops:
  0.6 6.0 %copy-start = (f32[16,160,128]{2,1,0:T(8,128)S(1)}, f32[16,160,128]{2,1,0:T(8,128)}, u32[]{:S(2)}) copy-start(f32[16,160,128]{2,1,0:T(8,128)} %refs_4_.5) | copy-start | bytes 3932164
  0.7 8.1 %copy-start.4 = (f32[1,16,160,128]{3,2,1,0:T(8,128)S(1)}, f32[1,16,160,128]{3,2,1,0:T(8,128)}, u32[]{:S(2)}) copy-start(f32[1,16,160,128]{3,2,1,0:T(8,128)} %param.14) | copy-start | bytes 3932164
  2.0 10.4 %collective-permute-start.2 = (f32[4,160,128]{2,1,0:T(8,128)S(1)}, f32[4,160,128]{2,1,0:T(8,128)S(1)}, u32[]{:S(2)}, u32[]{:S(2)}) collective-permute-start(f32[4,160,128]{2,1,0:T(8,128)S(1)} %get-tuple-element.27), channel_id=1, source_target_pairs={{0,1},{1,0},{2,3},{3,2},{4,5},{5,4},{6,7},{7,6},{8,9},{9,8},{10,11... | collective-permute-start | bytes 983048 | tf_op jit(solution)/shard_map/ppermute | solution.py:270
  2.0 8.4 %copy-start.13 = (s32[256]{0:T(256)S(1)}, s32[256]{0:T(256)}, u32[]{:S(2)}) copy-start(s32[256]{0:T(256)} %param.18) | copy-start | bytes 3076
  2.0 9.7 %copy-start.15 = (f32[2]{0:T(128)S(1)}, f32[2]{0:T(128)}, u32[]{:S(2)}) copy-start(f32[2]{0:T(128)} %param.16) | copy-start | bytes 28
  2.1 12.8 %collective-permute-start.3 = (f32[4,160,128]{2,1,0:T(8,128)S(1)}, f32[4,160,128]{2,1,0:T(8,128)S(1)}, u32[]{:S(2)}, u32[]{:S(2)}) collective-permute-start(f32[4,160,128]{2,1,0:T(8,128)S(1)} %get-tuple-element.26), channel_id=1, source_target_pairs={{1,2},{2,1},{5,6},{6,5},{9,10},{10,9},{13,14},{14,13},{17,18},{18,... | collective-permute-start | bytes 983048 | tf_op jit(solution)/shard_map/ppermute | solution.py:270
  6.7 11.0 %collective-permute-start.4 = (f32[4,160,128]{2,1,0:T(8,128)S(1)}, f32[4,160,128]{2,1,0:T(8,128)}, u32[]{:S(2)}, u32[]{:S(2)}) collective-permute-start(f32[4,160,128]{2,1,0:T(8,128)S(1)} %get-tuple-element.25), channel_id=1, source_target_pairs={{0,1},{1,0},{2,3},{3,2},{4,5},{5,4},{6,7},{7,6},{8,9},{9,8},{10,11... | collective-permute-start | bytes 983048 | tf_op jit(solution)/shard_map/ppermute | solution.py:270
  6.8 14.1 %collective-permute-start.5 = (f32[4,160,128]{2,1,0:T(8,128)S(1)}, f32[4,160,128]{2,1,0:T(8,128)}, u32[]{:S(2)}, u32[]{:S(2)}) collective-permute-start(f32[4,160,128]{2,1,0:T(8,128)S(1)} %get-tuple-element.24), channel_id=1, source_target_pairs={{1,2},{2,1},{5,6},{6,5},{9,10},{10,9},{13,14},{14,13},{17,18},{18,... | collective-permute-start | bytes 983048 | tf_op jit(solution)/shard_map/ppermute | solution.py:270
  8.8 28.4 %collective-permute-start = (f32[4,160,128]{2,1,0:T(8,128)S(1)}, f32[4,160,128]{2,1,0:T(8,128)S(1)}, u32[]{:S(2)}, u32[]{:S(2)}) collective-permute-start(f32[4,160,128]{2,1,0:T(8,128)S(1)} %get-tuple-element.29), channel_id=1, source_target_pairs={{0,1},{1,0},{2,3},{3,2},{4,5},{5,4},{6,7},{7,6},{8,9},{9,8},{10,11... | collective-permute-start | bytes 983048 | tf_op jit(solution)/shard_map/ppermute | solution.py:270
  12.4 8.5 %copy-start.11 = (f32[4,160,128]{2,1,0:T(8,128)}, f32[4,160,128]{2,1,0:T(8,128)S(1)}, u32[]{:S(2)}) copy-start(f32[4,160,128]{2,1,0:T(8,128)S(1)} %collective-permute-done.2.refs_1_) | copy-start | bytes 983044
  12.4 24.8 %collective-permute-start.1 = (f32[4,160,128]{2,1,0:T(8,128)S(1)}, f32[4,160,128]{2,1,0:T(8,128)S(1)}, u32[]{:S(2)}, u32[]{:S(2)}) collective-permute-start(f32[4,160,128]{2,1,0:T(8,128)S(1)} %get-tuple-element.28), channel_id=1, source_target_pairs={{1,2},{2,1},{5,6},{6,5},{9,10},{10,9},{13,14},{14,13},{17,18},{18,... | collective-permute-start | bytes 983048 | tf_op jit(solution)/shard_map/ppermute | solution.py:270
  14.9 6.0 %copy-start.12 = (f32[4,160,128]{2,1,0:T(8,128)}, f32[4,160,128]{2,1,0:T(8,128)S(1)}, u32[]{:S(2)}) copy-start(f32[4,160,128]{2,1,0:T(8,128)S(1)} %collective-permute-done.3.refs_3_) | copy-start | bytes 983044
  33.0 13.0 %collective-permute-start.6 = (f32[4,160,128]{2,1,0:T(8,128)}, f32[4,160,128]{2,1,0:T(8,128)S(1)}, u32[]{:S(2)}, u32[]{:S(2)}) collective-permute-start(f32[4,160,128]{2,1,0:T(8,128)} %get-tuple-element.16), channel_id=1, source_target_pairs={{0,1},{1,0},{2,3},{3,2},{4,5},{5,4},{6,7},{7,6},{8,9},{9,8},{10,11... | collective-permute-start | bytes 983048 | tf_op jit(solution)/shard_map/ppermute | solution.py:270
  33.1 12.9 %collective-permute-start.7 = (f32[4,160,128]{2,1,0:T(8,128)}, f32[4,160,128]{2,1,0:T(8,128)S(1)}, u32[]{:S(2)}, u32[]{:S(2)}) collective-permute-start(f32[4,160,128]{2,1,0:T(8,128)} %get-tuple-element.18), channel_id=1, source_target_pairs={{1,2},{2,1},{5,6},{6,5},{9,10},{10,9},{13,14},{14,13},{17,18},{18,... | collective-permute-start | bytes 983048 | tf_op jit(solution)/shard_map/ppermute | solution.py:270
  46.9 11.0 %copy-start.14 = (f32[2,256]{1,0:T(2,128)S(1)}, f32[2,256]{1,0:T(2,128)}, u32[]{:S(2)}) copy-start(f32[2,256]{1,0:T(2,128)} %param.19) | copy-start | bytes 6148
  46.9 11.1 %copy-start.1 = (f32[16,160,128]{2,1,0:T(8,128)S(1)}, f32[16,160,128]{2,1,0:T(8,128)}, u32[]{:S(2)}) copy-start(f32[16,160,128]{2,1,0:T(8,128)} %shard_map.114) | copy-start | bytes 3932164
  60.4 8.3 %copy-start.2 = (f32[327680]{0:T(1024)}, f32[327680]{0:T(1024)S(1)}, u32[]{:S(2)}) copy-start(f32[327680]{0:T(1024)S(1)} %scatter_fusion) | copy-start | bytes 3932164
  60.5 6.0 %collective-permute-start.8 = (f32[4,160,128]{2,1,0:T(8,128)S(1)}, f32[4,160,128]{2,1,0:T(8,128)S(1)}, u32[]{:S(2)}, u32[]{:S(2)}) collective-permute-start(f32[4,160,128]{2,1,0:T(8,128)S(1)} %get-tuple-element.23), channel_id=1, source_target_pairs={{0,1},{1,0},{2,3},{3,2},{4,5},{5,4},{6,7},{7,6},{8,9},{9,8},{10,11... | collective-permute-start | bytes 983048 | tf_op jit(solution)/shard_map/ppermute | solution.py:270
  60.5 8.1 %collective-permute-start.9 = (f32[4,160,128]{2,1,0:T(8,128)S(1)}, f32[4,160,128]{2,1,0:T(8,128)S(1)}, u32[]{:S(2)}, u32[]{:S(2)}) collective-permute-start(f32[4,160,128]{2,1,0:T(8,128)S(1)} %get-tuple-element.22), channel_id=1, source_target_pairs={{1,2},{2,1},{5,6},{6,5},{9,10},{10,9},{13,14},{14,13},{17,18},{18,... | collective-permute-start | bytes 983048 | tf_op jit(solution)/shard_map/ppermute | solution.py:270
  77.3 4.4 %copy-start.3 = (f32[327680]{0:T(1024)S(1)}, f32[327680]{0:T(1024)}, u32[]{:S(2)}) copy-start(f32[327680]{0:T(1024)} %copy-done.2) | copy-start | bytes 3932164
  84.3 6.3 %collective-permute-start.10 = (f32[1280,128]{1,0:T(8,128)S(1)}, f32[1280,128]{1,0:T(8,128)S(1)}, u32[]{:S(2)}, u32[]{:S(2)}) collective-permute-start(f32[1280,128]{1,0:T(8,128)S(1)} %constant_dynamic-slice_fusion.1), channel_id=1, source_target_pairs={{0,4},{4,0},{8,12},{12,8},{1,5},{5,1},{9,13},{13,9},{2,6},{6,2},{1... | collective-permute-start | bytes 1966088 | tf_op jit(solution)/shard_map/ppermute | solution.py:255
  90.6 9.0 %collective-permute-start.11 = (f32[640,128]{1,0:T(8,128)S(1)}, f32[640,128]{1,0:T(8,128)S(1)}, u32[]{:S(2)}, u32[]{:S(2)}) collective-permute-start(f32[640,128]{1,0:T(8,128)S(1)} %constant_dynamic-slice_fusion), channel_id=1, source_target_pairs={{0,8},{4,12},{8,0},{12,4},{1,9},{5,13},{9,1},{13,5},{2,10},{6,14},... | collective-permute-start | bytes 983048 | tf_op jit(solution)/shard_map/ppermute | solution.py:255
  99.6 8.1 %collective-permute-start.12 = (f32[640,128]{1,0:T(8,128)S(1)}, f32[640,128]{1,0:T(8,128)S(1)}, u32[]{:S(2)}, u32[]{:S(2)}) collective-permute-start(f32[640,128]{1,0:T(8,128)S(1)} %add_multiply_fusion), channel_id=1, source_target_pairs={{0,8},{4,12},{8,0},{12,4},{1,9},{5,13},{9,1},{13,5},{2,10},{6,14},... | collective-permute-start | bytes 983048 | tf_op jit(solution)/shard_map/ppermute | solution.py:261
  107.8 3.9 %collective-permute-start.13 = (f32[1280,128]{1,0:T(8,128)S(1)}, f32[1280,128]{1,0:T(8,128)S(1)}, u32[]{:S(2)}, u32[]{:S(2)}) collective-permute-start(f32[1280,128]{1,0:T(8,128)S(1)} %maximum_select_fusion.1), channel_id=1, source_target_pairs={{0,4},{4,0},{8,12},{12,8},{1,5},{5,1},{9,13},{13,9},{2,6},{6,2},{1... | collective-permute-start | bytes 1966088 | tf_op jit(solution)/shard_map/ppermute | solution.py:261
  (6 other events, 6.1 us)

commit v15 on v12

--- a/solution.py
+++ b/solution.py
@@ -153,6 +153,58 @@
             g0_ref[sl] = grads[0]
             g1_ref[sl] = grads[1]
             g2_ref[sl] = grads[2]
+
+
+def final_kernel(parity_ref, lo_ref, mid_ref, hi_ref, b_ref, g0_ref, g1_ref, g2_ref, c_ref, old_ref,
+                 rec_ref, valid_ref, amount_ref, new_ref, pad_ref, *, block, rows):
+    i = pl.program_id(0)
+    odd = parity_ref[0] == 1
+
+    @pl.when(i == 0)
+    def _():
+        fill_padded(pad_ref, lo_ref, mid_ref, hi_ref, odd)
+
+    planes, height, depth = mid_ref.shape
+    lane = lax.broadcasted_iota(jnp.int32, (rows, depth), 1)
+    for p in range(block):
+        plane = i * block + p + HALO
+        for y0 in range(0, height, rows):
+            sl = (p, pl.ds(y0, rows), slice(None))
+            centre, lap, grads = taps(pad_ref, plane, y0, rows, lane)
+            force = b_ref[sl] * lap + (g0_ref[sl] * grads[0] + g1_ref[sl] * grads[1] + g2_ref[sl] * grads[2])
+            new_ref[plane - HALO, pl.ds(y0, rows), :] = 2.0 * centre - old_ref[sl] + c_ref[sl] * force
+
+    @pl.when(i == pl.num_programs(0) - 1)
+    def _():
+        one_lane = lax.broadcasted_iota(jnp.int32, (1, depth), 1)
+
+        def add(r, carry):
+            x = rec_ref[0, r]
+            y = rec_ref[1, r]
+            hit = (one_lane == rec_ref[2, r]) & (valid_ref[r] == 1)
+            line = new_ref[x, pl.ds(y, 1), :]
+            new_ref[x, pl.ds(y, 1), :] = jnp.where(hit, line + amount_ref[r], line)
+            return carry
+
+        lax.fori_loop(0, amount_ref.shape[0], add, 0)
+
+
+def apply_final(parity, lo, mid, hi, b, g, c, old, receivers, valid, amount, rows=40):
+    planes, height, depth = mid.shape
+    block = pick_block(planes)
+    full, blk = specs(mid.shape, block)
+    out = jax.ShapeDtypeStruct(mid.shape, jnp.float32)
+    smem = pl.BlockSpec(memory_space=pltpu.SMEM)
+    return pl.pallas_call(
+        functools.partial(final_kernel, block=block, rows=rows),
+        grid=(planes // block,),
+        in_specs=[smem, full(lo.shape), full(mid.shape), full(hi.shape)] + [blk] * 6
+        + [smem, smem, smem],
+        out_specs=full(mid.shape),
+        out_shape=out,
+        scratch_shapes=[pltpu.VMEM((planes + 2 * HALO, height + 2 * PADY, depth), jnp.float32)],
+        compiler_params=pltpu.CompilerParams(dimension_semantics=("arbitrary",)),
+    )(parity, lo, mid, hi, b, g[0], g[1], g[2], c, old, receivers, valid, amount)
 
 
 def pick_block(planes):
@@ -342,8 +394,13 @@
     image_part = jnp.zeros(buoyancy.shape, jnp.float32)
     for j in range(steps):
         lo, hi = halos(now, "tile")
-        (newer,) = apply_step(parity, lo, now, hi, buoyancy, grad_b, speed, older, want_force=False)
-        newer = inject(newer, rec_local, rec_valid, residual[steps - 1 - j])
+        if j + 1 < steps:
+            (newer,) = apply_step(parity, lo, now, hi, buoyancy, grad_b, speed, older, want_force=False)
+            newer = inject(newer, rec_local, rec_valid, residual[steps - 1 - j])
+        else:
+            cells = jnp.stack([rec_local // (height * depth), (rec_local // depth) % height, rec_local % depth])
+            valid = rec_valid.astype(jnp.int32)
+            newer = apply_final(parity, lo, now, hi, buoyancy, grad_b, speed, older, cells, valid, residual[0])
         image_part = image_part + newer * forces[steps - 1 - j]
         older, now = (now, newer)
     image = reduce_members(image_part, "real")

time: 114 us -> 113 us (level)
  other arithmetic: 14 us -> 10.7 us
  Pallas kernels: 38.2 us -> 41.4 us
    pallas_call x0 -> x1, Pallas kernels: none -> 11.1 us  [apply_final(): pl.pallas_call(functools.partial(final_kernel, block=block, rows=rows), g...]
    pallas_call x4 -> x3, Pallas kernels: 38.2 us -> 30.3 us  [apply_step(): pl.pallas_call(kernel, grid=(planes // block,), in_specs=in_specs, out_sp...]
    scatter-add x2 -> x1, other arithmetic: 6.82 us -> 2.44 us  [inject(): flat = field.reshape(-1).at[where].add(jnp.where(valid, values, 0.0))]
  transfers between devices with their start and end apart: 14 -> 14, of which waited for: 8 -> 8; matrix products, arithmetic and copies ran while one was open for 3% -> 4% of each run, Pallas kernels for 18% -> 18%
where the time goes in v15:
time: 113 us
  Pallas kernels  41.4 us (37%)
  waiting for transfers between devices  29.3 us (26%)
  starting transfers between devices  24.8 us (22%)
  other arithmetic  10.7 us (9%)
  local copies, waits for them, and re-layouts  5.12 us (5%)
  between operations  1.73 us (2%)
    pallas_call x3, Pallas kernels, apply_step(): pl.pallas_call(kernel, grid=(planes // block,), in_specs=in_specs, out_sp...  30.3 us
    ppermute x5, starting transfers between devices, swap_halos(): lax.ppermute(sends[1], axis, second)  14.3 us
    pallas_call x1, Pallas kernels, apply_final(): pl.pallas_call(functools.partial(final_kernel, block=block, rows=rows), g...  11.1 us
    ppermute x2, waiting for transfers between devices, reduce_members(): rows = keep + lax.ppermute(give, axis, pairs)  9.44 us
    ppermute x2, waiting for transfers between devices, reduce_members(): other = lax.ppermute(rows, axis, pairs)  8.52 us
    ppermute x5, waiting for transfers between devices, swap_halos(): lax.ppermute(sends[0], axis, first)  5.94 us
    ppermute x2, starting transfers between devices, reduce_members(): rows = keep + lax.ppermute(give, axis, pairs)  5.81 us
    ppermute x5, waiting for transfers between devices, swap_halos(): lax.ppermute(sends[1], axis, second)  5.36 us
  transfers between devices with their start and end apart: 14, of which 8 were waited for; matrix products, arithmetic and copies ran while one was open for 4% of the time, Pallas kernels for 18%

profile of v15, /device:TPU:9, one launch (start us, length us, event | category | flops | bytes accessed | tf_op | source)
XLA Modules:
  0.0 112.9 jit_solution(6543577704528285299)
XLA Ops:
  0.7 1.3 %dynamic-slice_bitcast_fusion = (f32[4,160,128]{2,1,0:T(8,128)S(1)}, f32[4,160,128]{2,1,0:T(8,128)S(1)}) fusion(f32[1,16,160,128]{3,2,1,0:T(8,128)} %param.12, s32[]{:T(128)S(6)} %select_n.135, s32[]{:T(128)S(6)} %select_n.134), kind=kLoop, calls=%fused_computation.6 | loop fusion | bytes 1310728 | tf_op jit(solution)/shard_map/dynamic_slice | solution.py:329
  2.1 4.6 %collective-permute-start.3 = (f32[4,160,128]{2,1,0:T(8,128)S(1)}, f32[4,160,128]{2,1,0:T(8,128)S(1)}, u32[]{:S(2)}, u32[]{:S(2)}) collective-permute-start(f32[4,160,128]{2,1,0:T(8,128)S(1)} %get-tuple-element.30), channel_id=1, source_target_pairs={{1,2},{2,1},{5,6},{6,5},{9,10},{10,9},{13,14},{14,13},{17,18},{18,... | collective-permute-start | bytes 983048 | tf_op jit(solution)/shard_map/ppermute | solution.py:322
  6.8 1.9 %collective-permute-start.5 = (f32[4,160,128]{2,1,0:T(8,128)S(1)}, f32[4,160,128]{2,1,0:T(8,128)}, u32[]{:S(2)}, u32[]{:S(2)}) collective-permute-start(f32[4,160,128]{2,1,0:T(8,128)S(1)} %get-tuple-element.28), channel_id=1, source_target_pairs={{1,2},{2,1},{5,6},{6,5},{9,10},{10,9},{13,14},{14,13},{17,18},{18,... | collective-permute-start | bytes 983048 | tf_op jit(solution)/shard_map/ppermute | solution.py:322
  12.3 2.5 %collective-permute-start.1 = (f32[4,160,128]{2,1,0:T(8,128)S(1)}, f32[4,160,128]{2,1,0:T(8,128)S(1)}, u32[]{:S(2)}, u32[]{:S(2)}) collective-permute-start(f32[4,160,128]{2,1,0:T(8,128)S(1)} %get-tuple-element.32), channel_id=1, source_target_pairs={{1,2},{2,1},{5,6},{6,5},{9,10},{10,9},{13,14},{14,13},{17,18},{18,... | collective-permute-start | bytes 983048 | tf_op jit(solution)/shard_map/ppermute | solution.py:322
  14.8 2.9 %collective-permute-done.4.refs_4_ = f32[4,160,128]{2,1,0:T(8,128)} collective-permute-done((f32[4,160,128]{2,1,0:T(8,128)S(1)}, f32[4,160,128]{2,1,0:T(8,128)}, u32[]{:S(2)}, u32[]{:S(2)}) %collective-permute-start.4) | collective-permute-done | bytes 327712 | tf_op jit(solution)/shard_map/ppermute | solution.py:322
  17.7 3.2 %collective-permute-done.5.refs_6_ = f32[4,160,128]{2,1,0:T(8,128)} collective-permute-done((f32[4,160,128]{2,1,0:T(8,128)S(1)}, f32[4,160,128]{2,1,0:T(8,128)}, u32[]{:S(2)}, u32[]{:S(2)}) %collective-permute-start.5) | collective-permute-done | bytes 327712 | tf_op jit(solution)/shard_map/ppermute | solution.py:322
  20.9 12.2 %shard_map.113 = (f32[16,160,128]{2,1,0:T(8,128)}, f32[16,160,128]{2,1,0:T(8,128)}, f32[16,160,128]{2,1,0:T(8,128)}, f32[16,160,128]{2,1,0:T(8,128)}, f32[16,160...) custom-call(s32[1]{0:T(128)} %bitcast.refs_0_.parity_ref, ...), custom_call_target="tpu_custom_call" | custom-call | tf_op jit(solution)/shard_map/pallas_call | solution.py:266
  33.2 3.0 %collective-permute-start.7 = (f32[4,160,128]{2,1,0:T(8,128)}, f32[4,160,128]{2,1,0:T(8,128)S(1)}, u32[]{:S(2)}, u32[]{:S(2)}) collective-permute-start(f32[4,160,128]{2,1,0:T(8,128)} %get-tuple-element.18), channel_id=1, source_target_pairs={{1,2},{2,1},{5,6},{6,5},{9,10},{10,9},{13,14},{14,13},{17,18},{18,... | collective-permute-start | bytes 983048 | tf_op jit(solution)/shard_map/ppermute | solution.py:322
  38.7 8.0 %shard_map.114 = f32[16,160,128]{2,1,0:T(8,128)} custom-call(s32[1]{0:T(128)} %bitcast.refs_0_.parity_ref, f32[4,160,128]{2,1,0:T(8,128)} %copy-done.5, f32[16,160,128]{2,1,0:T(8,128)} %bitcast.43, f32[4,160,128]{2,1,0:T(8,128)} %copy-done.8, f32[16,160,128]{2,1,0:T(8,128)} %b_ref.1, f32[16,160,128]{2,1,0:T(8,128)} %get-tuple-element.12.refs_5_.g0_ref, ...), custom_call_target="tpu_custom_call" | custom-call | tf_op jit(solution)/shard_map/pallas_call | solution.py:266
  47.6 10.1 %shard_map.115 = (f32[16,160,128]{2,1,0:T(8,128)}, f32[16,160,128]{2,1,0:T(8,128)}, f32[256,128]{1,0:T(8,128)}) custom-call(s32[1]{0:T(128)} %bitcast.refs_0_.parity_ref, f32[4,160,128]{2,1,0:T(8,128)} %copy-done.9, f32[16,160,128]{2,1,0:T(8,128)} %get-tuple-element.17.refs_2_, f32[4,160,128]{2,1,0:T(8,128)} %copy-done.10, f32[16,160,128]{2,1,0:T(8,128)} %b_ref.1, ...), custom_call_target="tpu_custom_call" | custom-call | tf_op jit(solution)/shard_map/pallas_call | solution.py:266
  59.3 2.4 %scatter_fusion = f32[327680]{0:T(1024)S(1)} fusion(f32[327680]{0:T(1024)S(1)} %bitcast.33, s32[256]{0:T(256)S(1)} %get-tuple-element.38, f32[256]{0:T(256)S(1)} %broadcast_select_fusion), kind=kCustom, calls=%fused_computation | custom fusion | flops 256 | bytes 4096 | tf_op jit(solution)/shard_map/scatter-add | solution.py:334
  61.9 2.2 %collective-permute-start.9 = (f32[4,160,128]{2,1,0:T(8,128)S(1)}, f32[4,160,128]{2,1,0:T(8,128)S(1)}, u32[]{:S(2)}, u32[]{:S(2)}) collective-permute-start(f32[4,160,128]{2,1,0:T(8,128)S(1)} %get-tuple-element.26), channel_id=1, source_target_pairs={{1,2},{2,1},{5,6},{6,5},{9,10},{10,9},{13,14},{14,13},{17,18},{18,... | collective-permute-start | bytes 983048 | tf_op jit(solution)/shard_map/ppermute | solution.py:322
  64.7 3.0 %collective-permute-done.8.lo_ref = f32[4,160,128]{2,1,0:T(8,128)S(1)} collective-permute-done((f32[4,160,128]{2,1,0:T(8,128)S(1)}, f32[4,160,128]{2,1,0:T(8,128)S(1)}, u32[]{:S(2)}, u32[]{:S(2)}) %collective-permute-start.8) | collective-permute-done | bytes 327712 | tf_op jit(solution)/shard_map/ppermute | solution.py:322
  67.8 2.2 %collective-permute-done.9.hi_ref = f32[4,160,128]{2,1,0:T(8,128)S(1)} collective-permute-done((f32[4,160,128]{2,1,0:T(8,128)S(1)}, f32[4,160,128]{2,1,0:T(8,128)S(1)}, u32[]{:S(2)}, u32[]{:S(2)}) %collective-permute-start.9) | collective-permute-done | bytes 327712 | tf_op jit(solution)/shard_map/ppermute | solution.py:322
  70.7 11.1 %shard_map.116 = f32[16,160,128]{2,1,0:T(8,128)} custom-call(s32[1]{0:T(128)} %bitcast.refs_0_.parity_ref, f32[4,160,128]{2,1,0:T(8,128)} %copy-done.6, f32[16,160,128]{2,1,0:T(8,128)} %bitcast.35, f32[4,160,128]{2,1,0:T(8,128)} %copy-done.7, f32[16,160,128]{2,1,0:T(8,128)} %b_ref.1, f32[16,160,128]{2,1,0:T(8,128)} %get-tuple-element.12.refs_5_.g0_ref, ...), custom_call_target="tpu_custom_call" | custom-call | tf_op jit(solution)/shard_map/pallas_call | solution.py:198
  81.8 2.5 %multiply_add_fusion = f32[16,160,128]{2,1,0:T(8,128)S(1)} fusion(f32[16,160,128]{2,1,0:T(8,128)} %shard_map.116, f32[16,160,128]{2,1,0:T(8,128)S(1)} %copy-done.4, f32[16,160,128]{2,1,0:T(8,128)} %bitcast.36, f32[16,160,128]{2,1,0:T(8,128)} %get-tuple-element.20), kind=kLoop, calls=%fused_computation.2 | loop fusion | flops 983040 | bytes 6553600 | tf_op jit(solution)/shard_map/add | solution.py:404
  84.3 4.5 %collective-permute-start.10 = (f32[1280,128]{1,0:T(8,128)S(1)}, f32[1280,128]{1,0:T(8,128)S(1)}, u32[]{:S(2)}, u32[]{:S(2)}) collective-permute-start(f32[1280,128]{1,0:T(8,128)S(1)} %constant_dynamic-slice_fusion.1), channel_id=1, source_target_pairs={{0,4},{4,0},{8,12},{12,8},{1,5},{5,1},{9,13},{13,9},{2,6},{6,2},{1... | collective-permute-start | bytes 1966088 | tf_op jit(solution)/shard_map/ppermute | solution.py:307
  88.9 1.7 %collective-permute-done.10 = f32[1280,128]{1,0:T(8,128)S(1)} collective-permute-done((f32[1280,128]{1,0:T(8,128)S(1)}, f32[1280,128]{1,0:T(8,128)S(1)}, u32[]{:S(2)}, u32[]{:S(2)}) %collective-permute-start.10) | collective-permute-done | bytes 655392 | tf_op jit(solution)/shard_map/ppermute | solution.py:307
  90.7 1.3 %collective-permute-start.11 = (f32[640,128]{1,0:T(8,128)S(1)}, f32[640,128]{1,0:T(8,128)S(1)}, u32[]{:S(2)}, u32[]{:S(2)}) collective-permute-start(f32[640,128]{1,0:T(8,128)S(1)} %constant_dynamic-slice_fusion), channel_id=1, source_target_pairs={{0,8},{4,12},{8,0},{12,4},{1,9},{5,13},{9,1},{13,5},{2,10},{6,14},... | collective-permute-start | bytes 983048 | tf_op jit(solution)/shard_map/ppermute | solution.py:307
  92.0 7.7 %collective-permute-done.11 = f32[640,128]{1,0:T(8,128)S(1)} collective-permute-done((f32[640,128]{1,0:T(8,128)S(1)}, f32[640,128]{1,0:T(8,128)S(1)}, u32[]{:S(2)}, u32[]{:S(2)}) %collective-permute-start.11) | collective-permute-done | bytes 327712 | tf_op jit(solution)/shard_map/ppermute | solution.py:307
  99.7 1.3 %collective-permute-start.12 = (f32[640,128]{1,0:T(8,128)S(1)}, f32[640,128]{1,0:T(8,128)S(1)}, u32[]{:S(2)}, u32[]{:S(2)}) collective-permute-start(f32[640,128]{1,0:T(8,128)S(1)} %add_multiply_fusion), channel_id=1, source_target_pairs={{0,8},{4,12},{8,0},{12,4},{1,9},{5,13},{9,1},{13,5},{2,10},{6,14},... | collective-permute-start | bytes 983048 | tf_op jit(solution)/shard_map/ppermute | solution.py:313
  101.0 6.8 %collective-permute-done.12 = f32[640,128]{1,0:T(8,128)S(1)} collective-permute-done((f32[640,128]{1,0:T(8,128)S(1)}, f32[640,128]{1,0:T(8,128)S(1)}, u32[]{:S(2)}, u32[]{:S(2)}) %collective-permute-start.12) | collective-permute-done | bytes 327712 | tf_op jit(solution)/shard_map/ppermute | solution.py:313
  107.8 2.2 %collective-permute-start.13 = (f32[1280,128]{1,0:T(8,128)S(1)}, f32[1280,128]{1,0:T(8,128)S(1)}, u32[]{:S(2)}, u32[]{:S(2)}) collective-permute-start(f32[1280,128]{1,0:T(8,128)S(1)} %maximum_select_fusion.1), channel_id=1, source_target_pairs={{0,4},{4,0},{8,12},{12,8},{1,5},{5,1},{9,13},{13,9},{2,6},{6,2},{1... | collective-permute-start | bytes 1966088 | tf_op jit(solution)/shard_map/ppermute | solution.py:313
  110.0 1.7 %collective-permute-done.13 = f32[1280,128]{1,0:T(8,128)S(1)} collective-permute-done((f32[1280,128]{1,0:T(8,128)S(1)}, f32[1280,128]{1,0:T(8,128)S(1)}, u32[]{:S(2)}, u32[]{:S(2)}) %collective-permute-start.13) | collective-permute-done | bytes 655392 | tf_op jit(solution)/shard_map/ppermute | solution.py:313
  (64 shorter events, 10.9 us)
Async XLA Ops:
  0.6 6.0 %copy-start = (f32[16,160,128]{2,1,0:T(8,128)S(1)}, f32[16,160,128]{2,1,0:T(8,128)}, u32[]{:S(2)}) copy-start(f32[16,160,128]{2,1,0:T(8,128)} %b_ref.1) | copy-start | bytes 3932164
  0.7 8.1 %copy-start.3 = (f32[1,16,160,128]{3,2,1,0:T(8,128)S(1)}, f32[1,16,160,128]{3,2,1,0:T(8,128)}, u32[]{:S(2)}) copy-start(f32[1,16,160,128]{3,2,1,0:T(8,128)} %param.14) | copy-start | bytes 3932164
  2.0 10.4 %collective-permute-start.2 = (f32[4,160,128]{2,1,0:T(8,128)S(1)}, f32[4,160,128]{2,1,0:T(8,128)S(1)}, u32[]{:S(2)}, u32[]{:S(2)}) collective-permute-start(f32[4,160,128]{2,1,0:T(8,128)S(1)} %get-tuple-element.31), channel_id=1, source_target_pairs={{0,1},{1,0},{2,3},{3,2},{4,5},{5,4},{6,7},{7,6},{8,9},{9,8},{10,11... | collective-permute-start | bytes 983048 | tf_op jit(solution)/shard_map/ppermute | solution.py:322
  2.0 8.4 %copy-start.13 = (s32[256]{0:T(256)S(1)}, s32[256]{0:T(256)}, u32[]{:S(2)}) copy-start(s32[256]{0:T(256)} %param.18) | copy-start | bytes 3076
  2.0 9.7 %copy-start.15 = (f32[2]{0:T(128)S(1)}, f32[2]{0:T(128)}, u32[]{:S(2)}) copy-start(f32[2]{0:T(128)} %param.16) | copy-start | bytes 28
  2.1 12.8 %collective-permute-start.3 = (f32[4,160,128]{2,1,0:T(8,128)S(1)}, f32[4,160,128]{2,1,0:T(8,128)S(1)}, u32[]{:S(2)}, u32[]{:S(2)}) collective-permute-start(f32[4,160,128]{2,1,0:T(8,128)S(1)} %get-tuple-element.30), channel_id=1, source_target_pairs={{1,2},{2,1},{5,6},{6,5},{9,10},{10,9},{13,14},{14,13},{17,18},{18,... | collective-permute-start | bytes 983048 | tf_op jit(solution)/shard_map/ppermute | solution.py:322
  6.7 11.0 %collective-permute-start.4 = (f32[4,160,128]{2,1,0:T(8,128)S(1)}, f32[4,160,128]{2,1,0:T(8,128)}, u32[]{:S(2)}, u32[]{:S(2)}) collective-permute-start(f32[4,160,128]{2,1,0:T(8,128)S(1)} %get-tuple-element.29), channel_id=1, source_target_pairs={{0,1},{1,0},{2,3},{3,2},{4,5},{5,4},{6,7},{7,6},{8,9},{9,8},{10,11... | collective-permute-start | bytes 983048 | tf_op jit(solution)/shard_map/ppermute | solution.py:322
  6.8 14.1 %collective-permute-start.5 = (f32[4,160,128]{2,1,0:T(8,128)S(1)}, f32[4,160,128]{2,1,0:T(8,128)}, u32[]{:S(2)}, u32[]{:S(2)}) collective-permute-start(f32[4,160,128]{2,1,0:T(8,128)S(1)} %get-tuple-element.28), channel_id=1, source_target_pairs={{1,2},{2,1},{5,6},{6,5},{9,10},{10,9},{13,14},{14,13},{17,18},{18,... | collective-permute-start | bytes 983048 | tf_op jit(solution)/shard_map/ppermute | solution.py:322
  8.8 29.0 %collective-permute-start = (f32[4,160,128]{2,1,0:T(8,128)S(1)}, f32[4,160,128]{2,1,0:T(8,128)S(1)}, u32[]{:S(2)}, u32[]{:S(2)}) collective-permute-start(f32[4,160,128]{2,1,0:T(8,128)S(1)} %get-tuple-element.33), channel_id=1, source_target_pairs={{0,1},{1,0},{2,3},{3,2},{4,5},{5,4},{6,7},{7,6},{8,9},{9,8},{10,11... | collective-permute-start | bytes 983048 | tf_op jit(solution)/shard_map/ppermute | solution.py:322
  12.3 8.5 %copy-start.11 = (f32[4,160,128]{2,1,0:T(8,128)}, f32[4,160,128]{2,1,0:T(8,128)S(1)}, u32[]{:S(2)}) copy-start(f32[4,160,128]{2,1,0:T(8,128)S(1)} %collective-permute-done.2.refs_1_) | copy-start | bytes 983044
  12.3 25.5 %collective-permute-start.1 = (f32[4,160,128]{2,1,0:T(8,128)S(1)}, f32[4,160,128]{2,1,0:T(8,128)S(1)}, u32[]{:S(2)}, u32[]{:S(2)}) collective-permute-start(f32[4,160,128]{2,1,0:T(8,128)S(1)} %get-tuple-element.32), channel_id=1, source_target_pairs={{1,2},{2,1},{5,6},{6,5},{9,10},{10,9},{13,14},{14,13},{17,18},{18,... | collective-permute-start | bytes 983048 | tf_op jit(solution)/shard_map/ppermute | solution.py:322
  14.8 6.1 %copy-start.12 = (f32[4,160,128]{2,1,0:T(8,128)}, f32[4,160,128]{2,1,0:T(8,128)S(1)}, u32[]{:S(2)}) copy-start(f32[4,160,128]{2,1,0:T(8,128)S(1)} %collective-permute-done.3.refs_3_) | copy-start | bytes 983044
  33.1 13.5 %collective-permute-start.6 = (f32[4,160,128]{2,1,0:T(8,128)}, f32[4,160,128]{2,1,0:T(8,128)S(1)}, u32[]{:S(2)}, u32[]{:S(2)}) collective-permute-start(f32[4,160,128]{2,1,0:T(8,128)} %get-tuple-element.16), channel_id=1, source_target_pairs={{0,1},{1,0},{2,3},{3,2},{4,5},{5,4},{6,7},{7,6},{8,9},{9,8},{10,11... | collective-permute-start | bytes 983048 | tf_op jit(solution)/shard_map/ppermute | solution.py:322
  33.2 13.5 %collective-permute-start.7 = (f32[4,160,128]{2,1,0:T(8,128)}, f32[4,160,128]{2,1,0:T(8,128)S(1)}, u32[]{:S(2)}, u32[]{:S(2)}) collective-permute-start(f32[4,160,128]{2,1,0:T(8,128)} %get-tuple-element.18), channel_id=1, source_target_pairs={{1,2},{2,1},{5,6},{6,5},{9,10},{10,9},{13,14},{14,13},{17,18},{18,... | collective-permute-start | bytes 983048 | tf_op jit(solution)/shard_map/ppermute | solution.py:322
  47.6 11.1 %copy-start.14 = (f32[2,256]{1,0:T(2,128)S(1)}, f32[2,256]{1,0:T(2,128)}, u32[]{:S(2)}) copy-start(f32[2,256]{1,0:T(2,128)} %param.19) | copy-start | bytes 6148
  47.6 11.7 %copy-start.1 = (f32[16,160,128]{2,1,0:T(8,128)S(1)}, f32[16,160,128]{2,1,0:T(8,128)}, u32[]{:S(2)}) copy-start(f32[16,160,128]{2,1,0:T(8,128)} %shard_map.114) | copy-start | bytes 3932164
  61.7 8.3 %copy-start.2 = (f32[327680]{0:T(1024)}, f32[327680]{0:T(1024)S(1)}, u32[]{:S(2)}) copy-start(f32[327680]{0:T(1024)S(1)} %scatter_fusion) | copy-start | bytes 3932164
  61.8 6.0 %collective-permute-start.8 = (f32[4,160,128]{2,1,0:T(8,128)S(1)}, f32[4,160,128]{2,1,0:T(8,128)S(1)}, u32[]{:S(2)}, u32[]{:S(2)}) collective-permute-start(f32[4,160,128]{2,1,0:T(8,128)S(1)} %get-tuple-element.27), channel_id=1, source_target_pairs={{0,1},{1,0},{2,3},{3,2},{4,5},{5,4},{6,7},{7,6},{8,9},{9,8},{10,11... | collective-permute-start | bytes 983048 | tf_op jit(solution)/shard_map/ppermute | solution.py:322
  61.9 8.1 %collective-permute-start.9 = (f32[4,160,128]{2,1,0:T(8,128)S(1)}, f32[4,160,128]{2,1,0:T(8,128)S(1)}, u32[]{:S(2)}, u32[]{:S(2)}) collective-permute-start(f32[4,160,128]{2,1,0:T(8,128)S(1)} %get-tuple-element.26), channel_id=1, source_target_pairs={{1,2},{2,1},{5,6},{6,5},{9,10},{10,9},{13,14},{14,13},{17,18},{18,... | collective-permute-start | bytes 983048 | tf_op jit(solution)/shard_map/ppermute | solution.py:322
  70.7 11.1 %copy-start.4 = (f32[16,160,128]{2,1,0:T(8,128)S(1)}, f32[16,160,128]{2,1,0:T(8,128)}, u32[]{:S(2)}) copy-start(f32[16,160,128]{2,1,0:T(8,128)} %get-tuple-element.21) | copy-start | bytes 3932164
  84.3 6.3 %collective-permute-start.10 = (f32[1280,128]{1,0:T(8,128)S(1)}, f32[1280,128]{1,0:T(8,128)S(1)}, u32[]{:S(2)}, u32[]{:S(2)}) collective-permute-start(f32[1280,128]{1,0:T(8,128)S(1)} %constant_dynamic-slice_fusion.1), channel_id=1, source_target_pairs={{0,4},{4,0},{8,12},{12,8},{1,5},{5,1},{9,13},{13,9},{2,6},{6,2},{1... | collective-permute-start | bytes 1966088 | tf_op jit(solution)/shard_map/ppermute | solution.py:307
  90.7 9.0 %collective-permute-start.11 = (f32[640,128]{1,0:T(8,128)S(1)}, f32[640,128]{1,0:T(8,128)S(1)}, u32[]{:S(2)}, u32[]{:S(2)}) collective-permute-start(f32[640,128]{1,0:T(8,128)S(1)} %constant_dynamic-slice_fusion), channel_id=1, source_target_pairs={{0,8},{4,12},{8,0},{12,4},{1,9},{5,13},{9,1},{13,5},{2,10},{6,14},... | collective-permute-start | bytes 983048 | tf_op jit(solution)/shard_map/ppermute | solution.py:307
  99.7 8.1 %collective-permute-start.12 = (f32[640,128]{1,0:T(8,128)S(1)}, f32[640,128]{1,0:T(8,128)S(1)}, u32[]{:S(2)}, u32[]{:S(2)}) collective-permute-start(f32[640,128]{1,0:T(8,128)S(1)} %add_multiply_fusion), channel_id=1, source_target_pairs={{0,8},{4,12},{8,0},{12,4},{1,9},{5,13},{9,1},{13,5},{2,10},{6,14},... | collective-permute-start | bytes 983048 | tf_op jit(solution)/shard_map/ppermute | solution.py:313
  107.8 3.9 %collective-permute-start.13 = (f32[1280,128]{1,0:T(8,128)S(1)}, f32[1280,128]{1,0:T(8,128)S(1)}, u32[]{:S(2)}, u32[]{:S(2)}) collective-permute-start(f32[1280,128]{1,0:T(8,128)S(1)} %maximum_select_fusion.1), channel_id=1, source_target_pairs={{0,4},{4,0},{8,12},{12,8},{1,5},{5,1},{9,13},{13,9},{2,6},{6,2},{1... | collective-permute-start | bytes 1966088 | tf_op jit(solution)/shard_map/ppermute | solution.py:313
  (6 other events, 6.1 us)

commit v16 on v15

--- a/solution.py
+++ b/solution.py
@@ -186,7 +186,7 @@
             new_ref[x, pl.ds(y, 1), :] = jnp.where(hit, line + amount_ref[r], line)
             return carry
 
-        lax.fori_loop(0, amount_ref.shape[0], add, 0)
+        lax.fori_loop(0, amount_ref.shape[0], add, 0, unroll=8)
 
 
 def apply_final(parity, lo, mid, hi, b, g, c, old, receivers, valid, amount, rows=40):

time: 113 us -> 112 us (level)
  Pallas kernels: 41.4 us -> 40.2 us
    pallas_call x1, Pallas kernels: 11.1 us -> 9.9 us  [apply_final(): pl.pallas_call(functools.partial(final_kernel, block=block, rows=rows), g...]
where the time goes in v16:
time: 112 us
  Pallas kernels  40.2 us (36%)
  waiting for transfers between devices  29.2 us (26%)
  starting transfers between devices  24.8 us (22%)
  other arithmetic  10.7 us (10%)
  local copies, waits for them, and re-layouts  5.12 us (5%)
  between operations  1.73 us (2%)
    pallas_call x3, Pallas kernels, apply_step(): pl.pallas_call(kernel, grid=(planes // block,), in_specs=in_specs, out_sp...  30.3 us
    ppermute x5, starting transfers between devices, swap_halos(): lax.ppermute(sends[1], axis, second)  14.3 us
    pallas_call x1, Pallas kernels, apply_final(): pl.pallas_call(functools.partial(final_kernel, block=block, rows=rows), g...  9.9 us
    ppermute x2, waiting for transfers between devices, reduce_members(): rows = keep + lax.ppermute(give, axis, pairs)  9.44 us
    ppermute x2, waiting for transfers between devices, reduce_members(): other = lax.ppermute(rows, axis, pairs)  8.52 us
    ppermute x5, waiting for transfers between devices, swap_halos(): lax.ppermute(sends[0], axis, first)  5.93 us
    ppermute x2, starting transfers between devices, reduce_members(): rows = keep + lax.ppermute(give, axis, pairs)  5.81 us
    ppermute x5, waiting for transfers between devices, swap_halos(): lax.ppermute(sends[1], axis, second)  5.36 us
  transfers between devices with their start and end apart: 14, of which 8 were waited for; matrix products, arithmetic and copies ran while one was open for 4% of the time, Pallas kernels for 18%

profile of v16, /device:TPU:9, one launch (start us, length us, event | category | flops | bytes accessed | tf_op | source)
XLA Modules:
  0.0 111.7 jit_solution(10998005913252860150)
XLA Ops:
  0.7 1.3 %dynamic-slice_bitcast_fusion = (f32[4,160,128]{2,1,0:T(8,128)S(1)}, f32[4,160,128]{2,1,0:T(8,128)S(1)}) fusion(f32[1,16,160,128]{3,2,1,0:T(8,128)} %param.12, s32[]{:T(128)S(6)} %select_n.135, s32[]{:T(128)S(6)} %select_n.134), kind=kLoop, calls=%fused_computation.6 | loop fusion | bytes 1310728 | tf_op jit(solution)/shard_map/dynamic_slice | solution.py:329
  2.1 4.6 %collective-permute-start.3 = (f32[4,160,128]{2,1,0:T(8,128)S(1)}, f32[4,160,128]{2,1,0:T(8,128)S(1)}, u32[]{:S(2)}, u32[]{:S(2)}) collective-permute-start(f32[4,160,128]{2,1,0:T(8,128)S(1)} %get-tuple-element.30), channel_id=1, source_target_pairs={{1,2},{2,1},{5,6},{6,5},{9,10},{10,9},{13,14},{14,13},{17,18},{18,... | collective-permute-start | bytes 983048 | tf_op jit(solution)/shard_map/ppermute | solution.py:322
  6.8 1.9 %collective-permute-start.5 = (f32[4,160,128]{2,1,0:T(8,128)S(1)}, f32[4,160,128]{2,1,0:T(8,128)}, u32[]{:S(2)}, u32[]{:S(2)}) collective-permute-start(f32[4,160,128]{2,1,0:T(8,128)S(1)} %get-tuple-element.28), channel_id=1, source_target_pairs={{1,2},{2,1},{5,6},{6,5},{9,10},{10,9},{13,14},{14,13},{17,18},{18,... | collective-permute-start | bytes 983048 | tf_op jit(solution)/shard_map/ppermute | solution.py:322
  12.3 2.5 %collective-permute-start.1 = (f32[4,160,128]{2,1,0:T(8,128)S(1)}, f32[4,160,128]{2,1,0:T(8,128)S(1)}, u32[]{:S(2)}, u32[]{:S(2)}) collective-permute-start(f32[4,160,128]{2,1,0:T(8,128)S(1)} %get-tuple-element.32), channel_id=1, source_target_pairs={{1,2},{2,1},{5,6},{6,5},{9,10},{10,9},{13,14},{14,13},{17,18},{18,... | collective-permute-start | bytes 983048 | tf_op jit(solution)/shard_map/ppermute | solution.py:322
  14.8 2.9 %collective-permute-done.4.refs_4_ = f32[4,160,128]{2,1,0:T(8,128)} collective-permute-done((f32[4,160,128]{2,1,0:T(8,128)S(1)}, f32[4,160,128]{2,1,0:T(8,128)}, u32[]{:S(2)}, u32[]{:S(2)}) %collective-permute-start.4) | collective-permute-done | bytes 327712 | tf_op jit(solution)/shard_map/ppermute | solution.py:322
  17.7 3.2 %collective-permute-done.5.refs_6_ = f32[4,160,128]{2,1,0:T(8,128)} collective-permute-done((f32[4,160,128]{2,1,0:T(8,128)S(1)}, f32[4,160,128]{2,1,0:T(8,128)}, u32[]{:S(2)}, u32[]{:S(2)}) %collective-permute-start.5) | collective-permute-done | bytes 327712 | tf_op jit(solution)/shard_map/ppermute | solution.py:322
  20.9 12.2 %shard_map.113 = (f32[16,160,128]{2,1,0:T(8,128)}, f32[16,160,128]{2,1,0:T(8,128)}, f32[16,160,128]{2,1,0:T(8,128)}, f32[16,160,128]{2,1,0:T(8,128)}, f32[16,160...) custom-call(s32[1]{0:T(128)} %bitcast.refs_0_.parity_ref, ...), custom_call_target="tpu_custom_call" | custom-call | tf_op jit(solution)/shard_map/pallas_call | solution.py:266
  33.2 3.0 %collective-permute-start.7 = (f32[4,160,128]{2,1,0:T(8,128)}, f32[4,160,128]{2,1,0:T(8,128)S(1)}, u32[]{:S(2)}, u32[]{:S(2)}) collective-permute-start(f32[4,160,128]{2,1,0:T(8,128)} %get-tuple-element.18), channel_id=1, source_target_pairs={{1,2},{2,1},{5,6},{6,5},{9,10},{10,9},{13,14},{14,13},{17,18},{18,... | collective-permute-start | bytes 983048 | tf_op jit(solution)/shard_map/ppermute | solution.py:322
  38.7 8.0 %shard_map.114 = f32[16,160,128]{2,1,0:T(8,128)} custom-call(s32[1]{0:T(128)} %bitcast.refs_0_.parity_ref, f32[4,160,128]{2,1,0:T(8,128)} %copy-done.5, f32[16,160,128]{2,1,0:T(8,128)} %bitcast.43, f32[4,160,128]{2,1,0:T(8,128)} %copy-done.8, f32[16,160,128]{2,1,0:T(8,128)} %b_ref.1, f32[16,160,128]{2,1,0:T(8,128)} %get-tuple-element.12.refs_5_.g0_ref, ...), custom_call_target="tpu_custom_call" | custom-call | tf_op jit(solution)/shard_map/pallas_call | solution.py:266
  47.6 10.1 %shard_map.115 = (f32[16,160,128]{2,1,0:T(8,128)}, f32[16,160,128]{2,1,0:T(8,128)}, f32[256,128]{1,0:T(8,128)}) custom-call(s32[1]{0:T(128)} %bitcast.refs_0_.parity_ref, f32[4,160,128]{2,1,0:T(8,128)} %copy-done.9, f32[16,160,128]{2,1,0:T(8,128)} %get-tuple-element.17.refs_2_, f32[4,160,128]{2,1,0:T(8,128)} %copy-done.10, f32[16,160,128]{2,1,0:T(8,128)} %b_ref.1, ...), custom_call_target="tpu_custom_call" | custom-call | tf_op jit(solution)/shard_map/pallas_call | solution.py:266
  59.3 2.4 %scatter_fusion = f32[327680]{0:T(1024)S(1)} fusion(f32[327680]{0:T(1024)S(1)} %bitcast.33, s32[256]{0:T(256)S(1)} %get-tuple-element.38, f32[256]{0:T(256)S(1)} %broadcast_select_fusion), kind=kCustom, calls=%fused_computation | custom fusion | flops 256 | bytes 4096 | tf_op jit(solution)/shard_map/scatter-add | solution.py:334
  61.9 2.2 %collective-permute-start.9 = (f32[4,160,128]{2,1,0:T(8,128)S(1)}, f32[4,160,128]{2,1,0:T(8,128)S(1)}, u32[]{:S(2)}, u32[]{:S(2)}) collective-permute-start(f32[4,160,128]{2,1,0:T(8,128)S(1)} %get-tuple-element.26), channel_id=1, source_target_pairs={{1,2},{2,1},{5,6},{6,5},{9,10},{10,9},{13,14},{14,13},{17,18},{18,... | collective-permute-start | bytes 983048 | tf_op jit(solution)/shard_map/ppermute | solution.py:322
  64.7 3.0 %collective-permute-done.8.lo_ref = f32[4,160,128]{2,1,0:T(8,128)S(1)} collective-permute-done((f32[4,160,128]{2,1,0:T(8,128)S(1)}, f32[4,160,128]{2,1,0:T(8,128)S(1)}, u32[]{:S(2)}, u32[]{:S(2)}) %collective-permute-start.8) | collective-permute-done | bytes 327712 | tf_op jit(solution)/shard_map/ppermute | solution.py:322
  67.8 2.2 %collective-permute-done.9.hi_ref = f32[4,160,128]{2,1,0:T(8,128)S(1)} collective-permute-done((f32[4,160,128]{2,1,0:T(8,128)S(1)}, f32[4,160,128]{2,1,0:T(8,128)S(1)}, u32[]{:S(2)}, u32[]{:S(2)}) %collective-permute-start.9) | collective-permute-done | bytes 327712 | tf_op jit(solution)/shard_map/ppermute | solution.py:322
  70.7 9.9 %shard_map.116 = f32[16,160,128]{2,1,0:T(8,128)} custom-call(s32[1]{0:T(128)} %bitcast.refs_0_.parity_ref, f32[4,160,128]{2,1,0:T(8,128)} %copy-done.6, f32[16,160,128]{2,1,0:T(8,128)} %bitcast.35, f32[4,160,128]{2,1,0:T(8,128)} %copy-done.7, f32[16,160,128]{2,1,0:T(8,128)} %b_ref.1, f32[16,160,128]{2,1,0:T(8,128)} %get-tuple-element.12.refs_5_.g0_ref, ...), custom_call_target="tpu_custom_call" | custom-call | tf_op jit(solution)/shard_map/pallas_call | solution.py:198
  80.6 2.5 %multiply_add_fusion = f32[16,160,128]{2,1,0:T(8,128)S(1)} fusion(f32[16,160,128]{2,1,0:T(8,128)} %shard_map.116, f32[16,160,128]{2,1,0:T(8,128)S(1)} %copy-done.4, f32[16,160,128]{2,1,0:T(8,128)} %bitcast.36, f32[16,160,128]{2,1,0:T(8,128)} %get-tuple-element.20), kind=kLoop, calls=%fused_computation.2 | loop fusion | flops 983040 | bytes 6553600 | tf_op jit(solution)/shard_map/add | solution.py:404
  83.1 4.5 %collective-permute-start.10 = (f32[1280,128]{1,0:T(8,128)S(1)}, f32[1280,128]{1,0:T(8,128)S(1)}, u32[]{:S(2)}, u32[]{:S(2)}) collective-permute-start(f32[1280,128]{1,0:T(8,128)S(1)} %constant_dynamic-slice_fusion.1), channel_id=1, source_target_pairs={{0,4},{4,0},{8,12},{12,8},{1,5},{5,1},{9,13},{13,9},{2,6},{6,2},{1... | collective-permute-start | bytes 1966088 | tf_op jit(solution)/shard_map/ppermute | solution.py:307
  87.6 1.7 %collective-permute-done.10 = f32[1280,128]{1,0:T(8,128)S(1)} collective-permute-done((f32[1280,128]{1,0:T(8,128)S(1)}, f32[1280,128]{1,0:T(8,128)S(1)}, u32[]{:S(2)}, u32[]{:S(2)}) %collective-permute-start.10) | collective-permute-done | bytes 655392 | tf_op jit(solution)/shard_map/ppermute | solution.py:307
  89.5 1.3 %collective-permute-start.11 = (f32[640,128]{1,0:T(8,128)S(1)}, f32[640,128]{1,0:T(8,128)S(1)}, u32[]{:S(2)}, u32[]{:S(2)}) collective-permute-start(f32[640,128]{1,0:T(8,128)S(1)} %constant_dynamic-slice_fusion), channel_id=1, source_target_pairs={{0,8},{4,12},{8,0},{12,4},{1,9},{5,13},{9,1},{13,5},{2,10},{6,14},... | collective-permute-start | bytes 983048 | tf_op jit(solution)/shard_map/ppermute | solution.py:307
  90.7 7.7 %collective-permute-done.11 = f32[640,128]{1,0:T(8,128)S(1)} collective-permute-done((f32[640,128]{1,0:T(8,128)S(1)}, f32[640,128]{1,0:T(8,128)S(1)}, u32[]{:S(2)}, u32[]{:S(2)}) %collective-permute-start.11) | collective-permute-done | bytes 327712 | tf_op jit(solution)/shard_map/ppermute | solution.py:307
  98.5 1.3 %collective-permute-start.12 = (f32[640,128]{1,0:T(8,128)S(1)}, f32[640,128]{1,0:T(8,128)S(1)}, u32[]{:S(2)}, u32[]{:S(2)}) collective-permute-start(f32[640,128]{1,0:T(8,128)S(1)} %add_multiply_fusion), channel_id=1, source_target_pairs={{0,8},{4,12},{8,0},{12,4},{1,9},{5,13},{9,1},{13,5},{2,10},{6,14},... | collective-permute-start | bytes 983048 | tf_op jit(solution)/shard_map/ppermute | solution.py:313
  99.8 6.8 %collective-permute-done.12 = f32[640,128]{1,0:T(8,128)S(1)} collective-permute-done((f32[640,128]{1,0:T(8,128)S(1)}, f32[640,128]{1,0:T(8,128)S(1)}, u32[]{:S(2)}, u32[]{:S(2)}) %collective-permute-start.12) | collective-permute-done | bytes 327712 | tf_op jit(solution)/shard_map/ppermute | solution.py:313
  106.6 2.2 %collective-permute-start.13 = (f32[1280,128]{1,0:T(8,128)S(1)}, f32[1280,128]{1,0:T(8,128)S(1)}, u32[]{:S(2)}, u32[]{:S(2)}) collective-permute-start(f32[1280,128]{1,0:T(8,128)S(1)} %maximum_select_fusion.1), channel_id=1, source_target_pairs={{0,4},{4,0},{8,12},{12,8},{1,5},{5,1},{9,13},{13,9},{2,6},{6,2},{1... | collective-permute-start | bytes 1966088 | tf_op jit(solution)/shard_map/ppermute | solution.py:313
  108.8 1.7 %collective-permute-done.13 = f32[1280,128]{1,0:T(8,128)S(1)} collective-permute-done((f32[1280,128]{1,0:T(8,128)S(1)}, f32[1280,128]{1,0:T(8,128)S(1)}, u32[]{:S(2)}, u32[]{:S(2)}) %collective-permute-start.13) | collective-permute-done | bytes 655392 | tf_op jit(solution)/shard_map/ppermute | solution.py:313
  (64 shorter events, 10.9 us)
Async XLA Ops:
  0.6 6.0 %copy-start = (f32[16,160,128]{2,1,0:T(8,128)S(1)}, f32[16,160,128]{2,1,0:T(8,128)}, u32[]{:S(2)}) copy-start(f32[16,160,128]{2,1,0:T(8,128)} %b_ref.1) | copy-start | bytes 3932164
  0.7 8.1 %copy-start.3 = (f32[1,16,160,128]{3,2,1,0:T(8,128)S(1)}, f32[1,16,160,128]{3,2,1,0:T(8,128)}, u32[]{:S(2)}) copy-start(f32[1,16,160,128]{3,2,1,0:T(8,128)} %param.14) | copy-start | bytes 3932164
  2.0 10.4 %collective-permute-start.2 = (f32[4,160,128]{2,1,0:T(8,128)S(1)}, f32[4,160,128]{2,1,0:T(8,128)S(1)}, u32[]{:S(2)}, u32[]{:S(2)}) collective-permute-start(f32[4,160,128]{2,1,0:T(8,128)S(1)} %get-tuple-element.31), channel_id=1, source_target_pairs={{0,1},{1,0},{2,3},{3,2},{4,5},{5,4},{6,7},{7,6},{8,9},{9,8},{10,11... | collective-permute-start | bytes 983048 | tf_op jit(solution)/shard_map/ppermute | solution.py:322
  2.0 8.4 %copy-start.13 = (s32[256]{0:T(256)S(1)}, s32[256]{0:T(256)}, u32[]{:S(2)}) copy-start(s32[256]{0:T(256)} %param.18) | copy-start | bytes 3076
  2.0 9.7 %copy-start.15 = (f32[2]{0:T(128)S(1)}, f32[2]{0:T(128)}, u32[]{:S(2)}) copy-start(f32[2]{0:T(128)} %param.16) | copy-start | bytes 28
  2.1 12.8 %collective-permute-start.3 = (f32[4,160,128]{2,1,0:T(8,128)S(1)}, f32[4,160,128]{2,1,0:T(8,128)S(1)}, u32[]{:S(2)}, u32[]{:S(2)}) collective-permute-start(f32[4,160,128]{2,1,0:T(8,128)S(1)} %get-tuple-element.30), channel_id=1, source_target_pairs={{1,2},{2,1},{5,6},{6,5},{9,10},{10,9},{13,14},{14,13},{17,18},{18,... | collective-permute-start | bytes 983048 | tf_op jit(solution)/shard_map/ppermute | solution.py:322
  6.7 11.0 %collective-permute-start.4 = (f32[4,160,128]{2,1,0:T(8,128)S(1)}, f32[4,160,128]{2,1,0:T(8,128)}, u32[]{:S(2)}, u32[]{:S(2)}) collective-permute-start(f32[4,160,128]{2,1,0:T(8,128)S(1)} %get-tuple-element.29), channel_id=1, source_target_pairs={{0,1},{1,0},{2,3},{3,2},{4,5},{5,4},{6,7},{7,6},{8,9},{9,8},{10,11... | collective-permute-start | bytes 983048 | tf_op jit(solution)/shard_map/ppermute | solution.py:322
  6.8 14.1 %collective-permute-start.5 = (f32[4,160,128]{2,1,0:T(8,128)S(1)}, f32[4,160,128]{2,1,0:T(8,128)}, u32[]{:S(2)}, u32[]{:S(2)}) collective-permute-start(f32[4,160,128]{2,1,0:T(8,128)S(1)} %get-tuple-element.28), channel_id=1, source_target_pairs={{1,2},{2,1},{5,6},{6,5},{9,10},{10,9},{13,14},{14,13},{17,18},{18,... | collective-permute-start | bytes 983048 | tf_op jit(solution)/shard_map/ppermute | solution.py:322
  8.8 29.0 %collective-permute-start = (f32[4,160,128]{2,1,0:T(8,128)S(1)}, f32[4,160,128]{2,1,0:T(8,128)S(1)}, u32[]{:S(2)}, u32[]{:S(2)}) collective-permute-start(f32[4,160,128]{2,1,0:T(8,128)S(1)} %get-tuple-element.33), channel_id=1, source_target_pairs={{0,1},{1,0},{2,3},{3,2},{4,5},{5,4},{6,7},{7,6},{8,9},{9,8},{10,11... | collective-permute-start | bytes 983048 | tf_op jit(solution)/shard_map/ppermute | solution.py:322
  12.3 8.5 %copy-start.11 = (f32[4,160,128]{2,1,0:T(8,128)}, f32[4,160,128]{2,1,0:T(8,128)S(1)}, u32[]{:S(2)}) copy-start(f32[4,160,128]{2,1,0:T(8,128)S(1)} %collective-permute-done.2.refs_1_) | copy-start | bytes 983044
  12.3 25.5 %collective-permute-start.1 = (f32[4,160,128]{2,1,0:T(8,128)S(1)}, f32[4,160,128]{2,1,0:T(8,128)S(1)}, u32[]{:S(2)}, u32[]{:S(2)}) collective-permute-start(f32[4,160,128]{2,1,0:T(8,128)S(1)} %get-tuple-element.32), channel_id=1, source_target_pairs={{1,2},{2,1},{5,6},{6,5},{9,10},{10,9},{13,14},{14,13},{17,18},{18,... | collective-permute-start | bytes 983048 | tf_op jit(solution)/shard_map/ppermute | solution.py:322
  14.8 6.1 %copy-start.12 = (f32[4,160,128]{2,1,0:T(8,128)}, f32[4,160,128]{2,1,0:T(8,128)S(1)}, u32[]{:S(2)}) copy-start(f32[4,160,128]{2,1,0:T(8,128)S(1)} %collective-permute-done.3.refs_3_) | copy-start | bytes 983044
  33.1 13.5 %collective-permute-start.6 = (f32[4,160,128]{2,1,0:T(8,128)}, f32[4,160,128]{2,1,0:T(8,128)S(1)}, u32[]{:S(2)}, u32[]{:S(2)}) collective-permute-start(f32[4,160,128]{2,1,0:T(8,128)} %get-tuple-element.16), channel_id=1, source_target_pairs={{0,1},{1,0},{2,3},{3,2},{4,5},{5,4},{6,7},{7,6},{8,9},{9,8},{10,11... | collective-permute-start | bytes 983048 | tf_op jit(solution)/shard_map/ppermute | solution.py:322
  33.2 13.5 %collective-permute-start.7 = (f32[4,160,128]{2,1,0:T(8,128)}, f32[4,160,128]{2,1,0:T(8,128)S(1)}, u32[]{:S(2)}, u32[]{:S(2)}) collective-permute-start(f32[4,160,128]{2,1,0:T(8,128)} %get-tuple-element.18), channel_id=1, source_target_pairs={{1,2},{2,1},{5,6},{6,5},{9,10},{10,9},{13,14},{14,13},{17,18},{18,... | collective-permute-start | bytes 983048 | tf_op jit(solution)/shard_map/ppermute | solution.py:322
  47.6 11.1 %copy-start.14 = (f32[2,256]{1,0:T(2,128)S(1)}, f32[2,256]{1,0:T(2,128)}, u32[]{:S(2)}) copy-start(f32[2,256]{1,0:T(2,128)} %param.19) | copy-start | bytes 6148
  47.6 11.7 %copy-start.1 = (f32[16,160,128]{2,1,0:T(8,128)S(1)}, f32[16,160,128]{2,1,0:T(8,128)}, u32[]{:S(2)}) copy-start(f32[16,160,128]{2,1,0:T(8,128)} %shard_map.114) | copy-start | bytes 3932164
  61.7 8.3 %copy-start.2 = (f32[327680]{0:T(1024)}, f32[327680]{0:T(1024)S(1)}, u32[]{:S(2)}) copy-start(f32[327680]{0:T(1024)S(1)} %scatter_fusion) | copy-start | bytes 3932164
  61.8 6.0 %collective-permute-start.8 = (f32[4,160,128]{2,1,0:T(8,128)S(1)}, f32[4,160,128]{2,1,0:T(8,128)S(1)}, u32[]{:S(2)}, u32[]{:S(2)}) collective-permute-start(f32[4,160,128]{2,1,0:T(8,128)S(1)} %get-tuple-element.27), channel_id=1, source_target_pairs={{0,1},{1,0},{2,3},{3,2},{4,5},{5,4},{6,7},{7,6},{8,9},{9,8},{10,11... | collective-permute-start | bytes 983048 | tf_op jit(solution)/shard_map/ppermute | solution.py:322
  61.9 8.1 %collective-permute-start.9 = (f32[4,160,128]{2,1,0:T(8,128)S(1)}, f32[4,160,128]{2,1,0:T(8,128)S(1)}, u32[]{:S(2)}, u32[]{:S(2)}) collective-permute-start(f32[4,160,128]{2,1,0:T(8,128)S(1)} %get-tuple-element.26), channel_id=1, source_target_pairs={{1,2},{2,1},{5,6},{6,5},{9,10},{10,9},{13,14},{14,13},{17,18},{18,... | collective-permute-start | bytes 983048 | tf_op jit(solution)/shard_map/ppermute | solution.py:322
  70.7 9.9 %copy-start.4 = (f32[16,160,128]{2,1,0:T(8,128)S(1)}, f32[16,160,128]{2,1,0:T(8,128)}, u32[]{:S(2)}) copy-start(f32[16,160,128]{2,1,0:T(8,128)} %get-tuple-element.21) | copy-start | bytes 3932164
  83.1 6.3 %collective-permute-start.10 = (f32[1280,128]{1,0:T(8,128)S(1)}, f32[1280,128]{1,0:T(8,128)S(1)}, u32[]{:S(2)}, u32[]{:S(2)}) collective-permute-start(f32[1280,128]{1,0:T(8,128)S(1)} %constant_dynamic-slice_fusion.1), channel_id=1, source_target_pairs={{0,4},{4,0},{8,12},{12,8},{1,5},{5,1},{9,13},{13,9},{2,6},{6,2},{1... | collective-permute-start | bytes 1966088 | tf_op jit(solution)/shard_map/ppermute | solution.py:307
  89.5 9.0 %collective-permute-start.11 = (f32[640,128]{1,0:T(8,128)S(1)}, f32[640,128]{1,0:T(8,128)S(1)}, u32[]{:S(2)}, u32[]{:S(2)}) collective-permute-start(f32[640,128]{1,0:T(8,128)S(1)} %constant_dynamic-slice_fusion), channel_id=1, source_target_pairs={{0,8},{4,12},{8,0},{12,4},{1,9},{5,13},{9,1},{13,5},{2,10},{6,14},... | collective-permute-start | bytes 983048 | tf_op jit(solution)/shard_map/ppermute | solution.py:307
  98.5 8.1 %collective-permute-start.12 = (f32[640,128]{1,0:T(8,128)S(1)}, f32[640,128]{1,0:T(8,128)S(1)}, u32[]{:S(2)}, u32[]{:S(2)}) collective-permute-start(f32[640,128]{1,0:T(8,128)S(1)} %add_multiply_fusion), channel_id=1, source_target_pairs={{0,8},{4,12},{8,0},{12,4},{1,9},{5,13},{9,1},{13,5},{2,10},{6,14},... | collective-permute-start | bytes 983048 | tf_op jit(solution)/shard_map/ppermute | solution.py:313
  106.6 3.9 %collective-permute-start.13 = (f32[1280,128]{1,0:T(8,128)S(1)}, f32[1280,128]{1,0:T(8,128)S(1)}, u32[]{:S(2)}, u32[]{:S(2)}) collective-permute-start(f32[1280,128]{1,0:T(8,128)S(1)} %maximum_select_fusion.1), channel_id=1, source_target_pairs={{0,4},{4,0},{8,12},{12,8},{1,5},{5,1},{9,13},{13,9},{2,6},{6,2},{1... | collective-permute-start | bytes 1966088 | tf_op jit(solution)/shard_map/ppermute | solution.py:313
  (6 other events, 6.1 us)

commit v17 on v16

--- a/solution.py
+++ b/solution.py
@@ -186,7 +186,7 @@
             new_ref[x, pl.ds(y, 1), :] = jnp.where(hit, line + amount_ref[r], line)
             return carry
 
-        lax.fori_loop(0, amount_ref.shape[0], add, 0, unroll=8)
+        lax.fori_loop(0, amount_ref.shape[0], add, 0, unroll=32)
 
 
 def apply_final(parity, lo, mid, hi, b, g, c, old, receivers, valid, amount, rows=40):

time: 112 us -> 112 us (level)
  no operation moved by 1% of the time
where the time goes in v17:
time: 112 us
  Pallas kernels  40.1 us (36%)
  waiting for transfers between devices  29.2 us (26%)
  starting transfers between devices  24.8 us (22%)
  other arithmetic  10.7 us (10%)
  local copies, waits for them, and re-layouts  5.12 us (5%)
  between operations  1.73 us (2%)
    pallas_call x3, Pallas kernels, apply_step(): pl.pallas_call(kernel, grid=(planes // block,), in_specs=in_specs, out_sp...  30.3 us
    ppermute x5, starting transfers between devices, swap_halos(): lax.ppermute(sends[1], axis, second)  14.3 us
    pallas_call x1, Pallas kernels, apply_final(): pl.pallas_call(functools.partial(final_kernel, block=block, rows=rows), g...  9.88 us
    ppermute x2, waiting for transfers between devices, reduce_members(): rows = keep + lax.ppermute(give, axis, pairs)  9.44 us
    ppermute x2, waiting for transfers between devices, reduce_members(): other = lax.ppermute(rows, axis, pairs)  8.52 us
    ppermute x5, waiting for transfers between devices, swap_halos(): lax.ppermute(sends[0], axis, first)  5.93 us
    ppermute x2, starting transfers between devices, reduce_members(): rows = keep + lax.ppermute(give, axis, pairs)  5.81 us
    ppermute x5, waiting for transfers between devices, swap_halos(): lax.ppermute(sends[1], axis, second)  5.36 us
  transfers between devices with their start and end apart: 14, of which 8 were waited for; matrix products, arithmetic and copies ran while one was open for 4% of the time, Pallas kernels for 18%

profile of v17, /device:TPU:9, one launch (start us, length us, event | category | flops | bytes accessed | tf_op | source)
XLA Modules:
  0.0 111.7 jit_solution(4289726643587520402)
XLA Ops:
  0.7 1.3 %dynamic-slice_bitcast_fusion = (f32[4,160,128]{2,1,0:T(8,128)S(1)}, f32[4,160,128]{2,1,0:T(8,128)S(1)}) fusion(f32[1,16,160,128]{3,2,1,0:T(8,128)} %param.12, s32[]{:T(128)S(6)} %select_n.135, s32[]{:T(128)S(6)} %select_n.134), kind=kLoop, calls=%fused_computation.6 | loop fusion | bytes 1310728 | tf_op jit(solution)/shard_map/dynamic_slice | solution.py:329
  2.1 4.6 %collective-permute-start.3 = (f32[4,160,128]{2,1,0:T(8,128)S(1)}, f32[4,160,128]{2,1,0:T(8,128)S(1)}, u32[]{:S(2)}, u32[]{:S(2)}) collective-permute-start(f32[4,160,128]{2,1,0:T(8,128)S(1)} %get-tuple-element.30), channel_id=1, source_target_pairs={{1,2},{2,1},{5,6},{6,5},{9,10},{10,9},{13,14},{14,13},{17,18},{18,... | collective-permute-start | bytes 983048 | tf_op jit(solution)/shard_map/ppermute | solution.py:322
  6.8 1.9 %collective-permute-start.5 = (f32[4,160,128]{2,1,0:T(8,128)S(1)}, f32[4,160,128]{2,1,0:T(8,128)}, u32[]{:S(2)}, u32[]{:S(2)}) collective-permute-start(f32[4,160,128]{2,1,0:T(8,128)S(1)} %get-tuple-element.28), channel_id=1, source_target_pairs={{1,2},{2,1},{5,6},{6,5},{9,10},{10,9},{13,14},{14,13},{17,18},{18,... | collective-permute-start | bytes 983048 | tf_op jit(solution)/shard_map/ppermute | solution.py:322
  12.3 2.5 %collective-permute-start.1 = (f32[4,160,128]{2,1,0:T(8,128)S(1)}, f32[4,160,128]{2,1,0:T(8,128)S(1)}, u32[]{:S(2)}, u32[]{:S(2)}) collective-permute-start(f32[4,160,128]{2,1,0:T(8,128)S(1)} %get-tuple-element.32), channel_id=1, source_target_pairs={{1,2},{2,1},{5,6},{6,5},{9,10},{10,9},{13,14},{14,13},{17,18},{18,... | collective-permute-start | bytes 983048 | tf_op jit(solution)/shard_map/ppermute | solution.py:322
  14.8 2.9 %collective-permute-done.4.refs_4_ = f32[4,160,128]{2,1,0:T(8,128)} collective-permute-done((f32[4,160,128]{2,1,0:T(8,128)S(1)}, f32[4,160,128]{2,1,0:T(8,128)}, u32[]{:S(2)}, u32[]{:S(2)}) %collective-permute-start.4) | collective-permute-done | bytes 327712 | tf_op jit(solution)/shard_map/ppermute | solution.py:322
  17.7 3.2 %collective-permute-done.5.refs_6_ = f32[4,160,128]{2,1,0:T(8,128)} collective-permute-done((f32[4,160,128]{2,1,0:T(8,128)S(1)}, f32[4,160,128]{2,1,0:T(8,128)}, u32[]{:S(2)}, u32[]{:S(2)}) %collective-permute-start.5) | collective-permute-done | bytes 327712 | tf_op jit(solution)/shard_map/ppermute | solution.py:322
  20.9 12.2 %shard_map.113 = (f32[16,160,128]{2,1,0:T(8,128)}, f32[16,160,128]{2,1,0:T(8,128)}, f32[16,160,128]{2,1,0:T(8,128)}, f32[16,160,128]{2,1,0:T(8,128)}, f32[16,160...) custom-call(s32[1]{0:T(128)} %bitcast.refs_0_.parity_ref, ...), custom_call_target="tpu_custom_call" | custom-call | tf_op jit(solution)/shard_map/pallas_call | solution.py:266
  33.2 3.0 %collective-permute-start.7 = (f32[4,160,128]{2,1,0:T(8,128)}, f32[4,160,128]{2,1,0:T(8,128)S(1)}, u32[]{:S(2)}, u32[]{:S(2)}) collective-permute-start(f32[4,160,128]{2,1,0:T(8,128)} %get-tuple-element.18), channel_id=1, source_target_pairs={{1,2},{2,1},{5,6},{6,5},{9,10},{10,9},{13,14},{14,13},{17,18},{18,... | collective-permute-start | bytes 983048 | tf_op jit(solution)/shard_map/ppermute | solution.py:322
  38.7 8.0 %shard_map.114 = f32[16,160,128]{2,1,0:T(8,128)} custom-call(s32[1]{0:T(128)} %bitcast.refs_0_.parity_ref, f32[4,160,128]{2,1,0:T(8,128)} %copy-done.5, f32[16,160,128]{2,1,0:T(8,128)} %bitcast.43, f32[4,160,128]{2,1,0:T(8,128)} %copy-done.8, f32[16,160,128]{2,1,0:T(8,128)} %b_ref.1, f32[16,160,128]{2,1,0:T(8,128)} %get-tuple-element.12.refs_5_.g0_ref, ...), custom_call_target="tpu_custom_call" | custom-call | tf_op jit(solution)/shard_map/pallas_call | solution.py:266
  47.6 10.1 %shard_map.115 = (f32[16,160,128]{2,1,0:T(8,128)}, f32[16,160,128]{2,1,0:T(8,128)}, f32[256,128]{1,0:T(8,128)}) custom-call(s32[1]{0:T(128)} %bitcast.refs_0_.parity_ref, f32[4,160,128]{2,1,0:T(8,128)} %copy-done.9, f32[16,160,128]{2,1,0:T(8,128)} %get-tuple-element.17.refs_2_, f32[4,160,128]{2,1,0:T(8,128)} %copy-done.10, f32[16,160,128]{2,1,0:T(8,128)} %b_ref.1, ...), custom_call_target="tpu_custom_call" | custom-call | tf_op jit(solution)/shard_map/pallas_call | solution.py:266
  59.3 2.4 %scatter_fusion = f32[327680]{0:T(1024)S(1)} fusion(f32[327680]{0:T(1024)S(1)} %bitcast.33, s32[256]{0:T(256)S(1)} %get-tuple-element.38, f32[256]{0:T(256)S(1)} %broadcast_select_fusion), kind=kCustom, calls=%fused_computation | custom fusion | flops 256 | bytes 4096 | tf_op jit(solution)/shard_map/scatter-add | solution.py:334
  61.9 2.2 %collective-permute-start.9 = (f32[4,160,128]{2,1,0:T(8,128)S(1)}, f32[4,160,128]{2,1,0:T(8,128)S(1)}, u32[]{:S(2)}, u32[]{:S(2)}) collective-permute-start(f32[4,160,128]{2,1,0:T(8,128)S(1)} %get-tuple-element.26), channel_id=1, source_target_pairs={{1,2},{2,1},{5,6},{6,5},{9,10},{10,9},{13,14},{14,13},{17,18},{18,... | collective-permute-start | bytes 983048 | tf_op jit(solution)/shard_map/ppermute | solution.py:322
  64.7 3.0 %collective-permute-done.8.lo_ref = f32[4,160,128]{2,1,0:T(8,128)S(1)} collective-permute-done((f32[4,160,128]{2,1,0:T(8,128)S(1)}, f32[4,160,128]{2,1,0:T(8,128)S(1)}, u32[]{:S(2)}, u32[]{:S(2)}) %collective-permute-start.8) | collective-permute-done | bytes 327712 | tf_op jit(solution)/shard_map/ppermute | solution.py:322
  67.8 2.2 %collective-permute-done.9.hi_ref = f32[4,160,128]{2,1,0:T(8,128)S(1)} collective-permute-done((f32[4,160,128]{2,1,0:T(8,128)S(1)}, f32[4,160,128]{2,1,0:T(8,128)S(1)}, u32[]{:S(2)}, u32[]{:S(2)}) %collective-permute-start.9) | collective-permute-done | bytes 327712 | tf_op jit(solution)/shard_map/ppermute | solution.py:322
  70.7 9.9 %shard_map.116 = f32[16,160,128]{2,1,0:T(8,128)} custom-call(s32[1]{0:T(128)} %bitcast.refs_0_.parity_ref, f32[4,160,128]{2,1,0:T(8,128)} %copy-done.6, f32[16,160,128]{2,1,0:T(8,128)} %bitcast.35, f32[4,160,128]{2,1,0:T(8,128)} %copy-done.7, f32[16,160,128]{2,1,0:T(8,128)} %b_ref.1, f32[16,160,128]{2,1,0:T(8,128)} %get-tuple-element.12.refs_5_.g0_ref, ...), custom_call_target="tpu_custom_call" | custom-call | tf_op jit(solution)/shard_map/pallas_call | solution.py:198
  80.6 2.5 %multiply_add_fusion = f32[16,160,128]{2,1,0:T(8,128)S(1)} fusion(f32[16,160,128]{2,1,0:T(8,128)} %shard_map.116, f32[16,160,128]{2,1,0:T(8,128)S(1)} %copy-done.4, f32[16,160,128]{2,1,0:T(8,128)} %bitcast.36, f32[16,160,128]{2,1,0:T(8,128)} %get-tuple-element.20), kind=kLoop, calls=%fused_computation.2 | loop fusion | flops 983040 | bytes 6553600 | tf_op jit(solution)/shard_map/add | solution.py:404
  83.1 4.5 %collective-permute-start.10 = (f32[1280,128]{1,0:T(8,128)S(1)}, f32[1280,128]{1,0:T(8,128)S(1)}, u32[]{:S(2)}, u32[]{:S(2)}) collective-permute-start(f32[1280,128]{1,0:T(8,128)S(1)} %constant_dynamic-slice_fusion.1), channel_id=1, source_target_pairs={{0,4},{4,0},{8,12},{12,8},{1,5},{5,1},{9,13},{13,9},{2,6},{6,2},{1... | collective-permute-start | bytes 1966088 | tf_op jit(solution)/shard_map/ppermute | solution.py:307
  87.6 1.7 %collective-permute-done.10 = f32[1280,128]{1,0:T(8,128)S(1)} collective-permute-done((f32[1280,128]{1,0:T(8,128)S(1)}, f32[1280,128]{1,0:T(8,128)S(1)}, u32[]{:S(2)}, u32[]{:S(2)}) %collective-permute-start.10) | collective-permute-done | bytes 655392 | tf_op jit(solution)/shard_map/ppermute | solution.py:307
  89.5 1.3 %collective-permute-start.11 = (f32[640,128]{1,0:T(8,128)S(1)}, f32[640,128]{1,0:T(8,128)S(1)}, u32[]{:S(2)}, u32[]{:S(2)}) collective-permute-start(f32[640,128]{1,0:T(8,128)S(1)} %constant_dynamic-slice_fusion), channel_id=1, source_target_pairs={{0,8},{4,12},{8,0},{12,4},{1,9},{5,13},{9,1},{13,5},{2,10},{6,14},... | collective-permute-start | bytes 983048 | tf_op jit(solution)/shard_map/ppermute | solution.py:307
  90.7 7.7 %collective-permute-done.11 = f32[640,128]{1,0:T(8,128)S(1)} collective-permute-done((f32[640,128]{1,0:T(8,128)S(1)}, f32[640,128]{1,0:T(8,128)S(1)}, u32[]{:S(2)}, u32[]{:S(2)}) %collective-permute-start.11) | collective-permute-done | bytes 327712 | tf_op jit(solution)/shard_map/ppermute | solution.py:307
  98.5 1.3 %collective-permute-start.12 = (f32[640,128]{1,0:T(8,128)S(1)}, f32[640,128]{1,0:T(8,128)S(1)}, u32[]{:S(2)}, u32[]{:S(2)}) collective-permute-start(f32[640,128]{1,0:T(8,128)S(1)} %add_multiply_fusion), channel_id=1, source_target_pairs={{0,8},{4,12},{8,0},{12,4},{1,9},{5,13},{9,1},{13,5},{2,10},{6,14},... | collective-permute-start | bytes 983048 | tf_op jit(solution)/shard_map/ppermute | solution.py:313
  99.8 6.8 %collective-permute-done.12 = f32[640,128]{1,0:T(8,128)S(1)} collective-permute-done((f32[640,128]{1,0:T(8,128)S(1)}, f32[640,128]{1,0:T(8,128)S(1)}, u32[]{:S(2)}, u32[]{:S(2)}) %collective-permute-start.12) | collective-permute-done | bytes 327712 | tf_op jit(solution)/shard_map/ppermute | solution.py:313
  106.6 2.2 %collective-permute-start.13 = (f32[1280,128]{1,0:T(8,128)S(1)}, f32[1280,128]{1,0:T(8,128)S(1)}, u32[]{:S(2)}, u32[]{:S(2)}) collective-permute-start(f32[1280,128]{1,0:T(8,128)S(1)} %maximum_select_fusion.1), channel_id=1, source_target_pairs={{0,4},{4,0},{8,12},{12,8},{1,5},{5,1},{9,13},{13,9},{2,6},{6,2},{1... | collective-permute-start | bytes 1966088 | tf_op jit(solution)/shard_map/ppermute | solution.py:313
  108.8 1.7 %collective-permute-done.13 = f32[1280,128]{1,0:T(8,128)S(1)} collective-permute-done((f32[1280,128]{1,0:T(8,128)S(1)}, f32[1280,128]{1,0:T(8,128)S(1)}, u32[]{:S(2)}, u32[]{:S(2)}) %collective-permute-start.13) | collective-permute-done | bytes 655392 | tf_op jit(solution)/shard_map/ppermute | solution.py:313
  (64 shorter events, 10.9 us)
Async XLA Ops:
  0.6 6.0 %copy-start = (f32[16,160,128]{2,1,0:T(8,128)S(1)}, f32[16,160,128]{2,1,0:T(8,128)}, u32[]{:S(2)}) copy-start(f32[16,160,128]{2,1,0:T(8,128)} %b_ref.1) | copy-start | bytes 3932164
  0.7 8.1 %copy-start.3 = (f32[1,16,160,128]{3,2,1,0:T(8,128)S(1)}, f32[1,16,160,128]{3,2,1,0:T(8,128)}, u32[]{:S(2)}) copy-start(f32[1,16,160,128]{3,2,1,0:T(8,128)} %param.14) | copy-start | bytes 3932164
  2.0 10.4 %collective-permute-start.2 = (f32[4,160,128]{2,1,0:T(8,128)S(1)}, f32[4,160,128]{2,1,0:T(8,128)S(1)}, u32[]{:S(2)}, u32[]{:S(2)}) collective-permute-start(f32[4,160,128]{2,1,0:T(8,128)S(1)} %get-tuple-element.31), channel_id=1, source_target_pairs={{0,1},{1,0},{2,3},{3,2},{4,5},{5,4},{6,7},{7,6},{8,9},{9,8},{10,11... | collective-permute-start | bytes 983048 | tf_op jit(solution)/shard_map/ppermute | solution.py:322
  2.0 8.4 %copy-start.13 = (s32[256]{0:T(256)S(1)}, s32[256]{0:T(256)}, u32[]{:S(2)}) copy-start(s32[256]{0:T(256)} %param.18) | copy-start | bytes 3076
  2.0 9.7 %copy-start.15 = (f32[2]{0:T(128)S(1)}, f32[2]{0:T(128)}, u32[]{:S(2)}) copy-start(f32[2]{0:T(128)} %param.16) | copy-start | bytes 28
  2.1 12.8 %collective-permute-start.3 = (f32[4,160,128]{2,1,0:T(8,128)S(1)}, f32[4,160,128]{2,1,0:T(8,128)S(1)}, u32[]{:S(2)}, u32[]{:S(2)}) collective-permute-start(f32[4,160,128]{2,1,0:T(8,128)S(1)} %get-tuple-element.30), channel_id=1, source_target_pairs={{1,2},{2,1},{5,6},{6,5},{9,10},{10,9},{13,14},{14,13},{17,18},{18,... | collective-permute-start | bytes 983048 | tf_op jit(solution)/shard_map/ppermute | solution.py:322
  6.7 11.0 %collective-permute-start.4 = (f32[4,160,128]{2,1,0:T(8,128)S(1)}, f32[4,160,128]{2,1,0:T(8,128)}, u32[]{:S(2)}, u32[]{:S(2)}) collective-permute-start(f32[4,160,128]{2,1,0:T(8,128)S(1)} %get-tuple-element.29), channel_id=1, source_target_pairs={{0,1},{1,0},{2,3},{3,2},{4,5},{5,4},{6,7},{7,6},{8,9},{9,8},{10,11... | collective-permute-start | bytes 983048 | tf_op jit(solution)/shard_map/ppermute | solution.py:322
  6.8 14.1 %collective-permute-start.5 = (f32[4,160,128]{2,1,0:T(8,128)S(1)}, f32[4,160,128]{2,1,0:T(8,128)}, u32[]{:S(2)}, u32[]{:S(2)}) collective-permute-start(f32[4,160,128]{2,1,0:T(8,128)S(1)} %get-tuple-element.28), channel_id=1, source_target_pairs={{1,2},{2,1},{5,6},{6,5},{9,10},{10,9},{13,14},{14,13},{17,18},{18,... | collective-permute-start | bytes 983048 | tf_op jit(solution)/shard_map/ppermute | solution.py:322
  8.8 29.0 %collective-permute-start = (f32[4,160,128]{2,1,0:T(8,128)S(1)}, f32[4,160,128]{2,1,0:T(8,128)S(1)}, u32[]{:S(2)}, u32[]{:S(2)}) collective-permute-start(f32[4,160,128]{2,1,0:T(8,128)S(1)} %get-tuple-element.33), channel_id=1, source_target_pairs={{0,1},{1,0},{2,3},{3,2},{4,5},{5,4},{6,7},{7,6},{8,9},{9,8},{10,11... | collective-permute-start | bytes 983048 | tf_op jit(solution)/shard_map/ppermute | solution.py:322
  12.3 8.5 %copy-start.11 = (f32[4,160,128]{2,1,0:T(8,128)}, f32[4,160,128]{2,1,0:T(8,128)S(1)}, u32[]{:S(2)}) copy-start(f32[4,160,128]{2,1,0:T(8,128)S(1)} %collective-permute-done.2.refs_1_) | copy-start | bytes 983044
  12.3 25.5 %collective-permute-start.1 = (f32[4,160,128]{2,1,0:T(8,128)S(1)}, f32[4,160,128]{2,1,0:T(8,128)S(1)}, u32[]{:S(2)}, u32[]{:S(2)}) collective-permute-start(f32[4,160,128]{2,1,0:T(8,128)S(1)} %get-tuple-element.32), channel_id=1, source_target_pairs={{1,2},{2,1},{5,6},{6,5},{9,10},{10,9},{13,14},{14,13},{17,18},{18,... | collective-permute-start | bytes 983048 | tf_op jit(solution)/shard_map/ppermute | solution.py:322
  14.8 6.1 %copy-start.12 = (f32[4,160,128]{2,1,0:T(8,128)}, f32[4,160,128]{2,1,0:T(8,128)S(1)}, u32[]{:S(2)}) copy-start(f32[4,160,128]{2,1,0:T(8,128)S(1)} %collective-permute-done.3.refs_3_) | copy-start | bytes 983044
  33.1 13.5 %collective-permute-start.6 = (f32[4,160,128]{2,1,0:T(8,128)}, f32[4,160,128]{2,1,0:T(8,128)S(1)}, u32[]{:S(2)}, u32[]{:S(2)}) collective-permute-start(f32[4,160,128]{2,1,0:T(8,128)} %get-tuple-element.16), channel_id=1, source_target_pairs={{0,1},{1,0},{2,3},{3,2},{4,5},{5,4},{6,7},{7,6},{8,9},{9,8},{10,11... | collective-permute-start | bytes 983048 | tf_op jit(solution)/shard_map/ppermute | solution.py:322
  33.2 13.5 %collective-permute-start.7 = (f32[4,160,128]{2,1,0:T(8,128)}, f32[4,160,128]{2,1,0:T(8,128)S(1)}, u32[]{:S(2)}, u32[]{:S(2)}) collective-permute-start(f32[4,160,128]{2,1,0:T(8,128)} %get-tuple-element.18), channel_id=1, source_target_pairs={{1,2},{2,1},{5,6},{6,5},{9,10},{10,9},{13,14},{14,13},{17,18},{18,... | collective-permute-start | bytes 983048 | tf_op jit(solution)/shard_map/ppermute | solution.py:322
  47.6 11.1 %copy-start.14 = (f32[2,256]{1,0:T(2,128)S(1)}, f32[2,256]{1,0:T(2,128)}, u32[]{:S(2)}) copy-start(f32[2,256]{1,0:T(2,128)} %param.19) | copy-start | bytes 6148
  47.6 11.7 %copy-start.1 = (f32[16,160,128]{2,1,0:T(8,128)S(1)}, f32[16,160,128]{2,1,0:T(8,128)}, u32[]{:S(2)}) copy-start(f32[16,160,128]{2,1,0:T(8,128)} %shard_map.114) | copy-start | bytes 3932164
  61.7 8.3 %copy-start.2 = (f32[327680]{0:T(1024)}, f32[327680]{0:T(1024)S(1)}, u32[]{:S(2)}) copy-start(f32[327680]{0:T(1024)S(1)} %scatter_fusion) | copy-start | bytes 3932164
  61.8 6.0 %collective-permute-start.8 = (f32[4,160,128]{2,1,0:T(8,128)S(1)}, f32[4,160,128]{2,1,0:T(8,128)S(1)}, u32[]{:S(2)}, u32[]{:S(2)}) collective-permute-start(f32[4,160,128]{2,1,0:T(8,128)S(1)} %get-tuple-element.27), channel_id=1, source_target_pairs={{0,1},{1,0},{2,3},{3,2},{4,5},{5,4},{6,7},{7,6},{8,9},{9,8},{10,11... | collective-permute-start | bytes 983048 | tf_op jit(solution)/shard_map/ppermute | solution.py:322
  61.9 8.1 %collective-permute-start.9 = (f32[4,160,128]{2,1,0:T(8,128)S(1)}, f32[4,160,128]{2,1,0:T(8,128)S(1)}, u32[]{:S(2)}, u32[]{:S(2)}) collective-permute-start(f32[4,160,128]{2,1,0:T(8,128)S(1)} %get-tuple-element.26), channel_id=1, source_target_pairs={{1,2},{2,1},{5,6},{6,5},{9,10},{10,9},{13,14},{14,13},{17,18},{18,... | collective-permute-start | bytes 983048 | tf_op jit(solution)/shard_map/ppermute | solution.py:322
  70.7 9.9 %copy-start.4 = (f32[16,160,128]{2,1,0:T(8,128)S(1)}, f32[16,160,128]{2,1,0:T(8,128)}, u32[]{:S(2)}) copy-start(f32[16,160,128]{2,1,0:T(8,128)} %get-tuple-element.21) | copy-start | bytes 3932164
  83.1 6.3 %collective-permute-start.10 = (f32[1280,128]{1,0:T(8,128)S(1)}, f32[1280,128]{1,0:T(8,128)S(1)}, u32[]{:S(2)}, u32[]{:S(2)}) collective-permute-start(f32[1280,128]{1,0:T(8,128)S(1)} %constant_dynamic-slice_fusion.1), channel_id=1, source_target_pairs={{0,4},{4,0},{8,12},{12,8},{1,5},{5,1},{9,13},{13,9},{2,6},{6,2},{1... | collective-permute-start | bytes 1966088 | tf_op jit(solution)/shard_map/ppermute | solution.py:307
  89.5 9.0 %collective-permute-start.11 = (f32[640,128]{1,0:T(8,128)S(1)}, f32[640,128]{1,0:T(8,128)S(1)}, u32[]{:S(2)}, u32[]{:S(2)}) collective-permute-start(f32[640,128]{1,0:T(8,128)S(1)} %constant_dynamic-slice_fusion), channel_id=1, source_target_pairs={{0,8},{4,12},{8,0},{12,4},{1,9},{5,13},{9,1},{13,5},{2,10},{6,14},... | collective-permute-start | bytes 983048 | tf_op jit(solution)/shard_map/ppermute | solution.py:307
  98.5 8.1 %collective-permute-start.12 = (f32[640,128]{1,0:T(8,128)S(1)}, f32[640,128]{1,0:T(8,128)S(1)}, u32[]{:S(2)}, u32[]{:S(2)}) collective-permute-start(f32[640,128]{1,0:T(8,128)S(1)} %add_multiply_fusion), channel_id=1, source_target_pairs={{0,8},{4,12},{8,0},{12,4},{1,9},{5,13},{9,1},{13,5},{2,10},{6,14},... | collective-permute-start | bytes 983048 | tf_op jit(solution)/shard_map/ppermute | solution.py:313
  106.6 3.9 %collective-permute-start.13 = (f32[1280,128]{1,0:T(8,128)S(1)}, f32[1280,128]{1,0:T(8,128)S(1)}, u32[]{:S(2)}, u32[]{:S(2)}) collective-permute-start(f32[1280,128]{1,0:T(8,128)S(1)} %maximum_select_fusion.1), channel_id=1, source_target_pairs={{0,4},{4,0},{8,12},{12,8},{1,5},{5,1},{9,13},{13,9},{2,6},{6,2},{1... | collective-permute-start | bytes 1966088 | tf_op jit(solution)/shard_map/ppermute | solution.py:313
  (6 other events, 6.1 us)

commit v18 on v16

--- a/solution.py
+++ b/solution.py
@@ -394,13 +394,10 @@
     image_part = jnp.zeros(buoyancy.shape, jnp.float32)
     for j in range(steps):
         lo, hi = halos(now, "tile")
-        if j + 1 < steps:
-            (newer,) = apply_step(parity, lo, now, hi, buoyancy, grad_b, speed, older, want_force=False)
-            newer = inject(newer, rec_local, rec_valid, residual[steps - 1 - j])
-        else:
-            cells = jnp.stack([rec_local // (height * depth), (rec_local // depth) % height, rec_local % depth])
-            valid = rec_valid.astype(jnp.int32)
-            newer = apply_final(parity, lo, now, hi, buoyancy, grad_b, speed, older, cells, valid, residual[0])
+        cells = jnp.stack([rec_local // (height * depth), (rec_local // depth) % height, rec_local % depth])
+        valid = rec_valid.astype(jnp.int32)
+        values = residual[steps - 1 - j]
+        newer = apply_final(parity, lo, now, hi, buoyancy, grad_b, speed, older, cells, valid, values)
         image_part = image_part + newer * forces[steps - 1 - j]
         older, now = (now, newer)
     image = reduce_members(image_part, "real")

time: 112 us -> 117 us (1.045)
  waiting for transfers between devices: 29.2 us -> 32.4 us
  other arithmetic: 10.7 us -> 8.32 us
  Pallas kernels: 40.2 us -> 42 us
  local copies, waits for them, and re-layouts: 5.12 us -> 6.84 us
    pallas_call x1 -> x2, Pallas kernels: 9.9 us -> 19.7 us  [apply_final(): pl.pallas_call(functools.partial(final_kernel, block=block, rows=rows), g...]
    pallas_call x3 -> x2, Pallas kernels: 30.3 us -> 22.3 us  [apply_step(): pl.pallas_call(kernel, grid=(planes // block,), in_specs=in_specs, out_sp...]
    scatter-add x1 -> x0, other arithmetic: 2.44 us -> none  [inject(): flat = field.reshape(-1).at[where].add(jnp.where(valid, values, 0.0))]
    ppermute x5, waiting for transfers between devices: 5.36 us -> 7.23 us  [swap_halos(): lax.ppermute(sends[1], axis, second)]
    ppermute x5, waiting for transfers between devices: 5.93 us -> 7.21 us  [swap_halos(): lax.ppermute(sends[0], axis, first)]
    ppermute x5, starting transfers between devices: 14.3 us -> 15.5 us  [swap_halos(): lax.ppermute(sends[1], axis, second)]
    unnamed x32 -> x28, local copies, waits for them, and re-layouts: 2.46 us -> 3.03 us
  transfers between devices with their start and end apart: 14 -> 14, of which waited for: 8 -> 10; matrix products, arithmetic and copies ran while one was open for 4% -> 5% of each run, Pallas kernels for 18% -> 19%
where the time goes in v18:
time: 117 us
  Pallas kernels  42 us (36%)
  waiting for transfers between devices  32.4 us (28%)
  starting transfers between devices  25.4 us (22%)
  other arithmetic  8.32 us (7%)
  local copies, waits for them, and re-layouts  6.84 us (6%)
  between operations  1.66 us (1%)
    pallas_call x2, Pallas kernels, apply_step(): pl.pallas_call(kernel, grid=(planes // block,), in_specs=in_specs, out_sp...  22.3 us
    pallas_call x2, Pallas kernels, apply_final(): pl.pallas_call(functools.partial(final_kernel, block=block, rows=rows), g...  19.7 us
    ppermute x5, starting transfers between devices, swap_halos(): lax.ppermute(sends[1], axis, second)  15.5 us
    ppermute x2, waiting for transfers between devices, reduce_members(): rows = keep + lax.ppermute(give, axis, pairs)  9.44 us
    ppermute x2, waiting for transfers between devices, reduce_members(): other = lax.ppermute(rows, axis, pairs)  8.52 us
    ppermute x5, waiting for transfers between devices, swap_halos(): lax.ppermute(sends[1], axis, second)  7.23 us
    ppermute x5, waiting for transfers between devices, swap_halos(): lax.ppermute(sends[0], axis, first)  7.21 us
    ppermute x2, starting transfers between devices, reduce_members(): rows = keep + lax.ppermute(give, axis, pairs)  5.85 us
  transfers between devices with their start and end apart: 14, of which 10 were waited for; matrix products, arithmetic and copies ran while one was open for 5% of the time, Pallas kernels for 19%

profile of v18, /device:TPU:9, one launch (start us, length us, event | category | flops | bytes accessed | tf_op | source)
XLA Modules:
  0.0 116.6 jit_solution(13033282001966801043)
XLA Ops:
  2.1 4.6 %collective-permute-start.3 = (f32[4,160,128]{2,1,0:T(8,128)S(1)}, f32[4,160,128]{2,1,0:T(8,128)}, u32[]{:S(2)}, u32[]{:S(2)}) collective-permute-start(f32[4,160,128]{2,1,0:T(8,128)S(1)} %get-tuple-element.30), channel_id=1, source_target_pairs={{1,2},{2,1},{5,6},{6,5},{9,10},{10,9},{13,14},{14,13},{17,18},{18,... | collective-permute-start | bytes 983048 | tf_op jit(solution)/shard_map/ppermute | solution.py:322
  6.8 1.9 %collective-permute-start.5 = (f32[4,160,128]{2,1,0:T(8,128)S(1)}, f32[4,160,128]{2,1,0:T(8,128)S(1)}, u32[]{:S(2)}, u32[]{:S(2)}) collective-permute-start(f32[4,160,128]{2,1,0:T(8,128)S(1)} %get-tuple-element.28), channel_id=1, source_target_pairs={{1,2},{2,1},{5,6},{6,5},{9,10},{10,9},{13,14},{14,13},{17,18},{18,... | collective-permute-start | bytes 983048 | tf_op jit(solution)/shard_map/ppermute | solution.py:322
  11.8 3.2 %collective-permute-start.1 = (f32[4,160,128]{2,1,0:T(8,128)S(1)}, f32[4,160,128]{2,1,0:T(8,128)S(1)}, u32[]{:S(2)}, u32[]{:S(2)}) collective-permute-start(f32[4,160,128]{2,1,0:T(8,128)S(1)} %get-tuple-element.32), channel_id=1, source_target_pairs={{1,2},{2,1},{5,6},{6,5},{9,10},{10,9},{13,14},{14,13},{17,18},{18,... | collective-permute-start | bytes 983048 | tf_op jit(solution)/shard_map/ppermute | solution.py:322
  15.0 2.7 %collective-permute-done.4.refs_4_ = f32[4,160,128]{2,1,0:T(8,128)S(1)} collective-permute-done((f32[4,160,128]{2,1,0:T(8,128)S(1)}, f32[4,160,128]{2,1,0:T(8,128)S(1)}, u32[]{:S(2)}, u32[]{:S(2)}) %collective-permute-start.4) | collective-permute-done | bytes 327712 | tf_op jit(solution)/shard_map/ppermute | solution.py:322
  17.6 3.2 %collective-permute-done.5.refs_6_ = f32[4,160,128]{2,1,0:T(8,128)S(1)} collective-permute-done((f32[4,160,128]{2,1,0:T(8,128)S(1)}, f32[4,160,128]{2,1,0:T(8,128)S(1)}, u32[]{:S(2)}, u32[]{:S(2)}) %collective-permute-start.5) | collective-permute-done | bytes 327712 | tf_op jit(solution)/shard_map/ppermute | solution.py:322
  21.5 12.3 %shard_map.113 = (f32[16,160,128]{2,1,0:T(8,128)}, f32[16,160,128]{2,1,0:T(8,128)}, f32[16,160,128]{2,1,0:T(8,128)}, f32[16,160,128]{2,1,0:T(8,128)}, f32[16,160...) custom-call(s32[1]{0:T(128)} %bitcast.refs_0_.parity_ref, ...), custom_call_target="tpu_custom_call" | custom-call | tf_op jit(solution)/shard_map/pallas_call | solution.py:266
  33.9 3.0 %collective-permute-start.7 = (f32[4,160,128]{2,1,0:T(8,128)}, f32[4,160,128]{2,1,0:T(8,128)S(1)}, u32[]{:S(2)}, u32[]{:S(2)}) collective-permute-start(f32[4,160,128]{2,1,0:T(8,128)} %get-tuple-element.18), channel_id=1, source_target_pairs={{1,2},{2,1},{5,6},{6,5},{9,10},{10,9},{13,14},{14,13},{17,18},{18,... | collective-permute-start | bytes 983048 | tf_op jit(solution)/shard_map/ppermute | solution.py:322
  39.1 1.5 %collective-permute-done.6.refs_1_ = f32[4,160,128]{2,1,0:T(8,128)S(1)} collective-permute-done((f32[4,160,128]{2,1,0:T(8,128)}, f32[4,160,128]{2,1,0:T(8,128)S(1)}, u32[]{:S(2)}, u32[]{:S(2)}) %collective-permute-start.6) | collective-permute-done | bytes 327712 | tf_op jit(solution)/shard_map/ppermute | solution.py:322
  40.6 1.9 %collective-permute-done.7.refs_3_ = f32[4,160,128]{2,1,0:T(8,128)S(1)} collective-permute-done((f32[4,160,128]{2,1,0:T(8,128)}, f32[4,160,128]{2,1,0:T(8,128)S(1)}, u32[]{:S(2)}, u32[]{:S(2)}) %collective-permute-start.7) | collective-permute-done | bytes 327712 | tf_op jit(solution)/shard_map/ppermute | solution.py:322
  43.2 10.0 %shard_map.114 = (f32[16,160,128]{2,1,0:T(8,128)}, f32[16,160,128]{2,1,0:T(8,128)}, f32[256,128]{1,0:T(8,128)}) custom-call(s32[1]{0:T(128)} %bitcast.refs_0_.parity_ref, f32[4,160,128]{2,1,0:T(8,128)} %copy-done.7, f32[16,160,128]{2,1,0:T(8,128)} %get-tuple-element.17.refs_2_, f32[4,160,128]{2,1,0:T(8,128)} %copy-done.8, f32[16,160,128]{2,1,0:T(8,128)} %b_ref.3, ...), custom_call_target="tpu_custom_call" | custom-call | tf_op jit(solution)/shard_map/pallas_call | solution.py:266
  55.7 9.8 %shard_map.115.mid_ref = f32[16,160,128]{2,1,0:T(8,128)} custom-call(s32[1]{0:T(128)} %bitcast.refs_0_.parity_ref, f32[4,160,128]{2,1,0:T(8,128)} %copy-done.3, f32[16,160,128]{2,1,0:T(8,128)} %bitcast.37, f32[4,160,128]{2,1,0:T(8,128)} %copy-done.4, f32[16,160,128]{2,1,0:T(8,128)} %b_ref.3, f32[16,160,128]{2,1,0:T(8,128)} %get-tuple-element.12.refs_5_.g0_ref, ...), custom_call_target="tpu_custom_call" | custom-call | tf_op jit(solution)/shard_map/pallas_call | solution.py:198
  66.7 2.8 %collective-permute-start.9 = (f32[4,160,128]{2,1,0:T(8,128)S(1)}, f32[4,160,128]{2,1,0:T(8,128)S(1)}, u32[]{:S(2)}, u32[]{:S(2)}) collective-permute-start(f32[4,160,128]{2,1,0:T(8,128)S(1)} %get-tuple-element.26), channel_id=1, source_target_pairs={{1,2},{2,1},{5,6},{6,5},{9,10},{10,9},{13,14},{14,13},{17,18},{18,... | collective-permute-start | bytes 983048 | tf_op jit(solution)/shard_map/ppermute | solution.py:322
  69.5 3.1 %collective-permute-done.8.lo_ref = f32[4,160,128]{2,1,0:T(8,128)S(1)} collective-permute-done((f32[4,160,128]{2,1,0:T(8,128)S(1)}, f32[4,160,128]{2,1,0:T(8,128)S(1)}, u32[]{:S(2)}, u32[]{:S(2)}) %collective-permute-start.8) | collective-permute-done | bytes 327712 | tf_op jit(solution)/shard_map/ppermute | solution.py:322
  72.6 2.2 %collective-permute-done.9.hi_ref = f32[4,160,128]{2,1,0:T(8,128)S(1)} collective-permute-done((f32[4,160,128]{2,1,0:T(8,128)S(1)}, f32[4,160,128]{2,1,0:T(8,128)S(1)}, u32[]{:S(2)}, u32[]{:S(2)}) %collective-permute-start.9) | collective-permute-done | bytes 327712 | tf_op jit(solution)/shard_map/ppermute | solution.py:322
  75.5 9.9 %shard_map.116 = f32[16,160,128]{2,1,0:T(8,128)} custom-call(s32[1]{0:T(128)} %bitcast.refs_0_.parity_ref, f32[4,160,128]{2,1,0:T(8,128)} %copy-done.5, f32[16,160,128]{2,1,0:T(8,128)} %shard_map.115.mid_ref, f32[4,160,128]{2,1,0:T(8,128)} %copy-done.6, f32[16,160,128]{2,1,0:T(8,128)} %b_ref.3, f32[16,160,128]{2,1,0:T(8,128)} %get-tuple-element.12.refs_5_.g0_ref, ...), custom_call_target="tpu_custom_call" | custom-call | tf_op jit(solution)/shard_map/pallas_call | solution.py:198
  85.4 2.5 %multiply_add_fusion = f32[16,160,128]{2,1,0:T(8,128)S(1)} fusion(f32[16,160,128]{2,1,0:T(8,128)} %shard_map.116, f32[16,160,128]{2,1,0:T(8,128)} %get-tuple-element.21, f32[16,160,128]{2,1,0:T(8,128)S(1)} %copy-done.1, f32[16,160,128]{2,1,0:T(8,128)} %get-tuple-element.20), kind=kLoop, calls=%fused_computation.1 | loop fusion | flops 983040 | bytes 6553600 | tf_op jit(solution)/shard_map/add | solution.py:401
  88.0 4.6 %collective-permute-start.10 = (f32[1280,128]{1,0:T(8,128)S(1)}, f32[1280,128]{1,0:T(8,128)S(1)}, u32[]{:S(2)}, u32[]{:S(2)}) collective-permute-start(f32[1280,128]{1,0:T(8,128)S(1)} %constant_dynamic-slice_fusion.1), channel_id=1, source_target_pairs={{0,4},{4,0},{8,12},{12,8},{1,5},{5,1},{9,13},{13,9},{2,6},{6,2},{1... | collective-permute-start | bytes 1966088 | tf_op jit(solution)/shard_map/ppermute | solution.py:307
  92.5 1.7 %collective-permute-done.10 = f32[1280,128]{1,0:T(8,128)S(1)} collective-permute-done((f32[1280,128]{1,0:T(8,128)S(1)}, f32[1280,128]{1,0:T(8,128)S(1)}, u32[]{:S(2)}, u32[]{:S(2)}) %collective-permute-start.10) | collective-permute-done | bytes 655392 | tf_op jit(solution)/shard_map/ppermute | solution.py:307
  94.4 1.3 %collective-permute-start.11 = (f32[640,128]{1,0:T(8,128)S(1)}, f32[640,128]{1,0:T(8,128)S(1)}, u32[]{:S(2)}, u32[]{:S(2)}) collective-permute-start(f32[640,128]{1,0:T(8,128)S(1)} %constant_dynamic-slice_fusion), channel_id=1, source_target_pairs={{0,8},{4,12},{8,0},{12,4},{1,9},{5,13},{9,1},{13,5},{2,10},{6,14},... | collective-permute-start | bytes 983048 | tf_op jit(solution)/shard_map/ppermute | solution.py:307
  95.6 7.7 %collective-permute-done.11 = f32[640,128]{1,0:T(8,128)S(1)} collective-permute-done((f32[640,128]{1,0:T(8,128)S(1)}, f32[640,128]{1,0:T(8,128)S(1)}, u32[]{:S(2)}, u32[]{:S(2)}) %collective-permute-start.11) | collective-permute-done | bytes 327712 | tf_op jit(solution)/shard_map/ppermute | solution.py:307
  103.4 1.3 %collective-permute-start.12 = (f32[640,128]{1,0:T(8,128)S(1)}, f32[640,128]{1,0:T(8,128)S(1)}, u32[]{:S(2)}, u32[]{:S(2)}) collective-permute-start(f32[640,128]{1,0:T(8,128)S(1)} %add_multiply_fusion), channel_id=1, source_target_pairs={{0,8},{4,12},{8,0},{12,4},{1,9},{5,13},{9,1},{13,5},{2,10},{6,14},... | collective-permute-start | bytes 983048 | tf_op jit(solution)/shard_map/ppermute | solution.py:313
  104.7 6.8 %collective-permute-done.12 = f32[640,128]{1,0:T(8,128)S(1)} collective-permute-done((f32[640,128]{1,0:T(8,128)S(1)}, f32[640,128]{1,0:T(8,128)S(1)}, u32[]{:S(2)}, u32[]{:S(2)}) %collective-permute-start.12) | collective-permute-done | bytes 327712 | tf_op jit(solution)/shard_map/ppermute | solution.py:313
  111.5 2.2 %collective-permute-start.13 = (f32[1280,128]{1,0:T(8,128)S(1)}, f32[1280,128]{1,0:T(8,128)S(1)}, u32[]{:S(2)}, u32[]{:S(2)}) collective-permute-start(f32[1280,128]{1,0:T(8,128)S(1)} %maximum_select_fusion.1), channel_id=1, source_target_pairs={{0,4},{4,0},{8,12},{12,8},{1,5},{5,1},{9,13},{13,9},{2,6},{6,2},{1... | collective-permute-start | bytes 1966088 | tf_op jit(solution)/shard_map/ppermute | solution.py:313
  113.7 1.7 %collective-permute-done.13 = f32[1280,128]{1,0:T(8,128)S(1)} collective-permute-done((f32[1280,128]{1,0:T(8,128)S(1)}, f32[1280,128]{1,0:T(8,128)S(1)}, u32[]{:S(2)}, u32[]{:S(2)}) %collective-permute-start.13) | collective-permute-done | bytes 655392 | tf_op jit(solution)/shard_map/ppermute | solution.py:313
  (58 shorter events, 13.3 us)
Async XLA Ops:
  0.6 6.0 %copy-start = (f32[16,160,128]{2,1,0:T(8,128)S(1)}, f32[16,160,128]{2,1,0:T(8,128)}, u32[]{:S(2)}) copy-start(f32[16,160,128]{2,1,0:T(8,128)} %b_ref.3) | copy-start | bytes 3932164
  0.7 8.1 %copy-start.2 = (f32[1,16,160,128]{3,2,1,0:T(8,128)S(1)}, f32[1,16,160,128]{3,2,1,0:T(8,128)}, u32[]{:S(2)}) copy-start(f32[1,16,160,128]{3,2,1,0:T(8,128)} %param.14) | copy-start | bytes 3932164
  2.0 9.8 %collective-permute-start.2 = (f32[4,160,128]{2,1,0:T(8,128)S(1)}, f32[4,160,128]{2,1,0:T(8,128)}, u32[]{:S(2)}, u32[]{:S(2)}) collective-permute-start(f32[4,160,128]{2,1,0:T(8,128)S(1)} %get-tuple-element.31), channel_id=1, source_target_pairs={{0,1},{1,0},{2,3},{3,2},{4,5},{5,4},{6,7},{7,6},{8,9},{9,8},{10,11... | collective-permute-start | bytes 983048 | tf_op jit(solution)/shard_map/ppermute | solution.py:322
  2.0 7.7 %copy-start.11 = (s32[256]{0:T(256)S(1)}, s32[256]{0:T(256)}, u32[]{:S(2)}) copy-start(s32[256]{0:T(256)} %param.18) | copy-start | bytes 3076
  2.0 9.1 %copy-start.13 = (f32[2]{0:T(128)S(1)}, f32[2]{0:T(128)}, u32[]{:S(2)}) copy-start(f32[2]{0:T(128)} %param.16) | copy-start | bytes 28
  2.1 12.9 %collective-permute-start.3 = (f32[4,160,128]{2,1,0:T(8,128)S(1)}, f32[4,160,128]{2,1,0:T(8,128)}, u32[]{:S(2)}, u32[]{:S(2)}) collective-permute-start(f32[4,160,128]{2,1,0:T(8,128)S(1)} %get-tuple-element.30), channel_id=1, source_target_pairs={{1,2},{2,1},{5,6},{6,5},{9,10},{10,9},{13,14},{14,13},{17,18},{18,... | collective-permute-start | bytes 983048 | tf_op jit(solution)/shard_map/ppermute | solution.py:322
  6.7 10.9 %collective-permute-start.4 = (f32[4,160,128]{2,1,0:T(8,128)S(1)}, f32[4,160,128]{2,1,0:T(8,128)S(1)}, u32[]{:S(2)}, u32[]{:S(2)}) collective-permute-start(f32[4,160,128]{2,1,0:T(8,128)S(1)} %get-tuple-element.29), channel_id=1, source_target_pairs={{0,1},{1,0},{2,3},{3,2},{4,5},{5,4},{6,7},{7,6},{8,9},{9,8},{10,11... | collective-permute-start | bytes 983048 | tf_op jit(solution)/shard_map/ppermute | solution.py:322
  6.8 14.0 %collective-permute-start.5 = (f32[4,160,128]{2,1,0:T(8,128)S(1)}, f32[4,160,128]{2,1,0:T(8,128)S(1)}, u32[]{:S(2)}, u32[]{:S(2)}) collective-permute-start(f32[4,160,128]{2,1,0:T(8,128)S(1)} %get-tuple-element.28), channel_id=1, source_target_pairs={{1,2},{2,1},{5,6},{6,5},{9,10},{10,9},{13,14},{14,13},{17,18},{18,... | collective-permute-start | bytes 983048 | tf_op jit(solution)/shard_map/ppermute | solution.py:322
  8.8 46.0 %collective-permute-start = (f32[4,160,128]{2,1,0:T(8,128)S(1)}, f32[4,160,128]{2,1,0:T(8,128)S(1)}, u32[]{:S(2)}, u32[]{:S(2)}) collective-permute-start(f32[4,160,128]{2,1,0:T(8,128)S(1)} %get-tuple-element.33), channel_id=1, source_target_pairs={{0,1},{1,0},{2,3},{3,2},{4,5},{5,4},{6,7},{7,6},{8,9},{9,8},{10,11... | collective-permute-start | bytes 983048 | tf_op jit(solution)/shard_map/ppermute | solution.py:322
  11.8 43.1 %collective-permute-start.1 = (f32[4,160,128]{2,1,0:T(8,128)S(1)}, f32[4,160,128]{2,1,0:T(8,128)S(1)}, u32[]{:S(2)}, u32[]{:S(2)}) collective-permute-start(f32[4,160,128]{2,1,0:T(8,128)S(1)} %get-tuple-element.32), channel_id=1, source_target_pairs={{1,2},{2,1},{5,6},{6,5},{9,10},{10,9},{13,14},{14,13},{17,18},{18,... | collective-permute-start | bytes 983048 | tf_op jit(solution)/shard_map/ppermute | solution.py:322
  17.6 3.2 %copy-start.9 = (f32[4,160,128]{2,1,0:T(8,128)}, f32[4,160,128]{2,1,0:T(8,128)S(1)}, u32[]{:S(2)}) copy-start(f32[4,160,128]{2,1,0:T(8,128)S(1)} %collective-permute-done.4.refs_4_) | copy-start | bytes 983044
  33.8 6.8 %collective-permute-start.6 = (f32[4,160,128]{2,1,0:T(8,128)}, f32[4,160,128]{2,1,0:T(8,128)S(1)}, u32[]{:S(2)}, u32[]{:S(2)}) collective-permute-start(f32[4,160,128]{2,1,0:T(8,128)} %get-tuple-element.16), channel_id=1, source_target_pairs={{0,1},{1,0},{2,3},{3,2},{4,5},{5,4},{6,7},{7,6},{8,9},{9,8},{10,11... | collective-permute-start | bytes 983048 | tf_op jit(solution)/shard_map/ppermute | solution.py:322
  33.9 8.6 %collective-permute-start.7 = (f32[4,160,128]{2,1,0:T(8,128)}, f32[4,160,128]{2,1,0:T(8,128)S(1)}, u32[]{:S(2)}, u32[]{:S(2)}) collective-permute-start(f32[4,160,128]{2,1,0:T(8,128)} %get-tuple-element.18), channel_id=1, source_target_pairs={{1,2},{2,1},{5,6},{6,5},{9,10},{10,9},{13,14},{14,13},{17,18},{18,... | collective-permute-start | bytes 983048 | tf_op jit(solution)/shard_map/ppermute | solution.py:322
  40.6 1.9 %copy-start.7 = (f32[4,160,128]{2,1,0:T(8,128)}, f32[4,160,128]{2,1,0:T(8,128)S(1)}, u32[]{:S(2)}) copy-start(f32[4,160,128]{2,1,0:T(8,128)S(1)} %collective-permute-done.6.refs_1_) | copy-start | bytes 983044
  43.2 11.1 %copy-start.12 = (f32[2,256]{1,0:T(2,128)S(1)}, f32[2,256]{1,0:T(2,128)}, u32[]{:S(2)}) copy-start(f32[2,256]{1,0:T(2,128)} %param.19) | copy-start | bytes 6148
  54.8 0.8 copy-start.4
  66.6 6.0 %collective-permute-start.8 = (f32[4,160,128]{2,1,0:T(8,128)S(1)}, f32[4,160,128]{2,1,0:T(8,128)S(1)}, u32[]{:S(2)}, u32[]{:S(2)}) collective-permute-start(f32[4,160,128]{2,1,0:T(8,128)S(1)} %get-tuple-element.27), channel_id=1, source_target_pairs={{0,1},{1,0},{2,3},{3,2},{4,5},{5,4},{6,7},{7,6},{8,9},{9,8},{10,11... | collective-permute-start | bytes 983048 | tf_op jit(solution)/shard_map/ppermute | solution.py:322
  66.7 8.1 %collective-permute-start.9 = (f32[4,160,128]{2,1,0:T(8,128)S(1)}, f32[4,160,128]{2,1,0:T(8,128)S(1)}, u32[]{:S(2)}, u32[]{:S(2)}) collective-permute-start(f32[4,160,128]{2,1,0:T(8,128)S(1)} %get-tuple-element.26), channel_id=1, source_target_pairs={{1,2},{2,1},{5,6},{6,5},{9,10},{10,9},{13,14},{14,13},{17,18},{18,... | collective-permute-start | bytes 983048 | tf_op jit(solution)/shard_map/ppermute | solution.py:322
  72.6 2.2 %copy-start.5 = (f32[4,160,128]{2,1,0:T(8,128)}, f32[4,160,128]{2,1,0:T(8,128)S(1)}, u32[]{:S(2)}) copy-start(f32[4,160,128]{2,1,0:T(8,128)S(1)} %collective-permute-done.8.lo_ref) | copy-start | bytes 983044
  75.5 9.9 %copy-start.1 = (f32[16,160,128]{2,1,0:T(8,128)S(1)}, f32[16,160,128]{2,1,0:T(8,128)}, u32[]{:S(2)}) copy-start(f32[16,160,128]{2,1,0:T(8,128)} %shard_map.115.mid_ref) | copy-start | bytes 3932164
  88.0 6.3 %collective-permute-start.10 = (f32[1280,128]{1,0:T(8,128)S(1)}, f32[1280,128]{1,0:T(8,128)S(1)}, u32[]{:S(2)}, u32[]{:S(2)}) collective-permute-start(f32[1280,128]{1,0:T(8,128)S(1)} %constant_dynamic-slice_fusion.1), channel_id=1, source_target_pairs={{0,4},{4,0},{8,12},{12,8},{1,5},{5,1},{9,13},{13,9},{2,6},{6,2},{1... | collective-permute-start | bytes 1966088 | tf_op jit(solution)/shard_map/ppermute | solution.py:307
  94.4 9.0 %collective-permute-start.11 = (f32[640,128]{1,0:T(8,128)S(1)}, f32[640,128]{1,0:T(8,128)S(1)}, u32[]{:S(2)}, u32[]{:S(2)}) collective-permute-start(f32[640,128]{1,0:T(8,128)S(1)} %constant_dynamic-slice_fusion), channel_id=1, source_target_pairs={{0,8},{4,12},{8,0},{12,4},{1,9},{5,13},{9,1},{13,5},{2,10},{6,14},... | collective-permute-start | bytes 983048 | tf_op jit(solution)/shard_map/ppermute | solution.py:307
  103.4 8.1 %collective-permute-start.12 = (f32[640,128]{1,0:T(8,128)S(1)}, f32[640,128]{1,0:T(8,128)S(1)}, u32[]{:S(2)}, u32[]{:S(2)}) collective-permute-start(f32[640,128]{1,0:T(8,128)S(1)} %add_multiply_fusion), channel_id=1, source_target_pairs={{0,8},{4,12},{8,0},{12,4},{1,9},{5,13},{9,1},{13,5},{2,10},{6,14},... | collective-permute-start | bytes 983048 | tf_op jit(solution)/shard_map/ppermute | solution.py:313
  111.5 3.9 %collective-permute-start.13 = (f32[1280,128]{1,0:T(8,128)S(1)}, f32[1280,128]{1,0:T(8,128)S(1)}, u32[]{:S(2)}, u32[]{:S(2)}) collective-permute-start(f32[1280,128]{1,0:T(8,128)S(1)} %maximum_select_fusion.1), channel_id=1, source_target_pairs={{0,4},{4,0},{8,12},{12,8},{1,5},{5,1},{9,13},{13,9},{2,6},{6,2},{1... | collective-permute-start | bytes 1966088 | tf_op jit(solution)/shard_map/ppermute | solution.py:313
  (4 other events, 2.9 us)

commit v19 on v16

--- a/solution.py
+++ b/solution.py
@@ -290,14 +290,24 @@
     )(lo, mid, hi)
 
 
-def reduce_members(part, axis):
+def reduce_members(base, axis, scale=None, weight=None):
+    part = base if scale is None else base + scale * weight
     members = lax.axis_size(axis)
     if members & (members - 1) or part.size % (members * 1024):
         return lax.psum(part, axis) / members
     me = lax.axis_index(axis)
-    rows = part.reshape(-1, 128)
+    if scale is not None:
+        flat = [x.reshape(-1, 128) for x in (base, scale, weight)]
+        half = flat[0].shape[0] // 2
+        upper = me % 2
+        keep = [lax.dynamic_slice_in_dim(x, upper * half, half, 0) for x in flat]
+        give = [lax.dynamic_slice_in_dim(x, (1 - upper) * half, half, 0) for x in flat]
+        sent = lax.ppermute(give[0] + give[1] * give[2], axis, [(i, i ^ 1) for i in range(members)])
+        rows = (keep[0] + keep[1] * keep[2]) + sent
+    else:
+        rows = part.reshape(-1, 128)
     bits = members.bit_length() - 1
-    for b in range(bits):
+    for b in range(0 if scale is None else 1, bits):
         mask = 1 << b
         half = rows.shape[0] // 2
         upper = (me // mask) % 2
@@ -401,9 +411,10 @@
             cells = jnp.stack([rec_local // (height * depth), (rec_local // depth) % height, rec_local % depth])
             valid = rec_valid.astype(jnp.int32)
             newer = apply_final(parity, lo, now, hi, buoyancy, grad_b, speed, older, cells, valid, residual[0])
-        image_part = image_part + newer * forces[steps - 1 - j]
+        if j + 1 < steps:
+            image_part = image_part + newer * forces[steps - 1 - j]
         older, now = (now, newer)
-    image = reduce_members(image_part, "real")
+    image = reduce_members(image_part, "real", now, forces[0])
     return (image, now[None])
 
 

time: 112 us -> 114 us (1.018)
  other arithmetic: 10.7 us -> 12.5 us
    ppermute x0 -> x1, starting transfers between devices: none -> 4.53 us  [reduce_members(): lax.ppermute(give[0] + give[1] * give[2], axis, [(i, i ^ 1) for i in rang...]
    ppermute x2 -> x1, starting transfers between devices: 5.81 us -> 1.28 us  [reduce_members(): rows = keep + lax.ppermute(give, axis, pairs)]
    ppermute x0 -> x1, waiting for transfers between devices: none -> 1.86 us  [reduce_members(): lax.ppermute(give[0] + give[1] * give[2], axis, [(i, i ^ 1) for i in rang...]
    ppermute x2 -> x1, waiting for transfers between devices: 9.44 us -> 7.71 us  [reduce_members(): rows = keep + lax.ppermute(give, axis, pairs)]
    mul x0 -> x1, other arithmetic: none -> 1.46 us  [shards(): image_part = image_part + newer * forces[steps - 1 - j]]
    ppermute x5, waiting for transfers between devices: 5.93 us -> 4.69 us  [swap_halos(): lax.ppermute(sends[0], axis, first)]
  transfers between devices with their start and end apart: 14 -> 14, of which waited for: 8 -> 8; matrix products, arithmetic and copies ran while one was open for 4% -> 5% of each run, Pallas kernels for 18% -> 18%
where the time goes in v19:
time: 114 us; the launch traced here: 113 us
  Pallas kernels  40 us (35%)
  waiting for transfers between devices  28.1 us (25%)
  starting transfers between devices  24.7 us (22%)
  other arithmetic  12.5 us (11%)
  local copies, waits for them, and re-layouts  5.97 us (5%)
  between operations  1.72 us (2%)
    pallas_call x3, Pallas kernels, apply_step(): pl.pallas_call(kernel, grid=(planes // block,), in_specs=in_specs, out_sp...  30.2 us
    ppermute x5, starting transfers between devices, swap_halos(): lax.ppermute(sends[1], axis, second)  14.2 us
    pallas_call x1, Pallas kernels, apply_final(): pl.pallas_call(functools.partial(final_kernel, block=block, rows=rows), g...  9.81 us
    ppermute x2, waiting for transfers between devices, reduce_members(): other = lax.ppermute(rows, axis, pairs)  8.52 us
    ppermute x1, waiting for transfers between devices, reduce_members(): rows = keep + lax.ppermute(give, axis, pairs)  7.71 us
    ppermute x5, waiting for transfers between devices, swap_halos(): lax.ppermute(sends[1], axis, second)  5.34 us
    ppermute x5, waiting for transfers between devices, swap_halos(): lax.ppermute(sends[0], axis, first)  4.69 us
    ppermute x1, starting transfers between devices, reduce_members(): lax.ppermute(give[0] + give[1] * give[2], axis, [(i, i ^ 1) for i in rang...  4.53 us
  transfers between devices with their start and end apart: 14, of which 8 were waited for; matrix products, arithmetic and copies ran while one was open for 5% of the time, Pallas kernels for 18%

profile of v19, /device:TPU:9, one launch (start us, length us, event | category | flops | bytes accessed | tf_op | source)
XLA Modules:
  0.0 113.0 jit_solution(2851631451022225342)
XLA Ops:
  2.1 4.6 %collective-permute-start.5 = (f32[4,160,128]{2,1,0:T(8,128)S(1)}, f32[4,160,128]{2,1,0:T(8,128)S(1)}, u32[]{:S(2)}, u32[]{:S(2)}) collective-permute-start(f32[4,160,128]{2,1,0:T(8,128)S(1)} %get-tuple-element.30), channel_id=1, source_target_pairs={{1,2},{2,1},{5,6},{6,5},{9,10},{10,9},{13,14},{14,13},{17,18},{18,... | collective-permute-start | bytes 983048 | tf_op jit(solution)/shard_map/ppermute | solution.py:332
  6.8 1.9 %collective-permute-start.3 = (f32[4,160,128]{2,1,0:T(8,128)S(1)}, f32[4,160,128]{2,1,0:T(8,128)}, u32[]{:S(2)}, u32[]{:S(2)}) collective-permute-start(f32[4,160,128]{2,1,0:T(8,128)S(1)} %get-tuple-element.32), channel_id=1, source_target_pairs={{1,2},{2,1},{5,6},{6,5},{9,10},{10,9},{13,14},{14,13},{17,18},{18,... | collective-permute-start | bytes 983048 | tf_op jit(solution)/shard_map/ppermute | solution.py:332
  12.3 2.5 %collective-permute-start.1 = (f32[4,160,128]{2,1,0:T(8,128)S(1)}, f32[4,160,128]{2,1,0:T(8,128)S(1)}, u32[]{:S(2)}, u32[]{:S(2)}) collective-permute-start(f32[4,160,128]{2,1,0:T(8,128)S(1)} %get-tuple-element.28), channel_id=1, source_target_pairs={{1,2},{2,1},{5,6},{6,5},{9,10},{10,9},{13,14},{14,13},{17,18},{18,... | collective-permute-start | bytes 983048 | tf_op jit(solution)/shard_map/ppermute | solution.py:332
  14.8 2.9 %collective-permute-done.2.refs_1_ = f32[4,160,128]{2,1,0:T(8,128)} collective-permute-done((f32[4,160,128]{2,1,0:T(8,128)S(1)}, f32[4,160,128]{2,1,0:T(8,128)}, u32[]{:S(2)}, u32[]{:S(2)}) %collective-permute-start.2) | collective-permute-done | bytes 327712 | tf_op jit(solution)/shard_map/ppermute | solution.py:332
  17.7 3.2 %collective-permute-done.3.refs_3_ = f32[4,160,128]{2,1,0:T(8,128)} collective-permute-done((f32[4,160,128]{2,1,0:T(8,128)S(1)}, f32[4,160,128]{2,1,0:T(8,128)}, u32[]{:S(2)}, u32[]{:S(2)}) %collective-permute-start.3) | collective-permute-done | bytes 327712 | tf_op jit(solution)/shard_map/ppermute | solution.py:332
  20.9 12.2 %shard_map.113 = (f32[16,160,128]{2,1,0:T(8,128)}, f32[16,160,128]{2,1,0:T(8,128)}, f32[16,160,128]{2,1,0:T(8,128)}, f32[16,160,128]{2,1,0:T(8,128)}, f32[16,160...) custom-call(s32[1]{0:T(128)} %bitcast.refs_0_.parity_ref, ...), custom_call_target="tpu_custom_call" | custom-call | tf_op jit(solution)/shard_map/pallas_call | solution.py:266
  33.2 3.0 %collective-permute-start.7 = (f32[4,160,128]{2,1,0:T(8,128)}, f32[4,160,128]{2,1,0:T(8,128)S(1)}, u32[]{:S(2)}, u32[]{:S(2)}) collective-permute-start(f32[4,160,128]{2,1,0:T(8,128)} %get-tuple-element.18), channel_id=1, source_target_pairs={{1,2},{2,1},{5,6},{6,5},{9,10},{10,9},{13,14},{14,13},{17,18},{18,... | collective-permute-start | bytes 983048 | tf_op jit(solution)/shard_map/ppermute | solution.py:332
  38.6 8.0 %shard_map.114 = f32[16,160,128]{2,1,0:T(8,128)} custom-call(s32[1]{0:T(128)} %bitcast.refs_0_.parity_ref, f32[4,160,128]{2,1,0:T(8,128)} %copy-done.5, f32[16,160,128]{2,1,0:T(8,128)} %bitcast.45, f32[4,160,128]{2,1,0:T(8,128)} %copy-done.8, f32[16,160,128]{2,1,0:T(8,128)} %b_ref.1, f32[16,160,128]{2,1,0:T(8,128)} %get-tuple-element.12.refs_5_.g0_ref, ...), custom_call_target="tpu_custom_call" | custom-call | tf_op jit(solution)/shard_map/pallas_call | solution.py:266
  47.5 10.0 %shard_map.115 = (f32[16,160,128]{2,1,0:T(8,128)}, f32[16,160,128]{2,1,0:T(8,128)}, f32[256,128]{1,0:T(8,128)}) custom-call(s32[1]{0:T(128)} %bitcast.refs_0_.parity_ref, f32[4,160,128]{2,1,0:T(8,128)} %copy-done.9, f32[16,160,128]{2,1,0:T(8,128)} %get-tuple-element.17.refs_2_, f32[4,160,128]{2,1,0:T(8,128)} %copy-done.10, f32[16,160,128]{2,1,0:T(8,128)} %b_ref.1, ...), custom_call_target="tpu_custom_call" | custom-call | tf_op jit(solution)/shard_map/pallas_call | solution.py:266
  59.2 2.4 %scatter_fusion = f32[327680]{0:T(1024)S(1)} fusion(f32[327680]{0:T(1024)S(1)} %bitcast.35, s32[256]{0:T(256)S(1)} %get-tuple-element.38, f32[256]{0:T(256)S(1)} %broadcast_select_fusion), kind=kCustom, calls=%fused_computation | custom fusion | flops 256 | bytes 4096 | tf_op jit(solution)/shard_map/scatter-add | solution.py:344
  62.6 2.2 %collective-permute-start.9 = (f32[4,160,128]{2,1,0:T(8,128)}, f32[4,160,128]{2,1,0:T(8,128)S(1)}, u32[]{:S(2)}, u32[]{:S(2)}) collective-permute-start(f32[4,160,128]{2,1,0:T(8,128)} %get-tuple-element.26), channel_id=1, source_target_pairs={{1,2},{2,1},{5,6},{6,5},{9,10},{10,9},{13,14},{14,13},{17,18},{18,... | collective-permute-start | bytes 983048 | tf_op jit(solution)/shard_map/ppermute | solution.py:332
  65.5 1.5 %mul.43 = f32[16,160,128]{2,1,0:T(8,128)S(1)} multiply(f32[16,160,128]{2,1,0:T(8,128)S(1)} %bitcast.37, f32[16,160,128]{2,1,0:T(8,128)} %get-tuple-element.20) | non-fusion elementwise | flops 327680 | bytes 3932160 | tf_op jit(solution)/shard_map/mul | solution.py:415
  66.9 1.8 %collective-permute-done.8.lo_ref = f32[4,160,128]{2,1,0:T(8,128)S(1)} collective-permute-done((f32[4,160,128]{2,1,0:T(8,128)}, f32[4,160,128]{2,1,0:T(8,128)S(1)}, u32[]{:S(2)}, u32[]{:S(2)}) %collective-permute-start.8) | collective-permute-done | bytes 327712 | tf_op jit(solution)/shard_map/ppermute | solution.py:332
  68.7 2.2 %collective-permute-done.9.hi_ref = f32[4,160,128]{2,1,0:T(8,128)S(1)} collective-permute-done((f32[4,160,128]{2,1,0:T(8,128)}, f32[4,160,128]{2,1,0:T(8,128)S(1)}, u32[]{:S(2)}, u32[]{:S(2)}) %collective-permute-start.9) | collective-permute-done | bytes 327712 | tf_op jit(solution)/shard_map/ppermute | solution.py:332
  71.6 9.8 %shard_map.116 = f32[16,160,128]{2,1,0:T(8,128)} custom-call(s32[1]{0:T(128)} %bitcast.refs_0_.parity_ref, f32[4,160,128]{2,1,0:T(8,128)} %copy-done.6, f32[16,160,128]{2,1,0:T(8,128)} %bitcast.38, f32[4,160,128]{2,1,0:T(8,128)} %copy-done.7, f32[16,160,128]{2,1,0:T(8,128)} %b_ref.1, f32[16,160,128]{2,1,0:T(8,128)} %get-tuple-element.12.refs_5_.g0_ref, ...), custom_call_target="tpu_custom_call" | custom-call | tf_op jit(solution)/shard_map/pallas_call | solution.py:198
  81.4 1.5 %multiply_add_fusion = f32[1280,128]{1,0:T(8,128)S(1)} fusion(f32[2560,128]{1,0:T(8,128)} %bitcast.54, s32[]{:T(128)S(6)} %select_n.151, f32[2560,128]{1,0:T(8,128)} %bitcast.49, f32[2560,128]{1,0:T(8,128)S(1)} %bitcast.47), kind=kLoop, calls=%fused_computation.3 | loop fusion | flops 327680 | bytes 2621444 | tf_op jit(solution)/shard_map/add | solution.py:305
  82.9 4.5 %collective-permute-start.10 = (f32[1280,128]{1,0:T(8,128)S(1)}, f32[1280,128]{1,0:T(8,128)}, u32[]{:S(2)}, u32[]{:S(2)}) collective-permute-start(f32[1280,128]{1,0:T(8,128)S(1)} %multiply_add_fusion), channel_id=1, source_target_pairs={{0,4},{4,0},{8,12},{12,8},{1,5},{5,1},{9,13},{13,9},{2,6},{6,2},{1... | collective-permute-start | bytes 1966088 | tf_op jit(solution)/shard_map/ppermute | solution.py:305
  87.5 1.9 %collective-permute-done.10 = f32[1280,128]{1,0:T(8,128)} collective-permute-done((f32[1280,128]{1,0:T(8,128)S(1)}, f32[1280,128]{1,0:T(8,128)}, u32[]{:S(2)}, u32[]{:S(2)}) %collective-permute-start.10) | collective-permute-done | bytes 655392 | tf_op jit(solution)/shard_map/ppermute | solution.py:305
  89.3 1.4 %add_add_fusion = f32[1280,128]{1,0:T(8,128)S(1)} fusion(f32[1280,128]{1,0:T(8,128)} %collective-permute-done.10, f32[2560,128]{1,0:T(8,128)} %bitcast.55, s32[]{:T(128)S(6)} %select_n.148, f32[2560,128]{1,0:T(8,128)S(1)} %bitcast.51, f32[2560,128]{1,0:T(8,128)S(1)} %bitcast.48), kind=kLoop, calls=%fused_computation.4 | loop fusion | flops 491520 | bytes 3276804 | tf_op jit(solution)/shard_map/add | solution.py:306
  90.8 1.3 %collective-permute-start.11 = (f32[640,128]{1,0:T(8,128)S(1)}, f32[640,128]{1,0:T(8,128)S(1)}, u32[]{:S(2)}, u32[]{:S(2)}) collective-permute-start(f32[640,128]{1,0:T(8,128)S(1)} %constant_dynamic-slice_fusion), channel_id=1, source_target_pairs={{0,8},{4,12},{8,0},{12,4},{1,9},{5,13},{9,1},{13,5},{2,10},{6,14},... | collective-permute-start | bytes 983048 | tf_op jit(solution)/shard_map/ppermute | solution.py:317
  92.0 7.7 %collective-permute-done.11 = f32[640,128]{1,0:T(8,128)S(1)} collective-permute-done((f32[640,128]{1,0:T(8,128)S(1)}, f32[640,128]{1,0:T(8,128)S(1)}, u32[]{:S(2)}, u32[]{:S(2)}) %collective-permute-start.11) | collective-permute-done | bytes 327712 | tf_op jit(solution)/shard_map/ppermute | solution.py:317
  101.1 6.8 %collective-permute-done.12 = f32[640,128]{1,0:T(8,128)S(1)} collective-permute-done((f32[640,128]{1,0:T(8,128)S(1)}, f32[640,128]{1,0:T(8,128)S(1)}, u32[]{:S(2)}, u32[]{:S(2)}) %collective-permute-start.12) | collective-permute-done | bytes 327712 | tf_op jit(solution)/shard_map/ppermute | solution.py:323
  107.9 2.2 %collective-permute-start.13 = (f32[1280,128]{1,0:T(8,128)S(1)}, f32[1280,128]{1,0:T(8,128)S(1)}, u32[]{:S(2)}, u32[]{:S(2)}) collective-permute-start(f32[1280,128]{1,0:T(8,128)S(1)} %maximum_select_fusion.1), channel_id=1, source_target_pairs={{0,4},{4,0},{8,12},{12,8},{1,5},{5,1},{9,13},{13,9},{2,6},{6,2},{1... | collective-permute-start | bytes 1966088 | tf_op jit(solution)/shard_map/ppermute | solution.py:323
  110.1 1.7 %collective-permute-done.13 = f32[1280,128]{1,0:T(8,128)S(1)} collective-permute-done((f32[1280,128]{1,0:T(8,128)S(1)}, f32[1280,128]{1,0:T(8,128)S(1)}, u32[]{:S(2)}, u32[]{:S(2)}) %collective-permute-start.13) | collective-permute-done | bytes 655392 | tf_op jit(solution)/shard_map/ppermute | solution.py:323
  (64 shorter events, 14.2 us)
Async XLA Ops:
  0.6 6.0 %copy-start.2 = (f32[1,16,160,128]{3,2,1,0:T(8,128)S(1)}, f32[1,16,160,128]{3,2,1,0:T(8,128)}, u32[]{:S(2)}) copy-start(f32[1,16,160,128]{3,2,1,0:T(8,128)} %param.12) | copy-start | bytes 3932164
  0.7 8.1 %copy-start.3 = (f32[1,16,160,128]{3,2,1,0:T(8,128)S(1)}, f32[1,16,160,128]{3,2,1,0:T(8,128)}, u32[]{:S(2)}) copy-start(f32[1,16,160,128]{3,2,1,0:T(8,128)} %param.14) | copy-start | bytes 3932164
  2.0 10.4 %collective-permute-start.4 = (f32[4,160,128]{2,1,0:T(8,128)S(1)}, f32[4,160,128]{2,1,0:T(8,128)S(1)}, u32[]{:S(2)}, u32[]{:S(2)}) collective-permute-start(f32[4,160,128]{2,1,0:T(8,128)S(1)} %get-tuple-element.31), channel_id=1, source_target_pairs={{0,1},{1,0},{2,3},{3,2},{4,5},{5,4},{6,7},{7,6},{8,9},{9,8},{10,11... | collective-permute-start | bytes 983048 | tf_op jit(solution)/shard_map/ppermute | solution.py:332
  2.0 8.4 %copy-start.13 = (s32[256]{0:T(256)S(1)}, s32[256]{0:T(256)}, u32[]{:S(2)}) copy-start(s32[256]{0:T(256)} %param.18) | copy-start | bytes 3076
  2.0 9.7 %copy-start.15 = (f32[2]{0:T(128)S(1)}, f32[2]{0:T(128)}, u32[]{:S(2)}) copy-start(f32[2]{0:T(128)} %param.16) | copy-start | bytes 28
  2.1 12.8 %collective-permute-start.5 = (f32[4,160,128]{2,1,0:T(8,128)S(1)}, f32[4,160,128]{2,1,0:T(8,128)S(1)}, u32[]{:S(2)}, u32[]{:S(2)}) collective-permute-start(f32[4,160,128]{2,1,0:T(8,128)S(1)} %get-tuple-element.30), channel_id=1, source_target_pairs={{1,2},{2,1},{5,6},{6,5},{9,10},{10,9},{13,14},{14,13},{17,18},{18,... | collective-permute-start | bytes 983048 | tf_op jit(solution)/shard_map/ppermute | solution.py:332
  6.7 11.0 %collective-permute-start.2 = (f32[4,160,128]{2,1,0:T(8,128)S(1)}, f32[4,160,128]{2,1,0:T(8,128)}, u32[]{:S(2)}, u32[]{:S(2)}) collective-permute-start(f32[4,160,128]{2,1,0:T(8,128)S(1)} %get-tuple-element.33), channel_id=1, source_target_pairs={{0,1},{1,0},{2,3},{3,2},{4,5},{5,4},{6,7},{7,6},{8,9},{9,8},{10,11... | collective-permute-start | bytes 983048 | tf_op jit(solution)/shard_map/ppermute | solution.py:332
  6.8 14.1 %collective-permute-start.3 = (f32[4,160,128]{2,1,0:T(8,128)S(1)}, f32[4,160,128]{2,1,0:T(8,128)}, u32[]{:S(2)}, u32[]{:S(2)}) collective-permute-start(f32[4,160,128]{2,1,0:T(8,128)S(1)} %get-tuple-element.32), channel_id=1, source_target_pairs={{1,2},{2,1},{5,6},{6,5},{9,10},{10,9},{13,14},{14,13},{17,18},{18,... | collective-permute-start | bytes 983048 | tf_op jit(solution)/shard_map/ppermute | solution.py:332
  8.8 29.0 %collective-permute-start = (f32[4,160,128]{2,1,0:T(8,128)S(1)}, f32[4,160,128]{2,1,0:T(8,128)S(1)}, u32[]{:S(2)}, u32[]{:S(2)}) collective-permute-start(f32[4,160,128]{2,1,0:T(8,128)S(1)} %get-tuple-element.29), channel_id=1, source_target_pairs={{0,1},{1,0},{2,3},{3,2},{4,5},{5,4},{6,7},{7,6},{8,9},{9,8},{10,11... | collective-permute-start | bytes 983048 | tf_op jit(solution)/shard_map/ppermute | solution.py:332
  12.3 8.5 %copy-start.11 = (f32[4,160,128]{2,1,0:T(8,128)}, f32[4,160,128]{2,1,0:T(8,128)S(1)}, u32[]{:S(2)}) copy-start(f32[4,160,128]{2,1,0:T(8,128)S(1)} %collective-permute-done.4.refs_4_) | copy-start | bytes 983044
  12.3 25.5 %collective-permute-start.1 = (f32[4,160,128]{2,1,0:T(8,128)S(1)}, f32[4,160,128]{2,1,0:T(8,128)S(1)}, u32[]{:S(2)}, u32[]{:S(2)}) collective-permute-start(f32[4,160,128]{2,1,0:T(8,128)S(1)} %get-tuple-element.28), channel_id=1, source_target_pairs={{1,2},{2,1},{5,6},{6,5},{9,10},{10,9},{13,14},{14,13},{17,18},{18,... | collective-permute-start | bytes 983048 | tf_op jit(solution)/shard_map/ppermute | solution.py:332
  14.8 6.1 %copy-start.12 = (f32[4,160,128]{2,1,0:T(8,128)}, f32[4,160,128]{2,1,0:T(8,128)S(1)}, u32[]{:S(2)}) copy-start(f32[4,160,128]{2,1,0:T(8,128)S(1)} %collective-permute-done.5.refs_6_) | copy-start | bytes 983044
  33.1 13.5 %collective-permute-start.6 = (f32[4,160,128]{2,1,0:T(8,128)}, f32[4,160,128]{2,1,0:T(8,128)S(1)}, u32[]{:S(2)}, u32[]{:S(2)}) collective-permute-start(f32[4,160,128]{2,1,0:T(8,128)} %get-tuple-element.16), channel_id=1, source_target_pairs={{0,1},{1,0},{2,3},{3,2},{4,5},{5,4},{6,7},{7,6},{8,9},{9,8},{10,11... | collective-permute-start | bytes 983048 | tf_op jit(solution)/shard_map/ppermute | solution.py:332
  33.2 13.5 %collective-permute-start.7 = (f32[4,160,128]{2,1,0:T(8,128)}, f32[4,160,128]{2,1,0:T(8,128)S(1)}, u32[]{:S(2)}, u32[]{:S(2)}) collective-permute-start(f32[4,160,128]{2,1,0:T(8,128)} %get-tuple-element.18), channel_id=1, source_target_pairs={{1,2},{2,1},{5,6},{6,5},{9,10},{10,9},{13,14},{14,13},{17,18},{18,... | collective-permute-start | bytes 983048 | tf_op jit(solution)/shard_map/ppermute | solution.py:332
  47.5 11.1 %copy-start.14 = (f32[2,256]{1,0:T(2,128)S(1)}, f32[2,256]{1,0:T(2,128)}, u32[]{:S(2)}) copy-start(f32[2,256]{1,0:T(2,128)} %param.19) | copy-start | bytes 6148
  47.5 11.6 %copy-start = (f32[16,160,128]{2,1,0:T(8,128)S(1)}, f32[16,160,128]{2,1,0:T(8,128)}, u32[]{:S(2)}) copy-start(f32[16,160,128]{2,1,0:T(8,128)} %shard_map.114) | copy-start | bytes 3932164
  61.6 5.3 %copy-start.1 = (f32[327680]{0:T(1024)}, f32[327680]{0:T(1024)S(1)}, u32[]{:S(2)}) copy-start(f32[327680]{0:T(1024)S(1)} %scatter_fusion) | copy-start | bytes 3932164
  62.6 6.1 %collective-permute-start.8 = (f32[4,160,128]{2,1,0:T(8,128)}, f32[4,160,128]{2,1,0:T(8,128)S(1)}, u32[]{:S(2)}, u32[]{:S(2)}) collective-permute-start(f32[4,160,128]{2,1,0:T(8,128)} %get-tuple-element.27), channel_id=1, source_target_pairs={{0,1},{1,0},{2,3},{3,2},{4,5},{5,4},{6,7},{7,6},{8,9},{9,8},{10,11... | collective-permute-start | bytes 983048 | tf_op jit(solution)/shard_map/ppermute | solution.py:332
  62.6 8.3 %collective-permute-start.9 = (f32[4,160,128]{2,1,0:T(8,128)}, f32[4,160,128]{2,1,0:T(8,128)S(1)}, u32[]{:S(2)}, u32[]{:S(2)}) collective-permute-start(f32[4,160,128]{2,1,0:T(8,128)} %get-tuple-element.26), channel_id=1, source_target_pairs={{1,2},{2,1},{5,6},{6,5},{9,10},{10,9},{13,14},{14,13},{17,18},{18,... | collective-permute-start | bytes 983048 | tf_op jit(solution)/shard_map/ppermute | solution.py:332
  81.4 7.9 %copy-start.4 = (f32[16,160,128]{2,1,0:T(8,128)S(1)}, f32[16,160,128]{2,1,0:T(8,128)}, u32[]{:S(2)}) copy-start(f32[16,160,128]{2,1,0:T(8,128)} %shard_map.116) | copy-start | bytes 3932164
  82.9 6.4 %collective-permute-start.10 = (f32[1280,128]{1,0:T(8,128)S(1)}, f32[1280,128]{1,0:T(8,128)}, u32[]{:S(2)}, u32[]{:S(2)}) collective-permute-start(f32[1280,128]{1,0:T(8,128)S(1)} %multiply_add_fusion), channel_id=1, source_target_pairs={{0,4},{4,0},{8,12},{12,8},{1,5},{5,1},{9,13},{13,9},{2,6},{6,2},{1... | collective-permute-start | bytes 1966088 | tf_op jit(solution)/shard_map/ppermute | solution.py:305
  90.8 9.0 %collective-permute-start.11 = (f32[640,128]{1,0:T(8,128)S(1)}, f32[640,128]{1,0:T(8,128)S(1)}, u32[]{:S(2)}, u32[]{:S(2)}) collective-permute-start(f32[640,128]{1,0:T(8,128)S(1)} %constant_dynamic-slice_fusion), channel_id=1, source_target_pairs={{0,8},{4,12},{8,0},{12,4},{1,9},{5,13},{9,1},{13,5},{2,10},{6,14},... | collective-permute-start | bytes 983048 | tf_op jit(solution)/shard_map/ppermute | solution.py:317
  99.8 8.1 %collective-permute-start.12 = (f32[640,128]{1,0:T(8,128)S(1)}, f32[640,128]{1,0:T(8,128)S(1)}, u32[]{:S(2)}, u32[]{:S(2)}) collective-permute-start(f32[640,128]{1,0:T(8,128)S(1)} %add_multiply_fusion), channel_id=1, source_target_pairs={{0,8},{4,12},{8,0},{12,4},{1,9},{5,13},{9,1},{13,5},{2,10},{6,14},... | collective-permute-start | bytes 983048 | tf_op jit(solution)/shard_map/ppermute | solution.py:323
  107.9 3.9 %collective-permute-start.13 = (f32[1280,128]{1,0:T(8,128)S(1)}, f32[1280,128]{1,0:T(8,128)S(1)}, u32[]{:S(2)}, u32[]{:S(2)}) collective-permute-start(f32[1280,128]{1,0:T(8,128)S(1)} %maximum_select_fusion.1), channel_id=1, source_target_pairs={{0,4},{4,0},{8,12},{12,8},{1,5},{5,1},{9,13},{13,9},{2,6},{6,2},{1... | collective-permute-start | bytes 1966088 | tf_op jit(solution)/shard_map/ppermute | solution.py:323
  (6 other events, 6.1 us)

commit v20 on v16

--- a/solution.py
+++ b/solution.py
@@ -204,6 +204,7 @@
         out_shape=out,
         scratch_shapes=[pltpu.VMEM((planes + 2 * HALO, height + 2 * PADY, depth), jnp.float32)],
         compiler_params=pltpu.CompilerParams(dimension_semantics=("arbitrary",)),
+        cost_estimate=pl.CostEstimate(flops=100 * mid.size, transcendentals=0, bytes_accessed=40 * mid.size),
     )(parity, lo, mid, hi, b, g[0], g[1], g[2], c, old, receivers, valid, amount)
 
 
@@ -271,6 +272,7 @@
         out_shape=out_shape,
         scratch_shapes=scratch,
         compiler_params=pltpu.CompilerParams(dimension_semantics=("arbitrary",)),
+        cost_estimate=pl.CostEstimate(flops=100 * mid.size, transcendentals=0, bytes_accessed=40 * mid.size),
     )(*args)
 
 
@@ -287,6 +289,7 @@
         out_shape=[out, out, out],
         scratch_shapes=[pltpu.VMEM((planes + 2 * HALO, height + 2 * PADY, depth), jnp.float32)],
         compiler_params=pltpu.CompilerParams(dimension_semantics=("arbitrary",)),
+        cost_estimate=pl.CostEstimate(flops=100 * mid.size, transcendentals=0, bytes_accessed=40 * mid.size),
     )(lo, mid, hi)
 
 

time: 112 us -> 112 us (level)
  no operation moved by 1% of the time
where the time goes in v20:
time: 112 us
  Pallas kernels  40.2 us (36%)
  waiting for transfers between devices  29.2 us (26%)
  starting transfers between devices  24.8 us (22%)
  other arithmetic  10.7 us (10%)
  local copies, waits for them, and re-layouts  5.12 us (5%)
  between operations  1.73 us (2%)
    pallas_call x3, Pallas kernels, apply_step(): pl.pallas_call(kernel, grid=(planes // block,), in_specs=in_specs, out_sp...  30.3 us
    ppermute x5, starting transfers between devices, swap_halos(): lax.ppermute(sends[1], axis, second)  14.3 us
    pallas_call x1, Pallas kernels, apply_final(): pl.pallas_call(functools.partial(final_kernel, block=block, rows=rows), g...  9.91 us
    ppermute x2, waiting for transfers between devices, reduce_members(): rows = keep + lax.ppermute(give, axis, pairs)  9.44 us
    ppermute x2, waiting for transfers between devices, reduce_members(): other = lax.ppermute(rows, axis, pairs)  8.52 us
    ppermute x5, waiting for transfers between devices, swap_halos(): lax.ppermute(sends[0], axis, first)  5.93 us
    ppermute x2, starting transfers between devices, reduce_members(): rows = keep + lax.ppermute(give, axis, pairs)  5.81 us
    ppermute x5, waiting for transfers between devices, swap_halos(): lax.ppermute(sends[1], axis, second)  5.36 us
  transfers between devices with their start and end apart: 14, of which 8 were waited for; matrix products, arithmetic and copies ran while one was open for 4% of the time, Pallas kernels for 18%

profile of v20, /device:TPU:9, one launch (start us, length us, event | category | flops | bytes accessed | tf_op | source)
XLA Modules:
  0.0 111.7 jit_solution(10998005913252860150)
XLA Ops:
  0.7 1.3 %dynamic-slice_bitcast_fusion = (f32[4,160,128]{2,1,0:T(8,128)S(1)}, f32[4,160,128]{2,1,0:T(8,128)S(1)}) fusion(f32[1,16,160,128]{3,2,1,0:T(8,128)} %param.12, s32[]{:T(128)S(6)} %select_n.135, s32[]{:T(128)S(6)} %select_n.134), kind=kLoop, calls=%fused_computation.6 | loop fusion | bytes 1310728 | tf_op jit(solution)/shard_map/dynamic_slice | solution.py:332
  2.1 4.6 %collective-permute-start.3 = (f32[4,160,128]{2,1,0:T(8,128)S(1)}, f32[4,160,128]{2,1,0:T(8,128)S(1)}, u32[]{:S(2)}, u32[]{:S(2)}) collective-permute-start(f32[4,160,128]{2,1,0:T(8,128)S(1)} %get-tuple-element.30), channel_id=1, source_target_pairs={{1,2},{2,1},{5,6},{6,5},{9,10},{10,9},{13,14},{14,13},{17,18},{18,... | collective-permute-start | bytes 983048 | tf_op jit(solution)/shard_map/ppermute | solution.py:325
  6.8 1.9 %collective-permute-start.5 = (f32[4,160,128]{2,1,0:T(8,128)S(1)}, f32[4,160,128]{2,1,0:T(8,128)}, u32[]{:S(2)}, u32[]{:S(2)}) collective-permute-start(f32[4,160,128]{2,1,0:T(8,128)S(1)} %get-tuple-element.28), channel_id=1, source_target_pairs={{1,2},{2,1},{5,6},{6,5},{9,10},{10,9},{13,14},{14,13},{17,18},{18,... | collective-permute-start | bytes 983048 | tf_op jit(solution)/shard_map/ppermute | solution.py:325
  12.3 2.5 %collective-permute-start.1 = (f32[4,160,128]{2,1,0:T(8,128)S(1)}, f32[4,160,128]{2,1,0:T(8,128)S(1)}, u32[]{:S(2)}, u32[]{:S(2)}) collective-permute-start(f32[4,160,128]{2,1,0:T(8,128)S(1)} %get-tuple-element.32), channel_id=1, source_target_pairs={{1,2},{2,1},{5,6},{6,5},{9,10},{10,9},{13,14},{14,13},{17,18},{18,... | collective-permute-start | bytes 983048 | tf_op jit(solution)/shard_map/ppermute | solution.py:325
  14.8 2.9 %collective-permute-done.4.refs_4_ = f32[4,160,128]{2,1,0:T(8,128)} collective-permute-done((f32[4,160,128]{2,1,0:T(8,128)S(1)}, f32[4,160,128]{2,1,0:T(8,128)}, u32[]{:S(2)}, u32[]{:S(2)}) %collective-permute-start.4) | collective-permute-done | bytes 327712 | tf_op jit(solution)/shard_map/ppermute | solution.py:325
  17.7 3.2 %collective-permute-done.5.refs_6_ = f32[4,160,128]{2,1,0:T(8,128)} collective-permute-done((f32[4,160,128]{2,1,0:T(8,128)S(1)}, f32[4,160,128]{2,1,0:T(8,128)}, u32[]{:S(2)}, u32[]{:S(2)}) %collective-permute-start.5) | collective-permute-done | bytes 327712 | tf_op jit(solution)/shard_map/ppermute | solution.py:325
  20.9 12.2 %shard_map.113 = (f32[16,160,128]{2,1,0:T(8,128)}, f32[16,160,128]{2,1,0:T(8,128)}, f32[16,160,128]{2,1,0:T(8,128)}, f32[16,160,128]{2,1,0:T(8,128)}, f32[16,160...) custom-call(s32[1]{0:T(128)} %bitcast.refs_0_.parity_ref, ...), custom_call_target="tpu_custom_call" | custom-call | flops 32768000 | bytes 13107200 | tf_op jit(solution)/shard_map/pallas_call | solution.py:267
  33.2 3.0 %collective-permute-start.7 = (f32[4,160,128]{2,1,0:T(8,128)}, f32[4,160,128]{2,1,0:T(8,128)S(1)}, u32[]{:S(2)}, u32[]{:S(2)}) collective-permute-start(f32[4,160,128]{2,1,0:T(8,128)} %get-tuple-element.18), channel_id=1, source_target_pairs={{1,2},{2,1},{5,6},{6,5},{9,10},{10,9},{13,14},{14,13},{17,18},{18,... | collective-permute-start | bytes 983048 | tf_op jit(solution)/shard_map/ppermute | solution.py:325
  38.7 8.0 %shard_map.114 = f32[16,160,128]{2,1,0:T(8,128)} custom-call(s32[1]{0:T(128)} %bitcast.refs_0_.parity_ref, f32[4,160,128]{2,1,0:T(8,128)} %copy-done.5, f32[16,160,128]{2,1,0:T(8,128)} %bitcast.43, f32[4,160,128]{2,1,0:T(8,128)} %copy-done.8, f32[16,160,128]{2,1,0:T(8,128)} %b_ref.1, f32[16,160,128]{2,1,0:T(8,128)} %get-tuple-element.12.refs_5_.g0_ref, ...), custom_call_target="tpu_custom_call" | custom-call | flops 32768000 | bytes 13107200 | tf_op jit(solution)/shard_map/pallas_call | solution.py:267
  47.6 10.1 %shard_map.115 = (f32[16,160,128]{2,1,0:T(8,128)}, f32[16,160,128]{2,1,0:T(8,128)}, f32[256,128]{1,0:T(8,128)}) custom-call(s32[1]{0:T(128)} %bitcast.refs_0_.parity_ref, f32[4,160,128]{2,1,0:T(8,128)} %copy-done.9, f32[16,160,128]{2,1,0:T(8,128)} %get-tuple-element.17.refs_2_, f32[4,160,128]{2,1,0:T(8,128)} %copy-done.10, f32[16,160,128]{2,1,0:T(8,128)} %b_ref.1, ...), custom_call_target="tpu_custom_call" | custom-call | flops 32768000 | bytes 13107200 | tf_op jit(solution)/shard_map/pallas_call | solution.py:267
  59.3 2.4 %scatter_fusion = f32[327680]{0:T(1024)S(1)} fusion(f32[327680]{0:T(1024)S(1)} %bitcast.33, s32[256]{0:T(256)S(1)} %get-tuple-element.38, f32[256]{0:T(256)S(1)} %broadcast_select_fusion), kind=kCustom, calls=%fused_computation | custom fusion | flops 256 | bytes 4096 | tf_op jit(solution)/shard_map/scatter-add | solution.py:337
  61.9 2.2 %collective-permute-start.9 = (f32[4,160,128]{2,1,0:T(8,128)S(1)}, f32[4,160,128]{2,1,0:T(8,128)S(1)}, u32[]{:S(2)}, u32[]{:S(2)}) collective-permute-start(f32[4,160,128]{2,1,0:T(8,128)S(1)} %get-tuple-element.26), channel_id=1, source_target_pairs={{1,2},{2,1},{5,6},{6,5},{9,10},{10,9},{13,14},{14,13},{17,18},{18,... | collective-permute-start | bytes 983048 | tf_op jit(solution)/shard_map/ppermute | solution.py:325
  64.7 3.0 %collective-permute-done.8.lo_ref = f32[4,160,128]{2,1,0:T(8,128)S(1)} collective-permute-done((f32[4,160,128]{2,1,0:T(8,128)S(1)}, f32[4,160,128]{2,1,0:T(8,128)S(1)}, u32[]{:S(2)}, u32[]{:S(2)}) %collective-permute-start.8) | collective-permute-done | bytes 327712 | tf_op jit(solution)/shard_map/ppermute | solution.py:325
  67.8 2.2 %collective-permute-done.9.hi_ref = f32[4,160,128]{2,1,0:T(8,128)S(1)} collective-permute-done((f32[4,160,128]{2,1,0:T(8,128)S(1)}, f32[4,160,128]{2,1,0:T(8,128)S(1)}, u32[]{:S(2)}, u32[]{:S(2)}) %collective-permute-start.9) | collective-permute-done | bytes 327712 | tf_op jit(solution)/shard_map/ppermute | solution.py:325
  70.7 9.9 %shard_map.116 = f32[16,160,128]{2,1,0:T(8,128)} custom-call(s32[1]{0:T(128)} %bitcast.refs_0_.parity_ref, f32[4,160,128]{2,1,0:T(8,128)} %copy-done.6, f32[16,160,128]{2,1,0:T(8,128)} %bitcast.35, f32[4,160,128]{2,1,0:T(8,128)} %copy-done.7, f32[16,160,128]{2,1,0:T(8,128)} %b_ref.1, f32[16,160,128]{2,1,0:T(8,128)} %get-tuple-element.12.refs_5_.g0_ref, ...), custom_call_target="tpu_custom_call" | custom-call | flops 32768000 | bytes 13107200 | tf_op jit(solution)/shard_map/pallas_call | solution.py:198
  80.6 2.5 %multiply_add_fusion = f32[16,160,128]{2,1,0:T(8,128)S(1)} fusion(f32[16,160,128]{2,1,0:T(8,128)} %shard_map.116, f32[16,160,128]{2,1,0:T(8,128)S(1)} %copy-done.4, f32[16,160,128]{2,1,0:T(8,128)} %bitcast.36, f32[16,160,128]{2,1,0:T(8,128)} %get-tuple-element.20), kind=kLoop, calls=%fused_computation.2 | loop fusion | flops 983040 | bytes 6553600 | tf_op jit(solution)/shard_map/add | solution.py:407
  83.1 4.5 %collective-permute-start.10 = (f32[1280,128]{1,0:T(8,128)S(1)}, f32[1280,128]{1,0:T(8,128)S(1)}, u32[]{:S(2)}, u32[]{:S(2)}) collective-permute-start(f32[1280,128]{1,0:T(8,128)S(1)} %constant_dynamic-slice_fusion.1), channel_id=1, source_target_pairs={{0,4},{4,0},{8,12},{12,8},{1,5},{5,1},{9,13},{13,9},{2,6},{6,2},{1... | collective-permute-start | bytes 1966088 | tf_op jit(solution)/shard_map/ppermute | solution.py:310
  87.6 1.7 %collective-permute-done.10 = f32[1280,128]{1,0:T(8,128)S(1)} collective-permute-done((f32[1280,128]{1,0:T(8,128)S(1)}, f32[1280,128]{1,0:T(8,128)S(1)}, u32[]{:S(2)}, u32[]{:S(2)}) %collective-permute-start.10) | collective-permute-done | bytes 655392 | tf_op jit(solution)/shard_map/ppermute | solution.py:310
  89.5 1.3 %collective-permute-start.11 = (f32[640,128]{1,0:T(8,128)S(1)}, f32[640,128]{1,0:T(8,128)S(1)}, u32[]{:S(2)}, u32[]{:S(2)}) collective-permute-start(f32[640,128]{1,0:T(8,128)S(1)} %constant_dynamic-slice_fusion), channel_id=1, source_target_pairs={{0,8},{4,12},{8,0},{12,4},{1,9},{5,13},{9,1},{13,5},{2,10},{6,14},... | collective-permute-start | bytes 983048 | tf_op jit(solution)/shard_map/ppermute | solution.py:310
  90.8 7.7 %collective-permute-done.11 = f32[640,128]{1,0:T(8,128)S(1)} collective-permute-done((f32[640,128]{1,0:T(8,128)S(1)}, f32[640,128]{1,0:T(8,128)S(1)}, u32[]{:S(2)}, u32[]{:S(2)}) %collective-permute-start.11) | collective-permute-done | bytes 327712 | tf_op jit(solution)/shard_map/ppermute | solution.py:310
  98.5 1.3 %collective-permute-start.12 = (f32[640,128]{1,0:T(8,128)S(1)}, f32[640,128]{1,0:T(8,128)S(1)}, u32[]{:S(2)}, u32[]{:S(2)}) collective-permute-start(f32[640,128]{1,0:T(8,128)S(1)} %add_multiply_fusion), channel_id=1, source_target_pairs={{0,8},{4,12},{8,0},{12,4},{1,9},{5,13},{9,1},{13,5},{2,10},{6,14},... | collective-permute-start | bytes 983048 | tf_op jit(solution)/shard_map/ppermute | solution.py:316
  99.8 6.8 %collective-permute-done.12 = f32[640,128]{1,0:T(8,128)S(1)} collective-permute-done((f32[640,128]{1,0:T(8,128)S(1)}, f32[640,128]{1,0:T(8,128)S(1)}, u32[]{:S(2)}, u32[]{:S(2)}) %collective-permute-start.12) | collective-permute-done | bytes 327712 | tf_op jit(solution)/shard_map/ppermute | solution.py:316
  106.6 2.2 %collective-permute-start.13 = (f32[1280,128]{1,0:T(8,128)S(1)}, f32[1280,128]{1,0:T(8,128)S(1)}, u32[]{:S(2)}, u32[]{:S(2)}) collective-permute-start(f32[1280,128]{1,0:T(8,128)S(1)} %maximum_select_fusion.1), channel_id=1, source_target_pairs={{0,4},{4,0},{8,12},{12,8},{1,5},{5,1},{9,13},{13,9},{2,6},{6,2},{1... | collective-permute-start | bytes 1966088 | tf_op jit(solution)/shard_map/ppermute | solution.py:316
  108.8 1.7 %collective-permute-done.13 = f32[1280,128]{1,0:T(8,128)S(1)} collective-permute-done((f32[1280,128]{1,0:T(8,128)S(1)}, f32[1280,128]{1,0:T(8,128)S(1)}, u32[]{:S(2)}, u32[]{:S(2)}) %collective-permute-start.13) | collective-permute-done | bytes 655392 | tf_op jit(solution)/shard_map/ppermute | solution.py:316
  (64 shorter events, 10.9 us)
Async XLA Ops:
  0.6 6.0 %copy-start = (f32[16,160,128]{2,1,0:T(8,128)S(1)}, f32[16,160,128]{2,1,0:T(8,128)}, u32[]{:S(2)}) copy-start(f32[16,160,128]{2,1,0:T(8,128)} %b_ref.1) | copy-start | bytes 3932164
  0.7 8.1 %copy-start.3 = (f32[1,16,160,128]{3,2,1,0:T(8,128)S(1)}, f32[1,16,160,128]{3,2,1,0:T(8,128)}, u32[]{:S(2)}) copy-start(f32[1,16,160,128]{3,2,1,0:T(8,128)} %param.14) | copy-start | bytes 3932164
  2.0 10.4 %collective-permute-start.2 = (f32[4,160,128]{2,1,0:T(8,128)S(1)}, f32[4,160,128]{2,1,0:T(8,128)S(1)}, u32[]{:S(2)}, u32[]{:S(2)}) collective-permute-start(f32[4,160,128]{2,1,0:T(8,128)S(1)} %get-tuple-element.31), channel_id=1, source_target_pairs={{0,1},{1,0},{2,3},{3,2},{4,5},{5,4},{6,7},{7,6},{8,9},{9,8},{10,11... | collective-permute-start | bytes 983048 | tf_op jit(solution)/shard_map/ppermute | solution.py:325
  2.0 8.4 %copy-start.13 = (s32[256]{0:T(256)S(1)}, s32[256]{0:T(256)}, u32[]{:S(2)}) copy-start(s32[256]{0:T(256)} %param.18) | copy-start | bytes 3076
  2.0 9.7 %copy-start.15 = (f32[2]{0:T(128)S(1)}, f32[2]{0:T(128)}, u32[]{:S(2)}) copy-start(f32[2]{0:T(128)} %param.16) | copy-start | bytes 28
  2.1 12.8 %collective-permute-start.3 = (f32[4,160,128]{2,1,0:T(8,128)S(1)}, f32[4,160,128]{2,1,0:T(8,128)S(1)}, u32[]{:S(2)}, u32[]{:S(2)}) collective-permute-start(f32[4,160,128]{2,1,0:T(8,128)S(1)} %get-tuple-element.30), channel_id=1, source_target_pairs={{1,2},{2,1},{5,6},{6,5},{9,10},{10,9},{13,14},{14,13},{17,18},{18,... | collective-permute-start | bytes 983048 | tf_op jit(solution)/shard_map/ppermute | solution.py:325
  6.7 11.0 %collective-permute-start.4 = (f32[4,160,128]{2,1,0:T(8,128)S(1)}, f32[4,160,128]{2,1,0:T(8,128)}, u32[]{:S(2)}, u32[]{:S(2)}) collective-permute-start(f32[4,160,128]{2,1,0:T(8,128)S(1)} %get-tuple-element.29), channel_id=1, source_target_pairs={{0,1},{1,0},{2,3},{3,2},{4,5},{5,4},{6,7},{7,6},{8,9},{9,8},{10,11... | collective-permute-start | bytes 983048 | tf_op jit(solution)/shard_map/ppermute | solution.py:325
  6.8 14.1 %collective-permute-start.5 = (f32[4,160,128]{2,1,0:T(8,128)S(1)}, f32[4,160,128]{2,1,0:T(8,128)}, u32[]{:S(2)}, u32[]{:S(2)}) collective-permute-start(f32[4,160,128]{2,1,0:T(8,128)S(1)} %get-tuple-element.28), channel_id=1, source_target_pairs={{1,2},{2,1},{5,6},{6,5},{9,10},{10,9},{13,14},{14,13},{17,18},{18,... | collective-permute-start | bytes 983048 | tf_op jit(solution)/shard_map/ppermute | solution.py:325
  8.8 29.0 %collective-permute-start = (f32[4,160,128]{2,1,0:T(8,128)S(1)}, f32[4,160,128]{2,1,0:T(8,128)S(1)}, u32[]{:S(2)}, u32[]{:S(2)}) collective-permute-start(f32[4,160,128]{2,1,0:T(8,128)S(1)} %get-tuple-element.33), channel_id=1, source_target_pairs={{0,1},{1,0},{2,3},{3,2},{4,5},{5,4},{6,7},{7,6},{8,9},{9,8},{10,11... | collective-permute-start | bytes 983048 | tf_op jit(solution)/shard_map/ppermute | solution.py:325
  12.3 8.5 %copy-start.11 = (f32[4,160,128]{2,1,0:T(8,128)}, f32[4,160,128]{2,1,0:T(8,128)S(1)}, u32[]{:S(2)}) copy-start(f32[4,160,128]{2,1,0:T(8,128)S(1)} %collective-permute-done.2.refs_1_) | copy-start | bytes 983044
  12.3 25.5 %collective-permute-start.1 = (f32[4,160,128]{2,1,0:T(8,128)S(1)}, f32[4,160,128]{2,1,0:T(8,128)S(1)}, u32[]{:S(2)}, u32[]{:S(2)}) collective-permute-start(f32[4,160,128]{2,1,0:T(8,128)S(1)} %get-tuple-element.32), channel_id=1, source_target_pairs={{1,2},{2,1},{5,6},{6,5},{9,10},{10,9},{13,14},{14,13},{17,18},{18,... | collective-permute-start | bytes 983048 | tf_op jit(solution)/shard_map/ppermute | solution.py:325
  14.8 6.1 %copy-start.12 = (f32[4,160,128]{2,1,0:T(8,128)}, f32[4,160,128]{2,1,0:T(8,128)S(1)}, u32[]{:S(2)}) copy-start(f32[4,160,128]{2,1,0:T(8,128)S(1)} %collective-permute-done.3.refs_3_) | copy-start | bytes 983044
  33.1 13.5 %collective-permute-start.6 = (f32[4,160,128]{2,1,0:T(8,128)}, f32[4,160,128]{2,1,0:T(8,128)S(1)}, u32[]{:S(2)}, u32[]{:S(2)}) collective-permute-start(f32[4,160,128]{2,1,0:T(8,128)} %get-tuple-element.16), channel_id=1, source_target_pairs={{0,1},{1,0},{2,3},{3,2},{4,5},{5,4},{6,7},{7,6},{8,9},{9,8},{10,11... | collective-permute-start | bytes 983048 | tf_op jit(solution)/shard_map/ppermute | solution.py:325
  33.2 13.5 %collective-permute-start.7 = (f32[4,160,128]{2,1,0:T(8,128)}, f32[4,160,128]{2,1,0:T(8,128)S(1)}, u32[]{:S(2)}, u32[]{:S(2)}) collective-permute-start(f32[4,160,128]{2,1,0:T(8,128)} %get-tuple-element.18), channel_id=1, source_target_pairs={{1,2},{2,1},{5,6},{6,5},{9,10},{10,9},{13,14},{14,13},{17,18},{18,... | collective-permute-start | bytes 983048 | tf_op jit(solution)/shard_map/ppermute | solution.py:325
  47.6 11.1 %copy-start.14 = (f32[2,256]{1,0:T(2,128)S(1)}, f32[2,256]{1,0:T(2,128)}, u32[]{:S(2)}) copy-start(f32[2,256]{1,0:T(2,128)} %param.19) | copy-start | bytes 6148
  47.6 11.7 %copy-start.1 = (f32[16,160,128]{2,1,0:T(8,128)S(1)}, f32[16,160,128]{2,1,0:T(8,128)}, u32[]{:S(2)}) copy-start(f32[16,160,128]{2,1,0:T(8,128)} %shard_map.114) | copy-start | bytes 3932164
  61.7 8.3 %copy-start.2 = (f32[327680]{0:T(1024)}, f32[327680]{0:T(1024)S(1)}, u32[]{:S(2)}) copy-start(f32[327680]{0:T(1024)S(1)} %scatter_fusion) | copy-start | bytes 3932164
  61.8 6.0 %collective-permute-start.8 = (f32[4,160,128]{2,1,0:T(8,128)S(1)}, f32[4,160,128]{2,1,0:T(8,128)S(1)}, u32[]{:S(2)}, u32[]{:S(2)}) collective-permute-start(f32[4,160,128]{2,1,0:T(8,128)S(1)} %get-tuple-element.27), channel_id=1, source_target_pairs={{0,1},{1,0},{2,3},{3,2},{4,5},{5,4},{6,7},{7,6},{8,9},{9,8},{10,11... | collective-permute-start | bytes 983048 | tf_op jit(solution)/shard_map/ppermute | solution.py:325
  61.9 8.1 %collective-permute-start.9 = (f32[4,160,128]{2,1,0:T(8,128)S(1)}, f32[4,160,128]{2,1,0:T(8,128)S(1)}, u32[]{:S(2)}, u32[]{:S(2)}) collective-permute-start(f32[4,160,128]{2,1,0:T(8,128)S(1)} %get-tuple-element.26), channel_id=1, source_target_pairs={{1,2},{2,1},{5,6},{6,5},{9,10},{10,9},{13,14},{14,13},{17,18},{18,... | collective-permute-start | bytes 983048 | tf_op jit(solution)/shard_map/ppermute | solution.py:325
  70.7 9.9 %copy-start.4 = (f32[16,160,128]{2,1,0:T(8,128)S(1)}, f32[16,160,128]{2,1,0:T(8,128)}, u32[]{:S(2)}) copy-start(f32[16,160,128]{2,1,0:T(8,128)} %get-tuple-element.21) | copy-start | bytes 3932164
  83.1 6.3 %collective-permute-start.10 = (f32[1280,128]{1,0:T(8,128)S(1)}, f32[1280,128]{1,0:T(8,128)S(1)}, u32[]{:S(2)}, u32[]{:S(2)}) collective-permute-start(f32[1280,128]{1,0:T(8,128)S(1)} %constant_dynamic-slice_fusion.1), channel_id=1, source_target_pairs={{0,4},{4,0},{8,12},{12,8},{1,5},{5,1},{9,13},{13,9},{2,6},{6,2},{1... | collective-permute-start | bytes 1966088 | tf_op jit(solution)/shard_map/ppermute | solution.py:310
  89.5 9.0 %collective-permute-start.11 = (f32[640,128]{1,0:T(8,128)S(1)}, f32[640,128]{1,0:T(8,128)S(1)}, u32[]{:S(2)}, u32[]{:S(2)}) collective-permute-start(f32[640,128]{1,0:T(8,128)S(1)} %constant_dynamic-slice_fusion), channel_id=1, source_target_pairs={{0,8},{4,12},{8,0},{12,4},{1,9},{5,13},{9,1},{13,5},{2,10},{6,14},... | collective-permute-start | bytes 983048 | tf_op jit(solution)/shard_map/ppermute | solution.py:310
  98.5 8.1 %collective-permute-start.12 = (f32[640,128]{1,0:T(8,128)S(1)}, f32[640,128]{1,0:T(8,128)S(1)}, u32[]{:S(2)}, u32[]{:S(2)}) collective-permute-start(f32[640,128]{1,0:T(8,128)S(1)} %add_multiply_fusion), channel_id=1, source_target_pairs={{0,8},{4,12},{8,0},{12,4},{1,9},{5,13},{9,1},{13,5},{2,10},{6,14},... | collective-permute-start | bytes 983048 | tf_op jit(solution)/shard_map/ppermute | solution.py:316
  106.6 3.9 %collective-permute-start.13 = (f32[1280,128]{1,0:T(8,128)S(1)}, f32[1280,128]{1,0:T(8,128)S(1)}, u32[]{:S(2)}, u32[]{:S(2)}) collective-permute-start(f32[1280,128]{1,0:T(8,128)S(1)} %maximum_select_fusion.1), channel_id=1, source_target_pairs={{0,4},{4,0},{8,12},{12,8},{1,5},{5,1},{9,13},{13,9},{2,6},{6,2},{1... | collective-permute-start | bytes 1966088 | tf_op jit(solution)/shard_map/ppermute | solution.py:316
  (6 other events, 6.1 us)

commit v21 on v16

--- a/solution.py
+++ b/solution.py
@@ -191,7 +191,7 @@
 
 def apply_final(parity, lo, mid, hi, b, g, c, old, receivers, valid, amount, rows=40):
     planes, height, depth = mid.shape
-    block = pick_block(planes)
+    block = 8 if planes % 8 == 0 else pick_block(planes)
     full, blk = specs(mid.shape, block)
     out = jax.ShapeDtypeStruct(mid.shape, jnp.float32)
     smem = pl.BlockSpec(memory_space=pltpu.SMEM)

time: 112 us -> 112 us (level)
  no operation moved by 1% of the time
where the time goes in v21:
time: 112 us
  Pallas kernels  40.4 us (36%)
  waiting for transfers between devices  29.2 us (26%)
  starting transfers between devices  24.8 us (22%)
  other arithmetic  10.7 us (10%)
  local copies, waits for them, and re-layouts  5.12 us (5%)
  between operations  1.73 us (2%)
    pallas_call x3, Pallas kernels, apply_step(): pl.pallas_call(kernel, grid=(planes // block,), in_specs=in_specs, out_sp...  30.3 us
    ppermute x5, starting transfers between devices, swap_halos(): lax.ppermute(sends[1], axis, second)  14.3 us
    pallas_call x1, Pallas kernels, apply_final(): pl.pallas_call(functools.partial(final_kernel, block=block, rows=rows), g...  10.1 us
    ppermute x2, waiting for transfers between devices, reduce_members(): rows = keep + lax.ppermute(give, axis, pairs)  9.44 us
    ppermute x2, waiting for transfers between devices, reduce_members(): other = lax.ppermute(rows, axis, pairs)  8.52 us
    ppermute x5, waiting for transfers between devices, swap_halos(): lax.ppermute(sends[0], axis, first)  5.93 us
    ppermute x2, starting transfers between devices, reduce_members(): rows = keep + lax.ppermute(give, axis, pairs)  5.81 us
    ppermute x5, waiting for transfers between devices, swap_halos(): lax.ppermute(sends[1], axis, second)  5.36 us
  transfers between devices with their start and end apart: 14, of which 8 were waited for; matrix products, arithmetic and copies ran while one was open for 4% of the time, Pallas kernels for 18%

profile of v21, /device:TPU:9, one launch (start us, length us, event | category | flops | bytes accessed | tf_op | source)
XLA Modules:
  0.0 111.9 jit_solution(10123211015326564502)
XLA Ops:
  0.7 1.3 %dynamic-slice_bitcast_fusion = (f32[4,160,128]{2,1,0:T(8,128)S(1)}, f32[4,160,128]{2,1,0:T(8,128)S(1)}) fusion(f32[1,16,160,128]{3,2,1,0:T(8,128)} %param.12, s32[]{:T(128)S(6)} %select_n.135, s32[]{:T(128)S(6)} %select_n.134), kind=kLoop, calls=%fused_computation.6 | loop fusion | bytes 1310728 | tf_op jit(solution)/shard_map/dynamic_slice | solution.py:329
  2.1 4.6 %collective-permute-start.3 = (f32[4,160,128]{2,1,0:T(8,128)S(1)}, f32[4,160,128]{2,1,0:T(8,128)S(1)}, u32[]{:S(2)}, u32[]{:S(2)}) collective-permute-start(f32[4,160,128]{2,1,0:T(8,128)S(1)} %get-tuple-element.30), channel_id=1, source_target_pairs={{1,2},{2,1},{5,6},{6,5},{9,10},{10,9},{13,14},{14,13},{17,18},{18,... | collective-permute-start | bytes 983048 | tf_op jit(solution)/shard_map/ppermute | solution.py:322
  6.8 1.9 %collective-permute-start.5 = (f32[4,160,128]{2,1,0:T(8,128)S(1)}, f32[4,160,128]{2,1,0:T(8,128)}, u32[]{:S(2)}, u32[]{:S(2)}) collective-permute-start(f32[4,160,128]{2,1,0:T(8,128)S(1)} %get-tuple-element.28), channel_id=1, source_target_pairs={{1,2},{2,1},{5,6},{6,5},{9,10},{10,9},{13,14},{14,13},{17,18},{18,... | collective-permute-start | bytes 983048 | tf_op jit(solution)/shard_map/ppermute | solution.py:322
  12.3 2.5 %collective-permute-start.1 = (f32[4,160,128]{2,1,0:T(8,128)S(1)}, f32[4,160,128]{2,1,0:T(8,128)S(1)}, u32[]{:S(2)}, u32[]{:S(2)}) collective-permute-start(f32[4,160,128]{2,1,0:T(8,128)S(1)} %get-tuple-element.32), channel_id=1, source_target_pairs={{1,2},{2,1},{5,6},{6,5},{9,10},{10,9},{13,14},{14,13},{17,18},{18,... | collective-permute-start | bytes 983048 | tf_op jit(solution)/shard_map/ppermute | solution.py:322
  14.8 2.9 %collective-permute-done.4.refs_4_ = f32[4,160,128]{2,1,0:T(8,128)} collective-permute-done((f32[4,160,128]{2,1,0:T(8,128)S(1)}, f32[4,160,128]{2,1,0:T(8,128)}, u32[]{:S(2)}, u32[]{:S(2)}) %collective-permute-start.4) | collective-permute-done | bytes 327712 | tf_op jit(solution)/shard_map/ppermute | solution.py:322
  17.7 3.2 %collective-permute-done.5.refs_6_ = f32[4,160,128]{2,1,0:T(8,128)} collective-permute-done((f32[4,160,128]{2,1,0:T(8,128)S(1)}, f32[4,160,128]{2,1,0:T(8,128)}, u32[]{:S(2)}, u32[]{:S(2)}) %collective-permute-start.5) | collective-permute-done | bytes 327712 | tf_op jit(solution)/shard_map/ppermute | solution.py:322
  20.9 12.2 %shard_map.113 = (f32[16,160,128]{2,1,0:T(8,128)}, f32[16,160,128]{2,1,0:T(8,128)}, f32[16,160,128]{2,1,0:T(8,128)}, f32[16,160,128]{2,1,0:T(8,128)}, f32[16,160...) custom-call(s32[1]{0:T(128)} %bitcast.refs_0_.parity_ref, ...), custom_call_target="tpu_custom_call" | custom-call | tf_op jit(solution)/shard_map/pallas_call | solution.py:266
  33.2 3.0 %collective-permute-start.7 = (f32[4,160,128]{2,1,0:T(8,128)}, f32[4,160,128]{2,1,0:T(8,128)S(1)}, u32[]{:S(2)}, u32[]{:S(2)}) collective-permute-start(f32[4,160,128]{2,1,0:T(8,128)} %get-tuple-element.18), channel_id=1, source_target_pairs={{1,2},{2,1},{5,6},{6,5},{9,10},{10,9},{13,14},{14,13},{17,18},{18,... | collective-permute-start | bytes 983048 | tf_op jit(solution)/shard_map/ppermute | solution.py:322
  38.7 8.0 %shard_map.114 = f32[16,160,128]{2,1,0:T(8,128)} custom-call(s32[1]{0:T(128)} %bitcast.refs_0_.parity_ref, f32[4,160,128]{2,1,0:T(8,128)} %copy-done.5, f32[16,160,128]{2,1,0:T(8,128)} %bitcast.43, f32[4,160,128]{2,1,0:T(8,128)} %copy-done.8, f32[16,160,128]{2,1,0:T(8,128)} %b_ref.1, f32[16,160,128]{2,1,0:T(8,128)} %get-tuple-element.12.refs_5_.g0_ref, ...), custom_call_target="tpu_custom_call" | custom-call | tf_op jit(solution)/shard_map/pallas_call | solution.py:266
  47.6 10.1 %shard_map.115 = (f32[16,160,128]{2,1,0:T(8,128)}, f32[16,160,128]{2,1,0:T(8,128)}, f32[256,128]{1,0:T(8,128)}) custom-call(s32[1]{0:T(128)} %bitcast.refs_0_.parity_ref, f32[4,160,128]{2,1,0:T(8,128)} %copy-done.9, f32[16,160,128]{2,1,0:T(8,128)} %get-tuple-element.17.refs_2_, f32[4,160,128]{2,1,0:T(8,128)} %copy-done.10, f32[16,160,128]{2,1,0:T(8,128)} %b_ref.1, ...), custom_call_target="tpu_custom_call" | custom-call | tf_op jit(solution)/shard_map/pallas_call | solution.py:266
  59.3 2.4 %scatter_fusion = f32[327680]{0:T(1024)S(1)} fusion(f32[327680]{0:T(1024)S(1)} %bitcast.33, s32[256]{0:T(256)S(1)} %get-tuple-element.38, f32[256]{0:T(256)S(1)} %broadcast_select_fusion), kind=kCustom, calls=%fused_computation | custom fusion | flops 256 | bytes 4096 | tf_op jit(solution)/shard_map/scatter-add | solution.py:334
  61.9 2.2 %collective-permute-start.9 = (f32[4,160,128]{2,1,0:T(8,128)S(1)}, f32[4,160,128]{2,1,0:T(8,128)S(1)}, u32[]{:S(2)}, u32[]{:S(2)}) collective-permute-start(f32[4,160,128]{2,1,0:T(8,128)S(1)} %get-tuple-element.26), channel_id=1, source_target_pairs={{1,2},{2,1},{5,6},{6,5},{9,10},{10,9},{13,14},{14,13},{17,18},{18,... | collective-permute-start | bytes 983048 | tf_op jit(solution)/shard_map/ppermute | solution.py:322
  64.7 3.0 %collective-permute-done.8.lo_ref = f32[4,160,128]{2,1,0:T(8,128)S(1)} collective-permute-done((f32[4,160,128]{2,1,0:T(8,128)S(1)}, f32[4,160,128]{2,1,0:T(8,128)S(1)}, u32[]{:S(2)}, u32[]{:S(2)}) %collective-permute-start.8) | collective-permute-done | bytes 327712 | tf_op jit(solution)/shard_map/ppermute | solution.py:322
  67.8 2.2 %collective-permute-done.9.hi_ref = f32[4,160,128]{2,1,0:T(8,128)S(1)} collective-permute-done((f32[4,160,128]{2,1,0:T(8,128)S(1)}, f32[4,160,128]{2,1,0:T(8,128)S(1)}, u32[]{:S(2)}, u32[]{:S(2)}) %collective-permute-start.9) | collective-permute-done | bytes 327712 | tf_op jit(solution)/shard_map/ppermute | solution.py:322
  70.7 10.1 %shard_map.116 = f32[16,160,128]{2,1,0:T(8,128)} custom-call(s32[1]{0:T(128)} %bitcast.refs_0_.parity_ref, f32[4,160,128]{2,1,0:T(8,128)} %copy-done.6, f32[16,160,128]{2,1,0:T(8,128)} %bitcast.35, f32[4,160,128]{2,1,0:T(8,128)} %copy-done.7, f32[16,160,128]{2,1,0:T(8,128)} %b_ref.1, f32[16,160,128]{2,1,0:T(8,128)} %get-tuple-element.12.refs_5_.g0_ref, ...), custom_call_target="tpu_custom_call" | custom-call | tf_op jit(solution)/shard_map/pallas_call | solution.py:198
  80.8 2.5 %multiply_add_fusion = f32[16,160,128]{2,1,0:T(8,128)S(1)} fusion(f32[16,160,128]{2,1,0:T(8,128)} %shard_map.116, f32[16,160,128]{2,1,0:T(8,128)S(1)} %copy-done.4, f32[16,160,128]{2,1,0:T(8,128)} %bitcast.36, f32[16,160,128]{2,1,0:T(8,128)} %get-tuple-element.20), kind=kLoop, calls=%fused_computation.2 | loop fusion | flops 983040 | bytes 6553600 | tf_op jit(solution)/shard_map/add | solution.py:404
  83.3 4.5 %collective-permute-start.10 = (f32[1280,128]{1,0:T(8,128)S(1)}, f32[1280,128]{1,0:T(8,128)S(1)}, u32[]{:S(2)}, u32[]{:S(2)}) collective-permute-start(f32[1280,128]{1,0:T(8,128)S(1)} %constant_dynamic-slice_fusion.1), channel_id=1, source_target_pairs={{0,4},{4,0},{8,12},{12,8},{1,5},{5,1},{9,13},{13,9},{2,6},{6,2},{1... | collective-permute-start | bytes 1966088 | tf_op jit(solution)/shard_map/ppermute | solution.py:307
  87.8 1.7 %collective-permute-done.10 = f32[1280,128]{1,0:T(8,128)S(1)} collective-permute-done((f32[1280,128]{1,0:T(8,128)S(1)}, f32[1280,128]{1,0:T(8,128)S(1)}, u32[]{:S(2)}, u32[]{:S(2)}) %collective-permute-start.10) | collective-permute-done | bytes 655392 | tf_op jit(solution)/shard_map/ppermute | solution.py:307
  89.7 1.3 %collective-permute-start.11 = (f32[640,128]{1,0:T(8,128)S(1)}, f32[640,128]{1,0:T(8,128)S(1)}, u32[]{:S(2)}, u32[]{:S(2)}) collective-permute-start(f32[640,128]{1,0:T(8,128)S(1)} %constant_dynamic-slice_fusion), channel_id=1, source_target_pairs={{0,8},{4,12},{8,0},{12,4},{1,9},{5,13},{9,1},{13,5},{2,10},{6,14},... | collective-permute-start | bytes 983048 | tf_op jit(solution)/shard_map/ppermute | solution.py:307
  91.0 7.7 %collective-permute-done.11 = f32[640,128]{1,0:T(8,128)S(1)} collective-permute-done((f32[640,128]{1,0:T(8,128)S(1)}, f32[640,128]{1,0:T(8,128)S(1)}, u32[]{:S(2)}, u32[]{:S(2)}) %collective-permute-start.11) | collective-permute-done | bytes 327712 | tf_op jit(solution)/shard_map/ppermute | solution.py:307
  98.7 1.3 %collective-permute-start.12 = (f32[640,128]{1,0:T(8,128)S(1)}, f32[640,128]{1,0:T(8,128)S(1)}, u32[]{:S(2)}, u32[]{:S(2)}) collective-permute-start(f32[640,128]{1,0:T(8,128)S(1)} %add_multiply_fusion), channel_id=1, source_target_pairs={{0,8},{4,12},{8,0},{12,4},{1,9},{5,13},{9,1},{13,5},{2,10},{6,14},... | collective-permute-start | bytes 983048 | tf_op jit(solution)/shard_map/ppermute | solution.py:313
  100.0 6.8 %collective-permute-done.12 = f32[640,128]{1,0:T(8,128)S(1)} collective-permute-done((f32[640,128]{1,0:T(8,128)S(1)}, f32[640,128]{1,0:T(8,128)S(1)}, u32[]{:S(2)}, u32[]{:S(2)}) %collective-permute-start.12) | collective-permute-done | bytes 327712 | tf_op jit(solution)/shard_map/ppermute | solution.py:313
  106.8 2.2 %collective-permute-start.13 = (f32[1280,128]{1,0:T(8,128)S(1)}, f32[1280,128]{1,0:T(8,128)S(1)}, u32[]{:S(2)}, u32[]{:S(2)}) collective-permute-start(f32[1280,128]{1,0:T(8,128)S(1)} %maximum_select_fusion.1), channel_id=1, source_target_pairs={{0,4},{4,0},{8,12},{12,8},{1,5},{5,1},{9,13},{13,9},{2,6},{6,2},{1... | collective-permute-start | bytes 1966088 | tf_op jit(solution)/shard_map/ppermute | solution.py:313
  109.0 1.7 %collective-permute-done.13 = f32[1280,128]{1,0:T(8,128)S(1)} collective-permute-done((f32[1280,128]{1,0:T(8,128)S(1)}, f32[1280,128]{1,0:T(8,128)S(1)}, u32[]{:S(2)}, u32[]{:S(2)}) %collective-permute-start.13) | collective-permute-done | bytes 655392 | tf_op jit(solution)/shard_map/ppermute | solution.py:313
  (64 shorter events, 10.9 us)
Async XLA Ops:
  0.6 6.0 %copy-start = (f32[16,160,128]{2,1,0:T(8,128)S(1)}, f32[16,160,128]{2,1,0:T(8,128)}, u32[]{:S(2)}) copy-start(f32[16,160,128]{2,1,0:T(8,128)} %b_ref.1) | copy-start | bytes 3932164
  0.7 8.1 %copy-start.3 = (f32[1,16,160,128]{3,2,1,0:T(8,128)S(1)}, f32[1,16,160,128]{3,2,1,0:T(8,128)}, u32[]{:S(2)}) copy-start(f32[1,16,160,128]{3,2,1,0:T(8,128)} %param.14) | copy-start | bytes 3932164
  2.0 10.4 %collective-permute-start.2 = (f32[4,160,128]{2,1,0:T(8,128)S(1)}, f32[4,160,128]{2,1,0:T(8,128)S(1)}, u32[]{:S(2)}, u32[]{:S(2)}) collective-permute-start(f32[4,160,128]{2,1,0:T(8,128)S(1)} %get-tuple-element.31), channel_id=1, source_target_pairs={{0,1},{1,0},{2,3},{3,2},{4,5},{5,4},{6,7},{7,6},{8,9},{9,8},{10,11... | collective-permute-start | bytes 983048 | tf_op jit(solution)/shard_map/ppermute | solution.py:322
  2.0 8.4 %copy-start.13 = (s32[256]{0:T(256)S(1)}, s32[256]{0:T(256)}, u32[]{:S(2)}) copy-start(s32[256]{0:T(256)} %param.18) | copy-start | bytes 3076
  2.0 9.7 %copy-start.15 = (f32[2]{0:T(128)S(1)}, f32[2]{0:T(128)}, u32[]{:S(2)}) copy-start(f32[2]{0:T(128)} %param.16) | copy-start | bytes 28
  2.1 12.8 %collective-permute-start.3 = (f32[4,160,128]{2,1,0:T(8,128)S(1)}, f32[4,160,128]{2,1,0:T(8,128)S(1)}, u32[]{:S(2)}, u32[]{:S(2)}) collective-permute-start(f32[4,160,128]{2,1,0:T(8,128)S(1)} %get-tuple-element.30), channel_id=1, source_target_pairs={{1,2},{2,1},{5,6},{6,5},{9,10},{10,9},{13,14},{14,13},{17,18},{18,... | collective-permute-start | bytes 983048 | tf_op jit(solution)/shard_map/ppermute | solution.py:322
  6.7 11.0 %collective-permute-start.4 = (f32[4,160,128]{2,1,0:T(8,128)S(1)}, f32[4,160,128]{2,1,0:T(8,128)}, u32[]{:S(2)}, u32[]{:S(2)}) collective-permute-start(f32[4,160,128]{2,1,0:T(8,128)S(1)} %get-tuple-element.29), channel_id=1, source_target_pairs={{0,1},{1,0},{2,3},{3,2},{4,5},{5,4},{6,7},{7,6},{8,9},{9,8},{10,11... | collective-permute-start | bytes 983048 | tf_op jit(solution)/shard_map/ppermute | solution.py:322
  6.8 14.1 %collective-permute-start.5 = (f32[4,160,128]{2,1,0:T(8,128)S(1)}, f32[4,160,128]{2,1,0:T(8,128)}, u32[]{:S(2)}, u32[]{:S(2)}) collective-permute-start(f32[4,160,128]{2,1,0:T(8,128)S(1)} %get-tuple-element.28), channel_id=1, source_target_pairs={{1,2},{2,1},{5,6},{6,5},{9,10},{10,9},{13,14},{14,13},{17,18},{18,... | collective-permute-start | bytes 983048 | tf_op jit(solution)/shard_map/ppermute | solution.py:322
  8.8 29.0 %collective-permute-start = (f32[4,160,128]{2,1,0:T(8,128)S(1)}, f32[4,160,128]{2,1,0:T(8,128)S(1)}, u32[]{:S(2)}, u32[]{:S(2)}) collective-permute-start(f32[4,160,128]{2,1,0:T(8,128)S(1)} %get-tuple-element.33), channel_id=1, source_target_pairs={{0,1},{1,0},{2,3},{3,2},{4,5},{5,4},{6,7},{7,6},{8,9},{9,8},{10,11... | collective-permute-start | bytes 983048 | tf_op jit(solution)/shard_map/ppermute | solution.py:322
  12.3 8.5 %copy-start.11 = (f32[4,160,128]{2,1,0:T(8,128)}, f32[4,160,128]{2,1,0:T(8,128)S(1)}, u32[]{:S(2)}) copy-start(f32[4,160,128]{2,1,0:T(8,128)S(1)} %collective-permute-done.2.refs_1_) | copy-start | bytes 983044
  12.3 25.5 %collective-permute-start.1 = (f32[4,160,128]{2,1,0:T(8,128)S(1)}, f32[4,160,128]{2,1,0:T(8,128)S(1)}, u32[]{:S(2)}, u32[]{:S(2)}) collective-permute-start(f32[4,160,128]{2,1,0:T(8,128)S(1)} %get-tuple-element.32), channel_id=1, source_target_pairs={{1,2},{2,1},{5,6},{6,5},{9,10},{10,9},{13,14},{14,13},{17,18},{18,... | collective-permute-start | bytes 983048 | tf_op jit(solution)/shard_map/ppermute | solution.py:322
  14.8 6.1 %copy-start.12 = (f32[4,160,128]{2,1,0:T(8,128)}, f32[4,160,128]{2,1,0:T(8,128)S(1)}, u32[]{:S(2)}) copy-start(f32[4,160,128]{2,1,0:T(8,128)S(1)} %collective-permute-done.3.refs_3_) | copy-start | bytes 983044
  33.1 13.5 %collective-permute-start.6 = (f32[4,160,128]{2,1,0:T(8,128)}, f32[4,160,128]{2,1,0:T(8,128)S(1)}, u32[]{:S(2)}, u32[]{:S(2)}) collective-permute-start(f32[4,160,128]{2,1,0:T(8,128)} %get-tuple-element.16), channel_id=1, source_target_pairs={{0,1},{1,0},{2,3},{3,2},{4,5},{5,4},{6,7},{7,6},{8,9},{9,8},{10,11... | collective-permute-start | bytes 983048 | tf_op jit(solution)/shard_map/ppermute | solution.py:322
  33.2 13.5 %collective-permute-start.7 = (f32[4,160,128]{2,1,0:T(8,128)}, f32[4,160,128]{2,1,0:T(8,128)S(1)}, u32[]{:S(2)}, u32[]{:S(2)}) collective-permute-start(f32[4,160,128]{2,1,0:T(8,128)} %get-tuple-element.18), channel_id=1, source_target_pairs={{1,2},{2,1},{5,6},{6,5},{9,10},{10,9},{13,14},{14,13},{17,18},{18,... | collective-permute-start | bytes 983048 | tf_op jit(solution)/shard_map/ppermute | solution.py:322
  47.6 11.1 %copy-start.14 = (f32[2,256]{1,0:T(2,128)S(1)}, f32[2,256]{1,0:T(2,128)}, u32[]{:S(2)}) copy-start(f32[2,256]{1,0:T(2,128)} %param.19) | copy-start | bytes 6148
  47.6 11.7 %copy-start.1 = (f32[16,160,128]{2,1,0:T(8,128)S(1)}, f32[16,160,128]{2,1,0:T(8,128)}, u32[]{:S(2)}) copy-start(f32[16,160,128]{2,1,0:T(8,128)} %shard_map.114) | copy-start | bytes 3932164
  61.7 8.3 %copy-start.2 = (f32[327680]{0:T(1024)}, f32[327680]{0:T(1024)S(1)}, u32[]{:S(2)}) copy-start(f32[327680]{0:T(1024)S(1)} %scatter_fusion) | copy-start | bytes 3932164
  61.8 6.0 %collective-permute-start.8 = (f32[4,160,128]{2,1,0:T(8,128)S(1)}, f32[4,160,128]{2,1,0:T(8,128)S(1)}, u32[]{:S(2)}, u32[]{:S(2)}) collective-permute-start(f32[4,160,128]{2,1,0:T(8,128)S(1)} %get-tuple-element.27), channel_id=1, source_target_pairs={{0,1},{1,0},{2,3},{3,2},{4,5},{5,4},{6,7},{7,6},{8,9},{9,8},{10,11... | collective-permute-start | bytes 983048 | tf_op jit(solution)/shard_map/ppermute | solution.py:322
  61.9 8.1 %collective-permute-start.9 = (f32[4,160,128]{2,1,0:T(8,128)S(1)}, f32[4,160,128]{2,1,0:T(8,128)S(1)}, u32[]{:S(2)}, u32[]{:S(2)}) collective-permute-start(f32[4,160,128]{2,1,0:T(8,128)S(1)} %get-tuple-element.26), channel_id=1, source_target_pairs={{1,2},{2,1},{5,6},{6,5},{9,10},{10,9},{13,14},{14,13},{17,18},{18,... | collective-permute-start | bytes 983048 | tf_op jit(solution)/shard_map/ppermute | solution.py:322
  70.7 10.1 %copy-start.4 = (f32[16,160,128]{2,1,0:T(8,128)S(1)}, f32[16,160,128]{2,1,0:T(8,128)}, u32[]{:S(2)}) copy-start(f32[16,160,128]{2,1,0:T(8,128)} %get-tuple-element.21) | copy-start | bytes 3932164
  83.3 6.3 %collective-permute-start.10 = (f32[1280,128]{1,0:T(8,128)S(1)}, f32[1280,128]{1,0:T(8,128)S(1)}, u32[]{:S(2)}, u32[]{:S(2)}) collective-permute-start(f32[1280,128]{1,0:T(8,128)S(1)} %constant_dynamic-slice_fusion.1), channel_id=1, source_target_pairs={{0,4},{4,0},{8,12},{12,8},{1,5},{5,1},{9,13},{13,9},{2,6},{6,2},{1... | collective-permute-start | bytes 1966088 | tf_op jit(solution)/shard_map/ppermute | solution.py:307
  89.7 9.0 %collective-permute-start.11 = (f32[640,128]{1,0:T(8,128)S(1)}, f32[640,128]{1,0:T(8,128)S(1)}, u32[]{:S(2)}, u32[]{:S(2)}) collective-permute-start(f32[640,128]{1,0:T(8,128)S(1)} %constant_dynamic-slice_fusion), channel_id=1, source_target_pairs={{0,8},{4,12},{8,0},{12,4},{1,9},{5,13},{9,1},{13,5},{2,10},{6,14},... | collective-permute-start | bytes 983048 | tf_op jit(solution)/shard_map/ppermute | solution.py:307
  98.7 8.1 %collective-permute-start.12 = (f32[640,128]{1,0:T(8,128)S(1)}, f32[640,128]{1,0:T(8,128)S(1)}, u32[]{:S(2)}, u32[]{:S(2)}) collective-permute-start(f32[640,128]{1,0:T(8,128)S(1)} %add_multiply_fusion), channel_id=1, source_target_pairs={{0,8},{4,12},{8,0},{12,4},{1,9},{5,13},{9,1},{13,5},{2,10},{6,14},... | collective-permute-start | bytes 983048 | tf_op jit(solution)/shard_map/ppermute | solution.py:313
  106.8 3.9 %collective-permute-start.13 = (f32[1280,128]{1,0:T(8,128)S(1)}, f32[1280,128]{1,0:T(8,128)S(1)}, u32[]{:S(2)}, u32[]{:S(2)}) collective-permute-start(f32[1280,128]{1,0:T(8,128)S(1)} %maximum_select_fusion.1), channel_id=1, source_target_pairs={{0,4},{4,0},{8,12},{12,8},{1,5},{5,1},{9,13},{13,9},{2,6},{6,2},{1... | collective-permute-start | bytes 1966088 | tf_op jit(solution)/shard_map/ppermute | solution.py:313
  (6 other events, 6.1 us)
